TPU v7x, 32 devices: a whole 2x2x4 slice. The times are simulated.
32 devices in a mesh: grid: 8 (over z, y), band: 4 (over x, core).
Axes of the slice: x: 2, y: 2, z: 4, core: 2. Of those that a mesh axis runs over, the one named last changes fastest.
Arguments:
- orbitals: float32 [2048, 512], P('grid', 'band'), may hold values from -30 to 30
- potential: float32 [2048], P('grid'), may hold values from -1 to 1
- fitted: bfloat16 [512, 2048], P('band', 'grid'), may hold values from -6 to 6
- points: int32 [512], P('grid'), may hold values from -1 to 255, as said below
Outputs:
- updated: float32 [2048, 512], P('grid', 'band')
Inputs may be any that keep to these rules, and one draw needn't show every extreme that they name: Each block of 64 slots of one index of grid holds distinct grid points in its first slots and -1 in the rest; the numbers of filled slots of blocks 2i and 2i + 1 sum to 64, so that 256 slots are filled in all, and some block is full.
All inputs are finite; a program needn't handle non-finite values.
Results may differ from a plain program's by a relative error of at most 0.024.
Values may be sent and summed in bfloat16 or wider, within the bound.
No kernel may reach another device: no remote copies, remote signals or barrier semaphores. Data moves between devices by JAX's collectives and lax.ppermute only.
A program may use at most 64 MiB of HBM per device.

v0:
```python
import jax
import jax.numpy as jnp
from jax import lax
from jax.sharding import PartitionSpec as P

ITERS = 2


def body(orbitals, potential, fitted, points):
    rows = orbitals.shape[0]
    block_width = orbitals.shape[1]
    nbands = lax.axis_size("band")
    ngroups = lax.axis_size("grid")
    total_orbitals = block_width * nbands
    valid_mask = points >= 0
    safe_idx = jnp.where(valid_mask, points, 0)
    psi = orbitals
    for step in range(ITERS):
        orbital_block = psi.astype(jnp.bfloat16)
        selected_points = jnp.where(
            valid_mask[:, None], orbital_block[safe_idx], jnp.zeros((), jnp.bfloat16)
        )
        collocation_matrix = lax.all_gather(selected_points, "grid", axis=0, tiled=True)
        product = lax.dot_general(
            collocation_matrix,
            orbital_block,
            (((1,), (1,)), ((), ())),
            preferred_element_type=jnp.float32,
        )
        proj = lax.psum_scatter(
            (product / total_orbitals).astype(jnp.bfloat16), "band", scatter_dimension=0, tiled=True
        ).astype(jnp.float32)
        tile_blocks = (fitted.astype(jnp.float32) * proj).astype(jnp.bfloat16)
        orbitals_at_slots = lax.all_to_all(
            collocation_matrix, "band", split_axis=0, concat_axis=1, tiled=True
        )
        partial_value = lax.dot_general(
            tile_blocks,
            orbitals_at_slots,
            (((0,), (0,)), ((), ())),
            preferred_element_type=jnp.float32,
        )
        applied = lax.psum_scatter(
            partial_value.astype(jnp.bfloat16), "band", scatter_dimension=1, tiled=True
        ).astype(jnp.float32)
        fresh = psi - 0.25 * (potential[:, None] * psi - applied)
        squares = lax.psum(jnp.sum(fresh * fresh, axis=0), "grid")
        psi = fresh * lax.rsqrt(squares / (rows * ngroups) + 1e-06)
    return psi


def solution(mesh):
    in_specs = (P("grid", "band"), P("grid"), P("band", "grid"), P("grid"))
    out_specs = P("grid", "band")
    return jax.shard_map(body, mesh=mesh, in_specs=in_specs, out_specs=out_specs, check_vma=False)
```

profile of v0, /device:TPU:0, one launch (start us, length us, event | category | flops | bytes accessed | tf_op | source)
XLA Modules:
  0.0 209.6 jit_solution(11900437040815080563)
XLA Ops:
  6.5 0.0 copy-start.3
  6.5 0.0 reduce-scatter.9.cloned.1.call-start
  6.5 0.7 compare_select_fusion
  7.3 0.0 copy-done.3
  7.3 0.9 convert_element_type.41
  8.2 0.6 gather_fusion
  8.8 0.1 broadcast_select_fusion.1
  8.9 32.3 %all_gather.6 = bf16[512,128]{1,0:T(8,128)(2,1)S(1)} all-gather(bf16[64,128]{1,0:T(8,128)(2,1)S(1)} %broadcast_select_fusion.1), channel_id=1, replica_groups=mesh['grid'=8,'band'=4] {'grid'}, dimensions={0}, use_global_device_ids=true | all-gather | bytes 147456 | tf_op jit(solution)/shard_map/all_gather | solution.py:23
  41.2 0.9 fusion
  42.1 0.0 reduce-scatter.9.cloned.1.call-update
  42.2 0.0 reduce-scatter.13.cloned.1.call-start
  42.2 0.1 copy.7
  42.4 0.0 copy-start.1
  42.4 7.3 %all_to_all.38 = bf16[4,128,128]{1,2,0:T(8,128)(2,1)S(1)} all-to-all(bf16[4,128,128]{1,2,0:T(8,128)(2,1)S(1)} %copy.7), channel_id=1, replica_groups=mesh['grid'=8,'band'=4] {'band'}, dimensions={0} | all-to-all | bytes 262144 | tf_op jit(solution)/shard_map/all_to_all | solution.py:34
  49.7 13.6 %reduce-scatter.9.cloned.1.call-done = bf16[128,256]{1,0:T(8,128)(2,1)} async-done(((bf16[512,256]{1,0:T(8,128)(2,1)}), bf16[128,256]{1,0:T(8,128)(2,1)}) %reduce-scatter.9.cloned.1.call-update) | async-done | bytes 65552 | tf_op jit(solution)/shard_map/reduce_scatter | solution.py:30
  63.3 0.0 copy-done.1
  63.3 1.1 convolution_convert_fusion.1
  64.4 0.8 copy.9
  65.2 0.0 reduce-scatter.13.cloned.1.call-update
  65.2 0.0 copy-start
  65.2 0.0 reduce-scatter.11.cloned.1.call-start
  65.3 20.7 %reduce-scatter.13.cloned.1.call-done = bf16[128,256]{1,0:T(8,128)(2,1)} async-done(((bf16[512,256]{1,0:T(8,128)(2,1)}), bf16[128,256]{1,0:T(8,128)(2,1)}) %reduce-scatter.13.cloned.1.call-update) | async-done | bytes 65552
  86.0 0.0 copy-start.2
  86.0 1.0 copy.10
  86.9 0.0 copy-done
  86.9 0.0 copy-done.2
  86.9 0.1 multiply_reduce_fusion.1
  87.1 21.4 %psum.14 = f32[128]{0:T(128)S(1)} all-reduce(f32[128]{0:T(128)S(1)} %multiply_reduce_fusion.1), channel_id=1, replica_groups=mesh['grid'=8,'band'=4] {'grid'}, use_global_device_ids=true, to_apply=%region_3.4 | all-reduce | flops 128 | bytes 1024 | tf_op jit(solution)/shard_map/psum | solution.py:47
  108.4 0.1 multiply_convert_fusion
  108.5 0.6 gather_fusion.1
  109.2 0.1 broadcast_select_fusion
  109.3 30.5 %all_gather.7 = bf16[512,128]{1,0:T(8,128)(2,1)S(1)} all-gather(bf16[64,128]{1,0:T(8,128)(2,1)S(1)} %broadcast_select_fusion), channel_id=1, replica_groups=mesh['grid'=8,'band'=4] {'grid'}, dimensions={0}, use_global_device_ids=true | all-gather | bytes 147456 | tf_op jit(solution)/shard_map/all_gather | solution.py:23
  139.8 0.9 fusion.1
  140.7 0.0 reduce-scatter.11.cloned.1.call-update
  140.7 0.0 reduce-scatter.15.cloned.1.call-start
  140.8 0.1 copy.8
  140.9 7.0 %all_to_all.39 = bf16[4,128,128]{1,2,0:T(8,128)(2,1)S(1)} all-to-all(bf16[4,128,128]{1,2,0:T(8,128)(2,1)S(1)} %copy.8), channel_id=1, replica_groups=mesh['grid'=8,'band'=4] {'band'}, dimensions={0} | all-to-all | bytes 262144 | tf_op jit(solution)/shard_map/all_to_all | solution.py:34
  147.9 9.3 %reduce-scatter.11.cloned.1.call-done = bf16[128,256]{1,0:T(8,128)(2,1)} async-done(((bf16[512,256]{1,0:T(8,128)(2,1)}), bf16[128,256]{1,0:T(8,128)(2,1)}) %reduce-scatter.11.cloned.1.call-update) | async-done | bytes 65552 | tf_op jit(solution)/shard_map/reduce_scatter | solution.py:30
  157.2 1.1 convolution_convert_fusion
  158.3 0.8 copy.11
  159.1 0.0 reduce-scatter.15.cloned.1.call-update
  159.2 20.6 %reduce-scatter.15.cloned.1.call-done = bf16[128,256]{1,0:T(8,128)(2,1)} async-done(((bf16[512,256]{1,0:T(8,128)(2,1)}), bf16[128,256]{1,0:T(8,128)(2,1)}) %reduce-scatter.15.cloned.1.call-update) | async-done | bytes 65552
  179.8 0.9 copy.12
  180.7 0.1 multiply_reduce_fusion
  180.9 21.4 %psum.15 = f32[128]{0:T(128)S(1)} all-reduce(f32[128]{0:T(128)S(1)} %multiply_reduce_fusion), channel_id=1, replica_groups=mesh['grid'=8,'band'=4] {'grid'}, use_global_device_ids=true, to_apply=%region_7.8 | all-reduce | flops 128 | bytes 1024 | tf_op jit(solution)/shard_map/psum | solution.py:47
  202.2 0.8 broadcast_multiply_fusion
  (4 shorter events, 0.0 us)
Async XLA Ops:
  6.5 0.7 copy-start.3
  6.5 56.7 %reduce-scatter.9.cloned.1.call-start = ((), (), s32[]{:S(2)}) async-start(), calls=%async_computation.6 | async-start | bytes 327680 | tf_op jit(solution)/shard_map/reduce_scatter | solution.py:30
  42.2 43.8 %reduce-scatter.13.cloned.1.call-start = ((), (), s32[]{:S(2)}) async-start(), calls=%async_computation.8 | async-start | bytes 327680
  42.4 20.9 %copy-start.1 = (bf16[128,256]{1,0:T(8,128)(2,1)S(1)}, bf16[128,256]{1,0:T(8,128)(2,1)}, u32[]{:S(2)}) copy-start(bf16[128,256]{1,0:T(8,128)(2,1)} %param.6) | copy-start | bytes 196612
  65.2 21.7 %copy-start = (f32[256,128]{1,0:T(8,128)S(1)}, f32[256,128]{1,0:T(8,128)}, u32[]{:S(2)}) copy-start(f32[256,128]{1,0:T(8,128)} %param.4) | copy-start | bytes 393220
  65.2 92.0 %reduce-scatter.11.cloned.1.call-start = ((), (), s32[]{:S(2)}) async-start(), calls=%async_computation.7 | async-start | bytes 327680 | tf_op jit(solution)/shard_map/reduce_scatter | solution.py:30
  86.0 1.0 copy-start.2
  140.7 39.1 %reduce-scatter.15.cloned.1.call-start = ((), (), s32[]{:S(2)}) async-start(), calls=%async_computation.9 | async-start | bytes 327680
Sparse Core Ops, SparseCore 0:
  42.3 20.9 reduce-scatter.8
  65.9 20.0 reduce-scatter.12
  140.8 16.3 reduce-scatter.10
  159.7 20.0 reduce-scatter.14
where the time goes:
time: 210 us
  blocking collectives  120 us (57%)
  waiting for transfers between devices  64.2 us (31%)
  between operations  13.2 us (6%)
  local copies, waits for them, and re-layouts  5.13 us (2%)
  matrix products  4.01 us (2%)
  other arithmetic  2.98 us (1%)
    all_gather x2, blocking collectives, body(): lax.all_gather(selected_points, 'grid', axis=0, tiled=True)  62.8 us
    psum x2, blocking collectives, body(): squares = lax.psum(jnp.sum(fresh * fresh, axis=0), 'grid')  42.7 us
    unnamed x6, waiting for transfers between devices  41.3 us
    reduce_scatter x2, waiting for transfers between devices, body(): lax.psum_scatter((product / total_orbitals).astype(jnp.bfloat16), 'band',...  22.9 us
    all_to_all x2, blocking collectives, body(): lax.all_to_all(collocation_matrix, 'band', split_axis=0, concat_axis=1, t...  14.3 us
  transfers between devices with their start and end apart: 4, of which 4 were waited for; matrix products, arithmetic and copies ran while one was open for 0% of the time, Pallas kernels for 0%

commit v1 on v0

--- a/solution.py
+++ b/solution.py
@@ -6,7 +6,69 @@
 ITERS = 2
 
 
+def grid_gather(x):
+    ngroups = lax.axis_size("grid")
+    sent = jnp.broadcast_to(x[None], (ngroups,) + x.shape)
+    got = lax.all_to_all(sent, "grid", 0, 0, tiled=True)
+    return got.reshape((ngroups * x.shape[0],) + x.shape[1:])
+
+
+def band_gather(x, axis):
+    return lax.all_gather(x, "band", axis=axis, tiled=True)
+
+
 def body(orbitals, potential, fitted, points):
+    if lax.axis_size("grid") > 8:
+        return body_spread(orbitals, potential, fitted, points)
+    rows = orbitals.shape[0]
+    block_width = orbitals.shape[1]
+    nbands = lax.axis_size("band")
+    ngroups = lax.axis_size("grid")
+    band = lax.axis_index("band")
+    total_orbitals = block_width * nbands
+    valid_mask = points >= 0
+    safe_idx = jnp.where(valid_mask, points, 0)
+    psi = band_gather(orbitals, 1)
+    fitted_all = band_gather(fitted, 0).astype(jnp.float32)
+    pot = potential[:, None]
+    scale = None
+    for step in range(ITERS):
+        if scale is None:
+            orbital_block = psi.astype(jnp.bfloat16)
+            selected = jnp.where(valid_mask[:, None], orbital_block[safe_idx], jnp.zeros((), jnp.bfloat16))
+            coll = grid_gather(selected)
+        else:
+            at_slots = jnp.where(valid_mask[:, None], psi[safe_idx], 0.0)
+            got = grid_gather(jnp.concatenate([at_slots, sq[None]], 0)).reshape(ngroups, -1, total_orbitals)
+            total = jnp.sum(got[:, -1], axis=0)
+            scale = lax.rsqrt(total / (rows * ngroups) + 1e-06)
+            psi = psi * scale
+            orbital_block = psi.astype(jnp.bfloat16)
+            coll = (got[:, :-1] * scale).astype(jnp.bfloat16).reshape(-1, total_orbitals)
+        proj = None
+        for k in range(nbands):
+            part = lax.dot_general(
+                coll[:, k * block_width:(k + 1) * block_width],
+                orbital_block[:, k * block_width:(k + 1) * block_width],
+                (((1,), (1,)), ((), ())),
+                preferred_element_type=jnp.float32,
+            )
+            part = (part / total_orbitals).astype(jnp.bfloat16).astype(jnp.float32)
+            proj = part if proj is None else proj + part
+        tile_blocks = (fitted_all * proj).astype(jnp.bfloat16)
+        applied = lax.dot_general(
+            tile_blocks, coll, (((0,), (0,)), ((), ())), preferred_element_type=jnp.float32
+        )
+        psi = psi - 0.25 * (pot * psi - applied)
+        sq = jnp.sum(psi * psi, axis=0)
+        scale = sq
+    mine = lax.dynamic_slice_in_dim(psi, band * block_width, block_width, axis=1)
+    mine_sq = lax.dynamic_slice_in_dim(sq, band * block_width, block_width)
+    total = jnp.sum(grid_gather(mine_sq[None]), axis=0)
+    return mine * lax.rsqrt(total / (rows * ngroups) + 1e-06)
+
+
+def body_spread(orbitals, potential, fitted, points):
     rows = orbitals.shape[0]
     block_width = orbitals.shape[1]
     nbands = lax.axis_size("band")

time: 210 us -> 84.4 us (0.40)
  blocking collectives: 120 us -> 24.5 us
  waiting for transfers between devices: 64.2 us -> 38 us
  between operations: 13.2 us -> 0.12 us
  starting transfers between devices: 0.13 us -> 9.45 us
    all_gather x2, blocking collectives: 62.8 us -> 14.6 us  [band_gather(): return lax.all_gather(x, 'band', axis=axis, tiled=True)]
    psum x2 -> x0, blocking collectives: 42.7 us -> none  [body(): squares = lax.psum(jnp.sum(fresh * fresh, axis=0), 'grid')]
    unnamed x6 -> x0, waiting for transfers between devices: 41.3 us -> none
    all_to_all x0 -> x2, waiting for transfers between devices: none -> 38 us  [grid_gather(): got = lax.all_to_all(sent, 'grid', 0, 0, tiled=True)]
    reduce_scatter x2 -> x0, waiting for transfers between devices: 22.9 us -> none  [body(): lax.psum_scatter((product / total_orbitals).astype(jnp.bfloat16), 'band',...]
    all_to_all x0 -> x2, starting transfers between devices: none -> 9.45 us  [grid_gather(): got = lax.all_to_all(sent, 'grid', 0, 0, tiled=True)]
    all_to_all x2 -> x1, blocking collectives: 14.3 us -> 9.89 us  [grid_gather(): got = lax.all_to_all(sent, 'grid', 0, 0, tiled=True)]
    unnamed x12 -> x4, local copies, waits for them, and re-layouts: 3.59 us -> 0.01 us
  transfers between devices with their start and end apart: 4 -> 2, of which waited for: 4 -> 2; matrix products, arithmetic and copies ran while one was open for 0% -> 0% of each run, Pallas kernels for 0% -> 0%
where the time goes in v1:
time: 84.4 us; the launch traced here: 84 us
  waiting for transfers between devices  38 us (45%)
  blocking collectives  24.5 us (29%)
  starting transfers between devices  9.45 us (11%)
  matrix products  5.2 us (6%)
  local copies, waits for them, and re-layouts  3.44 us (4%)
  other arithmetic  3.33 us (4%)
    all_to_all x2, waiting for transfers between devices, grid_gather(): got = lax.all_to_all(sent, 'grid', 0, 0, tiled=True)  38 us
    all_gather x2, blocking collectives, band_gather(): return lax.all_gather(x, 'band', axis=axis, tiled=True)  14.6 us
    all_to_all x1, blocking collectives, grid_gather(): got = lax.all_to_all(sent, 'grid', 0, 0, tiled=True)  9.89 us
    all_to_all x2, starting transfers between devices, grid_gather(): got = lax.all_to_all(sent, 'grid', 0, 0, tiled=True)  9.45 us
    dot_general x2, matrix products, body(): lax.dot_general(tile_blocks, coll, (((0,), (0,)), ((), ())), preferred_el...  3.05 us
    dot_general x6, matrix products, body(): lax.dot_general(coll[:, k * block_width:(k + 1) * block_width], orbital_b...  2.15 us
    broadcast_in_dim x3, local copies, waits for them, and re-layouts, grid_gather(): sent = jnp.broadcast_to(x[None], (ngroups,) + x.shape)  1.99 us
  transfers between devices with their start and end apart: 2, of which 2 were waited for; matrix products, arithmetic and copies ran while one was open for 0% of the time, Pallas kernels for 0%

profile of v1, /device:TPU:0, one launch (start us, length us, event | category | flops | bytes accessed | tf_op | source)
XLA Modules:
  0.0 84.0 jit_solution(17447484352490558708)
XLA Ops:
  0.0 0.7 compare_select_fusion
  0.7 0.7 broadcast_compare_fusion
  1.3 8.8 %all_gather.6 = f32[256,512]{1,0:T(8,128)S(1)} all-gather(f32[256,128]{1,0:T(8,128)} %param.4), channel_id=1, replica_groups=mesh['grid'=8,'band'=4] {'band'}, dimensions={1}, use_global_device_ids=true | all-gather | bytes 655360 | tf_op jit(solution)/shard_map/all_gather | solution.py:17
  10.2 0.0 copy-start
  10.2 0.7 gather_fusion
  10.9 0.1 broadcast_select_fusion.1
  11.0 0.8 broadcast_in_dim.37
  11.8 5.8 %all-to-all-start = ((bf16[8,64,512]{2,1,0:T(8,128)(2,1)}), bf16[8,64,512]{2,1,0:T(8,128)(2,1)S(1)}, u32[]{:S(2)}, u32[]{:S(2)}) async-start(bf16[8,64,512]{2,1,0:T(8,128)(2,1)} %broadcast_in_dim.37), calls=%async_computation | async-start | bytes 1048576 | tf_op jit(solution)/shard_map/all_to_all | solution.py:12
  17.7 0.0 copy-done
  17.7 0.0 copy-start.1
  17.7 5.8 %all_gather.7 = bf16[512,256]{1,0:T(8,128)(2,1)S(1)} all-gather(bf16[128,256]{1,0:T(8,128)(2,1)S(1)} %copy-done), channel_id=1, replica_groups=mesh['grid'=8,'band'=4] {'band'}, dimensions={0}, use_global_device_ids=true | all-gather | bytes 327680 | tf_op jit(solution)/shard_map/all_gather | solution.py:17
  23.5 9.2 %all-to-all-done = bf16[8,64,512]{2,1,0:T(8,128)(2,1)S(1)} async-done(((bf16[8,64,512]{2,1,0:T(8,128)(2,1)}), bf16[8,64,512]{2,1,0:T(8,128)(2,1)S(1)}, u32[]{:S(2)}, u32[]{:S(2)}) %all-to-all-start) | async-done | bytes 524320 | tf_op jit(solution)/shard_map/all_to_all | solution.py:12
  32.7 0.2 fusion.11
  32.9 0.2 fusion.13
  33.1 1.0 %fusion.15 = f32[512,256]{1,0:T(8,128)} fusion(bf16[512,512]{1,0:T(8,128)(2,1)S(1)} %bitcast.12, bf16[256,512]{1,0:T(8,128)(2,1)S(1)} %convert_element_type.67), kind=kOutput, calls=%fused_computation.27 | convolution fusion | flops 33947648 | bytes 720896 | tf_op jit(solution)/shard_map/dot_general | solution.py:50
  34.1 0.0 copy-done.1
  34.1 1.7 %multiply_reduce_fusion.1 = (f32[512]{0:T(512)S(1)}, f32[256,512]{1,0:T(8,128)S(1)}) fusion(f32[256,512]{1,0:T(8,128)S(1)} %all_gather.6, bf16[512,512]{1,0:T(8,128)(2,1)S(1)} %bitcast.13, f32[512,256]{1,0:T(8,128)} %fusion.15, f32[512,256]{1,0:T(8,128)S(1)} %fusion.13, f32[512,256]{1,0:T(8,128)S(1)} %fusion.11, bf16[512,256]{1,0:T(8,128)(2,1)S(1)} %all_gather.7, ...), kind=kOutput, calls=%fused_computation.47 | convolution fusion | flops 169737728 | bytes 3607552 | tf_op jit(solution)/shard_map/dot_general | solution.py:59
  35.8 0.7 gather_fusion.1
  36.5 0.1 broadcast_select_fusion
  36.6 1.2 %broadcast_in_dim.60 = f32[8,65,512]{2,1,0:T(8,128)} broadcast(f32[65,512]{1,0:T(8,128)S(1)} %pad_maximum_fusion), dimensions={1,2} | broadcast | bytes 1198080 | tf_op jit(solution)/shard_map/broadcast_in_dim | solution.py:11
  37.7 3.6 %all-to-all-start.1 = ((f32[8,65,512]{2,1,0:T(8,128)}), f32[8,65,512]{2,1,0:T(8,128)S(1)}, u32[]{:S(2)}, u32[]{:S(2)}) async-start(f32[8,65,512]{2,1,0:T(8,128)} %broadcast_in_dim.60), calls=%async_computation.1 | async-start | bytes 2359296 | tf_op jit(solution)/shard_map/all_to_all | solution.py:12
  41.3 28.8 %all-to-all-done.1 = f32[8,65,512]{2,1,0:T(8,128)S(1)} async-done(((f32[8,65,512]{2,1,0:T(8,128)}), f32[8,65,512]{2,1,0:T(8,128)S(1)}, u32[]{:S(2)}, u32[]{:S(2)}) %all-to-all-start.1) | async-done | bytes 1064992 | tf_op jit(solution)/shard_map/all_to_all | solution.py:12
  70.1 0.1 multiply_convert_fusion
  70.2 0.1 fusion.30
  70.3 0.2 fusion.23
  70.6 0.2 fusion.25
  70.8 0.2 fusion.27
  71.0 1.4 %multiply_reduce_fusion = (f32[512]{0:T(512)S(1)}, f32[256,512]{1,0:T(8,128)}) fusion(bf16[512,512]{1,0:T(8,128)(2,1)S(1)} %bitcast.9, f32[512,256]{1,0:T(8,128)S(1)} %fusion.27, f32[512,256]{1,0:T(8,128)S(1)} %fusion.25, f32[512,256]{1,0:T(8,128)S(1)} %fusion.23, bf16[512,256]{1,0:T(8,128)(2,1)S(1)} %all_gather.7, ...), kind=kOutput, calls=%fused_computation.46 | convolution fusion | flops 169868800 | bytes 3609600 | tf_op jit(solution)/shard_map/dot_general | solution.py:59
  72.4 0.1 dynamic_slice.7
  72.5 9.9 %all_to_all.15 = f32[8,1,128]{2,1,0:T(1,128)S(1)} all-to-all(f32[8,1,128]{2,1,0:T(1,128)S(1)} %broadcast_in_dim.61), channel_id=1, replica_groups=mesh['grid'=8,'band'=4] {'grid'}, dimensions={0} | all-to-all | bytes 8192 | tf_op jit(solution)/shard_map/all_to_all | solution.py:12
  82.4 1.6 %dynamic-slice_multiply_fusion = f32[256,128]{1,0:T(8,128)} fusion(f32[256,512]{1,0:T(8,128)} %get-tuple-element.8, s32[]{:T(128)S(6)} %select_n.28, f32[128]{0:T(128)S(1)} %add_rsqrt_fusion.1), kind=kLoop, calls=%fused_computation.60 | loop fusion | flops 32768 | bytes 262660 | tf_op jit(solution)/shard_map/mul | solution.py:68
  (8 shorter events, 0.1 us)
Async XLA Ops:
  10.2 7.5 %copy-start = (bf16[128,256]{1,0:T(8,128)(2,1)S(1)}, bf16[128,256]{1,0:T(8,128)(2,1)}, u32[]{:S(2)}) copy-start(bf16[128,256]{1,0:T(8,128)(2,1)} %param.6) | copy-start | bytes 196612
  11.8 20.8 %all-to-all-start = ((bf16[8,64,512]{2,1,0:T(8,128)(2,1)}), bf16[8,64,512]{2,1,0:T(8,128)(2,1)S(1)}, u32[]{:S(2)}, u32[]{:S(2)}) async-start(bf16[8,64,512]{2,1,0:T(8,128)(2,1)} %broadcast_in_dim.37), calls=%async_computation | async-start | bytes 1048576 | tf_op jit(solution)/shard_map/all_to_all | solution.py:12
  17.7 16.5 %copy-start.1 = (f32[256]{0:T(256)S(1)}, f32[256]{0:T(256)}, u32[]{:S(2)}) copy-start(f32[256]{0:T(256)} %param.5) | copy-start | bytes 3076
  37.7 32.4 %all-to-all-start.1 = ((f32[8,65,512]{2,1,0:T(8,128)}), f32[8,65,512]{2,1,0:T(8,128)S(1)}, u32[]{:S(2)}, u32[]{:S(2)}) async-start(f32[8,65,512]{2,1,0:T(8,128)} %broadcast_in_dim.60), calls=%async_computation.1 | async-start | bytes 2359296 | tf_op jit(solution)/shard_map/all_to_all | solution.py:12

commit v2 on v1

--- a/solution.py
+++ b/solution.py
@@ -38,13 +38,18 @@
             selected = jnp.where(valid_mask[:, None], orbital_block[safe_idx], jnp.zeros((), jnp.bfloat16))
             coll = grid_gather(selected)
         else:
-            at_slots = jnp.where(valid_mask[:, None], psi[safe_idx], 0.0)
-            got = grid_gather(jnp.concatenate([at_slots, sq[None]], 0)).reshape(ngroups, -1, total_orbitals)
-            total = jnp.sum(got[:, -1], axis=0)
+            own = lax.dynamic_slice_in_dim(psi, band * block_width, block_width, axis=1)
+            at_slots = jnp.where(valid_mask[:, None], own[safe_idx], 0.0)
+            nslots = at_slots.shape[0]
+            payload = jnp.concatenate([at_slots, sq.reshape(nbands, block_width)], 0)
+            got = grid_gather(payload).reshape(ngroups, nslots + nbands, block_width)
+            total = jnp.sum(got[:, nslots:], axis=0).reshape(total_orbitals)
             scale = lax.rsqrt(total / (rows * ngroups) + 1e-06)
+            own_scale = lax.dynamic_slice_in_dim(scale, band * block_width, block_width)
+            coll_own = (got[:, :nslots] * own_scale).astype(jnp.bfloat16).reshape(-1, block_width)
+            coll = band_gather(coll_own, 1)
             psi = psi * scale
             orbital_block = psi.astype(jnp.bfloat16)
-            coll = (got[:, :-1] * scale).astype(jnp.bfloat16).reshape(-1, total_orbitals)
         proj = None
         for k in range(nbands):
             part = lax.dot_general(

time: 84.4 us -> 70.4 us (0.83)
  waiting for transfers between devices: 38 us -> 9.21 us
  blocking collectives: 24.5 us -> 44.5 us
  starting transfers between devices: 9.45 us -> 5.97 us
  local copies, waits for them, and re-layouts: 3.44 us -> 2.35 us
    all_to_all x2 -> x1, waiting for transfers between devices: 38 us -> 9.21 us  [grid_gather(): got = lax.all_to_all(sent, 'grid', 0, 0, tiled=True)]
    all_to_all x1 -> x2, blocking collectives: 9.89 us -> 23.1 us  [grid_gather(): got = lax.all_to_all(sent, 'grid', 0, 0, tiled=True)]
    all_gather x2 -> x3, blocking collectives: 14.6 us -> 21.5 us  [band_gather(): return lax.all_gather(x, 'band', axis=axis, tiled=True)]
    all_to_all x2 -> x1, starting transfers between devices: 9.45 us -> 5.97 us  [grid_gather(): got = lax.all_to_all(sent, 'grid', 0, 0, tiled=True)]
    broadcast_in_dim x3, local copies, waits for them, and re-layouts: 1.99 us -> 0.86 us  [grid_gather(): sent = jnp.broadcast_to(x[None], (ngroups,) + x.shape)]
  transfers between devices with their start and end apart: 2 -> 1, of which waited for: 2 -> 1; matrix products, arithmetic and copies ran while one was open for 0% -> 0% of each run, Pallas kernels for 0% -> 0%
where the time goes in v2:
time: 70.4 us; the launch traced here: 70 us
  blocking collectives  44.5 us (63%)
  waiting for transfers between devices  9.21 us (13%)
  starting transfers between devices  5.97 us (8%)
  matrix products  5.19 us (7%)
  other arithmetic  2.63 us (4%)
  local copies, waits for them, and re-layouts  2.35 us (3%)
    all_to_all x2, blocking collectives, grid_gather(): got = lax.all_to_all(sent, 'grid', 0, 0, tiled=True)  23.1 us
    all_gather x3, blocking collectives, band_gather(): return lax.all_gather(x, 'band', axis=axis, tiled=True)  21.5 us
    all_to_all x1, waiting for transfers between devices, grid_gather(): got = lax.all_to_all(sent, 'grid', 0, 0, tiled=True)  9.21 us
    all_to_all x1, starting transfers between devices, grid_gather(): got = lax.all_to_all(sent, 'grid', 0, 0, tiled=True)  5.97 us
    dot_general x2, matrix products, body(): lax.dot_general(tile_blocks, coll, (((0,), (0,)), ((), ())), preferred_el...  3.06 us
    dot_general x6, matrix products, body(): lax.dot_general(coll[:, k * block_width:(k + 1) * block_width], orbital_b...  2.13 us
    mul x1, other arithmetic, body(): return mine * lax.rsqrt(total / (rows * ngroups) + 1e-06)  1.57 us
  transfers between devices with their start and end apart: 1, of which 1 were waited for; matrix products, arithmetic and copies ran while one was open for 0% of the time, Pallas kernels for 0%

profile of v2, /device:TPU:0, one launch (start us, length us, event | category | flops | bytes accessed | tf_op | source)
XLA Modules:
  0.0 70.0 jit_solution(17747458119354516422)
XLA Ops:
  0.0 0.0 copy-start.2
  0.0 0.7 %broadcast_compare_fusion = pred[64]{0:T(512)(128)(4,1)S(1)} fusion(s32[64]{0:T(128)} %param.7), kind=kLoop, calls=%fused_computation.77 | loop fusion | flops 64 | bytes 320 | tf_op jit(solution)/shard_map/ge | solution.py:29
  0.7 0.0 copy-done.2
  0.8 8.8 %all_gather.9 = f32[256,512]{1,0:T(8,128)S(1)} all-gather(f32[256,128]{1,0:T(8,128)} %param.4), channel_id=1, replica_groups=mesh['grid'=8,'band'=4] {'band'}, dimensions={1}, use_global_device_ids=true | all-gather | bytes 655360 | tf_op jit(solution)/shard_map/all_gather | solution.py:17
  9.6 0.7 %gather_fusion = bf16[64,512]{1,0:T(8,128)(2,1)S(1)} fusion(bf16[256,512]{1,0:T(8,128)(2,1)S(1)} %convert_element_type.67, s32[1024]{0:T(1024)S(1)} %pad_clamp_fusion), kind=kCustom, calls=%fused_computation | custom fusion | bytes 131328 | tf_op jit(solution)/shard_map/gather | solution.py:38
  10.3 0.1 broadcast_select_fusion
  10.4 0.8 %broadcast_in_dim.56 = bf16[8,64,512]{2,1,0:T(8,128)(2,1)} broadcast(bf16[64,512]{1,0:T(8,128)(2,1)S(1)} %broadcast_select_fusion), dimensions={1,2} | broadcast | bytes 589824 | tf_op jit(solution)/shard_map/broadcast_in_dim | solution.py:11
  11.2 0.0 copy-start
  11.2 6.0 %all-to-all-start = ((bf16[8,64,512]{2,1,0:T(8,128)(2,1)}), bf16[8,64,512]{2,1,0:T(8,128)(2,1)S(1)}, u32[]{:S(2)}, u32[]{:S(2)}) async-start(bf16[8,64,512]{2,1,0:T(8,128)(2,1)} %broadcast_in_dim.56), calls=%async_computation | async-start | bytes 1048576 | tf_op jit(solution)/shard_map/all_to_all | solution.py:12
  17.2 0.0 copy-done
  17.2 5.8 %all_gather.10 = bf16[512,256]{1,0:T(8,128)(2,1)S(1)} all-gather(bf16[128,256]{1,0:T(8,128)(2,1)S(1)} %copy-done), channel_id=1, replica_groups=mesh['grid'=8,'band'=4] {'band'}, dimensions={0}, use_global_device_ids=true | all-gather | bytes 327680 | tf_op jit(solution)/shard_map/all_gather | solution.py:17
  23.0 9.2 %all-to-all-done = bf16[8,64,512]{2,1,0:T(8,128)(2,1)S(1)} async-done(((bf16[8,64,512]{2,1,0:T(8,128)(2,1)}), bf16[8,64,512]{2,1,0:T(8,128)(2,1)S(1)}, u32[]{:S(2)}, u32[]{:S(2)}) %all-to-all-start) | async-done | bytes 524320 | tf_op jit(solution)/shard_map/all_to_all | solution.py:12
  32.2 0.2 fusion.15
  32.4 0.2 fusion.13
  32.7 0.0 copy-start.1
  32.7 1.0 %fusion.11 = f32[512,256]{1,0:T(8,128)} fusion(bf16[512,512]{1,0:T(8,128)(2,1)S(1)} %bitcast.10, bf16[256,512]{1,0:T(8,128)(2,1)S(1)} %convert_element_type.67), kind=kOutput, calls=%fused_computation.23 | convolution fusion | flops 33947648 | bytes 720896 | tf_op jit(solution)/shard_map/dot_general | solution.py:55
  33.7 0.0 copy-done.1
  33.7 1.7 %multiply_reduce_fusion.1 = (f32[512]{0:T(512)S(1)}, f32[256,512]{1,0:T(8,128)S(1)}) fusion(f32[256,512]{1,0:T(8,128)S(1)} %all_gather.9, bf16[512,512]{1,0:T(8,128)(2,1)S(1)} %bitcast.11, f32[512,256]{1,0:T(8,128)S(1)} %fusion.15, f32[512,256]{1,0:T(8,128)S(1)} %fusion.13, f32[512,256]{1,0:T(8,128)} %fusion.11, bf16[512,256]{1,0:T(8,128)(2,1)S(1)} %all_gather.10, ...), kind=kOutput, calls=%fused_computation.45 | convolution fusion | flops 169737728 | bytes 3607552 | tf_op jit(solution)/shard_map/dot_general | solution.py:64
  35.4 0.6 gather_fusion.1
  36.0 0.1 broadcast_select_fusion.1
  36.1 14.0 %all_to_all.15 = f32[8,68,128]{2,1,0:T(8,128)S(1)} all-to-all(f32[8,68,128]{2,1,0:T(8,128)S(1)} %broadcast_in_dim.59), channel_id=1, replica_groups=mesh['grid'=8,'band'=4] {'grid'}, dimensions={0} | all-to-all | bytes 557056 | tf_op jit(solution)/shard_map/all_to_all | solution.py:12
  50.1 0.1 dynamic_slice.13
  50.3 6.8 %all_gather.11 = bf16[512,512]{1,0:T(8,128)(2,1)S(1)} all-gather(bf16[512,128]{1,0:T(8,128)(2,1)S(1)} %bitcast.12), channel_id=1, replica_groups=mesh['grid'=8,'band'=4] {'band'}, dimensions={1}, use_global_device_ids=true | all-gather | bytes 655360 | tf_op jit(solution)/shard_map/all_gather | solution.py:17
  57.1 0.2 fusion.27
  57.3 0.2 fusion.25
  57.6 0.2 fusion.23
  57.8 1.4 %multiply_reduce_fusion = (f32[512]{0:T(512)S(1)}, f32[256,512]{1,0:T(8,128)}) fusion(bf16[512,512]{1,0:T(8,128)(2,1)S(1)} %all_gather.11, f32[512,256]{1,0:T(8,128)S(1)} %fusion.27, f32[512,256]{1,0:T(8,128)S(1)} %fusion.25, f32[512,256]{1,0:T(8,128)S(1)} %fusion.23, bf16[512,256]{1,0:T(8,128)(2,1)S(1)} %all_gather.10, ...), kind=kOutput, calls=%fused_computation.44 | convolution fusion | flops 169868800 | bytes 3609600 | tf_op jit(solution)/shard_map/dot_general | solution.py:64
  59.2 0.1 dynamic_slice.15
  59.3 9.1 %all_to_all.16 = f32[8,1,128]{2,1,0:T(1,128)S(1)} all-to-all(f32[8,1,128]{2,1,0:T(1,128)S(1)} %broadcast_in_dim.60), channel_id=1, replica_groups=mesh['grid'=8,'band'=4] {'grid'}, dimensions={0} | all-to-all | bytes 8192 | tf_op jit(solution)/shard_map/all_to_all | solution.py:12
  68.4 1.6 %dynamic-slice_multiply_fusion = f32[256,128]{1,0:T(8,128)} fusion(f32[256,512]{1,0:T(8,128)} %get-tuple-element.8, s32[]{:T(128)S(6)} %select_n.29, f32[128]{0:T(128)S(1)} %add_rsqrt_fusion), kind=kLoop, calls=%fused_computation.59 | loop fusion | flops 32768 | bytes 262660 | tf_op jit(solution)/shard_map/mul | solution.py:73
  (13 shorter events, 0.2 us)
Async XLA Ops:
  0.0 0.7 %copy-start.2 = (s32[64]{0:T(128)S(1)}, s32[64]{0:T(128)}, u32[]{:S(2)}) copy-start(s32[64]{0:T(128)} %param.7) | copy-start | bytes 772
  11.2 6.0 %copy-start = (bf16[128,256]{1,0:T(8,128)(2,1)S(1)}, bf16[128,256]{1,0:T(8,128)(2,1)}, u32[]{:S(2)}) copy-start(bf16[128,256]{1,0:T(8,128)(2,1)} %param.6) | copy-start | bytes 196612
  11.2 21.0 %all-to-all-start = ((bf16[8,64,512]{2,1,0:T(8,128)(2,1)}), bf16[8,64,512]{2,1,0:T(8,128)(2,1)S(1)}, u32[]{:S(2)}, u32[]{:S(2)}) async-start(bf16[8,64,512]{2,1,0:T(8,128)(2,1)} %broadcast_in_dim.56), calls=%async_computation | async-start | bytes 1048576 | tf_op jit(solution)/shard_map/all_to_all | solution.py:12
  32.7 1.0 %copy-start.1 = (f32[256]{0:T(256)S(1)}, f32[256]{0:T(256)}, u32[]{:S(2)}) copy-start(f32[256]{0:T(256)} %param.5) | copy-start | bytes 3076

commit v3 on v2

--- a/solution.py
+++ b/solution.py
@@ -13,8 +13,12 @@
     return got.reshape((ngroups * x.shape[0],) + x.shape[1:])
 
 
-def band_gather(x, axis):
-    return lax.all_gather(x, "band", axis=axis, tiled=True)
+def band_swap(x):
+    nbands = lax.axis_size("band")
+    got = [x]
+    for k in range(1, nbands):
+        got.append(lax.ppermute(x, "band", [(i, i ^ k) for i in range(nbands)]))
+    return got
 
 
 def body(orbitals, potential, fitted, points):
@@ -28,26 +32,28 @@
     total_orbitals = block_width * nbands
     valid_mask = points >= 0
     safe_idx = jnp.where(valid_mask, points, 0)
-    psi = band_gather(orbitals, 1)
-    fitted_all = band_gather(fitted, 0).astype(jnp.float32)
+    psi = jnp.concatenate(band_swap(orbitals), 1)
+    fitted_got = jnp.stack(band_swap(fitted), 0)
+    fitted_all = jnp.take(fitted_got, jnp.arange(nbands, dtype=jnp.int32) ^ band, axis=0)
+    fitted_all = fitted_all.reshape(-1, fitted.shape[1]).astype(jnp.float32)
     pot = potential[:, None]
-    scale = None
+    sq = None
     for step in range(ITERS):
-        if scale is None:
+        if sq is None:
+            own_b = orbitals.astype(jnp.bfloat16)
+            selected = jnp.where(valid_mask[:, None], own_b[safe_idx], jnp.zeros((), jnp.bfloat16))
+            coll = jnp.concatenate(band_swap(grid_gather(selected)), 1)
             orbital_block = psi.astype(jnp.bfloat16)
-            selected = jnp.where(valid_mask[:, None], orbital_block[safe_idx], jnp.zeros((), jnp.bfloat16))
-            coll = grid_gather(selected)
         else:
-            own = lax.dynamic_slice_in_dim(psi, band * block_width, block_width, axis=1)
+            own = psi[:, :block_width]
             at_slots = jnp.where(valid_mask[:, None], own[safe_idx], 0.0)
             nslots = at_slots.shape[0]
             payload = jnp.concatenate([at_slots, sq.reshape(nbands, block_width)], 0)
             got = grid_gather(payload).reshape(ngroups, nslots + nbands, block_width)
             total = jnp.sum(got[:, nslots:], axis=0).reshape(total_orbitals)
             scale = lax.rsqrt(total / (rows * ngroups) + 1e-06)
-            own_scale = lax.dynamic_slice_in_dim(scale, band * block_width, block_width)
-            coll_own = (got[:, :nslots] * own_scale).astype(jnp.bfloat16).reshape(-1, block_width)
-            coll = band_gather(coll_own, 1)
+            coll_own = (got[:, :nslots] * scale[:block_width]).astype(jnp.bfloat16).reshape(-1, block_width)
+            coll = jnp.concatenate(band_swap(coll_own), 1)
             psi = psi * scale
             orbital_block = psi.astype(jnp.bfloat16)
         proj = None
@@ -66,11 +72,8 @@
         )
         psi = psi - 0.25 * (pot * psi - applied)
         sq = jnp.sum(psi * psi, axis=0)
-        scale = sq
-    mine = lax.dynamic_slice_in_dim(psi, band * block_width, block_width, axis=1)
-    mine_sq = lax.dynamic_slice_in_dim(sq, band * block_width, block_width)
-    total = jnp.sum(grid_gather(mine_sq[None]), axis=0)
-    return mine * lax.rsqrt(total / (rows * ngroups) + 1e-06)
+    total = jnp.sum(grid_gather(sq[None, :block_width]), axis=0)
+    return psi[:, :block_width] * lax.rsqrt(total / (rows * ngroups) + 1e-06)
 
 
 def body_spread(orbitals, potential, fitted, points):

time: 70.4 us -> 67.5 us (0.959)
  blocking collectives: 44.5 us -> 25.1 us
  starting transfers between devices: 5.97 us -> 15.3 us
  waiting for transfers between devices: 9.21 us -> 15.8 us
  local copies, waits for them, and re-layouts: 2.35 us -> 3.3 us
  matrix products: 5.19 us -> 4.46 us
    all_gather x3 -> x0, blocking collectives: 21.5 us -> none  [band_gather(): return lax.all_gather(x, 'band', axis=axis, tiled=True)]
    ppermute x0 -> x12, waiting for transfers between devices: none -> 9.52 us  [band_swap(): got.append(lax.ppermute(x, 'band', [(i, i ^ k) for i in range(nbands)]))]
    ppermute x0 -> x12, starting transfers between devices: none -> 9.36 us  [band_swap(): got.append(lax.ppermute(x, 'band', [(i, i ^ k) for i in range(nbands)]))]
    all_to_all x1, waiting for transfers between devices: 9.21 us -> 6.3 us  [grid_gather(): got = lax.all_to_all(sent, 'grid', 0, 0, tiled=True)]
    all_to_all x2, blocking collectives: 23.1 us -> 25.1 us  [grid_gather(): got = lax.all_to_all(sent, 'grid', 0, 0, tiled=True)]
    convert_element_type x1 -> x2, other arithmetic: 0.02 us -> 1.03 us  [the longest x1 1 us: body(): own_b = orbitals.astype(jnp.bfloat16)]
    mul x1, other arithmetic: 1.57 us -> 0.68 us  [body(): return psi[:, :block_width] * lax.rsqrt(total / (rows * ngroups) + 1e-06)]
    dot_general x6, matrix products: 2.13 us -> 1.33 us  [body(): lax.dot_general(coll[:, k * block_width:(k + 1) * block_width], orbital_b...]
  transfers between devices with their start and end apart: 1 -> 13, of which waited for: 1 -> 5; matrix products, arithmetic and copies ran while one was open for 0% -> 8% of each run, Pallas kernels for 0% -> 0%
where the time goes in v3:
time: 67.5 us; the launch traced here: 67.1 us
  blocking collectives  25.1 us (37%)
  waiting for transfers between devices  15.8 us (23%)
  starting transfers between devices  15.3 us (23%)
  matrix products  4.46 us (7%)
  local copies, waits for them, and re-layouts  3.3 us (5%)
  other arithmetic  2.86 us (4%)
    all_to_all x2, blocking collectives, grid_gather(): got = lax.all_to_all(sent, 'grid', 0, 0, tiled=True)  25.1 us
    ppermute x12, waiting for transfers between devices, band_swap(): got.append(lax.ppermute(x, 'band', [(i, i ^ k) for i in range(nbands)]))  9.52 us
    ppermute x12, starting transfers between devices, band_swap(): got.append(lax.ppermute(x, 'band', [(i, i ^ k) for i in range(nbands)]))  9.36 us
    all_to_all x1, waiting for transfers between devices, grid_gather(): got = lax.all_to_all(sent, 'grid', 0, 0, tiled=True)  6.3 us
    all_to_all x1, starting transfers between devices, grid_gather(): got = lax.all_to_all(sent, 'grid', 0, 0, tiled=True)  5.97 us
    dot_general x2, matrix products, body(): lax.dot_general(tile_blocks, coll, (((0,), (0,)), ((), ())), preferred_el...  3.12 us
  transfers between devices with their start and end apart: 13, of which 5 were waited for; matrix products, arithmetic and copies ran while one was open for 8% of the time, Pallas kernels for 0%

profile of v3, /device:TPU:0, one launch (start us, length us, event | category | flops | bytes accessed | tf_op | source)
XLA Modules:
  0.0 67.1 jit_solution(4403423508097010724)
XLA Ops:
  0.0 0.5 collective-permute-start.3
  0.5 2.6 %collective-permute-start.5 = (bf16[128,256]{1,0:T(8,128)(2,1)}, bf16[128,256]{1,0:T(8,128)(2,1)S(1)}, u32[]{:S(2)}, u32[]{:S(2)}) collective-permute-start(bf16[128,256]{1,0:T(8,128)(2,1)} %param.6), channel_id=1, source_target_pairs={{0,3},{1,2},{2,1},{3,0},{4,7},{5,6},{6,5},{7,4},{8,11},{9,10},{10,... | collective-permute-start | bytes 196616 | tf_op jit(solution)/shard_map/ppermute | solution.py:20
  3.1 0.1 collective-permute-start.4
  3.1 2.0 %collective-permute-start.1 = (f32[256,128]{1,0:T(8,128)}, f32[256,128]{1,0:T(8,128)S(1)}, u32[]{:S(2)}, u32[]{:S(2)}) collective-permute-start(f32[256,128]{1,0:T(8,128)} %param.4), channel_id=1, source_target_pairs={{0,2},{1,3},{2,0},{3,1},{4,6},{5,7},{6,4},{7,5},{8,10},{9,11},{10,... | collective-permute-start | bytes 393224 | tf_op jit(solution)/shard_map/ppermute | solution.py:20
  5.1 0.0 collective-permute-start
  5.1 0.7 broadcast_compare_fusion
  5.8 1.0 %fusion.67 = (bf16[256,128]{1,0:T(8,128)(2,1)S(1)}, f32[256,512]{1,0:T(8,128)S(1)}) fusion(f32[256,128]{1,0:T(8,128)} %param.4), kind=kLoop, calls=%fused_computation.100 | loop fusion | flops 32767 | bytes 327680 | tf_op jit(solution)/shard_map/convert_element_type | solution.py:43
  6.8 0.6 gather_fusion.1
  7.4 0.1 broadcast_select_fusion.1
  7.5 0.7 %broadcast_in_dim.72 = bf16[8,64,128]{2,1,0:T(8,128)(2,1)} broadcast(bf16[64,128]{1,0:T(8,128)(2,1)S(1)} %broadcast_select_fusion.1), dimensions={1,2} | broadcast | bytes 147456 | tf_op jit(solution)/shard_map/broadcast_in_dim | solution.py:11
  8.2 6.0 %all-to-all-start = ((bf16[8,64,128]{2,1,0:T(8,128)(2,1)}), bf16[8,64,128]{2,1,0:T(8,128)(2,1)S(1)}, u32[]{:S(2)}, u32[]{:S(2)}) async-start(bf16[8,64,128]{2,1,0:T(8,128)(2,1)} %broadcast_in_dim.72), calls=%async_computation | async-start | bytes 262144 | tf_op jit(solution)/shard_map/all_to_all | solution.py:12
  14.2 0.1 broadcast_bitcast_fusion
  14.2 0.0 collective-permute-done.3
  14.3 0.4 collective-permute-start.2
  14.7 0.0 collective-permute-done.5
  14.7 0.0 collective-permute-done.4
  14.7 0.6 gather_fusion
  15.3 0.1 bitcast_select_fusion
  15.5 0.0 collective-permute-done
  15.5 6.3 %all-to-all-done = bf16[8,64,128]{2,1,0:T(8,128)(2,1)S(1)} async-done(((bf16[8,64,128]{2,1,0:T(8,128)(2,1)}), bf16[8,64,128]{2,1,0:T(8,128)(2,1)S(1)}, u32[]{:S(2)}, u32[]{:S(2)}) %all-to-all-start) | async-done | bytes 131104 | tf_op jit(solution)/shard_map/all_to_all | solution.py:12
  21.8 0.0 collective-permute-start.8
  21.9 0.6 collective-permute-start.7
  22.5 1.3 %collective-permute-start.6 = (bf16[512,128]{1,0:T(8,128)(2,1)S(1)}, bf16[512,128]{1,0:T(8,128)(2,1)S(1)}, u32[]{:S(2)}, u32[]{:S(2)}) collective-permute-start(bf16[512,128]{1,0:T(8,128)(2,1)S(1)} %bitcast.33), channel_id=1, source_target_pairs={{0,1},{1,0},{2,3},{3,2},{4,5},{5,4},{6,7},{7,6},{8,9},{9,8},{10,11... | collective-permute-start | bytes 393224 | tf_op jit(solution)/shard_map/ppermute | solution.py:20
  23.8 3.8 %collective-permute-done.8 = bf16[512,128]{1,0:T(8,128)(2,1)S(1)} collective-permute-done((bf16[512,128]{1,0:T(8,128)(2,1)S(1)}, bf16[512,128]{1,0:T(8,128)(2,1)S(1)}, u32[]{:S(2)}, u32[]{:S(2)}) %collective-permute-start.8) | collective-permute-done | bytes 131104 | tf_op jit(solution)/shard_map/ppermute | solution.py:20
  27.6 0.2 fusion.11
  27.8 0.9 %collective-permute-done.7 = bf16[512,128]{1,0:T(8,128)(2,1)S(1)} collective-permute-done((bf16[512,128]{1,0:T(8,128)(2,1)S(1)}, bf16[512,128]{1,0:T(8,128)(2,1)S(1)}, u32[]{:S(2)}, u32[]{:S(2)}) %collective-permute-start.7) | collective-permute-done | bytes 131104 | tf_op jit(solution)/shard_map/ppermute | solution.py:20
  28.7 0.2 fusion.9
  28.9 0.0 copy-start.3
  28.9 0.0 collective-permute-done.6
  28.9 0.0 copy-start.1
  28.9 0.6 copy-done.1
  29.6 0.2 fusion.7
  29.8 1.5 %multiply_reduce_fusion.1 = (f32[512]{0:T(512)S(1)}, f32[256,512]{1,0:T(8,128)S(1)}) fusion(f32[256,512]{1,0:T(8,128)S(1)} %constant_dynamic-update-slice_fusion, bf16[512,128]{1,0:T(8,128)(2,1)S(1)} %collective-permute-done.8, bf16[512,128]{1,0:T(8,128)(2,1)S(1)} %collective-permute-done.7, bf16[512,128]{1,0:T(8,128)(2,1)} %copy-done.1, ...), kind=kOutput, calls=%fused_computation.57 | convolution fusion | flops 171834880 | bytes 3607552 | tf_op jit(solution)/shard_map/dot_general | solution.py:70
  31.4 0.6 gather_fusion.2
  32.0 0.1 broadcast_select_fusion
  32.1 14.8 %all_to_all.15 = f32[8,68,128]{2,1,0:T(8,128)S(1)} all-to-all(f32[8,68,128]{2,1,0:T(8,128)S(1)} %broadcast_in_dim.74), channel_id=1, replica_groups=mesh['grid'=8,'band'=4] {'grid'}, dimensions={0} | all-to-all | bytes 557056 | tf_op jit(solution)/shard_map/all_to_all | solution.py:12
  46.9 0.1 collective-permute-start.11
  47.0 0.8 %collective-permute-start.10 = (bf16[512,128]{1,0:T(8,128)(2,1)S(1)}, bf16[512,128]{1,0:T(8,128)(2,1)S(1)}, u32[]{:S(2)}, u32[]{:S(2)}) collective-permute-start(bf16[512,128]{1,0:T(8,128)(2,1)S(1)} %bitcast.27), channel_id=1, source_target_pairs={{0,2},{1,3},{2,0},{3,1},{4,6},{5,7},{6,4},{7,5},{8,10},{9,11},{10,... | collective-permute-start | bytes 393224 | tf_op jit(solution)/shard_map/ppermute | solution.py:20
  47.8 1.0 %collective-permute-start.9 = (bf16[512,128]{1,0:T(8,128)(2,1)S(1)}, bf16[512,128]{1,0:T(8,128)(2,1)}, u32[]{:S(2)}, u32[]{:S(2)}) collective-permute-start(bf16[512,128]{1,0:T(8,128)(2,1)S(1)} %bitcast.28), channel_id=1, source_target_pairs={{0,1},{1,0},{2,3},{3,2},{4,5},{5,4},{6,7},{7,6},{8,9},{9,8},{10,11... | collective-permute-start | bytes 393224 | tf_op jit(solution)/shard_map/ppermute | solution.py:20
  48.9 0.2 fusion.13
  49.1 3.6 %collective-permute-done.11 = bf16[512,128]{1,0:T(8,128)(2,1)S(1)} collective-permute-done((bf16[512,128]{1,0:T(8,128)(2,1)S(1)}, bf16[512,128]{1,0:T(8,128)(2,1)S(1)}, u32[]{:S(2)}, u32[]{:S(2)}) %collective-permute-start.11) | collective-permute-done | bytes 131104 | tf_op jit(solution)/shard_map/ppermute | solution.py:20
  52.7 0.2 fusion.23
  52.9 1.3 %collective-permute-done.10 = bf16[512,128]{1,0:T(8,128)(2,1)S(1)} collective-permute-done((bf16[512,128]{1,0:T(8,128)(2,1)S(1)}, bf16[512,128]{1,0:T(8,128)(2,1)S(1)}, u32[]{:S(2)}, u32[]{:S(2)}) %collective-permute-start.10) | collective-permute-done | bytes 131104 | tf_op jit(solution)/shard_map/ppermute | solution.py:20
  54.2 0.2 fusion.21
  54.5 0.0 collective-permute-done.9
  54.5 1.6 %multiply_reduce_fusion = (f32[512]{0:T(512)S(1)}, f32[256,512]{1,0:T(8,128)S(1)}) fusion(bf16[512,128]{1,0:T(8,128)(2,1)S(1)} %collective-permute-done.11, bf16[512,128]{1,0:T(8,128)(2,1)S(1)} %collective-permute-done.10, bf16[512,128]{1,0:T(8,128)(2,1)} %collective-permute-done.9, bf16[512,128]{1,0:T(8,128)(2,1)S(1)} %bitcast.30, ...), kind=kOutput, calls=%fused_computation.55 | convolution fusion | flops 171965952 | bytes 3609600 | tf_op jit(solution)/shard_map/dot_general | solution.py:70
  56.1 10.3 %all_to_all.16 = f32[8,1,128]{2,1,0:T(1,128)S(1)} all-to-all(f32[8,1,128]{2,1,0:T(1,128)S(1)} %broadcast_in_dim.75), channel_id=1, replica_groups=mesh['grid'=8,'band'=4] {'grid'}, dimensions={0} | all-to-all | bytes 8192 | tf_op jit(solution)/shard_map/all_to_all | solution.py:12
  66.4 0.7 %slice_multiply_fusion.1 = f32[256,128]{1,0:T(8,128)} fusion(f32[256,512]{1,0:T(8,128)S(1)} %get-tuple-element.12, f32[128]{0:T(128)S(1)} %add_rsqrt_fusion.1), kind=kLoop, calls=%fused_computation.66 | loop fusion | flops 32768 | bytes 262656 | tf_op jit(solution)/shard_map/mul | solution.py:76
  (31 shorter events, 0.3 us)
Async XLA Ops:
  0.0 5.7 %copy-start.4 = (s32[64]{0:T(128)S(1)}, s32[64]{0:T(128)}, u32[]{:S(2)}) copy-start(s32[64]{0:T(128)} %param.7) | copy-start | bytes 772
  0.0 14.2 %collective-permute-start.3 = (bf16[128,256]{1,0:T(8,128)(2,1)}, bf16[128,256]{1,0:T(8,128)(2,1)S(1)}, u32[]{:S(2)}, u32[]{:S(2)}) collective-permute-start(bf16[128,256]{1,0:T(8,128)(2,1)} %param.6), channel_id=1, source_target_pairs={{0,1},{1,0},{2,3},{3,2},{4,5},{5,4},{6,7},{7,6},{8,9},{9,8},{10,11... | collective-permute-start | bytes 196616 | tf_op jit(solution)/shard_map/ppermute | solution.py:20
  0.5 14.2 %collective-permute-start.5 = (bf16[128,256]{1,0:T(8,128)(2,1)}, bf16[128,256]{1,0:T(8,128)(2,1)S(1)}, u32[]{:S(2)}, u32[]{:S(2)}) collective-permute-start(bf16[128,256]{1,0:T(8,128)(2,1)} %param.6), channel_id=1, source_target_pairs={{0,3},{1,2},{2,1},{3,0},{4,7},{5,6},{6,5},{7,4},{8,11},{9,10},{10,... | collective-permute-start | bytes 196616 | tf_op jit(solution)/shard_map/ppermute | solution.py:20
  3.1 11.6 %collective-permute-start.4 = (bf16[128,256]{1,0:T(8,128)(2,1)}, bf16[128,256]{1,0:T(8,128)(2,1)S(1)}, u32[]{:S(2)}, u32[]{:S(2)}) collective-permute-start(bf16[128,256]{1,0:T(8,128)(2,1)} %param.6), channel_id=1, source_target_pairs={{0,2},{1,3},{2,0},{3,1},{4,6},{5,7},{6,4},{7,5},{8,10},{9,11},{10,... | collective-permute-start | bytes 196616 | tf_op jit(solution)/shard_map/ppermute | solution.py:20
  3.1 18.7 %collective-permute-start.1 = (f32[256,128]{1,0:T(8,128)}, f32[256,128]{1,0:T(8,128)S(1)}, u32[]{:S(2)}, u32[]{:S(2)}) collective-permute-start(f32[256,128]{1,0:T(8,128)} %param.4), channel_id=1, source_target_pairs={{0,2},{1,3},{2,0},{3,1},{4,6},{5,7},{6,4},{7,5},{8,10},{9,11},{10,... | collective-permute-start | bytes 393224 | tf_op jit(solution)/shard_map/ppermute | solution.py:20
  5.1 10.4 %collective-permute-start = (f32[256,128]{1,0:T(8,128)}, f32[256,128]{1,0:T(8,128)S(1)}, u32[]{:S(2)}, u32[]{:S(2)}) collective-permute-start(f32[256,128]{1,0:T(8,128)} %param.4), channel_id=1, source_target_pairs={{0,1},{1,0},{2,3},{3,2},{4,5},{5,4},{6,7},{7,6},{8,9},{9,8},{10,11... | collective-permute-start | bytes 393224 | tf_op jit(solution)/shard_map/ppermute | solution.py:20
  8.2 6.1 %copy-start = (f32[256,128]{1,0:T(8,128)S(1)}, f32[256,128]{1,0:T(8,128)}, u32[]{:S(2)}) copy-start(f32[256,128]{1,0:T(8,128)} %param.4) | copy-start | bytes 393220
  8.2 6.5 %copy-start.2 = (bf16[128,256]{1,0:T(8,128)(2,1)S(1)}, bf16[128,256]{1,0:T(8,128)(2,1)}, u32[]{:S(2)}) copy-start(bf16[128,256]{1,0:T(8,128)(2,1)} %param.6) | copy-start | bytes 196612
  8.2 13.6 %all-to-all-start = ((bf16[8,64,128]{2,1,0:T(8,128)(2,1)}), bf16[8,64,128]{2,1,0:T(8,128)(2,1)S(1)}, u32[]{:S(2)}, u32[]{:S(2)}) async-start(bf16[8,64,128]{2,1,0:T(8,128)(2,1)} %broadcast_in_dim.72), calls=%async_computation | async-start | bytes 262144 | tf_op jit(solution)/shard_map/all_to_all | solution.py:12
  14.3 7.6 %collective-permute-start.2 = (f32[256,128]{1,0:T(8,128)S(1)}, f32[256,128]{1,0:T(8,128)S(1)}, u32[]{:S(2)}, u32[]{:S(2)}) collective-permute-start(f32[256,128]{1,0:T(8,128)S(1)} %copy-done), channel_id=1, source_target_pairs={{0,3},{1,2},{2,1},{3,0},{4,7},{5,6},{6,5},{7,4},{8,11},{9,10},{10,... | collective-permute-start | bytes 393224 | tf_op jit(solution)/shard_map/ppermute | solution.py:20
  21.8 5.8 %collective-permute-start.8 = (bf16[512,128]{1,0:T(8,128)(2,1)S(1)}, bf16[512,128]{1,0:T(8,128)(2,1)S(1)}, u32[]{:S(2)}, u32[]{:S(2)}) collective-permute-start(bf16[512,128]{1,0:T(8,128)(2,1)S(1)} %bitcast.31), channel_id=1, source_target_pairs={{0,3},{1,2},{2,1},{3,0},{4,7},{5,6},{6,5},{7,4},{8,11},{9,10},{10,... | collective-permute-start | bytes 393224 | tf_op jit(solution)/shard_map/ppermute | solution.py:20
  21.9 6.8 %collective-permute-start.7 = (bf16[512,128]{1,0:T(8,128)(2,1)S(1)}, bf16[512,128]{1,0:T(8,128)(2,1)S(1)}, u32[]{:S(2)}, u32[]{:S(2)}) collective-permute-start(bf16[512,128]{1,0:T(8,128)(2,1)S(1)} %bitcast.32), channel_id=1, source_target_pairs={{0,2},{1,3},{2,0},{3,1},{4,6},{5,7},{6,4},{7,5},{8,10},{9,11},{10,... | collective-permute-start | bytes 393224 | tf_op jit(solution)/shard_map/ppermute | solution.py:20
  22.5 6.4 %collective-permute-start.6 = (bf16[512,128]{1,0:T(8,128)(2,1)S(1)}, bf16[512,128]{1,0:T(8,128)(2,1)S(1)}, u32[]{:S(2)}, u32[]{:S(2)}) collective-permute-start(bf16[512,128]{1,0:T(8,128)(2,1)S(1)} %bitcast.33), channel_id=1, source_target_pairs={{0,1},{1,0},{2,3},{3,2},{4,5},{5,4},{6,7},{7,6},{8,9},{9,8},{10,11... | collective-permute-start | bytes 393224 | tf_op jit(solution)/shard_map/ppermute | solution.py:20
  28.9 0.9 %copy-start.3 = (f32[256]{0:T(256)S(1)}, f32[256]{0:T(256)}, u32[]{:S(2)}) copy-start(f32[256]{0:T(256)} %param.5) | copy-start | bytes 3076
  28.9 0.7 copy-start.1
  46.9 5.8 %collective-permute-start.11 = (bf16[512,128]{1,0:T(8,128)(2,1)S(1)}, bf16[512,128]{1,0:T(8,128)(2,1)S(1)}, u32[]{:S(2)}, u32[]{:S(2)}) collective-permute-start(bf16[512,128]{1,0:T(8,128)(2,1)S(1)} %bitcast.26), channel_id=1, source_target_pairs={{0,3},{1,2},{2,1},{3,0},{4,7},{5,6},{6,5},{7,4},{8,11},{9,10},{10,... | collective-permute-start | bytes 393224 | tf_op jit(solution)/shard_map/ppermute | solution.py:20
  47.0 7.2 %collective-permute-start.10 = (bf16[512,128]{1,0:T(8,128)(2,1)S(1)}, bf16[512,128]{1,0:T(8,128)(2,1)S(1)}, u32[]{:S(2)}, u32[]{:S(2)}) collective-permute-start(bf16[512,128]{1,0:T(8,128)(2,1)S(1)} %bitcast.27), channel_id=1, source_target_pairs={{0,2},{1,3},{2,0},{3,1},{4,6},{5,7},{6,4},{7,5},{8,10},{9,11},{10,... | collective-permute-start | bytes 393224 | tf_op jit(solution)/shard_map/ppermute | solution.py:20
  47.8 6.7 %collective-permute-start.9 = (bf16[512,128]{1,0:T(8,128)(2,1)S(1)}, bf16[512,128]{1,0:T(8,128)(2,1)}, u32[]{:S(2)}, u32[]{:S(2)}) collective-permute-start(bf16[512,128]{1,0:T(8,128)(2,1)S(1)} %bitcast.28), channel_id=1, source_target_pairs={{0,1},{1,0},{2,3},{3,2},{4,5},{5,4},{6,7},{7,6},{8,9},{9,8},{10,11... | collective-permute-start | bytes 393224 | tf_op jit(solution)/shard_map/ppermute | solution.py:20

commit v4 on v3

--- a/solution.py
+++ b/solution.py
@@ -21,8 +21,14 @@
     return got
 
 
+def pair_up(slots):
+    ngroups, nslots = slots.shape[:2]
+    pairs = slots.reshape((ngroups // 2, 2) + slots.shape[1:])
+    return (pairs[:, 0] + jnp.flip(pairs[:, 1], axis=1)).reshape((ngroups // 2 * nslots,) + slots.shape[2:])
+
+
 def body(orbitals, potential, fitted, points):
-    if lax.axis_size("grid") > 8:
+    if lax.axis_size("grid") > 8 or lax.axis_size("grid") % 2 or points.shape[0] > orbitals.shape[1]:
         return body_spread(orbitals, potential, fitted, points)
     rows = orbitals.shape[0]
     block_width = orbitals.shape[1]
@@ -35,14 +41,21 @@
     psi = jnp.concatenate(band_swap(orbitals), 1)
     fitted_got = jnp.stack(band_swap(fitted), 0)
     fitted_all = jnp.take(fitted_got, jnp.arange(nbands, dtype=jnp.int32) ^ band, axis=0)
-    fitted_all = fitted_all.reshape(-1, fitted.shape[1]).astype(jnp.float32)
+    fitted_all = fitted_all.reshape(ngroups // 2, 2, points.shape[0], fitted.shape[1])
     pot = potential[:, None]
     sq = None
     for step in range(ITERS):
         if sq is None:
             own_b = orbitals.astype(jnp.bfloat16)
+            nslots = points.shape[0]
             selected = jnp.where(valid_mask[:, None], own_b[safe_idx], jnp.zeros((), jnp.bfloat16))
-            coll = jnp.concatenate(band_swap(grid_gather(selected)), 1)
+            filled = jnp.pad(valid_mask.astype(jnp.bfloat16), (0, block_width - nslots))
+            got = grid_gather(jnp.concatenate([selected, filled[None]], 0)).reshape(ngroups, nslots + 1, block_width)
+            coll = jnp.concatenate(band_swap(pair_up(got[:, :nslots])), 1)
+            first_filled = got[:, nslots, :nslots].reshape(ngroups // 2, 2, nslots)[:, 0] > 0
+            fitted_all = jnp.where(
+                first_filled[:, :, None], fitted_all[:, 0], jnp.flip(fitted_all[:, 1], axis=1)
+            ).reshape(-1, fitted.shape[1]).astype(jnp.float32)
             orbital_block = psi.astype(jnp.bfloat16)
         else:
             own = psi[:, :block_width]
@@ -52,7 +65,7 @@
             got = grid_gather(payload).reshape(ngroups, nslots + nbands, block_width)
             total = jnp.sum(got[:, nslots:], axis=0).reshape(total_orbitals)
             scale = lax.rsqrt(total / (rows * ngroups) + 1e-06)
-            coll_own = (got[:, :nslots] * scale[:block_width]).astype(jnp.bfloat16).reshape(-1, block_width)
+            coll_own = pair_up((got[:, :nslots] * scale[:block_width]).astype(jnp.bfloat16))
             coll = jnp.concatenate(band_swap(coll_own), 1)
             psi = psi * scale
             orbital_block = psi.astype(jnp.bfloat16)

time: 67.5 us -> 60.9 us (0.902)
  waiting for transfers between devices: 15.8 us -> 11.9 us
  matrix products: 4.46 us -> 2.1 us
    all_to_all x1, waiting for transfers between devices: 6.3 us -> 2.24 us  [grid_gather(): got = lax.all_to_all(sent, 'grid', 0, 0, tiled=True)]
    dot_general x2, matrix products: 3.12 us -> 0.98 us  [body(): lax.dot_general(tile_blocks, coll, (((0,), (0,)), ((), ())), preferred_el...]
  transfers between devices with their start and end apart: 13 -> 13, of which waited for: 5 -> 6; matrix products, arithmetic and copies ran while one was open for 8% -> 8% of each run, Pallas kernels for 0% -> 0%
where the time goes in v4:
time: 60.9 us; the launch traced here: 60.6 us
  blocking collectives  24.5 us (40%)
  starting transfers between devices  15.3 us (25%)
  waiting for transfers between devices  11.9 us (20%)
  local copies, waits for them, and re-layouts  3.5 us (6%)
  other arithmetic  2.97 us (5%)
  matrix products  2.1 us (3%)
    all_to_all x2, blocking collectives, grid_gather(): got = lax.all_to_all(sent, 'grid', 0, 0, tiled=True)  24.5 us
    ppermute x12, waiting for transfers between devices, band_swap(): got.append(lax.ppermute(x, 'band', [(i, i ^ k) for i in range(nbands)]))  9.66 us
    ppermute x12, starting transfers between devices, band_swap(): got.append(lax.ppermute(x, 'band', [(i, i ^ k) for i in range(nbands)]))  9.35 us
    all_to_all x1, starting transfers between devices, grid_gather(): got = lax.all_to_all(sent, 'grid', 0, 0, tiled=True)  5.96 us
    all_to_all x1, waiting for transfers between devices, grid_gather(): got = lax.all_to_all(sent, 'grid', 0, 0, tiled=True)  2.24 us
  transfers between devices with their start and end apart: 13, of which 6 were waited for; matrix products, arithmetic and copies ran while one was open for 8% of the time, Pallas kernels for 0%

profile of v4, /device:TPU:0, one launch (start us, length us, event | category | flops | bytes accessed | tf_op | source)
XLA Modules:
  0.0 60.6 jit_solution(1355913239798761246)
XLA Ops:
  0.0 0.5 collective-permute-start.3
  0.5 2.6 %collective-permute-start.5 = (bf16[128,256]{1,0:T(8,128)(2,1)}, bf16[128,256]{1,0:T(8,128)(2,1)S(1)}, u32[]{:S(2)}, u32[]{:S(2)}) collective-permute-start(bf16[128,256]{1,0:T(8,128)(2,1)} %param.6), channel_id=1, source_target_pairs={{0,3},{1,2},{2,1},{3,0},{4,7},{5,6},{6,5},{7,4},{8,11},{9,10},{10,... | collective-permute-start | bytes 196616 | tf_op jit(solution)/shard_map/ppermute | solution.py:20
  3.1 0.1 collective-permute-start.4
  3.1 2.0 %collective-permute-start.1 = (f32[256,128]{1,0:T(8,128)}, f32[256,128]{1,0:T(8,128)S(1)}, u32[]{:S(2)}, u32[]{:S(2)}) collective-permute-start(f32[256,128]{1,0:T(8,128)} %param.4), channel_id=1, source_target_pairs={{0,2},{1,3},{2,0},{3,1},{4,6},{5,7},{6,4},{7,5},{8,10},{9,11},{10,... | collective-permute-start | bytes 393224 | tf_op jit(solution)/shard_map/ppermute | solution.py:20
  5.1 0.0 collective-permute-start
  5.1 0.7 %broadcast_compare_fusion = pred[64]{0:T(512)(128)(4,1)S(1)} fusion(s32[64]{0:T(128)} %param.7), kind=kLoop, calls=%fused_computation.107 | loop fusion | flops 64 | bytes 320 | tf_op jit(solution)/shard_map/ge | solution.py:39
  5.8 1.0 %fusion.67 = (bf16[256,128]{1,0:T(8,128)(2,1)S(1)}, f32[256,512]{1,0:T(8,128)S(1)}) fusion(f32[256,128]{1,0:T(8,128)} %param.4), kind=kLoop, calls=%fused_computation.113 | loop fusion | flops 32767 | bytes 327680 | tf_op jit(solution)/shard_map/convert_element_type | solution.py:49
  6.8 0.6 %gather_fusion = bf16[64,128]{1,0:T(8,128)(2,1)S(1)} fusion(bf16[256,128]{1,0:T(8,128)(2,1)S(1)} %get-tuple-element.5, s32[1024]{0:T(1024)S(1)} %pad_clamp_fusion.1), kind=kCustom, calls=%fused_computation | custom fusion | bytes 33024 | tf_op jit(solution)/shard_map/gather | solution.py:51
  7.4 0.1 broadcast_select_fusion.1
  7.5 0.7 %broadcast_in_dim.81 = bf16[8,65,128]{2,1,0:T(8,128)(2,1)} broadcast(bf16[65,128]{1,0:T(8,128)(2,1)S(1)} %pad_maximum_fusion.2), dimensions={1,2} | broadcast | bytes 149760 | tf_op jit(solution)/shard_map/broadcast_in_dim | solution.py:11
  8.2 6.0 %all-to-all-start = ((bf16[8,65,128]{2,1,0:T(8,128)(2,1)}), bf16[8,65,128]{2,1,0:T(8,128)(2,1)S(1)}, u32[]{:S(2)}, u32[]{:S(2)}) async-start(bf16[8,65,128]{2,1,0:T(8,128)(2,1)} %broadcast_in_dim.81), calls=%async_computation | async-start | bytes 294912 | tf_op jit(solution)/shard_map/all_to_all | solution.py:12
  14.2 0.0 collective-permute-done.3
  14.2 0.4 collective-permute-start.2
  14.6 0.0 collective-permute-done.5
  14.7 0.0 collective-permute-done.4
  14.7 0.6 gather_fusion.1
  15.3 0.1 copy_select_fusion
  15.4 0.1 rev.11
  15.5 0.0 collective-permute-done
  15.6 4.2 %collective-permute-done.2 = f32[256,128]{1,0:T(8,128)S(1)} collective-permute-done((f32[256,128]{1,0:T(8,128)S(1)}, f32[256,128]{1,0:T(8,128)S(1)}, u32[]{:S(2)}, u32[]{:S(2)}) %collective-permute-start.2) | collective-permute-done | bytes 131104 | tf_op jit(solution)/shard_map/ppermute | solution.py:20
  19.8 2.2 %all-to-all-done = bf16[8,65,128]{2,1,0:T(8,128)(2,1)S(1)} async-done(((bf16[8,65,128]{2,1,0:T(8,128)(2,1)}), bf16[8,65,128]{2,1,0:T(8,128)(2,1)S(1)}, u32[]{:S(2)}, u32[]{:S(2)}) %all-to-all-start) | async-done | bytes 133152 | tf_op jit(solution)/shard_map/all_to_all | solution.py:12
  22.1 0.1 collective-permute-start.8
  22.2 0.6 collective-permute-start.7
  22.8 1.2 %collective-permute-start.6 = (bf16[256,128]{1,0:T(8,128)(2,1)S(1)}, bf16[256,128]{1,0:T(8,128)(2,1)S(1)}, u32[]{:S(2)}, u32[]{:S(2)}) collective-permute-start(bf16[256,128]{1,0:T(8,128)(2,1)S(1)} %bitcast.65), channel_id=1, source_target_pairs={{0,1},{1,0},{2,3},{3,2},{4,5},{5,4},{6,7},{7,6},{8,9},{9,8},{10,11... | collective-permute-start | bytes 196616 | tf_op jit(solution)/shard_map/ppermute | solution.py:20
  24.1 0.1 fusion.45
  24.2 1.8 %collective-permute-done.8 = bf16[256,128]{1,0:T(8,128)(2,1)S(1)} collective-permute-done((bf16[256,128]{1,0:T(8,128)(2,1)S(1)}, bf16[256,128]{1,0:T(8,128)(2,1)S(1)}, u32[]{:S(2)}, u32[]{:S(2)}) %collective-permute-start.8) | collective-permute-done | bytes 65568 | tf_op jit(solution)/shard_map/ppermute | solution.py:20
  26.0 0.2 fusion.11
  26.2 1.0 %collective-permute-done.7 = bf16[256,128]{1,0:T(8,128)(2,1)S(1)} collective-permute-done((bf16[256,128]{1,0:T(8,128)(2,1)S(1)}, bf16[256,128]{1,0:T(8,128)(2,1)S(1)}, u32[]{:S(2)}, u32[]{:S(2)}) %collective-permute-start.7) | collective-permute-done | bytes 65568 | tf_op jit(solution)/shard_map/ppermute | solution.py:20
  27.2 0.2 fusion.9
  27.4 0.2 fusion.7
  27.6 0.0 copy-start.2
  27.6 0.7 %copy-done.2 = f32[256]{0:T(256)S(1)} copy-done((f32[256]{0:T(256)S(1)}, f32[256]{0:T(256)}, u32[]{:S(2)}) %copy-start.2) | copy-done | bytes 1048
  28.3 0.5 multiply_reduce_fusion.1
  28.8 0.6 gather_fusion.2
  29.4 0.1 broadcast_select_fusion
  29.5 14.9 %all_to_all.15 = f32[8,68,128]{2,1,0:T(8,128)S(1)} all-to-all(f32[8,68,128]{2,1,0:T(8,128)S(1)} %broadcast_in_dim.86), channel_id=1, replica_groups=mesh['grid'=8,'band'=4] {'grid'}, dimensions={0} | all-to-all | bytes 557056 | tf_op jit(solution)/shard_map/all_to_all | solution.py:12
  44.5 0.1 collective-permute-start.11
  44.6 0.6 collective-permute-start.10
  45.2 1.3 %collective-permute-start.9 = (bf16[256,128]{1,0:T(8,128)(2,1)S(1)}, bf16[256,128]{1,0:T(8,128)(2,1)S(1)}, u32[]{:S(2)}, u32[]{:S(2)}) collective-permute-start(bf16[256,128]{1,0:T(8,128)(2,1)S(1)} %bitcast.58), channel_id=1, source_target_pairs={{0,1},{1,0},{2,3},{3,2},{4,5},{5,4},{6,7},{7,6},{8,9},{9,8},{10,11... | collective-permute-start | bytes 196616 | tf_op jit(solution)/shard_map/ppermute | solution.py:20
  46.5 0.2 fusion.13
  46.7 1.7 %collective-permute-done.11 = bf16[256,128]{1,0:T(8,128)(2,1)S(1)} collective-permute-done((bf16[256,128]{1,0:T(8,128)(2,1)S(1)}, bf16[256,128]{1,0:T(8,128)(2,1)S(1)}, u32[]{:S(2)}, u32[]{:S(2)}) %collective-permute-start.11) | collective-permute-done | bytes 65568 | tf_op jit(solution)/shard_map/ppermute | solution.py:20
  48.4 0.2 fusion.23
  48.6 1.0 %collective-permute-done.10 = bf16[256,128]{1,0:T(8,128)(2,1)S(1)} collective-permute-done((bf16[256,128]{1,0:T(8,128)(2,1)S(1)}, bf16[256,128]{1,0:T(8,128)(2,1)S(1)}, u32[]{:S(2)}, u32[]{:S(2)}) %collective-permute-start.10) | collective-permute-done | bytes 65568 | tf_op jit(solution)/shard_map/ppermute | solution.py:20
  49.6 0.2 fusion.21
  49.8 0.0 collective-permute-done.9
  49.8 0.5 multiply_reduce_fusion
  50.3 9.6 %all_to_all.16 = f32[8,1,128]{2,1,0:T(1,128)S(1)} all-to-all(f32[8,1,128]{2,1,0:T(1,128)S(1)} %broadcast_in_dim.87), channel_id=1, replica_groups=mesh['grid'=8,'band'=4] {'grid'}, dimensions={0} | all-to-all | bytes 8192 | tf_op jit(solution)/shard_map/all_to_all | solution.py:12
  59.9 0.7 %slice_multiply_fusion.1 = f32[256,128]{1,0:T(8,128)} fusion(f32[256,512]{1,0:T(8,128)S(1)} %get-tuple-element.12, f32[128]{0:T(128)S(1)} %add_rsqrt_fusion.1), kind=kLoop, calls=%fused_computation.64 | loop fusion | flops 32768 | bytes 262656 | tf_op jit(solution)/shard_map/mul | solution.py:89
  (44 shorter events, 0.5 us)
Async XLA Ops:
  0.0 5.7 %copy-start.3 = (s32[64]{0:T(128)S(1)}, s32[64]{0:T(128)}, u32[]{:S(2)}) copy-start(s32[64]{0:T(128)} %param.7) | copy-start | bytes 772
  0.0 14.2 %collective-permute-start.3 = (bf16[128,256]{1,0:T(8,128)(2,1)}, bf16[128,256]{1,0:T(8,128)(2,1)S(1)}, u32[]{:S(2)}, u32[]{:S(2)}) collective-permute-start(bf16[128,256]{1,0:T(8,128)(2,1)} %param.6), channel_id=1, source_target_pairs={{0,1},{1,0},{2,3},{3,2},{4,5},{5,4},{6,7},{7,6},{8,9},{9,8},{10,11... | collective-permute-start | bytes 196616 | tf_op jit(solution)/shard_map/ppermute | solution.py:20
  0.5 14.2 %collective-permute-start.5 = (bf16[128,256]{1,0:T(8,128)(2,1)}, bf16[128,256]{1,0:T(8,128)(2,1)S(1)}, u32[]{:S(2)}, u32[]{:S(2)}) collective-permute-start(bf16[128,256]{1,0:T(8,128)(2,1)} %param.6), channel_id=1, source_target_pairs={{0,3},{1,2},{2,1},{3,0},{4,7},{5,6},{6,5},{7,4},{8,11},{9,10},{10,... | collective-permute-start | bytes 196616 | tf_op jit(solution)/shard_map/ppermute | solution.py:20
  3.1 11.6 %collective-permute-start.4 = (bf16[128,256]{1,0:T(8,128)(2,1)}, bf16[128,256]{1,0:T(8,128)(2,1)S(1)}, u32[]{:S(2)}, u32[]{:S(2)}) collective-permute-start(bf16[128,256]{1,0:T(8,128)(2,1)} %param.6), channel_id=1, source_target_pairs={{0,2},{1,3},{2,0},{3,1},{4,6},{5,7},{6,4},{7,5},{8,10},{9,11},{10,... | collective-permute-start | bytes 196616 | tf_op jit(solution)/shard_map/ppermute | solution.py:20
  3.1 12.5 %collective-permute-start.1 = (f32[256,128]{1,0:T(8,128)}, f32[256,128]{1,0:T(8,128)S(1)}, u32[]{:S(2)}, u32[]{:S(2)}) collective-permute-start(f32[256,128]{1,0:T(8,128)} %param.4), channel_id=1, source_target_pairs={{0,2},{1,3},{2,0},{3,1},{4,6},{5,7},{6,4},{7,5},{8,10},{9,11},{10,... | collective-permute-start | bytes 393224 | tf_op jit(solution)/shard_map/ppermute | solution.py:20
  5.1 10.5 %collective-permute-start = (f32[256,128]{1,0:T(8,128)}, f32[256,128]{1,0:T(8,128)S(1)}, u32[]{:S(2)}, u32[]{:S(2)}) collective-permute-start(f32[256,128]{1,0:T(8,128)} %param.4), channel_id=1, source_target_pairs={{0,1},{1,0},{2,3},{3,2},{4,5},{5,4},{6,7},{7,6},{8,9},{9,8},{10,11... | collective-permute-start | bytes 393224 | tf_op jit(solution)/shard_map/ppermute | solution.py:20
  8.2 6.0 %copy-start = (f32[256,128]{1,0:T(8,128)S(1)}, f32[256,128]{1,0:T(8,128)}, u32[]{:S(2)}) copy-start(f32[256,128]{1,0:T(8,128)} %param.4) | copy-start | bytes 393220
  8.2 6.5 %copy-start.1 = (bf16[128,256]{1,0:T(8,128)(2,1)S(1)}, bf16[128,256]{1,0:T(8,128)(2,1)}, u32[]{:S(2)}) copy-start(bf16[128,256]{1,0:T(8,128)(2,1)} %param.6) | copy-start | bytes 196612
  8.2 13.9 %all-to-all-start = ((bf16[8,65,128]{2,1,0:T(8,128)(2,1)}), bf16[8,65,128]{2,1,0:T(8,128)(2,1)S(1)}, u32[]{:S(2)}, u32[]{:S(2)}) async-start(bf16[8,65,128]{2,1,0:T(8,128)(2,1)} %broadcast_in_dim.81), calls=%async_computation | async-start | bytes 294912 | tf_op jit(solution)/shard_map/all_to_all | solution.py:12
  14.2 5.5 %collective-permute-start.2 = (f32[256,128]{1,0:T(8,128)S(1)}, f32[256,128]{1,0:T(8,128)S(1)}, u32[]{:S(2)}, u32[]{:S(2)}) collective-permute-start(f32[256,128]{1,0:T(8,128)S(1)} %copy-done), channel_id=1, source_target_pairs={{0,3},{1,2},{2,1},{3,0},{4,7},{5,6},{6,5},{7,4},{8,11},{9,10},{10,... | collective-permute-start | bytes 393224 | tf_op jit(solution)/shard_map/ppermute | solution.py:20
  22.1 3.8 %collective-permute-start.8 = (bf16[256,128]{1,0:T(8,128)(2,1)S(1)}, bf16[256,128]{1,0:T(8,128)(2,1)S(1)}, u32[]{:S(2)}, u32[]{:S(2)}) collective-permute-start(bf16[256,128]{1,0:T(8,128)(2,1)S(1)} %bitcast.63), channel_id=1, source_target_pairs={{0,3},{1,2},{2,1},{3,0},{4,7},{5,6},{6,5},{7,4},{8,11},{9,10},{10,... | collective-permute-start | bytes 196616 | tf_op jit(solution)/shard_map/ppermute | solution.py:20
  22.2 5.0 %collective-permute-start.7 = (bf16[256,128]{1,0:T(8,128)(2,1)S(1)}, bf16[256,128]{1,0:T(8,128)(2,1)S(1)}, u32[]{:S(2)}, u32[]{:S(2)}) collective-permute-start(bf16[256,128]{1,0:T(8,128)(2,1)S(1)} %bitcast.64), channel_id=1, source_target_pairs={{0,2},{1,3},{2,0},{3,1},{4,6},{5,7},{6,4},{7,5},{8,10},{9,11},{10,... | collective-permute-start | bytes 196616 | tf_op jit(solution)/shard_map/ppermute | solution.py:20
  22.8 4.6 %collective-permute-start.6 = (bf16[256,128]{1,0:T(8,128)(2,1)S(1)}, bf16[256,128]{1,0:T(8,128)(2,1)S(1)}, u32[]{:S(2)}, u32[]{:S(2)}) collective-permute-start(bf16[256,128]{1,0:T(8,128)(2,1)S(1)} %bitcast.65), channel_id=1, source_target_pairs={{0,1},{1,0},{2,3},{3,2},{4,5},{5,4},{6,7},{7,6},{8,9},{9,8},{10,11... | collective-permute-start | bytes 196616 | tf_op jit(solution)/shard_map/ppermute | solution.py:20
  27.6 0.7 %copy-start.2 = (f32[256]{0:T(256)S(1)}, f32[256]{0:T(256)}, u32[]{:S(2)}) copy-start(f32[256]{0:T(256)} %param.5) | copy-start | bytes 3076
  44.5 3.8 %collective-permute-start.11 = (bf16[256,128]{1,0:T(8,128)(2,1)S(1)}, bf16[256,128]{1,0:T(8,128)(2,1)S(1)}, u32[]{:S(2)}, u32[]{:S(2)}) collective-permute-start(bf16[256,128]{1,0:T(8,128)(2,1)S(1)} %bitcast.56), channel_id=1, source_target_pairs={{0,3},{1,2},{2,1},{3,0},{4,7},{5,6},{6,5},{7,4},{8,11},{9,10},{10,... | collective-permute-start | bytes 196616 | tf_op jit(solution)/shard_map/ppermute | solution.py:20
  44.6 5.0 %collective-permute-start.10 = (bf16[256,128]{1,0:T(8,128)(2,1)S(1)}, bf16[256,128]{1,0:T(8,128)(2,1)S(1)}, u32[]{:S(2)}, u32[]{:S(2)}) collective-permute-start(bf16[256,128]{1,0:T(8,128)(2,1)S(1)} %bitcast.57), channel_id=1, source_target_pairs={{0,2},{1,3},{2,0},{3,1},{4,6},{5,7},{6,4},{7,5},{8,10},{9,11},{10,... | collective-permute-start | bytes 196616 | tf_op jit(solution)/shard_map/ppermute | solution.py:20
  45.2 4.6 %collective-permute-start.9 = (bf16[256,128]{1,0:T(8,128)(2,1)S(1)}, bf16[256,128]{1,0:T(8,128)(2,1)S(1)}, u32[]{:S(2)}, u32[]{:S(2)}) collective-permute-start(bf16[256,128]{1,0:T(8,128)(2,1)S(1)} %bitcast.58), channel_id=1, source_target_pairs={{0,1},{1,0},{2,3},{3,2},{4,5},{5,4},{6,7},{7,6},{8,9},{9,8},{10,11... | collective-permute-start | bytes 196616 | tf_op jit(solution)/shard_map/ppermute | solution.py:20

commit v5 on v4

--- a/solution.py
+++ b/solution.py
@@ -6,11 +6,18 @@
 ITERS = 2
 
 
+def grid_copies(x):
+    ngroups = lax.axis_size("grid")
+    return jnp.broadcast_to(x[None], (ngroups,) + x.shape)
+
+
+def grid_exchange(sent):
+    got = lax.all_to_all(sent, "grid", 0, 0, tiled=True)
+    return got.reshape((sent.shape[0] * sent.shape[1],) + sent.shape[2:])
+
+
 def grid_gather(x):
-    ngroups = lax.axis_size("grid")
-    sent = jnp.broadcast_to(x[None], (ngroups,) + x.shape)
-    got = lax.all_to_all(sent, "grid", 0, 0, tiled=True)
-    return got.reshape((ngroups * x.shape[0],) + x.shape[1:])
+    return grid_exchange(grid_copies(x))
 
 
 def band_swap(x):
@@ -38,10 +45,6 @@
     total_orbitals = block_width * nbands
     valid_mask = points >= 0
     safe_idx = jnp.where(valid_mask, points, 0)
-    psi = jnp.concatenate(band_swap(orbitals), 1)
-    fitted_got = jnp.stack(band_swap(fitted), 0)
-    fitted_all = jnp.take(fitted_got, jnp.arange(nbands, dtype=jnp.int32) ^ band, axis=0)
-    fitted_all = fitted_all.reshape(ngroups // 2, 2, points.shape[0], fitted.shape[1])
     pot = potential[:, None]
     sq = None
     for step in range(ITERS):
@@ -50,7 +53,13 @@
             nslots = points.shape[0]
             selected = jnp.where(valid_mask[:, None], own_b[safe_idx], jnp.zeros((), jnp.bfloat16))
             filled = jnp.pad(valid_mask.astype(jnp.bfloat16), (0, block_width - nslots))
-            got = grid_gather(jnp.concatenate([selected, filled[None]], 0)).reshape(ngroups, nslots + 1, block_width)
+            payload = jnp.concatenate([selected, filled[None]], 0)
+            sent, rows_own, fitted_own = lax.optimization_barrier((grid_copies(payload), orbitals, fitted))
+            got = grid_exchange(sent).reshape(ngroups, nslots + 1, block_width)
+            psi = jnp.concatenate(band_swap(rows_own), 1)
+            fitted_got = jnp.stack(band_swap(fitted_own), 0)
+            fitted_all = jnp.take(fitted_got, jnp.arange(nbands, dtype=jnp.int32) ^ band, axis=0)
+            fitted_all = fitted_all.reshape(ngroups // 2, 2, nslots, fitted.shape[1])
             coll = jnp.concatenate(band_swap(pair_up(got[:, :nslots])), 1)
             first_filled = got[:, nslots, :nslots].reshape(ngroups // 2, 2, nslots)[:, 0] > 0
             fitted_all = jnp.where(

time: 60.9 us -> 59.9 us (0.984)
  blocking collectives: 24.5 us -> 22.5 us
  waiting for transfers between devices: 11.9 us -> 13.2 us
    all_to_all x1, waiting for transfers between devices: 2.24 us -> 5.65 us  [grid_exchange(): got = lax.all_to_all(sent, 'grid', 0, 0, tiled=True)]
    ppermute x12, waiting for transfers between devices: 9.66 us -> 7.51 us  [band_swap(): got.append(lax.ppermute(x, 'band', [(i, i ^ k) for i in range(nbands)]))]
    all_to_all x2, blocking collectives: 24.5 us -> 22.5 us  [grid_exchange(): got = lax.all_to_all(sent, 'grid', 0, 0, tiled=True)]
  transfers between devices with their start and end apart: 13 -> 13, of which waited for: 6 -> 7; matrix products, arithmetic and copies ran while one was open for 8% -> 3% of each run, Pallas kernels for 0% -> 0%
where the time goes in v5:
time: 59.9 us; the launch traced here: 59.5 us
  blocking collectives  22.5 us (38%)
  starting transfers between devices  14.9 us (25%)
  waiting for transfers between devices  13.2 us (22%)
  local copies, waits for them, and re-layouts  3.66 us (6%)
  other arithmetic  2.96 us (5%)
  matrix products  2.09 us (3%)
    all_to_all x2, blocking collectives, grid_exchange(): got = lax.all_to_all(sent, 'grid', 0, 0, tiled=True)  22.5 us
    ppermute x12, starting transfers between devices, band_swap(): got.append(lax.ppermute(x, 'band', [(i, i ^ k) for i in range(nbands)]))  9.04 us
    ppermute x12, waiting for transfers between devices, band_swap(): got.append(lax.ppermute(x, 'band', [(i, i ^ k) for i in range(nbands)]))  7.51 us
    all_to_all x1, starting transfers between devices, grid_exchange(): got = lax.all_to_all(sent, 'grid', 0, 0, tiled=True)  5.82 us
    all_to_all x1, waiting for transfers between devices, grid_exchange(): got = lax.all_to_all(sent, 'grid', 0, 0, tiled=True)  5.65 us
  transfers between devices with their start and end apart: 13, of which 7 were waited for; matrix products, arithmetic and copies ran while one was open for 3% of the time, Pallas kernels for 0%

profile of v5, /device:TPU:0, one launch (start us, length us, event | category | flops | bytes accessed | tf_op | source)
XLA Modules:
  0.0 59.5 jit_solution(18225009313632390643)
XLA Ops:
  0.0 0.7 %broadcast_compare_fusion = pred[64]{0:T(512)(128)(4,1)S(1)} fusion(s32[64]{0:T(128)} %param.7), kind=kLoop, calls=%fused_computation.107 | loop fusion | flops 64 | bytes 320 | tf_op jit(solution)/shard_map/ge | solution.py:46
  0.8 0.9 %convert_element_type.75 = bf16[256,128]{1,0:T(8,128)(2,1)S(1)} convert(f32[256,128]{1,0:T(8,128)} %param.4) | non-fusion elementwise | flops 32768 | bytes 196608 | tf_op jit(solution)/shard_map/convert_element_type | solution.py:52
  1.7 0.6 %gather_fusion = bf16[64,128]{1,0:T(8,128)(2,1)S(1)} fusion(bf16[256,128]{1,0:T(8,128)(2,1)S(1)} %convert_element_type.75, s32[1024]{0:T(1024)S(1)} %pad_clamp_fusion.1), kind=kCustom, calls=%fused_computation | custom fusion | bytes 33024 | tf_op jit(solution)/shard_map/gather | solution.py:54
  2.3 0.1 broadcast_select_fusion.1
  2.4 0.0 copy-start.1
  2.4 0.7 %broadcast_in_dim.81 = bf16[8,65,128]{2,1,0:T(8,128)(2,1)} broadcast(bf16[65,128]{1,0:T(8,128)(2,1)S(1)} %pad_maximum_fusion.2), dimensions={1,2} | broadcast | bytes 149760 | tf_op jit(solution)/shard_map/broadcast_in_dim | solution.py:11
  3.1 0.2 copy-done.1
  3.3 2.4 %collective-permute-start.5 = (bf16[128,256]{1,0:T(8,128)(2,1)S(1)}, bf16[128,256]{1,0:T(8,128)(2,1)S(1)}, u32[]{:S(2)}, u32[]{:S(2)}) collective-permute-start(bf16[128,256]{1,0:T(8,128)(2,1)S(1)} %copy-done.1), channel_id=1, source_target_pairs={{0,3},{1,2},{2,1},{3,0},{4,7},{5,6},{6,5},{7,4},{8,11},{9,10},{10,... | collective-permute-start | bytes 196616 | tf_op jit(solution)/shard_map/ppermute | solution.py:27
  5.6 0.6 collective-permute-start.4
  6.2 0.1 collective-permute-start.3
  6.3 1.5 %collective-permute-start.2 = (f32[256,128]{1,0:T(8,128)S(1)}, f32[256,128]{1,0:T(8,128)S(1)}, u32[]{:S(2)}, u32[]{:S(2)}) collective-permute-start(f32[256,128]{1,0:T(8,128)S(1)} %copy-done), channel_id=1, source_target_pairs={{0,3},{1,2},{2,1},{3,0},{4,7},{5,6},{6,5},{7,4},{8,11},{9,10},{10,... | collective-permute-start | bytes 393224 | tf_op jit(solution)/shard_map/ppermute | solution.py:27
  7.8 0.6 %collective-permute-start.1 = (f32[256,128]{1,0:T(8,128)S(1)}, f32[256,128]{1,0:T(8,128)S(1)}, u32[]{:S(2)}, u32[]{:S(2)}) collective-permute-start(f32[256,128]{1,0:T(8,128)S(1)} %copy-done), channel_id=1, source_target_pairs={{0,2},{1,3},{2,0},{3,1},{4,6},{5,7},{6,4},{7,5},{8,10},{9,11},{10,... | collective-permute-start | bytes 393224 | tf_op jit(solution)/shard_map/ppermute | solution.py:27
  8.4 5.8 %all-to-all-start = ((bf16[8,65,128]{2,1,0:T(8,128)(2,1)}), bf16[8,65,128]{2,1,0:T(8,128)(2,1)S(1)}, u32[]{:S(2)}, u32[]{:S(2)}) async-start(bf16[8,65,128]{2,1,0:T(8,128)(2,1)} %broadcast_in_dim.81), calls=%async_computation | async-start | bytes 294912 | tf_op jit(solution)/shard_map/all_to_all | solution.py:15
  14.3 0.1 collective-permute-start
  14.4 0.6 gather_fusion.1
  15.0 0.1 copy_select_fusion
  15.1 0.1 rev.11
  15.3 0.4 collective-permute-done
  15.7 0.2 collective-permute-done.1
  15.9 0.0 collective-permute-done.2
  16.0 5.7 %all-to-all-done = bf16[8,65,128]{2,1,0:T(8,128)(2,1)S(1)} async-done(((bf16[8,65,128]{2,1,0:T(8,128)(2,1)}), bf16[8,65,128]{2,1,0:T(8,128)(2,1)S(1)}, u32[]{:S(2)}, u32[]{:S(2)}) %all-to-all-start) | async-done | bytes 133152 | tf_op jit(solution)/shard_map/all_to_all | solution.py:15
  21.7 0.1 collective-permute-start.8
  21.8 1.6 %collective-permute-start.7 = (bf16[256,128]{1,0:T(8,128)(2,1)S(1)}, bf16[256,128]{1,0:T(8,128)(2,1)S(1)}, u32[]{:S(2)}, u32[]{:S(2)}) collective-permute-start(bf16[256,128]{1,0:T(8,128)(2,1)S(1)} %bitcast.64), channel_id=1, source_target_pairs={{0,2},{1,3},{2,0},{3,1},{4,6},{5,7},{6,4},{7,5},{8,10},{9,11},{10,... | collective-permute-start | bytes 196616 | tf_op jit(solution)/shard_map/ppermute | solution.py:27
  23.4 0.3 collective-permute-start.6
  23.7 0.1 fusion.45
  23.8 2.3 %collective-permute-done.8 = bf16[256,128]{1,0:T(8,128)(2,1)S(1)} collective-permute-done((bf16[256,128]{1,0:T(8,128)(2,1)S(1)}, bf16[256,128]{1,0:T(8,128)(2,1)S(1)}, u32[]{:S(2)}, u32[]{:S(2)}) %collective-permute-start.8) | collective-permute-done | bytes 65568 | tf_op jit(solution)/shard_map/ppermute | solution.py:27
  26.1 0.2 fusion.11
  26.3 1.3 %collective-permute-done.7 = bf16[256,128]{1,0:T(8,128)(2,1)S(1)} collective-permute-done((bf16[256,128]{1,0:T(8,128)(2,1)S(1)}, bf16[256,128]{1,0:T(8,128)(2,1)S(1)}, u32[]{:S(2)}, u32[]{:S(2)}) %collective-permute-start.7) | collective-permute-done | bytes 65568 | tf_op jit(solution)/shard_map/ppermute | solution.py:27
  27.6 0.2 fusion.9
  27.8 0.2 fusion.7
  28.0 0.0 copy-start.2
  28.0 0.7 %copy-done.2 = f32[256]{0:T(256)S(1)} copy-done((f32[256]{0:T(256)S(1)}, f32[256]{0:T(256)}, u32[]{:S(2)}) %copy-start.2) | copy-done | bytes 1048
  28.7 0.5 multiply_reduce_fusion.1
  29.2 0.6 %gather_fusion.2 = f32[64,128]{1,0:T(8,128)S(1)} fusion(f32[256,128]{1,0:T(8,128)S(1)} %slice.113, s32[1024]{0:T(1024)S(1)} %pad_clamp_fusion.1), kind=kCustom, calls=%fused_computation.2 | custom fusion | bytes 65792 | tf_op jit(solution)/shard_map/gather | solution.py:71
  29.8 0.1 broadcast_select_fusion
  29.9 13.2 %all_to_all.15 = f32[8,68,128]{2,1,0:T(8,128)S(1)} all-to-all(f32[8,68,128]{2,1,0:T(8,128)S(1)} %broadcast_in_dim.86), channel_id=1, replica_groups=mesh['grid'=8,'band'=4] {'grid'}, dimensions={0} | all-to-all | bytes 557056 | tf_op jit(solution)/shard_map/all_to_all | solution.py:15
  43.2 0.1 collective-permute-start.11
  43.3 1.4 %collective-permute-start.10 = (bf16[256,128]{1,0:T(8,128)(2,1)S(1)}, bf16[256,128]{1,0:T(8,128)(2,1)S(1)}, u32[]{:S(2)}, u32[]{:S(2)}) collective-permute-start(bf16[256,128]{1,0:T(8,128)(2,1)S(1)} %bitcast.57), channel_id=1, source_target_pairs={{0,2},{1,3},{2,0},{3,1},{4,6},{5,7},{6,4},{7,5},{8,10},{9,11},{10,... | collective-permute-start | bytes 196616 | tf_op jit(solution)/shard_map/ppermute | solution.py:27
  44.7 0.5 collective-permute-start.9
  45.2 0.2 fusion.13
  45.4 2.3 %collective-permute-done.11 = bf16[256,128]{1,0:T(8,128)(2,1)S(1)} collective-permute-done((bf16[256,128]{1,0:T(8,128)(2,1)S(1)}, bf16[256,128]{1,0:T(8,128)(2,1)S(1)}, u32[]{:S(2)}, u32[]{:S(2)}) %collective-permute-start.11) | collective-permute-done | bytes 65568 | tf_op jit(solution)/shard_map/ppermute | solution.py:27
  47.7 0.2 fusion.23
  47.9 1.0 %collective-permute-done.10 = bf16[256,128]{1,0:T(8,128)(2,1)S(1)} collective-permute-done((bf16[256,128]{1,0:T(8,128)(2,1)S(1)}, bf16[256,128]{1,0:T(8,128)(2,1)S(1)}, u32[]{:S(2)}, u32[]{:S(2)}) %collective-permute-start.10) | collective-permute-done | bytes 65568 | tf_op jit(solution)/shard_map/ppermute | solution.py:27
  48.9 0.2 fusion.21
  49.0 0.0 collective-permute-done.9
  49.1 0.5 multiply_reduce_fusion
  49.6 9.3 %all_to_all.16 = f32[8,1,128]{2,1,0:T(1,128)S(1)} all-to-all(f32[8,1,128]{2,1,0:T(1,128)S(1)} %broadcast_in_dim.87), channel_id=1, replica_groups=mesh['grid'=8,'band'=4] {'grid'}, dimensions={0} | all-to-all | bytes 8192 | tf_op jit(solution)/shard_map/all_to_all | solution.py:15
  58.9 0.7 %slice_multiply_fusion.1 = f32[256,128]{1,0:T(8,128)} fusion(f32[256,512]{1,0:T(8,128)S(1)} %get-tuple-element.16, f32[128]{0:T(128)S(1)} %add_rsqrt_fusion.1), kind=kLoop, calls=%fused_computation.64 | loop fusion | flops 32768 | bytes 262656 | tf_op jit(solution)/shard_map/mul | solution.py:98
  (45 shorter events, 0.5 us)
Async XLA Ops:
  0.0 0.7 %copy-start.3 = (s32[64]{0:T(128)S(1)}, s32[64]{0:T(128)}, u32[]{:S(2)}) copy-start(s32[64]{0:T(128)} %param.7) | copy-start | bytes 772
  2.3 4.0 %copy-start = (f32[256,128]{1,0:T(8,128)S(1)}, f32[256,128]{1,0:T(8,128)}, u32[]{:S(2)}) copy-start(f32[256,128]{1,0:T(8,128)} %param.4) | copy-start | bytes 393220
  2.4 0.8 %copy-start.1 = (bf16[128,256]{1,0:T(8,128)(2,1)S(1)}, bf16[128,256]{1,0:T(8,128)(2,1)}, u32[]{:S(2)}) copy-start(bf16[128,256]{1,0:T(8,128)(2,1)} %param.6) | copy-start | bytes 196612
  3.3 11.0 %collective-permute-start.5 = (bf16[128,256]{1,0:T(8,128)(2,1)S(1)}, bf16[128,256]{1,0:T(8,128)(2,1)S(1)}, u32[]{:S(2)}, u32[]{:S(2)}) collective-permute-start(bf16[128,256]{1,0:T(8,128)(2,1)S(1)} %copy-done.1), channel_id=1, source_target_pairs={{0,3},{1,2},{2,1},{3,0},{4,7},{5,6},{6,5},{7,4},{8,11},{9,10},{10,... | collective-permute-start | bytes 196616 | tf_op jit(solution)/shard_map/ppermute | solution.py:27
  5.6 8.7 %collective-permute-start.4 = (bf16[128,256]{1,0:T(8,128)(2,1)S(1)}, bf16[128,256]{1,0:T(8,128)(2,1)S(1)}, u32[]{:S(2)}, u32[]{:S(2)}) collective-permute-start(bf16[128,256]{1,0:T(8,128)(2,1)S(1)} %copy-done.1), channel_id=1, source_target_pairs={{0,2},{1,3},{2,0},{3,1},{4,6},{5,7},{6,4},{7,5},{8,10},{9,11},{10,... | collective-permute-start | bytes 196616 | tf_op jit(solution)/shard_map/ppermute | solution.py:27
  6.2 8.1 %collective-permute-start.3 = (bf16[128,256]{1,0:T(8,128)(2,1)S(1)}, bf16[128,256]{1,0:T(8,128)(2,1)S(1)}, u32[]{:S(2)}, u32[]{:S(2)}) collective-permute-start(bf16[128,256]{1,0:T(8,128)(2,1)S(1)} %copy-done.1), channel_id=1, source_target_pairs={{0,1},{1,0},{2,3},{3,2},{4,5},{5,4},{6,7},{7,6},{8,9},{9,8},{10,11... | collective-permute-start | bytes 196616 | tf_op jit(solution)/shard_map/ppermute | solution.py:27
  6.3 9.6 %collective-permute-start.2 = (f32[256,128]{1,0:T(8,128)S(1)}, f32[256,128]{1,0:T(8,128)S(1)}, u32[]{:S(2)}, u32[]{:S(2)}) collective-permute-start(f32[256,128]{1,0:T(8,128)S(1)} %copy-done), channel_id=1, source_target_pairs={{0,3},{1,2},{2,1},{3,0},{4,7},{5,6},{6,5},{7,4},{8,11},{9,10},{10,... | collective-permute-start | bytes 393224 | tf_op jit(solution)/shard_map/ppermute | solution.py:27
  7.8 8.1 %collective-permute-start.1 = (f32[256,128]{1,0:T(8,128)S(1)}, f32[256,128]{1,0:T(8,128)S(1)}, u32[]{:S(2)}, u32[]{:S(2)}) collective-permute-start(f32[256,128]{1,0:T(8,128)S(1)} %copy-done), channel_id=1, source_target_pairs={{0,2},{1,3},{2,0},{3,1},{4,6},{5,7},{6,4},{7,5},{8,10},{9,11},{10,... | collective-permute-start | bytes 393224 | tf_op jit(solution)/shard_map/ppermute | solution.py:27
  8.4 13.3 %all-to-all-start = ((bf16[8,65,128]{2,1,0:T(8,128)(2,1)}), bf16[8,65,128]{2,1,0:T(8,128)(2,1)S(1)}, u32[]{:S(2)}, u32[]{:S(2)}) async-start(bf16[8,65,128]{2,1,0:T(8,128)(2,1)} %broadcast_in_dim.81), calls=%async_computation | async-start | bytes 294912 | tf_op jit(solution)/shard_map/all_to_all | solution.py:15
  14.3 1.4 %collective-permute-start = (f32[256,128]{1,0:T(8,128)S(1)}, f32[256,128]{1,0:T(8,128)S(1)}, u32[]{:S(2)}, u32[]{:S(2)}) collective-permute-start(f32[256,128]{1,0:T(8,128)S(1)} %copy-done), channel_id=1, source_target_pairs={{0,1},{1,0},{2,3},{3,2},{4,5},{5,4},{6,7},{7,6},{8,9},{9,8},{10,11... | collective-permute-start | bytes 393224 | tf_op jit(solution)/shard_map/ppermute | solution.py:27
  21.7 4.4 %collective-permute-start.8 = (bf16[256,128]{1,0:T(8,128)(2,1)S(1)}, bf16[256,128]{1,0:T(8,128)(2,1)S(1)}, u32[]{:S(2)}, u32[]{:S(2)}) collective-permute-start(bf16[256,128]{1,0:T(8,128)(2,1)S(1)} %bitcast.63), channel_id=1, source_target_pairs={{0,3},{1,2},{2,1},{3,0},{4,7},{5,6},{6,5},{7,4},{8,11},{9,10},{10,... | collective-permute-start | bytes 196616 | tf_op jit(solution)/shard_map/ppermute | solution.py:27
  21.8 5.8 %collective-permute-start.7 = (bf16[256,128]{1,0:T(8,128)(2,1)S(1)}, bf16[256,128]{1,0:T(8,128)(2,1)S(1)}, u32[]{:S(2)}, u32[]{:S(2)}) collective-permute-start(bf16[256,128]{1,0:T(8,128)(2,1)S(1)} %bitcast.64), channel_id=1, source_target_pairs={{0,2},{1,3},{2,0},{3,1},{4,6},{5,7},{6,4},{7,5},{8,10},{9,11},{10,... | collective-permute-start | bytes 196616 | tf_op jit(solution)/shard_map/ppermute | solution.py:27
  23.4 4.4 %collective-permute-start.6 = (bf16[256,128]{1,0:T(8,128)(2,1)S(1)}, bf16[256,128]{1,0:T(8,128)(2,1)S(1)}, u32[]{:S(2)}, u32[]{:S(2)}) collective-permute-start(bf16[256,128]{1,0:T(8,128)(2,1)S(1)} %bitcast.65), channel_id=1, source_target_pairs={{0,1},{1,0},{2,3},{3,2},{4,5},{5,4},{6,7},{7,6},{8,9},{9,8},{10,11... | collective-permute-start | bytes 196616 | tf_op jit(solution)/shard_map/ppermute | solution.py:27
  28.0 0.7 %copy-start.2 = (f32[256]{0:T(256)S(1)}, f32[256]{0:T(256)}, u32[]{:S(2)}) copy-start(f32[256]{0:T(256)} %param.5) | copy-start | bytes 3076
  43.2 4.5 %collective-permute-start.11 = (bf16[256,128]{1,0:T(8,128)(2,1)S(1)}, bf16[256,128]{1,0:T(8,128)(2,1)S(1)}, u32[]{:S(2)}, u32[]{:S(2)}) collective-permute-start(bf16[256,128]{1,0:T(8,128)(2,1)S(1)} %bitcast.56), channel_id=1, source_target_pairs={{0,3},{1,2},{2,1},{3,0},{4,7},{5,6},{6,5},{7,4},{8,11},{9,10},{10,... | collective-permute-start | bytes 196616 | tf_op jit(solution)/shard_map/ppermute | solution.py:27
  43.3 5.5 %collective-permute-start.10 = (bf16[256,128]{1,0:T(8,128)(2,1)S(1)}, bf16[256,128]{1,0:T(8,128)(2,1)S(1)}, u32[]{:S(2)}, u32[]{:S(2)}) collective-permute-start(bf16[256,128]{1,0:T(8,128)(2,1)S(1)} %bitcast.57), channel_id=1, source_target_pairs={{0,2},{1,3},{2,0},{3,1},{4,6},{5,7},{6,4},{7,5},{8,10},{9,11},{10,... | collective-permute-start | bytes 196616 | tf_op jit(solution)/shard_map/ppermute | solution.py:27
  44.7 4.3 %collective-permute-start.9 = (bf16[256,128]{1,0:T(8,128)(2,1)S(1)}, bf16[256,128]{1,0:T(8,128)(2,1)S(1)}, u32[]{:S(2)}, u32[]{:S(2)}) collective-permute-start(bf16[256,128]{1,0:T(8,128)(2,1)S(1)} %bitcast.58), channel_id=1, source_target_pairs={{0,1},{1,0},{2,3},{3,2},{4,5},{5,4},{6,7},{7,6},{8,9},{9,8},{10,11... | collective-permute-start | bytes 196616 | tf_op jit(solution)/shard_map/ppermute | solution.py:27

commit v6 on v5

--- a/solution.py
+++ b/solution.py
@@ -34,8 +34,33 @@
     return (pairs[:, 0] + jnp.flip(pairs[:, 1], axis=1)).reshape((ngroups // 2 * nslots,) + slots.shape[2:])
 
 
+def tree_gather(slots, extra, merge_first, merge_extra):
+    ngroups = lax.axis_size("grid")
+    g = lax.axis_index("grid")
+    nslots = slots.shape[0]
+    got = lax.ppermute(jnp.concatenate([slots, extra], 0), "grid", [(i, i ^ 1) for i in range(ngroups)])
+    lower = (g & 1) == 1
+    first = jnp.where(lower, got[:nslots], slots)
+    second = jnp.where(lower, slots, got[:nslots])
+    cur = first + jnp.flip(second, axis=0)
+    extra = merge_first(extra, got[nslots:], lower)
+    step = 2
+    while step < ngroups:
+        got = lax.ppermute(jnp.concatenate([cur, extra], 0), "grid", [(i, i ^ step) for i in range(ngroups)])
+        lower = (g & step) != 0
+        n = cur.shape[0]
+        cur = jnp.where(lower, jnp.concatenate([got[:n], cur], 0), jnp.concatenate([cur, got[:n]], 0))
+        extra = merge_extra(extra, got[n:], lower)
+        step *= 2
+    return cur, extra
+
+
+def add_extra(own, got, lower):
+    return own + got
+
+
 def body(orbitals, potential, fitted, points):
-    if lax.axis_size("grid") > 8 or lax.axis_size("grid") % 2 or points.shape[0] > orbitals.shape[1]:
+    if lax.axis_size("grid") > 8 or lax.axis_size("grid") & (lax.axis_size("grid") - 1) or points.shape[0] > orbitals.shape[1]:
         return body_spread(orbitals, potential, fitted, points)
     rows = orbitals.shape[0]
     block_width = orbitals.shape[1]
@@ -49,19 +74,23 @@
     sq = None
     for step in range(ITERS):
         if sq is None:
-            own_b = orbitals.astype(jnp.bfloat16)
             nslots = points.shape[0]
-            selected = jnp.where(valid_mask[:, None], own_b[safe_idx], jnp.zeros((), jnp.bfloat16))
+            selected = jnp.where(valid_mask[:, None], orbitals[safe_idx], 0.0).astype(jnp.bfloat16)
             filled = jnp.pad(valid_mask.astype(jnp.bfloat16), (0, block_width - nslots))
-            payload = jnp.concatenate([selected, filled[None]], 0)
-            sent, rows_own, fitted_own = lax.optimization_barrier((grid_copies(payload), orbitals, fitted))
-            got = grid_exchange(sent).reshape(ngroups, nslots + 1, block_width)
+            def pick_first(own, got, lower):
+                return jnp.where(lower, got, own)
+
+            def in_order(own, got, lower):
+                return jnp.where(lower, jnp.concatenate([got, own], 0), jnp.concatenate([own, got], 0))
+
+            sel, mask_row, rows_own, fitted_own = lax.optimization_barrier((selected, filled[None], orbitals, fitted))
+            merged, first_rows = tree_gather(sel, mask_row, pick_first, in_order)
             psi = jnp.concatenate(band_swap(rows_own), 1)
             fitted_got = jnp.stack(band_swap(fitted_own), 0)
             fitted_all = jnp.take(fitted_got, jnp.arange(nbands, dtype=jnp.int32) ^ band, axis=0)
             fitted_all = fitted_all.reshape(ngroups // 2, 2, nslots, fitted.shape[1])
-            coll = jnp.concatenate(band_swap(pair_up(got[:, :nslots])), 1)
-            first_filled = got[:, nslots, :nslots].reshape(ngroups // 2, 2, nslots)[:, 0] > 0
+            coll = jnp.concatenate(band_swap(merged), 1)
+            first_filled = first_rows[:, :nslots] > 0
             fitted_all = jnp.where(
                 first_filled[:, :, None], fitted_all[:, 0], jnp.flip(fitted_all[:, 1], axis=1)
             ).reshape(-1, fitted.shape[1]).astype(jnp.float32)
@@ -70,11 +99,9 @@
             own = psi[:, :block_width]
             at_slots = jnp.where(valid_mask[:, None], own[safe_idx], 0.0)
             nslots = at_slots.shape[0]
-            payload = jnp.concatenate([at_slots, sq.reshape(nbands, block_width)], 0)
-            got = grid_gather(payload).reshape(ngroups, nslots + nbands, block_width)
-            total = jnp.sum(got[:, nslots:], axis=0).reshape(total_orbitals)
-            scale = lax.rsqrt(total / (rows * ngroups) + 1e-06)
-            coll_own = pair_up((got[:, :nslots] * scale[:block_width]).astype(jnp.bfloat16))
+            merged, total = tree_gather(at_slots, sq.reshape(nbands, block_width), add_extra, add_extra)
+            scale = lax.rsqrt(total.reshape(total_orbitals) / (rows * ngroups) + 1e-06)
+            coll_own = (merged * scale[:block_width]).astype(jnp.bfloat16)
             coll = jnp.concatenate(band_swap(coll_own), 1)
             psi = psi * scale
             orbital_block = psi.astype(jnp.bfloat16)
@@ -94,7 +121,11 @@
         )
         psi = psi - 0.25 * (pot * psi - applied)
         sq = jnp.sum(psi * psi, axis=0)
-    total = jnp.sum(grid_gather(sq[None, :block_width]), axis=0)
+    total = sq[None, :block_width]
+    step = 1
+    while step < ngroups:
+        total = total + lax.ppermute(total, "grid", [(i, i ^ step) for i in range(ngroups)])
+        step *= 2
     return psi[:, :block_width] * lax.rsqrt(total / (rows * ngroups) + 1e-06)
 
 

time: 59.9 us -> 59.8 us (level)
  blocking collectives: 22.5 us -> 0 us
  starting transfers between devices: 14.9 us -> 29.6 us
  waiting for transfers between devices: 13.2 us -> 21.7 us
  other arithmetic: 2.96 us -> 2.26 us
    all_to_all x2 -> x0, blocking collectives: 22.5 us -> none  [grid_exchange(): got = lax.all_to_all(sent, 'grid', 0, 0, tiled=True)]
    ppermute x0 -> x9, starting transfers between devices: none -> 19.9 us  [the longest x4 9.82 us: tree_gather(): lax.ppermute(jnp.concatenate([cur, extra], 0), 'grid', [(i, i ^ step) for...]
    ppermute x0 -> x9, waiting for transfers between devices: none -> 16.4 us  [the longest x4 7.82 us: tree_gather(): lax.ppermute(jnp.concatenate([cur, extra], 0), 'grid', [(i, i ^ step) for...]
    all_to_all x1 -> x0, starting transfers between devices: 5.82 us -> none  [grid_exchange(): got = lax.all_to_all(sent, 'grid', 0, 0, tiled=True)]
    all_to_all x1 -> x0, waiting for transfers between devices: 5.65 us -> none  [grid_exchange(): got = lax.all_to_all(sent, 'grid', 0, 0, tiled=True)]
    ppermute x12, waiting for transfers between devices: 7.51 us -> 5.33 us  [band_swap(): got.append(lax.ppermute(x, 'band', [(i, i ^ k) for i in range(nbands)]))]
    gather x1, local copies, waits for them, and re-layouts: 0.63 us -> 1.51 us  [body(): orbitals[safe_idx]]
    convert_element_type x2, other arithmetic: 0.94 us -> 0.1 us  [the longest x1 0.08 us: body(): jnp.where(valid_mask[:, None], orbitals[safe_idx], 0.0).astype(jnp.bfloat16)]
  transfers between devices with their start and end apart: 13 -> 21, of which waited for: 7 -> 13; matrix products, arithmetic and copies ran while one was open for 3% -> 4% of each run, Pallas kernels for 0% -> 0%
where the time goes in v6:
time: 59.8 us; the launch traced here: 59.7 us
  starting transfers between devices  29.6 us (49%)
  waiting for transfers between devices  21.7 us (36%)
  local copies, waits for them, and re-layouts  3.63 us (6%)
  other arithmetic  2.26 us (4%)
  matrix products  2.09 us (3%)
    ppermute x4, starting transfers between devices, tree_gather(): lax.ppermute(jnp.concatenate([cur, extra], 0), 'grid', [(i, i ^ step) for...  9.82 us
    ppermute x12, starting transfers between devices, band_swap(): got.append(lax.ppermute(x, 'band', [(i, i ^ k) for i in range(nbands)]))  9.72 us
    ppermute x4, waiting for transfers between devices, tree_gather(): lax.ppermute(jnp.concatenate([cur, extra], 0), 'grid', [(i, i ^ step) for...  7.82 us
    ppermute x3, starting transfers between devices, body(): lax.ppermute(total, 'grid', [(i, i ^ step) for i in range(ngroups)])  6.7 us
    ppermute x12, waiting for transfers between devices, band_swap(): got.append(lax.ppermute(x, 'band', [(i, i ^ k) for i in range(nbands)]))  5.33 us
    ppermute x3, waiting for transfers between devices, body(): lax.ppermute(total, 'grid', [(i, i ^ step) for i in range(ngroups)])  5.06 us
    ppermute x2, waiting for transfers between devices, tree_gather(): lax.ppermute(jnp.concatenate([slots, extra], 0), 'grid', [(i, i ^ 1) for...  3.48 us
    ppermute x2, starting transfers between devices, tree_gather(): lax.ppermute(jnp.concatenate([slots, extra], 0), 'grid', [(i, i ^ 1) for...  3.36 us
  transfers between devices with their start and end apart: 21, of which 13 were waited for; matrix products, arithmetic and copies ran while one was open for 4% of the time, Pallas kernels for 0%

profile of v6, /device:TPU:0, one launch (start us, length us, event | category | flops | bytes accessed | tf_op | source)
XLA Modules:
  0.0 59.7 jit_solution(17557585465809946603)
XLA Ops:
  0.0 0.7 %broadcast_compare_fusion = pred[64]{0:T(512)(128)(4,1)S(1)} fusion(s32[64]{0:T(128)} %param.7), kind=kLoop, calls=%fused_computation.120 | loop fusion | flops 64 | bytes 320 | tf_op jit(solution)/shard_map/ge | solution.py:71
  0.8 1.5 %gather_fusion = bf16[64,128]{1,0:T(8,128)(2,1)S(1)} fusion(f32[256,128]{1,0:T(8,128)} %param.4, s32[1024]{0:T(1024)S(1)} %pad_clamp_fusion.1), kind=kCustom, calls=%fused_computation | custom fusion | bytes 33024 | tf_op jit(solution)/shard_map/gather | solution.py:78
  2.4 2.4 %collective-permute-start.8 = (bf16[128,256]{1,0:T(8,128)(2,1)}, bf16[128,256]{1,0:T(8,128)(2,1)S(1)}, u32[]{:S(2)}, u32[]{:S(2)}) collective-permute-start(bf16[128,256]{1,0:T(8,128)(2,1)} %param.6), channel_id=1, source_target_pairs={{0,3},{1,2},{2,1},{3,0},{4,7},{5,6},{6,5},{7,4},{8,11},{9,10},{10,... | collective-permute-start | bytes 196616 | tf_op jit(solution)/shard_map/ppermute | solution.py:27
  4.8 0.6 %collective-permute-start.7 = (bf16[128,256]{1,0:T(8,128)(2,1)}, bf16[128,256]{1,0:T(8,128)(2,1)S(1)}, u32[]{:S(2)}, u32[]{:S(2)}) collective-permute-start(bf16[128,256]{1,0:T(8,128)(2,1)} %param.6), channel_id=1, source_target_pairs={{0,2},{1,3},{2,0},{3,1},{4,6},{5,7},{6,4},{7,5},{8,10},{9,11},{10,... | collective-permute-start | bytes 196616 | tf_op jit(solution)/shard_map/ppermute | solution.py:27
  5.5 1.8 %collective-permute-start.3 = (bf16[65,128]{1,0:T(8,128)(2,1)S(1)}, bf16[65,128]{1,0:T(8,128)(2,1)S(1)}, u32[]{:S(2)}, u32[]{:S(2)}) collective-permute-start(bf16[65,128]{1,0:T(8,128)(2,1)S(1)} %pad_maximum_fusion.5), channel_id=1, source_target_pairs={{0,4},{4,0},{8,12},{12,8},{16,20},{20,16},{24,28},{28,24},{1,5},{5... | collective-permute-start | bytes 49928 | tf_op jit(solution)/shard_map/ppermute | solution.py:41
  7.2 0.9 %collective-permute-start.2 = (f32[256,128]{1,0:T(8,128)S(1)}, f32[256,128]{1,0:T(8,128)S(1)}, u32[]{:S(2)}, u32[]{:S(2)}) collective-permute-start(f32[256,128]{1,0:T(8,128)S(1)} %copy-done), channel_id=1, source_target_pairs={{0,3},{1,2},{2,1},{3,0},{4,7},{5,6},{6,5},{7,4},{8,11},{9,10},{10,... | collective-permute-start | bytes 393224 | tf_op jit(solution)/shard_map/ppermute | solution.py:27
  8.2 1.0 %collective-permute-done.3 = bf16[65,128]{1,0:T(8,128)(2,1)S(1)} collective-permute-done((bf16[65,128]{1,0:T(8,128)(2,1)S(1)}, bf16[65,128]{1,0:T(8,128)(2,1)S(1)}, u32[]{:S(2)}, u32[]{:S(2)}) %collective-permute-start.3) | collective-permute-done | bytes 16672 | tf_op jit(solution)/shard_map/ppermute | solution.py:41
  9.3 1.9 %collective-permute-start.4 = (bf16[65,128]{1,0:T(8,128)(2,1)S(1)}, bf16[65,128]{1,0:T(8,128)(2,1)S(1)}, u32[]{:S(2)}, u32[]{:S(2)}) collective-permute-start(bf16[65,128]{1,0:T(8,128)(2,1)S(1)} %pad_maximum_fusion.6), channel_id=1, source_target_pairs={{0,8},{4,12},{8,0},{12,4},{16,24},{20,28},{24,16},{28,20},{1,9},{5... | collective-permute-start | bytes 49928 | tf_op jit(solution)/shard_map/ppermute | solution.py:49
  11.2 2.0 %collective-permute-done.4 = bf16[65,128]{1,0:T(8,128)(2,1)S(1)} collective-permute-done((bf16[65,128]{1,0:T(8,128)(2,1)S(1)}, bf16[65,128]{1,0:T(8,128)(2,1)S(1)}, u32[]{:S(2)}, u32[]{:S(2)}) %collective-permute-start.4) | collective-permute-done | bytes 16672 | tf_op jit(solution)/shard_map/ppermute | solution.py:49
  13.2 1.7 %collective-permute-start.1 = (f32[256,128]{1,0:T(8,128)S(1)}, f32[256,128]{1,0:T(8,128)S(1)}, u32[]{:S(2)}, u32[]{:S(2)}) collective-permute-start(f32[256,128]{1,0:T(8,128)S(1)} %copy-done), channel_id=1, source_target_pairs={{0,2},{1,3},{2,0},{3,1},{4,6},{5,7},{6,4},{7,5},{8,10},{9,11},{10,... | collective-permute-start | bytes 393224 | tf_op jit(solution)/shard_map/ppermute | solution.py:27
  15.0 2.7 %collective-permute-start.5 = (bf16[130,128]{1,0:T(8,128)(2,1)S(1)}, bf16[130,128]{1,0:T(8,128)(2,1)S(1)}, u32[]{:S(2)}, u32[]{:S(2)}) collective-permute-start(bf16[130,128]{1,0:T(8,128)(2,1)S(1)} %pad_maximum_fusion.4), channel_id=1, source_target_pairs={{0,16},{4,20},{8,24},{12,28},{16,0},{20,4},{24,8},{28,12},{1,17},{... | collective-permute-start | bytes 99848 | tf_op jit(solution)/shard_map/ppermute | solution.py:49
  17.7 0.6 gather_fusion.1
  18.3 0.1 broadcast_select_fusion
  18.4 0.1 rev.13
  18.6 1.4 %collective-permute-done.5 = bf16[130,128]{1,0:T(8,128)(2,1)S(1)} collective-permute-done((bf16[130,128]{1,0:T(8,128)(2,1)S(1)}, bf16[130,128]{1,0:T(8,128)(2,1)S(1)}, u32[]{:S(2)}, u32[]{:S(2)}) %collective-permute-start.5) | collective-permute-done | bytes 33312 | tf_op jit(solution)/shard_map/ppermute | solution.py:49
  20.1 0.9 %collective-permute-start.10 = (bf16[256,128]{1,0:T(8,128)(2,1)S(1)}, bf16[256,128]{1,0:T(8,128)(2,1)S(1)}, u32[]{:S(2)}, u32[]{:S(2)}) collective-permute-start(bf16[256,128]{1,0:T(8,128)(2,1)S(1)} %maximum_select_fusion.1), channel_id=1, source_target_pairs={{0,2},{1,3},{2,0},{3,1},{4,6},{5,7},{6,4},{7,5},{8,10},{9,11},{10,... | collective-permute-start | bytes 196616 | tf_op jit(solution)/shard_map/ppermute | solution.py:27
  21.0 0.1 fusion.44
  21.1 1.0 %collective-permute-start.9 = (bf16[256,128]{1,0:T(8,128)(2,1)S(1)}, bf16[256,128]{1,0:T(8,128)(2,1)S(1)}, u32[]{:S(2)}, u32[]{:S(2)}) collective-permute-start(bf16[256,128]{1,0:T(8,128)(2,1)S(1)} %maximum_select_fusion.1), channel_id=1, source_target_pairs={{0,1},{1,0},{2,3},{3,2},{4,5},{5,4},{6,7},{7,6},{8,9},{9,8},{10,11... | collective-permute-start | bytes 196616 | tf_op jit(solution)/shard_map/ppermute | solution.py:27
  22.2 1.9 %collective-permute-done.11 = bf16[256,128]{1,0:T(8,128)(2,1)S(1)} collective-permute-done((bf16[256,128]{1,0:T(8,128)(2,1)S(1)}, bf16[256,128]{1,0:T(8,128)(2,1)S(1)}, u32[]{:S(2)}, u32[]{:S(2)}) %collective-permute-start.11) | collective-permute-done | bytes 65568 | tf_op jit(solution)/shard_map/ppermute | solution.py:27
  24.2 0.2 fusion.11
  24.4 0.7 %collective-permute-done.10 = bf16[256,128]{1,0:T(8,128)(2,1)S(1)} collective-permute-done((bf16[256,128]{1,0:T(8,128)(2,1)S(1)}, bf16[256,128]{1,0:T(8,128)(2,1)S(1)}, u32[]{:S(2)}, u32[]{:S(2)}) %collective-permute-start.10) | collective-permute-done | bytes 65568 | tf_op jit(solution)/shard_map/ppermute | solution.py:27
  25.0 0.2 fusion.9
  25.2 0.2 fusion.7
  25.4 0.7 %copy-done.2 = f32[256]{0:T(256)S(1)} copy-done((f32[256]{0:T(256)S(1)}, f32[256]{0:T(256)}, u32[]{:S(2)}) %copy-start.2) | copy-done | bytes 1048
  26.1 0.5 multiply_reduce_fusion.1
  26.6 0.6 %gather_fusion.2 = f32[64,128]{1,0:T(8,128)S(1)} fusion(f32[256,128]{1,0:T(8,128)S(1)} %slice.136, s32[1024]{0:T(1024)S(1)} %pad_clamp_fusion.1), kind=kCustom, calls=%fused_computation.2 | custom fusion | bytes 65792 | tf_op jit(solution)/shard_map/gather | solution.py:100
  27.3 1.6 %collective-permute-start.12 = (f32[68,128]{1,0:T(8,128)S(1)}, f32[68,128]{1,0:T(8,128)S(1)}, u32[]{:S(2)}, u32[]{:S(2)}) collective-permute-start(f32[68,128]{1,0:T(8,128)S(1)} %pad_maximum_fusion.2), channel_id=1, source_target_pairs={{0,4},{4,0},{8,12},{12,8},{16,20},{20,16},{24,28},{28,24},{1,5},{5... | collective-permute-start | bytes 104456 | tf_op jit(solution)/shard_map/ppermute | solution.py:41
  28.9 2.4 %collective-permute-done.12 = f32[68,128]{1,0:T(8,128)S(1)} collective-permute-done((f32[68,128]{1,0:T(8,128)S(1)}, f32[68,128]{1,0:T(8,128)S(1)}, u32[]{:S(2)}, u32[]{:S(2)}) %collective-permute-start.12) | collective-permute-done | bytes 34848 | tf_op jit(solution)/shard_map/ppermute | solution.py:41
  31.4 0.1 select_add_fusion
  31.5 1.8 %collective-permute-start.13 = (f32[68,128]{1,0:T(8,128)S(1)}, f32[68,128]{1,0:T(8,128)S(1)}, u32[]{:S(2)}, u32[]{:S(2)}) collective-permute-start(f32[68,128]{1,0:T(8,128)S(1)} %pad_maximum_fusion.3), channel_id=1, source_target_pairs={{0,8},{4,12},{8,0},{12,4},{16,24},{20,28},{24,16},{28,20},{1,9},{5... | collective-permute-start | bytes 104456 | tf_op jit(solution)/shard_map/ppermute | solution.py:49
  33.3 2.2 %collective-permute-done.13 = f32[68,128]{1,0:T(8,128)S(1)} collective-permute-done((f32[68,128]{1,0:T(8,128)S(1)}, f32[68,128]{1,0:T(8,128)S(1)}, u32[]{:S(2)}, u32[]{:S(2)}) %collective-permute-start.13) | collective-permute-done | bytes 34848 | tf_op jit(solution)/shard_map/ppermute | solution.py:49
  35.6 3.5 %collective-permute-start.14 = (f32[132,128]{1,0:T(8,128)S(1)}, f32[132,128]{1,0:T(8,128)S(1)}, u32[]{:S(2)}, u32[]{:S(2)}) collective-permute-start(f32[132,128]{1,0:T(8,128)S(1)} %pad_maximum_fusion.1), channel_id=1, source_target_pairs={{0,16},{4,20},{8,24},{12,28},{16,0},{20,4},{24,8},{28,12},{1,17},{... | collective-permute-start | bytes 202760 | tf_op jit(solution)/shard_map/ppermute | solution.py:49
  39.1 2.3 %collective-permute-done.14 = f32[132,128]{1,0:T(8,128)S(1)} collective-permute-done((f32[132,128]{1,0:T(8,128)S(1)}, f32[132,128]{1,0:T(8,128)S(1)}, u32[]{:S(2)}, u32[]{:S(2)}) %collective-permute-start.14) | collective-permute-done | bytes 67616 | tf_op jit(solution)/shard_map/ppermute | solution.py:49
  41.5 0.6 %collective-permute-start.16 = (bf16[256,128]{1,0:T(8,128)(2,1)S(1)}, bf16[256,128]{1,0:T(8,128)(2,1)S(1)}, u32[]{:S(2)}, u32[]{:S(2)}) collective-permute-start(bf16[256,128]{1,0:T(8,128)(2,1)S(1)} %fusion.46), channel_id=1, source_target_pairs={{0,2},{1,3},{2,0},{3,1},{4,6},{5,7},{6,4},{7,5},{8,10},{9,11},{10,... | collective-permute-start | bytes 196616 | tf_op jit(solution)/shard_map/ppermute | solution.py:27
  42.1 1.2 %collective-permute-start.15 = (bf16[256,128]{1,0:T(8,128)(2,1)S(1)}, bf16[256,128]{1,0:T(8,128)(2,1)S(1)}, u32[]{:S(2)}, u32[]{:S(2)}) collective-permute-start(bf16[256,128]{1,0:T(8,128)(2,1)S(1)} %fusion.46), channel_id=1, source_target_pairs={{0,1},{1,0},{2,3},{3,2},{4,5},{5,4},{6,7},{7,6},{8,9},{9,8},{10,11... | collective-permute-start | bytes 196616 | tf_op jit(solution)/shard_map/ppermute | solution.py:27
  43.4 0.2 fusion.13
  43.6 1.7 %collective-permute-done.17 = bf16[256,128]{1,0:T(8,128)(2,1)S(1)} collective-permute-done((bf16[256,128]{1,0:T(8,128)(2,1)S(1)}, bf16[256,128]{1,0:T(8,128)(2,1)S(1)}, u32[]{:S(2)}, u32[]{:S(2)}) %collective-permute-start.17) | collective-permute-done | bytes 65568 | tf_op jit(solution)/shard_map/ppermute | solution.py:27
  45.3 0.2 fusion.23
  45.5 1.0 %collective-permute-done.16 = bf16[256,128]{1,0:T(8,128)(2,1)S(1)} collective-permute-done((bf16[256,128]{1,0:T(8,128)(2,1)S(1)}, bf16[256,128]{1,0:T(8,128)(2,1)S(1)}, u32[]{:S(2)}, u32[]{:S(2)}) %collective-permute-start.16) | collective-permute-done | bytes 65568 | tf_op jit(solution)/shard_map/ppermute | solution.py:27
  46.5 0.2 fusion.21
  46.7 0.5 multiply_reduce_fusion
  47.2 1.6 %collective-permute-start.18 = (f32[1,128]{1,0:T(1,128)S(1)}, f32[1,128]{1,0:T(1,128)S(1)}, u32[]{:S(2)}, u32[]{:S(2)}) collective-permute-start(f32[1,128]{1,0:T(1,128)S(1)} %slice_bitcast_fusion.2), channel_id=1, source_target_pairs={{0,4},{4,0},{8,12},{12,8},{16,20},{20,16},{24,28},{28,24},{1,5},{5... | collective-permute-start | bytes 1544 | tf_op jit(solution)/shard_map/ppermute | solution.py:127
  48.8 2.0 %collective-permute-done.18 = f32[1,128]{1,0:T(1,128)S(1)} collective-permute-done((f32[1,128]{1,0:T(1,128)S(1)}, f32[1,128]{1,0:T(1,128)S(1)}, u32[]{:S(2)}, u32[]{:S(2)}) %collective-permute-start.18) | collective-permute-done | bytes 544 | tf_op jit(solution)/shard_map/ppermute | solution.py:127
  50.8 2.0 %collective-permute-start.19 = (f32[1,128]{1,0:T(1,128)S(1)}, f32[1,128]{1,0:T(1,128)S(1)}, u32[]{:S(2)}, u32[]{:S(2)}) collective-permute-start(f32[1,128]{1,0:T(1,128)S(1)} %fusion.68), channel_id=1, source_target_pairs={{0,8},{4,12},{8,0},{12,4},{16,24},{20,28},{24,16},{28,20},{1,9},{5... | collective-permute-start | bytes 1544 | tf_op jit(solution)/shard_map/ppermute | solution.py:127
  52.8 1.5 %collective-permute-done.19 = f32[1,128]{1,0:T(1,128)S(1)} collective-permute-done((f32[1,128]{1,0:T(1,128)S(1)}, f32[1,128]{1,0:T(1,128)S(1)}, u32[]{:S(2)}, u32[]{:S(2)}) %collective-permute-start.19) | collective-permute-done | bytes 544 | tf_op jit(solution)/shard_map/ppermute | solution.py:127
  54.4 3.1 %collective-permute-start.20 = (f32[1,128]{1,0:T(1,128)S(1)}, f32[1,128]{1,0:T(1,128)S(1)}, u32[]{:S(2)}, u32[]{:S(2)}) collective-permute-start(f32[1,128]{1,0:T(1,128)S(1)} %add.95), channel_id=1, source_target_pairs={{0,16},{4,20},{8,24},{12,28},{16,0},{20,4},{24,8},{28,12},{1,17},{... | collective-permute-start | bytes 1544 | tf_op jit(solution)/shard_map/ppermute | solution.py:127
  57.4 1.5 %collective-permute-done.20 = f32[1,128]{1,0:T(1,128)S(1)} collective-permute-done((f32[1,128]{1,0:T(1,128)S(1)}, f32[1,128]{1,0:T(1,128)S(1)}, u32[]{:S(2)}, u32[]{:S(2)}) %collective-permute-start.20) | collective-permute-done | bytes 544 | tf_op jit(solution)/shard_map/ppermute | solution.py:127
  59.0 0.7 %slice_multiply_fusion = f32[256,128]{1,0:T(8,128)} fusion(f32[256,512]{1,0:T(8,128)S(1)} %get-tuple-element.16, f32[128]{0:T(128)S(1)} %rsqrt_bitcast_fusion), kind=kLoop, calls=%fused_computation.62 | loop fusion | flops 32768 | bytes 262656 | tf_op jit(solution)/shard_map/mul | solution.py:129
  (69 shorter events, 1.0 us)
Async XLA Ops:
  0.0 0.7 %copy-start.3 = (s32[64]{0:T(128)S(1)}, s32[64]{0:T(128)}, u32[]{:S(2)}) copy-start(s32[64]{0:T(128)} %param.7) | copy-start | bytes 772
  0.0 7.2 %copy-start = (f32[256,128]{1,0:T(8,128)S(1)}, f32[256,128]{1,0:T(8,128)}, u32[]{:S(2)}) copy-start(f32[256,128]{1,0:T(8,128)} %param.4) | copy-start | bytes 393220
  2.4 12.6 %collective-permute-start.8 = (bf16[128,256]{1,0:T(8,128)(2,1)}, bf16[128,256]{1,0:T(8,128)(2,1)S(1)}, u32[]{:S(2)}, u32[]{:S(2)}) collective-permute-start(bf16[128,256]{1,0:T(8,128)(2,1)} %param.6), channel_id=1, source_target_pairs={{0,3},{1,2},{2,1},{3,0},{4,7},{5,6},{6,5},{7,4},{8,11},{9,10},{10,... | collective-permute-start | bytes 196616 | tf_op jit(solution)/shard_map/ppermute | solution.py:27
  4.8 10.3 %collective-permute-start.7 = (bf16[128,256]{1,0:T(8,128)(2,1)}, bf16[128,256]{1,0:T(8,128)(2,1)S(1)}, u32[]{:S(2)}, u32[]{:S(2)}) collective-permute-start(bf16[128,256]{1,0:T(8,128)(2,1)} %param.6), channel_id=1, source_target_pairs={{0,2},{1,3},{2,0},{3,1},{4,6},{5,7},{6,4},{7,5},{8,10},{9,11},{10,... | collective-permute-start | bytes 196616 | tf_op jit(solution)/shard_map/ppermute | solution.py:27
  5.4 12.3 %collective-permute-start.6 = (bf16[128,256]{1,0:T(8,128)(2,1)}, bf16[128,256]{1,0:T(8,128)(2,1)S(1)}, u32[]{:S(2)}, u32[]{:S(2)}) collective-permute-start(bf16[128,256]{1,0:T(8,128)(2,1)} %param.6), channel_id=1, source_target_pairs={{0,1},{1,0},{2,3},{3,2},{4,5},{5,4},{6,7},{7,6},{8,9},{9,8},{10,11... | collective-permute-start | bytes 196616 | tf_op jit(solution)/shard_map/ppermute | solution.py:27
  5.5 3.8 %collective-permute-start.3 = (bf16[65,128]{1,0:T(8,128)(2,1)S(1)}, bf16[65,128]{1,0:T(8,128)(2,1)S(1)}, u32[]{:S(2)}, u32[]{:S(2)}) collective-permute-start(bf16[65,128]{1,0:T(8,128)(2,1)S(1)} %pad_maximum_fusion.5), channel_id=1, source_target_pairs={{0,4},{4,0},{8,12},{12,8},{16,20},{20,16},{24,28},{28,24},{1,5},{5... | collective-permute-start | bytes 49928 | tf_op jit(solution)/shard_map/ppermute | solution.py:41
  7.2 14.9 %collective-permute-start.2 = (f32[256,128]{1,0:T(8,128)S(1)}, f32[256,128]{1,0:T(8,128)S(1)}, u32[]{:S(2)}, u32[]{:S(2)}) collective-permute-start(f32[256,128]{1,0:T(8,128)S(1)} %copy-done), channel_id=1, source_target_pairs={{0,3},{1,2},{2,1},{3,0},{4,7},{5,6},{6,5},{7,4},{8,11},{9,10},{10,... | collective-permute-start | bytes 393224 | tf_op jit(solution)/shard_map/ppermute | solution.py:27
  9.3 3.8 %collective-permute-start.4 = (bf16[65,128]{1,0:T(8,128)(2,1)S(1)}, bf16[65,128]{1,0:T(8,128)(2,1)S(1)}, u32[]{:S(2)}, u32[]{:S(2)}) collective-permute-start(bf16[65,128]{1,0:T(8,128)(2,1)S(1)} %pad_maximum_fusion.6), channel_id=1, source_target_pairs={{0,8},{4,12},{8,0},{12,4},{16,24},{20,28},{24,16},{28,20},{1,9},{5... | collective-permute-start | bytes 49928 | tf_op jit(solution)/shard_map/ppermute | solution.py:49
  13.2 9.0 %collective-permute-start.1 = (f32[256,128]{1,0:T(8,128)S(1)}, f32[256,128]{1,0:T(8,128)S(1)}, u32[]{:S(2)}, u32[]{:S(2)}) collective-permute-start(f32[256,128]{1,0:T(8,128)S(1)} %copy-done), channel_id=1, source_target_pairs={{0,2},{1,3},{2,0},{3,1},{4,6},{5,7},{6,4},{7,5},{8,10},{9,11},{10,... | collective-permute-start | bytes 393224 | tf_op jit(solution)/shard_map/ppermute | solution.py:27
  14.9 2.8 %copy-start.1 = (bf16[128,256]{1,0:T(8,128)(2,1)S(1)}, bf16[128,256]{1,0:T(8,128)(2,1)}, u32[]{:S(2)}) copy-start(bf16[128,256]{1,0:T(8,128)(2,1)} %param.6) | copy-start | bytes 196612
  15.0 6.1 %collective-permute-start = (f32[256,128]{1,0:T(8,128)S(1)}, f32[256,128]{1,0:T(8,128)S(1)}, u32[]{:S(2)}, u32[]{:S(2)}) collective-permute-start(f32[256,128]{1,0:T(8,128)S(1)} %copy-done), channel_id=1, source_target_pairs={{0,1},{1,0},{2,3},{3,2},{4,5},{5,4},{6,7},{7,6},{8,9},{9,8},{10,11... | collective-permute-start | bytes 393224 | tf_op jit(solution)/shard_map/ppermute | solution.py:27
  15.0 4.9 %collective-permute-start.5 = (bf16[130,128]{1,0:T(8,128)(2,1)S(1)}, bf16[130,128]{1,0:T(8,128)(2,1)S(1)}, u32[]{:S(2)}, u32[]{:S(2)}) collective-permute-start(bf16[130,128]{1,0:T(8,128)(2,1)S(1)} %pad_maximum_fusion.4), channel_id=1, source_target_pairs={{0,16},{4,20},{8,24},{12,28},{16,0},{20,4},{24,8},{28,12},{1,17},{... | collective-permute-start | bytes 99848 | tf_op jit(solution)/shard_map/ppermute | solution.py:49
  20.0 4.2 %collective-permute-start.11 = (bf16[256,128]{1,0:T(8,128)(2,1)S(1)}, bf16[256,128]{1,0:T(8,128)(2,1)S(1)}, u32[]{:S(2)}, u32[]{:S(2)}) collective-permute-start(bf16[256,128]{1,0:T(8,128)(2,1)S(1)} %maximum_select_fusion.1), channel_id=1, source_target_pairs={{0,3},{1,2},{2,1},{3,0},{4,7},{5,6},{6,5},{7,4},{8,11},{9,10},{10,... | collective-permute-start | bytes 196616 | tf_op jit(solution)/shard_map/ppermute | solution.py:27
  20.1 5.0 %collective-permute-start.10 = (bf16[256,128]{1,0:T(8,128)(2,1)S(1)}, bf16[256,128]{1,0:T(8,128)(2,1)S(1)}, u32[]{:S(2)}, u32[]{:S(2)}) collective-permute-start(bf16[256,128]{1,0:T(8,128)(2,1)S(1)} %maximum_select_fusion.1), channel_id=1, source_target_pairs={{0,2},{1,3},{2,0},{3,1},{4,6},{5,7},{6,4},{7,5},{8,10},{9,11},{10,... | collective-permute-start | bytes 196616 | tf_op jit(solution)/shard_map/ppermute | solution.py:27
  21.1 4.1 %collective-permute-start.9 = (bf16[256,128]{1,0:T(8,128)(2,1)S(1)}, bf16[256,128]{1,0:T(8,128)(2,1)S(1)}, u32[]{:S(2)}, u32[]{:S(2)}) collective-permute-start(bf16[256,128]{1,0:T(8,128)(2,1)S(1)} %maximum_select_fusion.1), channel_id=1, source_target_pairs={{0,1},{1,0},{2,3},{3,2},{4,5},{5,4},{6,7},{7,6},{8,9},{9,8},{10,11... | collective-permute-start | bytes 196616 | tf_op jit(solution)/shard_map/ppermute | solution.py:27
  25.4 0.7 %copy-start.2 = (f32[256]{0:T(256)S(1)}, f32[256]{0:T(256)}, u32[]{:S(2)}) copy-start(f32[256]{0:T(256)} %param.5) | copy-start | bytes 3076
  27.3 4.0 %collective-permute-start.12 = (f32[68,128]{1,0:T(8,128)S(1)}, f32[68,128]{1,0:T(8,128)S(1)}, u32[]{:S(2)}, u32[]{:S(2)}) collective-permute-start(f32[68,128]{1,0:T(8,128)S(1)} %pad_maximum_fusion.2), channel_id=1, source_target_pairs={{0,4},{4,0},{8,12},{12,8},{16,20},{20,16},{24,28},{28,24},{1,5},{5... | collective-permute-start | bytes 104456 | tf_op jit(solution)/shard_map/ppermute | solution.py:41
  31.5 4.0 %collective-permute-start.13 = (f32[68,128]{1,0:T(8,128)S(1)}, f32[68,128]{1,0:T(8,128)S(1)}, u32[]{:S(2)}, u32[]{:S(2)}) collective-permute-start(f32[68,128]{1,0:T(8,128)S(1)} %pad_maximum_fusion.3), channel_id=1, source_target_pairs={{0,8},{4,12},{8,0},{12,4},{16,24},{20,28},{24,16},{28,20},{1,9},{5... | collective-permute-start | bytes 104456 | tf_op jit(solution)/shard_map/ppermute | solution.py:49
  35.6 5.8 %collective-permute-start.14 = (f32[132,128]{1,0:T(8,128)S(1)}, f32[132,128]{1,0:T(8,128)S(1)}, u32[]{:S(2)}, u32[]{:S(2)}) collective-permute-start(f32[132,128]{1,0:T(8,128)S(1)} %pad_maximum_fusion.1), channel_id=1, source_target_pairs={{0,16},{4,20},{8,24},{12,28},{16,0},{20,4},{24,8},{28,12},{1,17},{... | collective-permute-start | bytes 202760 | tf_op jit(solution)/shard_map/ppermute | solution.py:49
  41.4 3.8 %collective-permute-start.17 = (bf16[256,128]{1,0:T(8,128)(2,1)S(1)}, bf16[256,128]{1,0:T(8,128)(2,1)S(1)}, u32[]{:S(2)}, u32[]{:S(2)}) collective-permute-start(bf16[256,128]{1,0:T(8,128)(2,1)S(1)} %fusion.46), channel_id=1, source_target_pairs={{0,3},{1,2},{2,1},{3,0},{4,7},{5,6},{6,5},{7,4},{8,11},{9,10},{10,... | collective-permute-start | bytes 196616 | tf_op jit(solution)/shard_map/ppermute | solution.py:27
  41.5 5.0 %collective-permute-start.16 = (bf16[256,128]{1,0:T(8,128)(2,1)S(1)}, bf16[256,128]{1,0:T(8,128)(2,1)S(1)}, u32[]{:S(2)}, u32[]{:S(2)}) collective-permute-start(bf16[256,128]{1,0:T(8,128)(2,1)S(1)} %fusion.46), channel_id=1, source_target_pairs={{0,2},{1,3},{2,0},{3,1},{4,6},{5,7},{6,4},{7,5},{8,10},{9,11},{10,... | collective-permute-start | bytes 196616 | tf_op jit(solution)/shard_map/ppermute | solution.py:27
  42.1 4.6 %collective-permute-start.15 = (bf16[256,128]{1,0:T(8,128)(2,1)S(1)}, bf16[256,128]{1,0:T(8,128)(2,1)S(1)}, u32[]{:S(2)}, u32[]{:S(2)}) collective-permute-start(bf16[256,128]{1,0:T(8,128)(2,1)S(1)} %fusion.46), channel_id=1, source_target_pairs={{0,1},{1,0},{2,3},{3,2},{4,5},{5,4},{6,7},{7,6},{8,9},{9,8},{10,11... | collective-permute-start | bytes 196616 | tf_op jit(solution)/shard_map/ppermute | solution.py:27
  47.2 3.6 %collective-permute-start.18 = (f32[1,128]{1,0:T(1,128)S(1)}, f32[1,128]{1,0:T(1,128)S(1)}, u32[]{:S(2)}, u32[]{:S(2)}) collective-permute-start(f32[1,128]{1,0:T(1,128)S(1)} %slice_bitcast_fusion.2), channel_id=1, source_target_pairs={{0,4},{4,0},{8,12},{12,8},{16,20},{20,16},{24,28},{28,24},{1,5},{5... | collective-permute-start | bytes 1544 | tf_op jit(solution)/shard_map/ppermute | solution.py:127
  50.8 3.5 %collective-permute-start.19 = (f32[1,128]{1,0:T(1,128)S(1)}, f32[1,128]{1,0:T(1,128)S(1)}, u32[]{:S(2)}, u32[]{:S(2)}) collective-permute-start(f32[1,128]{1,0:T(1,128)S(1)} %fusion.68), channel_id=1, source_target_pairs={{0,8},{4,12},{8,0},{12,4},{16,24},{20,28},{24,16},{28,20},{1,9},{5... | collective-permute-start | bytes 1544 | tf_op jit(solution)/shard_map/ppermute | solution.py:127
  54.4 4.6 %collective-permute-start.20 = (f32[1,128]{1,0:T(1,128)S(1)}, f32[1,128]{1,0:T(1,128)S(1)}, u32[]{:S(2)}, u32[]{:S(2)}) collective-permute-start(f32[1,128]{1,0:T(1,128)S(1)} %add.95), channel_id=1, source_target_pairs={{0,16},{4,20},{8,24},{12,28},{16,0},{20,4},{24,8},{28,12},{1,17},{... | collective-permute-start | bytes 1544 | tf_op jit(solution)/shard_map/ppermute | solution.py:127

commit v7 on v6

--- a/solution.py
+++ b/solution.py
@@ -55,10 +55,6 @@
     return cur, extra
 
 
-def add_extra(own, got, lower):
-    return own + got
-
-
 def body(orbitals, potential, fitted, points):
     if lax.axis_size("grid") > 8 or lax.axis_size("grid") & (lax.axis_size("grid") - 1) or points.shape[0] > orbitals.shape[1]:
         return body_spread(orbitals, potential, fitted, points)
@@ -99,9 +95,11 @@
             own = psi[:, :block_width]
             at_slots = jnp.where(valid_mask[:, None], own[safe_idx], 0.0)
             nslots = at_slots.shape[0]
-            merged, total = tree_gather(at_slots, sq.reshape(nbands, block_width), add_extra, add_extra)
-            scale = lax.rsqrt(total.reshape(total_orbitals) / (rows * ngroups) + 1e-06)
-            coll_own = (merged * scale[:block_width]).astype(jnp.bfloat16)
+            payload = jnp.concatenate([at_slots, sq.reshape(nbands, block_width)], 0)
+            got = grid_gather(payload).reshape(ngroups, nslots + nbands, block_width)
+            total = jnp.sum(got[:, nslots:], axis=0).reshape(total_orbitals)
+            scale = lax.rsqrt(total / (rows * ngroups) + 1e-06)
+            coll_own = pair_up((got[:, :nslots] * scale[:block_width]).astype(jnp.bfloat16))
             coll = jnp.concatenate(band_swap(coll_own), 1)
             psi = psi * scale
             orbital_block = psi.astype(jnp.bfloat16)
@@ -121,11 +119,7 @@
         )
         psi = psi - 0.25 * (pot * psi - applied)
         sq = jnp.sum(psi * psi, axis=0)
-    total = sq[None, :block_width]
-    step = 1
-    while step < ngroups:
-        total = total + lax.ppermute(total, "grid", [(i, i ^ step) for i in range(ngroups)])
-        step *= 2
+    total = jnp.sum(grid_gather(sq[None, :block_width]), axis=0)
     return psi[:, :block_width] * lax.rsqrt(total / (rows * ngroups) + 1e-06)
 
 

time: 59.8 us -> 61.3 us (1.025)
  blocking collectives: 0 us -> 27.1 us
  starting transfers between devices: 29.6 us -> 16 us
  waiting for transfers between devices: 21.7 us -> 9.69 us
    all_to_all x0 -> x2, blocking collectives: none -> 27.1 us  [grid_exchange(): got = lax.all_to_all(sent, 'grid', 0, 0, tiled=True)]
    ppermute x3 -> x0, starting transfers between devices: 6.7 us -> none  [body(): lax.ppermute(total, 'grid', [(i, i ^ step) for i in range(ngroups)])]
    ppermute x4 -> x2, starting transfers between devices: 9.82 us -> 4.52 us  [tree_gather(): lax.ppermute(jnp.concatenate([cur, extra], 0), 'grid', [(i, i ^ step) for...]
    ppermute x3 -> x0, waiting for transfers between devices: 5.06 us -> none  [body(): lax.ppermute(total, 'grid', [(i, i ^ step) for i in range(ngroups)])]
    ppermute x4 -> x2, waiting for transfers between devices: 7.82 us -> 3.32 us  [tree_gather(): lax.ppermute(jnp.concatenate([cur, extra], 0), 'grid', [(i, i ^ step) for...]
    ppermute x2 -> x1, waiting for transfers between devices: 3.48 us -> 1.04 us  [tree_gather(): lax.ppermute(jnp.concatenate([slots, extra], 0), 'grid', [(i, i ^ 1) for...]
    ppermute x2 -> x1, starting transfers between devices: 3.36 us -> 1.77 us  [tree_gather(): lax.ppermute(jnp.concatenate([slots, extra], 0), 'grid', [(i, i ^ 1) for...]
  transfers between devices with their start and end apart: 21 -> 15, of which waited for: 13 -> 7; matrix products, arithmetic and copies ran while one was open for 4% -> 4% of each run, Pallas kernels for 0% -> 0%
where the time goes in v7:
time: 61.3 us; the launch traced here: 61.1 us
  blocking collectives  27.1 us (44%)
  starting transfers between devices  16 us (26%)
  waiting for transfers between devices  9.69 us (16%)
  local copies, waits for them, and re-layouts  3.67 us (6%)
  other arithmetic  2.11 us (3%)
  matrix products  2.09 us (3%)
    all_to_all x2, blocking collectives, grid_exchange(): got = lax.all_to_all(sent, 'grid', 0, 0, tiled=True)  27.1 us
    ppermute x12, starting transfers between devices, band_swap(): got.append(lax.ppermute(x, 'band', [(i, i ^ k) for i in range(nbands)]))  9.72 us
    ppermute x12, waiting for transfers between devices, band_swap(): got.append(lax.ppermute(x, 'band', [(i, i ^ k) for i in range(nbands)]))  5.32 us
    ppermute x2, starting transfers between devices, tree_gather(): lax.ppermute(jnp.concatenate([cur, extra], 0), 'grid', [(i, i ^ step) for...  4.52 us
    ppermute x2, waiting for transfers between devices, tree_gather(): lax.ppermute(jnp.concatenate([cur, extra], 0), 'grid', [(i, i ^ step) for...  3.32 us
    ppermute x1, starting transfers between devices, tree_gather(): lax.ppermute(jnp.concatenate([slots, extra], 0), 'grid', [(i, i ^ 1) for...  1.77 us
    gather x1, local copies, waits for them, and re-layouts, body(): orbitals[safe_idx]  1.51 us
  transfers between devices with their start and end apart: 15, of which 7 were waited for; matrix products, arithmetic and copies ran while one was open for 4% of the time, Pallas kernels for 0%

profile of v7, /device:TPU:0, one launch (start us, length us, event | category | flops | bytes accessed | tf_op | source)
XLA Modules:
  0.0 61.1 jit_solution(12776394738015474588)
XLA Ops:
  0.0 0.7 %broadcast_compare_fusion = pred[64]{0:T(512)(128)(4,1)S(1)} fusion(s32[64]{0:T(128)} %param.7), kind=kLoop, calls=%fused_computation.112 | loop fusion | flops 64 | bytes 320 | tf_op jit(solution)/shard_map/ge | solution.py:67
  0.8 1.5 %gather_fusion = bf16[64,128]{1,0:T(8,128)(2,1)S(1)} fusion(f32[256,128]{1,0:T(8,128)} %param.4, s32[1024]{0:T(1024)S(1)} %pad_clamp_fusion.1), kind=kCustom, calls=%fused_computation | custom fusion | bytes 33024 | tf_op jit(solution)/shard_map/gather | solution.py:74
  2.3 0.1 select_convert_fusion
  2.4 2.4 %collective-permute-start.8 = (bf16[128,256]{1,0:T(8,128)(2,1)}, bf16[128,256]{1,0:T(8,128)(2,1)S(1)}, u32[]{:S(2)}, u32[]{:S(2)}) collective-permute-start(bf16[128,256]{1,0:T(8,128)(2,1)} %param.6), channel_id=1, source_target_pairs={{0,3},{1,2},{2,1},{3,0},{4,7},{5,6},{6,5},{7,4},{8,11},{9,10},{10,... | collective-permute-start | bytes 196616 | tf_op jit(solution)/shard_map/ppermute | solution.py:27
  4.8 0.6 %collective-permute-start.7 = (bf16[128,256]{1,0:T(8,128)(2,1)}, bf16[128,256]{1,0:T(8,128)(2,1)S(1)}, u32[]{:S(2)}, u32[]{:S(2)}) collective-permute-start(bf16[128,256]{1,0:T(8,128)(2,1)} %param.6), channel_id=1, source_target_pairs={{0,2},{1,3},{2,0},{3,1},{4,6},{5,7},{6,4},{7,5},{8,10},{9,11},{10,... | collective-permute-start | bytes 196616 | tf_op jit(solution)/shard_map/ppermute | solution.py:27
  5.4 0.0 collective-permute-start.6
  5.5 1.8 %collective-permute-start.3 = (bf16[65,128]{1,0:T(8,128)(2,1)S(1)}, bf16[65,128]{1,0:T(8,128)(2,1)S(1)}, u32[]{:S(2)}, u32[]{:S(2)}) collective-permute-start(bf16[65,128]{1,0:T(8,128)(2,1)S(1)} %pad_maximum_fusion.3), channel_id=1, source_target_pairs={{0,4},{4,0},{8,12},{12,8},{16,20},{20,16},{24,28},{28,24},{1,5},{5... | collective-permute-start | bytes 49928 | tf_op jit(solution)/shard_map/ppermute | solution.py:41
  7.2 0.9 %collective-permute-start.2 = (f32[256,128]{1,0:T(8,128)S(1)}, f32[256,128]{1,0:T(8,128)S(1)}, u32[]{:S(2)}, u32[]{:S(2)}) collective-permute-start(f32[256,128]{1,0:T(8,128)S(1)} %copy-done), channel_id=1, source_target_pairs={{0,3},{1,2},{2,1},{3,0},{4,7},{5,6},{6,5},{7,4},{8,11},{9,10},{10,... | collective-permute-start | bytes 393224 | tf_op jit(solution)/shard_map/ppermute | solution.py:27
  8.2 1.0 %collective-permute-done.3 = bf16[65,128]{1,0:T(8,128)(2,1)S(1)} collective-permute-done((bf16[65,128]{1,0:T(8,128)(2,1)S(1)}, bf16[65,128]{1,0:T(8,128)(2,1)S(1)}, u32[]{:S(2)}, u32[]{:S(2)}) %collective-permute-start.3) | collective-permute-done | bytes 16672 | tf_op jit(solution)/shard_map/ppermute | solution.py:41
  9.3 1.9 %collective-permute-start.4 = (bf16[65,128]{1,0:T(8,128)(2,1)S(1)}, bf16[65,128]{1,0:T(8,128)(2,1)S(1)}, u32[]{:S(2)}, u32[]{:S(2)}) collective-permute-start(bf16[65,128]{1,0:T(8,128)(2,1)S(1)} %pad_maximum_fusion.4), channel_id=1, source_target_pairs={{0,8},{4,12},{8,0},{12,4},{16,24},{20,28},{24,16},{28,20},{1,9},{5... | collective-permute-start | bytes 49928 | tf_op jit(solution)/shard_map/ppermute | solution.py:49
  11.2 2.0 %collective-permute-done.4 = bf16[65,128]{1,0:T(8,128)(2,1)S(1)} collective-permute-done((bf16[65,128]{1,0:T(8,128)(2,1)S(1)}, bf16[65,128]{1,0:T(8,128)(2,1)S(1)}, u32[]{:S(2)}, u32[]{:S(2)}) %collective-permute-start.4) | collective-permute-done | bytes 16672 | tf_op jit(solution)/shard_map/ppermute | solution.py:49
  13.2 1.7 %collective-permute-start.1 = (f32[256,128]{1,0:T(8,128)S(1)}, f32[256,128]{1,0:T(8,128)S(1)}, u32[]{:S(2)}, u32[]{:S(2)}) collective-permute-start(f32[256,128]{1,0:T(8,128)S(1)} %copy-done), channel_id=1, source_target_pairs={{0,2},{1,3},{2,0},{3,1},{4,6},{5,7},{6,4},{7,5},{8,10},{9,11},{10,... | collective-permute-start | bytes 393224 | tf_op jit(solution)/shard_map/ppermute | solution.py:27
  14.9 0.0 copy-start.1
  15.0 0.1 collective-permute-start
  15.0 0.0 collective-permute-done.7
  15.0 2.7 %collective-permute-start.5 = (bf16[130,128]{1,0:T(8,128)(2,1)S(1)}, bf16[130,128]{1,0:T(8,128)(2,1)S(1)}, u32[]{:S(2)}, u32[]{:S(2)}) collective-permute-start(bf16[130,128]{1,0:T(8,128)(2,1)S(1)} %pad_maximum_fusion.2), channel_id=1, source_target_pairs={{0,16},{4,20},{8,24},{12,28},{16,0},{20,4},{24,8},{28,12},{1,17},{... | collective-permute-start | bytes 99848 | tf_op jit(solution)/shard_map/ppermute | solution.py:49
  17.7 0.6 gather_fusion.1
  18.3 0.1 copy_select_fusion
  18.4 0.1 rev.13
  18.6 1.4 %collective-permute-done.5 = bf16[130,128]{1,0:T(8,128)(2,1)S(1)} collective-permute-done((bf16[130,128]{1,0:T(8,128)(2,1)S(1)}, bf16[130,128]{1,0:T(8,128)(2,1)S(1)}, u32[]{:S(2)}, u32[]{:S(2)}) %collective-permute-start.5) | collective-permute-done | bytes 33312 | tf_op jit(solution)/shard_map/ppermute | solution.py:49
  20.0 0.1 collective-permute-start.11
  20.1 0.9 %collective-permute-start.10 = (bf16[256,128]{1,0:T(8,128)(2,1)S(1)}, bf16[256,128]{1,0:T(8,128)(2,1)S(1)}, u32[]{:S(2)}, u32[]{:S(2)}) collective-permute-start(bf16[256,128]{1,0:T(8,128)(2,1)S(1)} %maximum_select_fusion), channel_id=1, source_target_pairs={{0,2},{1,3},{2,0},{3,1},{4,6},{5,7},{6,4},{7,5},{8,10},{9,11},{10,... | collective-permute-start | bytes 196616 | tf_op jit(solution)/shard_map/ppermute | solution.py:27
  21.0 0.1 fusion.45
  21.1 1.0 %collective-permute-start.9 = (bf16[256,128]{1,0:T(8,128)(2,1)S(1)}, bf16[256,128]{1,0:T(8,128)(2,1)S(1)}, u32[]{:S(2)}, u32[]{:S(2)}) collective-permute-start(bf16[256,128]{1,0:T(8,128)(2,1)S(1)} %maximum_select_fusion), channel_id=1, source_target_pairs={{0,1},{1,0},{2,3},{3,2},{4,5},{5,4},{6,7},{7,6},{8,9},{9,8},{10,11... | collective-permute-start | bytes 196616 | tf_op jit(solution)/shard_map/ppermute | solution.py:27
  22.1 0.0 collective-permute-done.1
  22.2 0.0 collective-permute-done.2
  22.2 1.9 %collective-permute-done.11 = bf16[256,128]{1,0:T(8,128)(2,1)S(1)} collective-permute-done((bf16[256,128]{1,0:T(8,128)(2,1)S(1)}, bf16[256,128]{1,0:T(8,128)(2,1)S(1)}, u32[]{:S(2)}, u32[]{:S(2)}) %collective-permute-start.11) | collective-permute-done | bytes 65568 | tf_op jit(solution)/shard_map/ppermute | solution.py:27
  24.2 0.2 fusion.11
  24.4 0.7 %collective-permute-done.10 = bf16[256,128]{1,0:T(8,128)(2,1)S(1)} collective-permute-done((bf16[256,128]{1,0:T(8,128)(2,1)S(1)}, bf16[256,128]{1,0:T(8,128)(2,1)S(1)}, u32[]{:S(2)}, u32[]{:S(2)}) %collective-permute-start.10) | collective-permute-done | bytes 65568 | tf_op jit(solution)/shard_map/ppermute | solution.py:27
  25.0 0.2 fusion.9
  25.2 0.2 fusion.7
  25.4 0.0 copy-start.2
  25.4 0.7 %copy-done.2 = f32[256]{0:T(256)S(1)} copy-done((f32[256]{0:T(256)S(1)}, f32[256]{0:T(256)}, u32[]{:S(2)}) %copy-start.2) | copy-done | bytes 1048
  26.1 0.5 multiply_reduce_fusion.1
  26.6 0.6 gather_fusion.2
  27.2 0.1 broadcast_select_fusion
  27.3 17.4 %all_to_all.10 = f32[8,68,128]{2,1,0:T(8,128)S(1)} all-to-all(f32[8,68,128]{2,1,0:T(8,128)S(1)} %broadcast_in_dim.72), channel_id=1, replica_groups=mesh['grid'=8,'band'=4] {'grid'}, dimensions={0} | all-to-all | bytes 557056 | tf_op jit(solution)/shard_map/all_to_all | solution.py:15
  44.9 0.1 collective-permute-start.14
  44.9 0.4 collective-permute-start.13
  45.4 1.4 %collective-permute-start.12 = (bf16[256,128]{1,0:T(8,128)(2,1)S(1)}, bf16[256,128]{1,0:T(8,128)(2,1)S(1)}, u32[]{:S(2)}, u32[]{:S(2)}) collective-permute-start(bf16[256,128]{1,0:T(8,128)(2,1)S(1)} %bitcast.44), channel_id=1, source_target_pairs={{0,1},{1,0},{2,3},{3,2},{4,5},{5,4},{6,7},{7,6},{8,9},{9,8},{10,11... | collective-permute-start | bytes 196616 | tf_op jit(solution)/shard_map/ppermute | solution.py:27
  46.8 0.2 fusion.13
  47.0 1.7 %collective-permute-done.14 = bf16[256,128]{1,0:T(8,128)(2,1)S(1)} collective-permute-done((bf16[256,128]{1,0:T(8,128)(2,1)S(1)}, bf16[256,128]{1,0:T(8,128)(2,1)S(1)}, u32[]{:S(2)}, u32[]{:S(2)}) %collective-permute-start.14) | collective-permute-done | bytes 65568 | tf_op jit(solution)/shard_map/ppermute | solution.py:27
  48.7 0.2 fusion.23
  48.9 1.0 %collective-permute-done.13 = bf16[256,128]{1,0:T(8,128)(2,1)S(1)} collective-permute-done((bf16[256,128]{1,0:T(8,128)(2,1)S(1)}, bf16[256,128]{1,0:T(8,128)(2,1)S(1)}, u32[]{:S(2)}, u32[]{:S(2)}) %collective-permute-start.13) | collective-permute-done | bytes 65568 | tf_op jit(solution)/shard_map/ppermute | solution.py:27
  49.9 0.2 fusion.21
  50.1 0.5 multiply_reduce_fusion
  50.7 9.7 %all_to_all.11 = f32[8,1,128]{2,1,0:T(1,128)S(1)} all-to-all(f32[8,1,128]{2,1,0:T(1,128)S(1)} %broadcast_in_dim.73), channel_id=1, replica_groups=mesh['grid'=8,'band'=4] {'grid'}, dimensions={0} | all-to-all | bytes 8192 | tf_op jit(solution)/shard_map/all_to_all | solution.py:15
  60.4 0.7 %slice_multiply_fusion.1 = f32[256,128]{1,0:T(8,128)} fusion(f32[256,512]{1,0:T(8,128)S(1)} %get-tuple-element.18, f32[128]{0:T(128)S(1)} %add_rsqrt_fusion.1), kind=kLoop, calls=%fused_computation.64 | loop fusion | flops 32768 | bytes 262656 | tf_op jit(solution)/shard_map/mul | solution.py:123
  (54 shorter events, 0.6 us)
Async XLA Ops:
  0.0 0.7 %copy-start.3 = (s32[64]{0:T(128)S(1)}, s32[64]{0:T(128)}, u32[]{:S(2)}) copy-start(s32[64]{0:T(128)} %param.7) | copy-start | bytes 772
  0.0 7.2 %copy-start = (f32[256,128]{1,0:T(8,128)S(1)}, f32[256,128]{1,0:T(8,128)}, u32[]{:S(2)}) copy-start(f32[256,128]{1,0:T(8,128)} %param.4) | copy-start | bytes 393220
  2.4 12.6 %collective-permute-start.8 = (bf16[128,256]{1,0:T(8,128)(2,1)}, bf16[128,256]{1,0:T(8,128)(2,1)S(1)}, u32[]{:S(2)}, u32[]{:S(2)}) collective-permute-start(bf16[128,256]{1,0:T(8,128)(2,1)} %param.6), channel_id=1, source_target_pairs={{0,3},{1,2},{2,1},{3,0},{4,7},{5,6},{6,5},{7,4},{8,11},{9,10},{10,... | collective-permute-start | bytes 196616 | tf_op jit(solution)/shard_map/ppermute | solution.py:27
  4.8 10.3 %collective-permute-start.7 = (bf16[128,256]{1,0:T(8,128)(2,1)}, bf16[128,256]{1,0:T(8,128)(2,1)S(1)}, u32[]{:S(2)}, u32[]{:S(2)}) collective-permute-start(bf16[128,256]{1,0:T(8,128)(2,1)} %param.6), channel_id=1, source_target_pairs={{0,2},{1,3},{2,0},{3,1},{4,6},{5,7},{6,4},{7,5},{8,10},{9,11},{10,... | collective-permute-start | bytes 196616 | tf_op jit(solution)/shard_map/ppermute | solution.py:27
  5.4 12.3 %collective-permute-start.6 = (bf16[128,256]{1,0:T(8,128)(2,1)}, bf16[128,256]{1,0:T(8,128)(2,1)S(1)}, u32[]{:S(2)}, u32[]{:S(2)}) collective-permute-start(bf16[128,256]{1,0:T(8,128)(2,1)} %param.6), channel_id=1, source_target_pairs={{0,1},{1,0},{2,3},{3,2},{4,5},{5,4},{6,7},{7,6},{8,9},{9,8},{10,11... | collective-permute-start | bytes 196616 | tf_op jit(solution)/shard_map/ppermute | solution.py:27
  5.5 3.8 %collective-permute-start.3 = (bf16[65,128]{1,0:T(8,128)(2,1)S(1)}, bf16[65,128]{1,0:T(8,128)(2,1)S(1)}, u32[]{:S(2)}, u32[]{:S(2)}) collective-permute-start(bf16[65,128]{1,0:T(8,128)(2,1)S(1)} %pad_maximum_fusion.3), channel_id=1, source_target_pairs={{0,4},{4,0},{8,12},{12,8},{16,20},{20,16},{24,28},{28,24},{1,5},{5... | collective-permute-start | bytes 49928 | tf_op jit(solution)/shard_map/ppermute | solution.py:41
  7.2 14.9 %collective-permute-start.2 = (f32[256,128]{1,0:T(8,128)S(1)}, f32[256,128]{1,0:T(8,128)S(1)}, u32[]{:S(2)}, u32[]{:S(2)}) collective-permute-start(f32[256,128]{1,0:T(8,128)S(1)} %copy-done), channel_id=1, source_target_pairs={{0,3},{1,2},{2,1},{3,0},{4,7},{5,6},{6,5},{7,4},{8,11},{9,10},{10,... | collective-permute-start | bytes 393224 | tf_op jit(solution)/shard_map/ppermute | solution.py:27
  9.3 3.8 %collective-permute-start.4 = (bf16[65,128]{1,0:T(8,128)(2,1)S(1)}, bf16[65,128]{1,0:T(8,128)(2,1)S(1)}, u32[]{:S(2)}, u32[]{:S(2)}) collective-permute-start(bf16[65,128]{1,0:T(8,128)(2,1)S(1)} %pad_maximum_fusion.4), channel_id=1, source_target_pairs={{0,8},{4,12},{8,0},{12,4},{16,24},{20,28},{24,16},{28,20},{1,9},{5... | collective-permute-start | bytes 49928 | tf_op jit(solution)/shard_map/ppermute | solution.py:49
  13.2 9.0 %collective-permute-start.1 = (f32[256,128]{1,0:T(8,128)S(1)}, f32[256,128]{1,0:T(8,128)S(1)}, u32[]{:S(2)}, u32[]{:S(2)}) collective-permute-start(f32[256,128]{1,0:T(8,128)S(1)} %copy-done), channel_id=1, source_target_pairs={{0,2},{1,3},{2,0},{3,1},{4,6},{5,7},{6,4},{7,5},{8,10},{9,11},{10,... | collective-permute-start | bytes 393224 | tf_op jit(solution)/shard_map/ppermute | solution.py:27
  14.9 2.8 %copy-start.1 = (bf16[128,256]{1,0:T(8,128)(2,1)S(1)}, bf16[128,256]{1,0:T(8,128)(2,1)}, u32[]{:S(2)}) copy-start(bf16[128,256]{1,0:T(8,128)(2,1)} %param.6) | copy-start | bytes 196612
  15.0 6.1 %collective-permute-start = (f32[256,128]{1,0:T(8,128)S(1)}, f32[256,128]{1,0:T(8,128)S(1)}, u32[]{:S(2)}, u32[]{:S(2)}) collective-permute-start(f32[256,128]{1,0:T(8,128)S(1)} %copy-done), channel_id=1, source_target_pairs={{0,1},{1,0},{2,3},{3,2},{4,5},{5,4},{6,7},{7,6},{8,9},{9,8},{10,11... | collective-permute-start | bytes 393224 | tf_op jit(solution)/shard_map/ppermute | solution.py:27
  15.0 4.9 %collective-permute-start.5 = (bf16[130,128]{1,0:T(8,128)(2,1)S(1)}, bf16[130,128]{1,0:T(8,128)(2,1)S(1)}, u32[]{:S(2)}, u32[]{:S(2)}) collective-permute-start(bf16[130,128]{1,0:T(8,128)(2,1)S(1)} %pad_maximum_fusion.2), channel_id=1, source_target_pairs={{0,16},{4,20},{8,24},{12,28},{16,0},{20,4},{24,8},{28,12},{1,17},{... | collective-permute-start | bytes 99848 | tf_op jit(solution)/shard_map/ppermute | solution.py:49
  20.0 4.2 %collective-permute-start.11 = (bf16[256,128]{1,0:T(8,128)(2,1)S(1)}, bf16[256,128]{1,0:T(8,128)(2,1)S(1)}, u32[]{:S(2)}, u32[]{:S(2)}) collective-permute-start(bf16[256,128]{1,0:T(8,128)(2,1)S(1)} %maximum_select_fusion), channel_id=1, source_target_pairs={{0,3},{1,2},{2,1},{3,0},{4,7},{5,6},{6,5},{7,4},{8,11},{9,10},{10,... | collective-permute-start | bytes 196616 | tf_op jit(solution)/shard_map/ppermute | solution.py:27
  20.1 5.0 %collective-permute-start.10 = (bf16[256,128]{1,0:T(8,128)(2,1)S(1)}, bf16[256,128]{1,0:T(8,128)(2,1)S(1)}, u32[]{:S(2)}, u32[]{:S(2)}) collective-permute-start(bf16[256,128]{1,0:T(8,128)(2,1)S(1)} %maximum_select_fusion), channel_id=1, source_target_pairs={{0,2},{1,3},{2,0},{3,1},{4,6},{5,7},{6,4},{7,5},{8,10},{9,11},{10,... | collective-permute-start | bytes 196616 | tf_op jit(solution)/shard_map/ppermute | solution.py:27
  21.1 4.1 %collective-permute-start.9 = (bf16[256,128]{1,0:T(8,128)(2,1)S(1)}, bf16[256,128]{1,0:T(8,128)(2,1)S(1)}, u32[]{:S(2)}, u32[]{:S(2)}) collective-permute-start(bf16[256,128]{1,0:T(8,128)(2,1)S(1)} %maximum_select_fusion), channel_id=1, source_target_pairs={{0,1},{1,0},{2,3},{3,2},{4,5},{5,4},{6,7},{7,6},{8,9},{9,8},{10,11... | collective-permute-start | bytes 196616 | tf_op jit(solution)/shard_map/ppermute | solution.py:27
  25.4 0.7 %copy-start.2 = (f32[256]{0:T(256)S(1)}, f32[256]{0:T(256)}, u32[]{:S(2)}) copy-start(f32[256]{0:T(256)} %param.5) | copy-start | bytes 3076
  44.9 3.8 %collective-permute-start.14 = (bf16[256,128]{1,0:T(8,128)(2,1)S(1)}, bf16[256,128]{1,0:T(8,128)(2,1)S(1)}, u32[]{:S(2)}, u32[]{:S(2)}) collective-permute-start(bf16[256,128]{1,0:T(8,128)(2,1)S(1)} %bitcast.42), channel_id=1, source_target_pairs={{0,3},{1,2},{2,1},{3,0},{4,7},{5,6},{6,5},{7,4},{8,11},{9,10},{10,... | collective-permute-start | bytes 196616 | tf_op jit(solution)/shard_map/ppermute | solution.py:27
  44.9 5.0 %collective-permute-start.13 = (bf16[256,128]{1,0:T(8,128)(2,1)S(1)}, bf16[256,128]{1,0:T(8,128)(2,1)S(1)}, u32[]{:S(2)}, u32[]{:S(2)}) collective-permute-start(bf16[256,128]{1,0:T(8,128)(2,1)S(1)} %bitcast.43), channel_id=1, source_target_pairs={{0,2},{1,3},{2,0},{3,1},{4,6},{5,7},{6,4},{7,5},{8,10},{9,11},{10,... | collective-permute-start | bytes 196616 | tf_op jit(solution)/shard_map/ppermute | solution.py:27
  45.4 4.7 %collective-permute-start.12 = (bf16[256,128]{1,0:T(8,128)(2,1)S(1)}, bf16[256,128]{1,0:T(8,128)(2,1)S(1)}, u32[]{:S(2)}, u32[]{:S(2)}) collective-permute-start(bf16[256,128]{1,0:T(8,128)(2,1)S(1)} %bitcast.44), channel_id=1, source_target_pairs={{0,1},{1,0},{2,3},{3,2},{4,5},{5,4},{6,7},{7,6},{8,9},{9,8},{10,11... | collective-permute-start | bytes 196616 | tf_op jit(solution)/shard_map/ppermute | solution.py:27

commit v8 on v5

--- a/solution.py
+++ b/solution.py
@@ -35,54 +35,51 @@
 
 
 def body(orbitals, potential, fitted, points):
-    if lax.axis_size("grid") > 8 or lax.axis_size("grid") % 2 or points.shape[0] > orbitals.shape[1]:
+    ngroups = lax.axis_size("grid")
+    nbands = lax.axis_size("band")
+    nslots = points.shape[0]
+    block_width = orbitals.shape[1]
+    if ngroups > 8 or ngroups % 2 or nbands & (nbands - 1) or nslots > block_width:
         return body_spread(orbitals, potential, fitted, points)
     rows = orbitals.shape[0]
-    block_width = orbitals.shape[1]
-    nbands = lax.axis_size("band")
-    ngroups = lax.axis_size("grid")
     band = lax.axis_index("band")
     total_orbitals = block_width * nbands
     valid_mask = points >= 0
     safe_idx = jnp.where(valid_mask, points, 0)
+    selected = jnp.where(valid_mask[:, None], orbitals[safe_idx], 0.0).astype(jnp.bfloat16)
+    filled = jnp.pad(valid_mask.astype(jnp.bfloat16), (0, block_width - nslots))
+    to_band = jnp.concatenate([orbitals.astype(jnp.bfloat16), fitted.reshape(-1, block_width)], 0)
+    sent, to_band = lax.optimization_barrier((grid_copies(jnp.concatenate([selected, filled[None]], 0)), to_band))
+    got = grid_exchange(sent).reshape(ngroups, nslots + 1, block_width)
+    swapped = band_swap(to_band)
+    rows_b = jnp.concatenate([part[:rows] for part in swapped], 1)
+    fitted_got = jnp.stack([part[rows:].reshape(fitted.shape) for part in swapped], 0)
+    fitted_all = jnp.take(fitted_got, jnp.arange(nbands, dtype=jnp.int32) ^ band, axis=0)
+    fitted_all = fitted_all.reshape(ngroups // 2, 2, nslots, fitted.shape[1])
+    coll = jnp.concatenate(band_swap(pair_up(got[:, :nslots])), 1)
+    first_filled = got[:, nslots, :nslots].reshape(ngroups // 2, 2, nslots)[:, 0] > 0
+    fitted_all = jnp.where(
+        first_filled[:, :, None], fitted_all[:, 0], jnp.flip(fitted_all[:, 1], axis=1)
+    ).reshape(-1, fitted.shape[1]).astype(jnp.float32)
+    psi = orbitals
     pot = potential[:, None]
-    sq = None
     for step in range(ITERS):
-        if sq is None:
-            own_b = orbitals.astype(jnp.bfloat16)
-            nslots = points.shape[0]
-            selected = jnp.where(valid_mask[:, None], own_b[safe_idx], jnp.zeros((), jnp.bfloat16))
-            filled = jnp.pad(valid_mask.astype(jnp.bfloat16), (0, block_width - nslots))
-            payload = jnp.concatenate([selected, filled[None]], 0)
-            sent, rows_own, fitted_own = lax.optimization_barrier((grid_copies(payload), orbitals, fitted))
-            got = grid_exchange(sent).reshape(ngroups, nslots + 1, block_width)
-            psi = jnp.concatenate(band_swap(rows_own), 1)
-            fitted_got = jnp.stack(band_swap(fitted_own), 0)
-            fitted_all = jnp.take(fitted_got, jnp.arange(nbands, dtype=jnp.int32) ^ band, axis=0)
-            fitted_all = fitted_all.reshape(ngroups // 2, 2, nslots, fitted.shape[1])
-            coll = jnp.concatenate(band_swap(pair_up(got[:, :nslots])), 1)
-            first_filled = got[:, nslots, :nslots].reshape(ngroups // 2, 2, nslots)[:, 0] > 0
-            fitted_all = jnp.where(
-                first_filled[:, :, None], fitted_all[:, 0], jnp.flip(fitted_all[:, 1], axis=1)
-            ).reshape(-1, fitted.shape[1]).astype(jnp.float32)
-            orbital_block = psi.astype(jnp.bfloat16)
-        else:
-            own = psi[:, :block_width]
-            at_slots = jnp.where(valid_mask[:, None], own[safe_idx], 0.0)
-            nslots = at_slots.shape[0]
-            payload = jnp.concatenate([at_slots, sq.reshape(nbands, block_width)], 0)
-            got = grid_gather(payload).reshape(ngroups, nslots + nbands, block_width)
-            total = jnp.sum(got[:, nslots:], axis=0).reshape(total_orbitals)
+        if step:
+            at_slots = jnp.where(valid_mask[:, None], psi[safe_idx], 0.0)
+            got = grid_gather(jnp.concatenate([at_slots, sq[None]], 0)).reshape(ngroups, nslots + 1, block_width)
+            total = jnp.sum(got[:, nslots], axis=0)
             scale = lax.rsqrt(total / (rows * ngroups) + 1e-06)
-            coll_own = pair_up((got[:, :nslots] * scale[:block_width]).astype(jnp.bfloat16))
-            coll = jnp.concatenate(band_swap(coll_own), 1)
+            coll_own = pair_up((got[:, :nslots] * scale).astype(jnp.bfloat16))
             psi = psi * scale
-            orbital_block = psi.astype(jnp.bfloat16)
+            ncoll = coll_own.shape[0]
+            swapped = band_swap(jnp.concatenate([coll_own, psi.astype(jnp.bfloat16)], 0))
+            coll = jnp.concatenate([part[:ncoll] for part in swapped], 1)
+            rows_b = jnp.concatenate([part[ncoll:] for part in swapped], 1)
         proj = None
         for k in range(nbands):
             part = lax.dot_general(
                 coll[:, k * block_width:(k + 1) * block_width],
-                orbital_block[:, k * block_width:(k + 1) * block_width],
+                rows_b[:, k * block_width:(k + 1) * block_width],
                 (((1,), (1,)), ((), ())),
                 preferred_element_type=jnp.float32,
             )
@@ -90,12 +87,12 @@
             proj = part if proj is None else proj + part
         tile_blocks = (fitted_all * proj).astype(jnp.bfloat16)
         applied = lax.dot_general(
-            tile_blocks, coll, (((0,), (0,)), ((), ())), preferred_element_type=jnp.float32
+            tile_blocks, coll[:, :block_width], (((0,), (0,)), ((), ())), preferred_element_type=jnp.float32
         )
         psi = psi - 0.25 * (pot * psi - applied)
         sq = jnp.sum(psi * psi, axis=0)
-    total = jnp.sum(grid_gather(sq[None, :block_width]), axis=0)
-    return psi[:, :block_width] * lax.rsqrt(total / (rows * ngroups) + 1e-06)
+    total = jnp.sum(grid_gather(sq[None]), axis=0)
+    return psi * lax.rsqrt(total / (rows * ngroups) + 1e-06)
 
 
 def body_spread(orbitals, potential, fitted, points):

time: 59.9 us -> 59.2 us (0.988)
  starting transfers between devices: 14.9 us -> 13.6 us
  waiting for transfers between devices: 13.2 us -> 14.1 us
    ppermute x12 -> x9, starting transfers between devices: 9.04 us -> 7.57 us  [band_swap(): got.append(lax.ppermute(x, 'band', [(i, i ^ k) for i in range(nbands)]))]
    ppermute x12 -> x9, waiting for transfers between devices: 7.51 us -> 7.92 us  [band_swap(): got.append(lax.ppermute(x, 'band', [(i, i ^ k) for i in range(nbands)]))]
  transfers between devices with their start and end apart: 13 -> 10, of which waited for: 7 -> 6; matrix products, arithmetic and copies ran while one was open for 3% -> 4% of each run, Pallas kernels for 0% -> 0%
where the time goes in v8:
time: 59.2 us; the launch traced here: 58.9 us
  blocking collectives  22.2 us (38%)
  waiting for transfers between devices  14.1 us (24%)
  starting transfers between devices  13.6 us (23%)
  local copies, waits for them, and re-layouts  3.7 us (6%)
  other arithmetic  2.91 us (5%)
  matrix products  2.02 us (3%)
    all_to_all x2, blocking collectives, grid_exchange(): got = lax.all_to_all(sent, 'grid', 0, 0, tiled=True)  22.2 us
    ppermute x9, waiting for transfers between devices, band_swap(): got.append(lax.ppermute(x, 'band', [(i, i ^ k) for i in range(nbands)]))  7.92 us
    ppermute x9, starting transfers between devices, band_swap(): got.append(lax.ppermute(x, 'band', [(i, i ^ k) for i in range(nbands)]))  7.57 us
    all_to_all x1, waiting for transfers between devices, grid_exchange(): got = lax.all_to_all(sent, 'grid', 0, 0, tiled=True)  6.17 us
    all_to_all x1, starting transfers between devices, grid_exchange(): got = lax.all_to_all(sent, 'grid', 0, 0, tiled=True)  6.06 us
  transfers between devices with their start and end apart: 10, of which 6 were waited for; matrix products, arithmetic and copies ran while one was open for 4% of the time, Pallas kernels for 0%

profile of v8, /device:TPU:0, one launch (start us, length us, event | category | flops | bytes accessed | tf_op | source)
XLA Modules:
  0.0 58.9 jit_solution(4174036328749021536)
XLA Ops:
  0.0 0.7 %broadcast_compare_fusion = pred[64]{0:T(512)(128)(4,1)S(1)} fusion(s32[64]{0:T(128)} %param.7), kind=kLoop, calls=%fused_computation.94 | loop fusion | flops 64 | bytes 320 | tf_op jit(solution)/shard_map/ge | solution.py:47
  0.7 0.0 copy-done.3
  0.8 0.9 %convert_element_type.76 = bf16[256,128]{1,0:T(8,128)(2,1)S(1)} convert(f32[256,128]{1,0:T(8,128)} %param.4) | non-fusion elementwise | flops 32768 | bytes 196608 | tf_op jit(solution)/shard_map/convert_element_type | solution.py:51
  1.7 0.0 copy-done
  1.7 0.0 copy-start.1
  1.7 0.6 %gather_fusion = bf16[64,128]{1,0:T(8,128)(2,1)S(1)} fusion(f32[256,128]{1,0:T(8,128)S(1)} %copy-done, s32[1024]{0:T(1024)S(1)} %pad_clamp_fusion.1), kind=kCustom, calls=%fused_computation | custom fusion | bytes 33024 | tf_op jit(solution)/shard_map/gather | solution.py:49
  2.3 0.1 select_convert_fusion
  2.4 0.1 copy-done.1
  2.6 0.7 %broadcast_in_dim.78 = bf16[8,65,128]{2,1,0:T(8,128)(2,1)} broadcast(bf16[65,128]{1,0:T(8,128)(2,1)S(1)} %pad_maximum_fusion.4), dimensions={1,2} | broadcast | bytes 149760 | tf_op jit(solution)/shard_map/broadcast_in_dim | solution.py:11
  3.3 0.5 collective-permute-start
  3.7 2.5 %collective-permute-start.1 = (bf16[512,128]{1,0:T(8,128)(2,1)S(1)}, bf16[512,128]{1,0:T(8,128)(2,1)S(1)}, u32[]{:S(2)}, u32[]{:S(2)}) collective-permute-start(bf16[512,128]{1,0:T(8,128)(2,1)S(1)} %pad_maximum_fusion.1), channel_id=1, source_target_pairs={{0,2},{1,3},{2,0},{3,1},{4,6},{5,7},{6,4},{7,5},{8,10},{9,11},{10,... | collective-permute-start | bytes 393224 | tf_op jit(solution)/shard_map/ppermute | solution.py:27
  6.2 0.1 collective-permute-start.2
  6.3 6.1 %all-to-all-start = ((bf16[8,65,128]{2,1,0:T(8,128)(2,1)}), bf16[8,65,128]{2,1,0:T(8,128)(2,1)S(1)}, u32[]{:S(2)}, u32[]{:S(2)}) async-start(bf16[8,65,128]{2,1,0:T(8,128)(2,1)} %broadcast_in_dim.78), calls=%async_computation | async-start | bytes 294912 | tf_op jit(solution)/shard_map/all_to_all | solution.py:15
  12.5 0.0 collective-permute-done
  12.5 0.0 collective-permute-done.1
  12.6 0.4 collective-permute-done.2
  13.1 0.6 gather_fusion.1
  13.6 0.1 broadcast_select_fusion
  13.8 0.1 rev.11
  13.9 6.2 %all-to-all-done = bf16[8,65,128]{2,1,0:T(8,128)(2,1)S(1)} async-done(((bf16[8,65,128]{2,1,0:T(8,128)(2,1)}), bf16[8,65,128]{2,1,0:T(8,128)(2,1)S(1)}, u32[]{:S(2)}, u32[]{:S(2)}) %all-to-all-start) | async-done | bytes 133152 | tf_op jit(solution)/shard_map/all_to_all | solution.py:15
  20.1 1.6 %collective-permute-start.4 = (bf16[256,128]{1,0:T(8,128)(2,1)S(1)}, bf16[256,128]{1,0:T(8,128)(2,1)S(1)}, u32[]{:S(2)}, u32[]{:S(2)}) collective-permute-start(bf16[256,128]{1,0:T(8,128)(2,1)S(1)} %bitcast.53), channel_id=1, source_target_pairs={{0,2},{1,3},{2,0},{3,1},{4,6},{5,7},{6,4},{7,5},{8,10},{9,11},{10,... | collective-permute-start | bytes 196616 | tf_op jit(solution)/shard_map/ppermute | solution.py:27
  21.7 0.0 collective-permute-start.5
  21.7 0.2 fusion.1
  21.9 0.7 %collective-permute-start.3 = (bf16[256,128]{1,0:T(8,128)(2,1)S(1)}, bf16[256,128]{1,0:T(8,128)(2,1)S(1)}, u32[]{:S(2)}, u32[]{:S(2)}) collective-permute-start(bf16[256,128]{1,0:T(8,128)(2,1)S(1)} %bitcast.56), channel_id=1, source_target_pairs={{0,1},{1,0},{2,3},{3,2},{4,5},{5,4},{6,7},{7,6},{8,9},{9,8},{10,11... | collective-permute-start | bytes 196616 | tf_op jit(solution)/shard_map/ppermute | solution.py:27
  22.7 0.1 fusion.33
  22.8 1.7 %collective-permute-done.4 = bf16[256,128]{1,0:T(8,128)(2,1)S(1)} collective-permute-done((bf16[256,128]{1,0:T(8,128)(2,1)S(1)}, bf16[256,128]{1,0:T(8,128)(2,1)S(1)}, u32[]{:S(2)}, u32[]{:S(2)}) %collective-permute-start.4) | collective-permute-done | bytes 65568 | tf_op jit(solution)/shard_map/ppermute | solution.py:27
  24.5 0.2 fusion.9
  24.7 1.2 %collective-permute-done.5 = bf16[256,128]{1,0:T(8,128)(2,1)S(1)} collective-permute-done((bf16[256,128]{1,0:T(8,128)(2,1)S(1)}, bf16[256,128]{1,0:T(8,128)(2,1)S(1)}, u32[]{:S(2)}, u32[]{:S(2)}) %collective-permute-start.5) | collective-permute-done | bytes 65568 | tf_op jit(solution)/shard_map/ppermute | solution.py:27
  25.9 0.2 fusion.11
  26.1 0.0 copy-start.2
  26.1 0.0 collective-permute-done.3
  26.1 0.7 %copy-done.2 = f32[256]{0:T(256)S(1)} copy-done((f32[256]{0:T(256)S(1)}, f32[256]{0:T(256)}, u32[]{:S(2)}) %copy-start.2) | copy-done | bytes 1048
  26.8 0.5 multiply_reduce_fusion.1
  27.2 0.6 %gather_fusion.2 = f32[64,128]{1,0:T(8,128)S(1)} fusion(f32[256,128]{1,0:T(8,128)S(1)} %get-tuple-element.10, s32[1024]{0:T(1024)S(1)} %pad_clamp_fusion.1), kind=kCustom, calls=%fused_computation.2 | custom fusion | bytes 65792 | tf_op jit(solution)/shard_map/gather | solution.py:68
  27.8 0.1 broadcast_select_fusion.1
  27.9 13.1 %all_to_all.15 = f32[8,65,128]{2,1,0:T(8,128)S(1)} all-to-all(f32[8,65,128]{2,1,0:T(8,128)S(1)} %broadcast_in_dim.83), channel_id=1, replica_groups=mesh['grid'=8,'band'=4] {'grid'}, dimensions={0} | all-to-all | bytes 532480 | tf_op jit(solution)/shard_map/all_to_all | solution.py:15
  41.2 1.4 %collective-permute-start.7 = (bf16[512,128]{1,0:T(8,128)(2,1)S(1)}, bf16[512,128]{1,0:T(8,128)(2,1)S(1)}, u32[]{:S(2)}, u32[]{:S(2)}) collective-permute-start(bf16[512,128]{1,0:T(8,128)(2,1)S(1)} %pad_maximum_fusion.2), channel_id=1, source_target_pairs={{0,2},{1,3},{2,0},{3,1},{4,6},{5,7},{6,4},{7,5},{8,10},{9,11},{10,... | collective-permute-start | bytes 393224 | tf_op jit(solution)/shard_map/ppermute | solution.py:27
  42.6 0.0 collective-permute-start.8
  42.6 0.8 %collective-permute-start.6 = (bf16[512,128]{1,0:T(8,128)(2,1)S(1)}, bf16[512,128]{1,0:T(8,128)(2,1)S(1)}, u32[]{:S(2)}, u32[]{:S(2)}) collective-permute-start(bf16[512,128]{1,0:T(8,128)(2,1)S(1)} %pad_maximum_fusion.2), channel_id=1, source_target_pairs={{0,1},{1,0},{2,3},{3,2},{4,5},{5,4},{6,7},{7,6},{8,9},{9,8},{10,11... | collective-permute-start | bytes 393224 | tf_op jit(solution)/shard_map/ppermute | solution.py:27
  43.4 0.2 fusion.13
  43.6 3.3 %collective-permute-done.7 = bf16[512,128]{1,0:T(8,128)(2,1)S(1)} collective-permute-done((bf16[512,128]{1,0:T(8,128)(2,1)S(1)}, bf16[512,128]{1,0:T(8,128)(2,1)S(1)}, u32[]{:S(2)}, u32[]{:S(2)}) %collective-permute-start.7) | collective-permute-done | bytes 131104 | tf_op jit(solution)/shard_map/ppermute | solution.py:27
  46.9 0.2 fusion.21
  47.1 1.3 %collective-permute-done.8 = bf16[512,128]{1,0:T(8,128)(2,1)S(1)} collective-permute-done((bf16[512,128]{1,0:T(8,128)(2,1)S(1)}, bf16[512,128]{1,0:T(8,128)(2,1)S(1)}, u32[]{:S(2)}, u32[]{:S(2)}) %collective-permute-start.8) | collective-permute-done | bytes 131104 | tf_op jit(solution)/shard_map/ppermute | solution.py:27
  48.4 0.2 fusion.23
  48.6 0.0 collective-permute-done.6
  48.6 0.5 multiply_reduce_fusion
  49.0 9.1 %all_to_all.16 = f32[8,1,128]{2,1,0:T(1,128)S(1)} all-to-all(f32[8,1,128]{2,1,0:T(1,128)S(1)} %broadcast_in_dim.84), channel_id=1, replica_groups=mesh['grid'=8,'band'=4] {'grid'}, dimensions={0} | all-to-all | bytes 8192 | tf_op jit(solution)/shard_map/all_to_all | solution.py:15
  58.2 0.7 %broadcast_multiply_fusion = f32[256,128]{1,0:T(8,128)} fusion(f32[256,128]{1,0:T(8,128)S(1)} %get-tuple-element.12, f32[128]{0:T(128)S(1)} %add_rsqrt_fusion), kind=kLoop, calls=%fused_computation.74 | loop fusion | flops 32768 | bytes 262656 | tf_op jit(solution)/shard_map/mul | solution.py:95
  (42 shorter events, 0.6 us)
Async XLA Ops:
  0.0 0.7 %copy-start.3 = (s32[64]{0:T(128)S(1)}, s32[64]{0:T(128)}, u32[]{:S(2)}) copy-start(s32[64]{0:T(128)} %param.7) | copy-start | bytes 772
  0.0 1.7 %copy-start = (f32[256,128]{1,0:T(8,128)S(1)}, f32[256,128]{1,0:T(8,128)}, u32[]{:S(2)}) copy-start(f32[256,128]{1,0:T(8,128)} %param.4) | copy-start | bytes 393220
  1.7 0.8 %copy-start.1 = (bf16[128,256]{1,0:T(8,128)(2,1)S(1)}, bf16[128,256]{1,0:T(8,128)(2,1)}, u32[]{:S(2)}) copy-start(bf16[128,256]{1,0:T(8,128)(2,1)} %param.6) | copy-start | bytes 196612
  3.3 9.2 %collective-permute-start = (bf16[512,128]{1,0:T(8,128)(2,1)S(1)}, bf16[512,128]{1,0:T(8,128)(2,1)S(1)}, u32[]{:S(2)}, u32[]{:S(2)}) collective-permute-start(bf16[512,128]{1,0:T(8,128)(2,1)S(1)} %pad_maximum_fusion.1), channel_id=1, source_target_pairs={{0,1},{1,0},{2,3},{3,2},{4,5},{5,4},{6,7},{7,6},{8,9},{9,8},{10,11... | collective-permute-start | bytes 393224 | tf_op jit(solution)/shard_map/ppermute | solution.py:27
  3.7 8.8 %collective-permute-start.1 = (bf16[512,128]{1,0:T(8,128)(2,1)S(1)}, bf16[512,128]{1,0:T(8,128)(2,1)S(1)}, u32[]{:S(2)}, u32[]{:S(2)}) collective-permute-start(bf16[512,128]{1,0:T(8,128)(2,1)S(1)} %pad_maximum_fusion.1), channel_id=1, source_target_pairs={{0,2},{1,3},{2,0},{3,1},{4,6},{5,7},{6,4},{7,5},{8,10},{9,11},{10,... | collective-permute-start | bytes 393224 | tf_op jit(solution)/shard_map/ppermute | solution.py:27
  6.2 6.8 %collective-permute-start.2 = (bf16[512,128]{1,0:T(8,128)(2,1)S(1)}, bf16[512,128]{1,0:T(8,128)(2,1)S(1)}, u32[]{:S(2)}, u32[]{:S(2)}) collective-permute-start(bf16[512,128]{1,0:T(8,128)(2,1)S(1)} %pad_maximum_fusion.1), channel_id=1, source_target_pairs={{0,3},{1,2},{2,1},{3,0},{4,7},{5,6},{6,5},{7,4},{8,11},{9,10},{10,... | collective-permute-start | bytes 393224 | tf_op jit(solution)/shard_map/ppermute | solution.py:27
  6.3 13.7 %all-to-all-start = ((bf16[8,65,128]{2,1,0:T(8,128)(2,1)}), bf16[8,65,128]{2,1,0:T(8,128)(2,1)S(1)}, u32[]{:S(2)}, u32[]{:S(2)}) async-start(bf16[8,65,128]{2,1,0:T(8,128)(2,1)} %broadcast_in_dim.78), calls=%async_computation | async-start | bytes 294912 | tf_op jit(solution)/shard_map/all_to_all | solution.py:15
  20.1 4.3 %collective-permute-start.4 = (bf16[256,128]{1,0:T(8,128)(2,1)S(1)}, bf16[256,128]{1,0:T(8,128)(2,1)S(1)}, u32[]{:S(2)}, u32[]{:S(2)}) collective-permute-start(bf16[256,128]{1,0:T(8,128)(2,1)S(1)} %bitcast.53), channel_id=1, source_target_pairs={{0,2},{1,3},{2,0},{3,1},{4,6},{5,7},{6,4},{7,5},{8,10},{9,11},{10,... | collective-permute-start | bytes 196616 | tf_op jit(solution)/shard_map/ppermute | solution.py:27
  21.7 4.2 %collective-permute-start.5 = (bf16[256,128]{1,0:T(8,128)(2,1)S(1)}, bf16[256,128]{1,0:T(8,128)(2,1)S(1)}, u32[]{:S(2)}, u32[]{:S(2)}) collective-permute-start(bf16[256,128]{1,0:T(8,128)(2,1)S(1)} %bitcast.54), channel_id=1, source_target_pairs={{0,3},{1,2},{2,1},{3,0},{4,7},{5,6},{6,5},{7,4},{8,11},{9,10},{10,... | collective-permute-start | bytes 196616 | tf_op jit(solution)/shard_map/ppermute | solution.py:27
  21.9 4.2 %collective-permute-start.3 = (bf16[256,128]{1,0:T(8,128)(2,1)S(1)}, bf16[256,128]{1,0:T(8,128)(2,1)S(1)}, u32[]{:S(2)}, u32[]{:S(2)}) collective-permute-start(bf16[256,128]{1,0:T(8,128)(2,1)S(1)} %bitcast.56), channel_id=1, source_target_pairs={{0,1},{1,0},{2,3},{3,2},{4,5},{5,4},{6,7},{7,6},{8,9},{9,8},{10,11... | collective-permute-start | bytes 196616 | tf_op jit(solution)/shard_map/ppermute | solution.py:27
  26.1 0.7 %copy-start.2 = (f32[256]{0:T(256)S(1)}, f32[256]{0:T(256)}, u32[]{:S(2)}) copy-start(f32[256]{0:T(256)} %param.5) | copy-start | bytes 3076
  41.2 5.7 %collective-permute-start.7 = (bf16[512,128]{1,0:T(8,128)(2,1)S(1)}, bf16[512,128]{1,0:T(8,128)(2,1)S(1)}, u32[]{:S(2)}, u32[]{:S(2)}) collective-permute-start(bf16[512,128]{1,0:T(8,128)(2,1)S(1)} %pad_maximum_fusion.2), channel_id=1, source_target_pairs={{0,2},{1,3},{2,0},{3,1},{4,6},{5,7},{6,4},{7,5},{8,10},{9,11},{10,... | collective-permute-start | bytes 393224 | tf_op jit(solution)/shard_map/ppermute | solution.py:27
  42.6 5.8 %collective-permute-start.8 = (bf16[512,128]{1,0:T(8,128)(2,1)S(1)}, bf16[512,128]{1,0:T(8,128)(2,1)S(1)}, u32[]{:S(2)}, u32[]{:S(2)}) collective-permute-start(bf16[512,128]{1,0:T(8,128)(2,1)S(1)} %pad_maximum_fusion.2), channel_id=1, source_target_pairs={{0,3},{1,2},{2,1},{3,0},{4,7},{5,6},{6,5},{7,4},{8,11},{9,10},{10,... | collective-permute-start | bytes 393224 | tf_op jit(solution)/shard_map/ppermute | solution.py:27
  42.6 6.0 %collective-permute-start.6 = (bf16[512,128]{1,0:T(8,128)(2,1)S(1)}, bf16[512,128]{1,0:T(8,128)(2,1)S(1)}, u32[]{:S(2)}, u32[]{:S(2)}) collective-permute-start(bf16[512,128]{1,0:T(8,128)(2,1)S(1)} %pad_maximum_fusion.2), channel_id=1, source_target_pairs={{0,1},{1,0},{2,3},{3,2},{4,5},{5,4},{6,7},{7,6},{8,9},{9,8},{10,11... | collective-permute-start | bytes 393224 | tf_op jit(solution)/shard_map/ppermute | solution.py:27

commit v9 on v8

--- a/solution.py
+++ b/solution.py
@@ -65,11 +65,17 @@
     pot = potential[:, None]
     for step in range(ITERS):
         if step:
-            at_slots = jnp.where(valid_mask[:, None], psi[safe_idx], 0.0)
-            got = grid_gather(jnp.concatenate([at_slots, sq[None]], 0)).reshape(ngroups, nslots + 1, block_width)
-            total = jnp.sum(got[:, nslots], axis=0)
+            at_slots = jnp.where(valid_mask[:, None], psi[safe_idx], 0.0).astype(jnp.bfloat16)
+            high = lax.reduce_precision(sq, exponent_bits=8, mantissa_bits=7)
+            rest = sq - high
+            middle = lax.reduce_precision(rest, exponent_bits=8, mantissa_bits=7)
+            low = lax.reduce_precision(rest - middle, exponent_bits=8, mantissa_bits=7)
+            parts = jnp.stack([high, middle, low], 0).astype(jnp.bfloat16)
+            got = grid_gather(jnp.concatenate([at_slots, parts], 0)).reshape(ngroups, nslots + 3, block_width)
+            sums = got[:, nslots:].astype(jnp.float32)
+            total = jnp.sum((sums[:, 0] + sums[:, 1]) + sums[:, 2], axis=0)
             scale = lax.rsqrt(total / (rows * ngroups) + 1e-06)
-            coll_own = pair_up((got[:, :nslots] * scale).astype(jnp.bfloat16))
+            coll_own = pair_up((got[:, :nslots].astype(jnp.float32) * scale).astype(jnp.bfloat16))
             psi = psi * scale
             ncoll = coll_own.shape[0]
             swapped = band_swap(jnp.concatenate([coll_own, psi.astype(jnp.bfloat16)], 0))

time: 59.2 us -> 56.1 us (0.948)
  blocking collectives: 22.2 us -> 19.2 us
    all_to_all x2, blocking collectives: 22.2 us -> 19.2 us  [grid_exchange(): got = lax.all_to_all(sent, 'grid', 0, 0, tiled=True)]
where the time goes in v9:
time: 56.1 us; the launch traced here: 55.8 us
  blocking collectives  19.2 us (34%)
  waiting for transfers between devices  14 us (25%)
  starting transfers between devices  13.6 us (24%)
  local copies, waits for them, and re-layouts  3.71 us (7%)
  other arithmetic  2.94 us (5%)
  matrix products  2.02 us (4%)
    all_to_all x2, blocking collectives, grid_exchange(): got = lax.all_to_all(sent, 'grid', 0, 0, tiled=True)  19.2 us
    ppermute x9, waiting for transfers between devices, band_swap(): got.append(lax.ppermute(x, 'band', [(i, i ^ k) for i in range(nbands)]))  7.81 us
    ppermute x9, starting transfers between devices, band_swap(): got.append(lax.ppermute(x, 'band', [(i, i ^ k) for i in range(nbands)]))  7.56 us
    all_to_all x1, waiting for transfers between devices, grid_exchange(): got = lax.all_to_all(sent, 'grid', 0, 0, tiled=True)  6.17 us
    all_to_all x1, starting transfers between devices, grid_exchange(): got = lax.all_to_all(sent, 'grid', 0, 0, tiled=True)  6.06 us
  transfers between devices with their start and end apart: 10, of which 6 were waited for; matrix products, arithmetic and copies ran while one was open for 4% of the time, Pallas kernels for 0%

profile of v9, /device:TPU:0, one launch (start us, length us, event | category | flops | bytes accessed | tf_op | source)
XLA Modules:
  0.0 55.8 jit_solution(13368391493359075001)
XLA Ops:
  0.0 0.7 %broadcast_compare_fusion = pred[64]{0:T(512)(128)(4,1)S(1)} fusion(s32[64]{0:T(128)} %param.7), kind=kLoop, calls=%fused_computation.102 | loop fusion | flops 64 | bytes 320 | tf_op jit(solution)/shard_map/ge | solution.py:47
  0.7 0.0 copy-done.3
  0.8 0.9 %convert_element_type.86 = bf16[256,128]{1,0:T(8,128)(2,1)S(1)} convert(f32[256,128]{1,0:T(8,128)} %param.4) | non-fusion elementwise | flops 32768 | bytes 196608 | tf_op jit(solution)/shard_map/convert_element_type | solution.py:51
  1.7 0.0 copy-done
  1.7 0.0 copy-start.1
  1.7 0.6 %gather_fusion = bf16[64,128]{1,0:T(8,128)(2,1)S(1)} fusion(f32[256,128]{1,0:T(8,128)S(1)} %copy-done, s32[1024]{0:T(1024)S(1)} %pad_clamp_fusion.1), kind=kCustom, calls=%fused_computation | custom fusion | bytes 33024 | tf_op jit(solution)/shard_map/gather | solution.py:49
  2.3 0.1 select_convert_fusion.1
  2.4 0.1 copy-done.1
  2.6 0.7 %broadcast_in_dim.75 = bf16[8,65,128]{2,1,0:T(8,128)(2,1)} broadcast(bf16[65,128]{1,0:T(8,128)(2,1)S(1)} %pad_maximum_fusion.3), dimensions={1,2} | broadcast | bytes 149760 | tf_op jit(solution)/shard_map/broadcast_in_dim | solution.py:11
  3.3 0.5 collective-permute-start
  3.7 2.5 %collective-permute-start.1 = (bf16[512,128]{1,0:T(8,128)(2,1)S(1)}, bf16[512,128]{1,0:T(8,128)(2,1)S(1)}, u32[]{:S(2)}, u32[]{:S(2)}) collective-permute-start(bf16[512,128]{1,0:T(8,128)(2,1)S(1)} %pad_maximum_fusion.1), channel_id=1, source_target_pairs={{0,2},{1,3},{2,0},{3,1},{4,6},{5,7},{6,4},{7,5},{8,10},{9,11},{10,... | collective-permute-start | bytes 393224 | tf_op jit(solution)/shard_map/ppermute | solution.py:27
  6.2 0.1 collective-permute-start.2
  6.3 6.1 %all-to-all-start = ((bf16[8,65,128]{2,1,0:T(8,128)(2,1)}), bf16[8,65,128]{2,1,0:T(8,128)(2,1)S(1)}, u32[]{:S(2)}, u32[]{:S(2)}) async-start(bf16[8,65,128]{2,1,0:T(8,128)(2,1)} %broadcast_in_dim.75), calls=%async_computation | async-start | bytes 294912 | tf_op jit(solution)/shard_map/all_to_all | solution.py:15
  12.5 0.0 collective-permute-done
  12.5 0.0 collective-permute-done.1
  12.6 0.4 collective-permute-done.2
  13.1 0.6 %gather_fusion.1 = bf16[4,128,256]{2,1,0:T(8,128)(2,1)S(1)} fusion(bf16[4,128,256]{2,1,0:T(8,128)(2,1)S(1)} %pad_maximum_fusion, s32[1024]{0:T(1024)S(1)} %pad_clamp_fusion), kind=kCustom, calls=%fused_computation.1 | custom fusion | bytes 524304 | tf_op jit(solution)/shard_map/jit(_take)/gather | solution.py:57
  13.6 0.1 broadcast_select_fusion
  13.8 0.1 rev.11
  13.9 6.2 %all-to-all-done = bf16[8,65,128]{2,1,0:T(8,128)(2,1)S(1)} async-done(((bf16[8,65,128]{2,1,0:T(8,128)(2,1)}), bf16[8,65,128]{2,1,0:T(8,128)(2,1)S(1)}, u32[]{:S(2)}, u32[]{:S(2)}) %all-to-all-start) | async-done | bytes 133152 | tf_op jit(solution)/shard_map/all_to_all | solution.py:15
  20.2 1.6 %collective-permute-start.4 = (bf16[256,128]{1,0:T(8,128)(2,1)S(1)}, bf16[256,128]{1,0:T(8,128)(2,1)S(1)}, u32[]{:S(2)}, u32[]{:S(2)}) collective-permute-start(bf16[256,128]{1,0:T(8,128)(2,1)S(1)} %bitcast.59), channel_id=1, source_target_pairs={{0,2},{1,3},{2,0},{3,1},{4,6},{5,7},{6,4},{7,5},{8,10},{9,11},{10,... | collective-permute-start | bytes 196616 | tf_op jit(solution)/shard_map/ppermute | solution.py:27
  21.7 0.0 collective-permute-start.5
  21.7 0.2 fusion.1
  21.9 0.7 %collective-permute-start.3 = (bf16[256,128]{1,0:T(8,128)(2,1)S(1)}, bf16[256,128]{1,0:T(8,128)(2,1)S(1)}, u32[]{:S(2)}, u32[]{:S(2)}) collective-permute-start(bf16[256,128]{1,0:T(8,128)(2,1)S(1)} %bitcast.62), channel_id=1, source_target_pairs={{0,1},{1,0},{2,3},{3,2},{4,5},{5,4},{6,7},{7,6},{8,9},{9,8},{10,11... | collective-permute-start | bytes 196616 | tf_op jit(solution)/shard_map/ppermute | solution.py:27
  22.7 0.1 fusion.32
  22.8 1.7 %collective-permute-done.4 = bf16[256,128]{1,0:T(8,128)(2,1)S(1)} collective-permute-done((bf16[256,128]{1,0:T(8,128)(2,1)S(1)}, bf16[256,128]{1,0:T(8,128)(2,1)S(1)}, u32[]{:S(2)}, u32[]{:S(2)}) %collective-permute-start.4) | collective-permute-done | bytes 65568 | tf_op jit(solution)/shard_map/ppermute | solution.py:27
  24.5 0.2 fusion.9
  24.7 1.2 %collective-permute-done.5 = bf16[256,128]{1,0:T(8,128)(2,1)S(1)} collective-permute-done((bf16[256,128]{1,0:T(8,128)(2,1)S(1)}, bf16[256,128]{1,0:T(8,128)(2,1)S(1)}, u32[]{:S(2)}, u32[]{:S(2)}) %collective-permute-start.5) | collective-permute-done | bytes 65568 | tf_op jit(solution)/shard_map/ppermute | solution.py:27
  25.9 0.2 fusion.11
  26.1 0.0 copy-start.2
  26.1 0.0 collective-permute-done.3
  26.1 0.7 %copy-done.2 = f32[256]{0:T(256)S(1)} copy-done((f32[256]{0:T(256)S(1)}, f32[256]{0:T(256)}, u32[]{:S(2)}) %copy-start.2) | copy-done | bytes 1048
  26.8 0.5 multiply_reduce_fusion.1
  27.2 0.6 %gather_fusion.2 = bf16[64,128]{1,0:T(8,128)(2,1)S(1)} fusion(f32[256,128]{1,0:T(8,128)S(1)} %get-tuple-element.13, s32[1024]{0:T(1024)S(1)} %pad_clamp_fusion.1), kind=kCustom, calls=%fused_computation.2 | custom fusion | bytes 33024 | tf_op jit(solution)/shard_map/gather | solution.py:68
  27.8 0.1 select_convert_fusion
  28.0 10.1 %all_to_all.15 = bf16[8,67,128]{2,1,0:T(8,128)(2,1)S(1)} all-to-all(bf16[8,67,128]{2,1,0:T(8,128)(2,1)S(1)} %broadcast_in_dim.79), channel_id=1, replica_groups=mesh['grid'=8,'band'=4] {'grid'}, dimensions={0} | all-to-all | bytes 274432 | tf_op jit(solution)/shard_map/all_to_all | solution.py:15
  38.2 1.3 %collective-permute-start.7 = (bf16[512,128]{1,0:T(8,128)(2,1)S(1)}, bf16[512,128]{1,0:T(8,128)(2,1)S(1)}, u32[]{:S(2)}, u32[]{:S(2)}) collective-permute-start(bf16[512,128]{1,0:T(8,128)(2,1)S(1)} %pad_maximum_fusion.2), channel_id=1, source_target_pairs={{0,2},{1,3},{2,0},{3,1},{4,6},{5,7},{6,4},{7,5},{8,10},{9,11},{10,... | collective-permute-start | bytes 393224 | tf_op jit(solution)/shard_map/ppermute | solution.py:27
  39.6 0.0 collective-permute-start.8
  39.6 0.9 %collective-permute-start.6 = (bf16[512,128]{1,0:T(8,128)(2,1)S(1)}, bf16[512,128]{1,0:T(8,128)(2,1)S(1)}, u32[]{:S(2)}, u32[]{:S(2)}) collective-permute-start(bf16[512,128]{1,0:T(8,128)(2,1)S(1)} %pad_maximum_fusion.2), channel_id=1, source_target_pairs={{0,1},{1,0},{2,3},{3,2},{4,5},{5,4},{6,7},{7,6},{8,9},{9,8},{10,11... | collective-permute-start | bytes 393224 | tf_op jit(solution)/shard_map/ppermute | solution.py:27
  40.4 0.2 fusion.13
  40.6 3.4 %collective-permute-done.7 = bf16[512,128]{1,0:T(8,128)(2,1)S(1)} collective-permute-done((bf16[512,128]{1,0:T(8,128)(2,1)S(1)}, bf16[512,128]{1,0:T(8,128)(2,1)S(1)}, u32[]{:S(2)}, u32[]{:S(2)}) %collective-permute-start.7) | collective-permute-done | bytes 131104 | tf_op jit(solution)/shard_map/ppermute | solution.py:27
  44.0 0.2 fusion.21
  44.2 1.1 %collective-permute-done.8 = bf16[512,128]{1,0:T(8,128)(2,1)S(1)} collective-permute-done((bf16[512,128]{1,0:T(8,128)(2,1)S(1)}, bf16[512,128]{1,0:T(8,128)(2,1)S(1)}, u32[]{:S(2)}, u32[]{:S(2)}) %collective-permute-start.8) | collective-permute-done | bytes 131104 | tf_op jit(solution)/shard_map/ppermute | solution.py:27
  45.3 0.2 fusion.23
  45.5 0.0 collective-permute-done.6
  45.5 0.5 multiply_reduce_fusion
  46.0 9.1 %all_to_all.16 = f32[8,1,128]{2,1,0:T(1,128)S(1)} all-to-all(f32[8,1,128]{2,1,0:T(1,128)S(1)} %broadcast_in_dim.80), channel_id=1, replica_groups=mesh['grid'=8,'band'=4] {'grid'}, dimensions={0} | all-to-all | bytes 8192 | tf_op jit(solution)/shard_map/all_to_all | solution.py:15
  55.1 0.7 %broadcast_multiply_fusion = f32[256,128]{1,0:T(8,128)} fusion(f32[256,128]{1,0:T(8,128)S(1)} %get-tuple-element.15, f32[128]{0:T(128)S(1)} %add_rsqrt_fusion), kind=kLoop, calls=%fused_computation.73 | loop fusion | flops 32768 | bytes 262656 | tf_op jit(solution)/shard_map/mul | solution.py:101
  (44 shorter events, 0.6 us)
Async XLA Ops:
  0.0 0.7 %copy-start.3 = (s32[64]{0:T(128)S(1)}, s32[64]{0:T(128)}, u32[]{:S(2)}) copy-start(s32[64]{0:T(128)} %param.7) | copy-start | bytes 772
  0.0 1.7 %copy-start = (f32[256,128]{1,0:T(8,128)S(1)}, f32[256,128]{1,0:T(8,128)}, u32[]{:S(2)}) copy-start(f32[256,128]{1,0:T(8,128)} %param.4) | copy-start | bytes 393220
  1.7 0.8 %copy-start.1 = (bf16[128,256]{1,0:T(8,128)(2,1)S(1)}, bf16[128,256]{1,0:T(8,128)(2,1)}, u32[]{:S(2)}) copy-start(bf16[128,256]{1,0:T(8,128)(2,1)} %param.6) | copy-start | bytes 196612
  3.3 9.2 %collective-permute-start = (bf16[512,128]{1,0:T(8,128)(2,1)S(1)}, bf16[512,128]{1,0:T(8,128)(2,1)S(1)}, u32[]{:S(2)}, u32[]{:S(2)}) collective-permute-start(bf16[512,128]{1,0:T(8,128)(2,1)S(1)} %pad_maximum_fusion.1), channel_id=1, source_target_pairs={{0,1},{1,0},{2,3},{3,2},{4,5},{5,4},{6,7},{7,6},{8,9},{9,8},{10,11... | collective-permute-start | bytes 393224 | tf_op jit(solution)/shard_map/ppermute | solution.py:27
  3.7 8.8 %collective-permute-start.1 = (bf16[512,128]{1,0:T(8,128)(2,1)S(1)}, bf16[512,128]{1,0:T(8,128)(2,1)S(1)}, u32[]{:S(2)}, u32[]{:S(2)}) collective-permute-start(bf16[512,128]{1,0:T(8,128)(2,1)S(1)} %pad_maximum_fusion.1), channel_id=1, source_target_pairs={{0,2},{1,3},{2,0},{3,1},{4,6},{5,7},{6,4},{7,5},{8,10},{9,11},{10,... | collective-permute-start | bytes 393224 | tf_op jit(solution)/shard_map/ppermute | solution.py:27
  6.2 6.8 %collective-permute-start.2 = (bf16[512,128]{1,0:T(8,128)(2,1)S(1)}, bf16[512,128]{1,0:T(8,128)(2,1)S(1)}, u32[]{:S(2)}, u32[]{:S(2)}) collective-permute-start(bf16[512,128]{1,0:T(8,128)(2,1)S(1)} %pad_maximum_fusion.1), channel_id=1, source_target_pairs={{0,3},{1,2},{2,1},{3,0},{4,7},{5,6},{6,5},{7,4},{8,11},{9,10},{10,... | collective-permute-start | bytes 393224 | tf_op jit(solution)/shard_map/ppermute | solution.py:27
  6.3 13.7 %all-to-all-start = ((bf16[8,65,128]{2,1,0:T(8,128)(2,1)}), bf16[8,65,128]{2,1,0:T(8,128)(2,1)S(1)}, u32[]{:S(2)}, u32[]{:S(2)}) async-start(bf16[8,65,128]{2,1,0:T(8,128)(2,1)} %broadcast_in_dim.75), calls=%async_computation | async-start | bytes 294912 | tf_op jit(solution)/shard_map/all_to_all | solution.py:15
  20.2 4.3 %collective-permute-start.4 = (bf16[256,128]{1,0:T(8,128)(2,1)S(1)}, bf16[256,128]{1,0:T(8,128)(2,1)S(1)}, u32[]{:S(2)}, u32[]{:S(2)}) collective-permute-start(bf16[256,128]{1,0:T(8,128)(2,1)S(1)} %bitcast.59), channel_id=1, source_target_pairs={{0,2},{1,3},{2,0},{3,1},{4,6},{5,7},{6,4},{7,5},{8,10},{9,11},{10,... | collective-permute-start | bytes 196616 | tf_op jit(solution)/shard_map/ppermute | solution.py:27
  21.7 4.2 %collective-permute-start.5 = (bf16[256,128]{1,0:T(8,128)(2,1)S(1)}, bf16[256,128]{1,0:T(8,128)(2,1)S(1)}, u32[]{:S(2)}, u32[]{:S(2)}) collective-permute-start(bf16[256,128]{1,0:T(8,128)(2,1)S(1)} %bitcast.60), channel_id=1, source_target_pairs={{0,3},{1,2},{2,1},{3,0},{4,7},{5,6},{6,5},{7,4},{8,11},{9,10},{10,... | collective-permute-start | bytes 196616 | tf_op jit(solution)/shard_map/ppermute | solution.py:27
  21.9 4.2 %collective-permute-start.3 = (bf16[256,128]{1,0:T(8,128)(2,1)S(1)}, bf16[256,128]{1,0:T(8,128)(2,1)S(1)}, u32[]{:S(2)}, u32[]{:S(2)}) collective-permute-start(bf16[256,128]{1,0:T(8,128)(2,1)S(1)} %bitcast.62), channel_id=1, source_target_pairs={{0,1},{1,0},{2,3},{3,2},{4,5},{5,4},{6,7},{7,6},{8,9},{9,8},{10,11... | collective-permute-start | bytes 196616 | tf_op jit(solution)/shard_map/ppermute | solution.py:27
  26.1 0.7 %copy-start.2 = (f32[256]{0:T(256)S(1)}, f32[256]{0:T(256)}, u32[]{:S(2)}) copy-start(f32[256]{0:T(256)} %param.5) | copy-start | bytes 3076
  38.2 5.8 %collective-permute-start.7 = (bf16[512,128]{1,0:T(8,128)(2,1)S(1)}, bf16[512,128]{1,0:T(8,128)(2,1)S(1)}, u32[]{:S(2)}, u32[]{:S(2)}) collective-permute-start(bf16[512,128]{1,0:T(8,128)(2,1)S(1)} %pad_maximum_fusion.2), channel_id=1, source_target_pairs={{0,2},{1,3},{2,0},{3,1},{4,6},{5,7},{6,4},{7,5},{8,10},{9,11},{10,... | collective-permute-start | bytes 393224 | tf_op jit(solution)/shard_map/ppermute | solution.py:27
  39.6 5.7 %collective-permute-start.8 = (bf16[512,128]{1,0:T(8,128)(2,1)S(1)}, bf16[512,128]{1,0:T(8,128)(2,1)S(1)}, u32[]{:S(2)}, u32[]{:S(2)}) collective-permute-start(bf16[512,128]{1,0:T(8,128)(2,1)S(1)} %pad_maximum_fusion.2), channel_id=1, source_target_pairs={{0,3},{1,2},{2,1},{3,0},{4,7},{5,6},{6,5},{7,4},{8,11},{9,10},{10,... | collective-permute-start | bytes 393224 | tf_op jit(solution)/shard_map/ppermute | solution.py:27
  39.6 5.9 %collective-permute-start.6 = (bf16[512,128]{1,0:T(8,128)(2,1)S(1)}, bf16[512,128]{1,0:T(8,128)(2,1)S(1)}, u32[]{:S(2)}, u32[]{:S(2)}) collective-permute-start(bf16[512,128]{1,0:T(8,128)(2,1)S(1)} %pad_maximum_fusion.2), channel_id=1, source_target_pairs={{0,1},{1,0},{2,3},{3,2},{4,5},{5,4},{6,7},{7,6},{8,9},{9,8},{10,11... | collective-permute-start | bytes 393224 | tf_op jit(solution)/shard_map/ppermute | solution.py:27

commit v10 on v9

--- a/solution.py
+++ b/solution.py
@@ -34,6 +34,19 @@
     return (pairs[:, 0] + jnp.flip(pairs[:, 1], axis=1)).reshape((ngroups // 2 * nslots,) + slots.shape[2:])
 
 
+def band_hops(x):
+    nbands = lax.axis_size("band")
+    held = {0: x}
+    bit = nbands // 2
+    while bit:
+        keys = sorted(held)
+        got = lax.ppermute(jnp.concatenate([held[k] for k in keys], 0), "band", [(i, i ^ bit) for i in range(nbands)])
+        for n, k in enumerate(keys):
+            held[k ^ bit] = got[n * x.shape[0]:(n + 1) * x.shape[0]]
+        bit //= 2
+    return [held[k] for k in range(nbands)]
+
+
 def body(orbitals, potential, fitted, points):
     ngroups = lax.axis_size("grid")
     nbands = lax.axis_size("band")
@@ -56,7 +69,7 @@
     fitted_got = jnp.stack([part[rows:].reshape(fitted.shape) for part in swapped], 0)
     fitted_all = jnp.take(fitted_got, jnp.arange(nbands, dtype=jnp.int32) ^ band, axis=0)
     fitted_all = fitted_all.reshape(ngroups // 2, 2, nslots, fitted.shape[1])
-    coll = jnp.concatenate(band_swap(pair_up(got[:, :nslots])), 1)
+    coll = jnp.concatenate(band_hops(pair_up(got[:, :nslots])), 1)
     first_filled = got[:, nslots, :nslots].reshape(ngroups // 2, 2, nslots)[:, 0] > 0
     fitted_all = jnp.where(
         first_filled[:, :, None], fitted_all[:, 0], jnp.flip(fitted_all[:, 1], axis=1)
@@ -78,7 +91,7 @@
             coll_own = pair_up((got[:, :nslots].astype(jnp.float32) * scale).astype(jnp.bfloat16))
             psi = psi * scale
             ncoll = coll_own.shape[0]
-            swapped = band_swap(jnp.concatenate([coll_own, psi.astype(jnp.bfloat16)], 0))
+            swapped = band_hops(jnp.concatenate([coll_own, psi.astype(jnp.bfloat16)], 0))
             coll = jnp.concatenate([part[:ncoll] for part in swapped], 1)
             rows_b = jnp.concatenate([part[ncoll:] for part in swapped], 1)
         proj = None

time: 56.1 us -> 56 us (level)
  starting transfers between devices: 13.6 us -> 12.4 us
  waiting for transfers between devices: 14 us -> 14.8 us
    ppermute x0 -> x4, waiting for transfers between devices: none -> 8.23 us  [band_hops(): lax.ppermute(jnp.concatenate([held[k] for k in keys], 0), 'band', [(i, i...]
    ppermute x9 -> x3, waiting for transfers between devices: 7.81 us -> 0.39 us  [band_swap(): got.append(lax.ppermute(x, 'band', [(i, i ^ k) for i in range(nbands)]))]
    ppermute x9 -> x3, starting transfers between devices: 7.56 us -> 3.09 us  [band_swap(): got.append(lax.ppermute(x, 'band', [(i, i ^ k) for i in range(nbands)]))]
    ppermute x0 -> x4, starting transfers between devices: none -> 3.25 us  [band_hops(): lax.ppermute(jnp.concatenate([held[k] for k in keys], 0), 'band', [(i, i...]
  transfers between devices with their start and end apart: 10 -> 8, of which waited for: 6 -> 6; matrix products, arithmetic and copies ran while one was open for 4% -> 3% of each run, Pallas kernels for 0% -> 0%
where the time goes in v10:
time: 56 us; the launch traced here: 55.7 us
  blocking collectives  19.4 us (35%)
  waiting for transfers between devices  14.8 us (26%)
  starting transfers between devices  12.4 us (22%)
  local copies, waits for them, and re-layouts  3.72 us (7%)
  other arithmetic  2.96 us (5%)
  matrix products  2.04 us (4%)
    all_to_all x2, blocking collectives, grid_exchange(): got = lax.all_to_all(sent, 'grid', 0, 0, tiled=True)  19.4 us
    ppermute x4, waiting for transfers between devices, band_hops(): lax.ppermute(jnp.concatenate([held[k] for k in keys], 0), 'band', [(i, i...  8.23 us
    all_to_all x1, waiting for transfers between devices, grid_exchange(): got = lax.all_to_all(sent, 'grid', 0, 0, tiled=True)  6.17 us
    all_to_all x1, starting transfers between devices, grid_exchange(): got = lax.all_to_all(sent, 'grid', 0, 0, tiled=True)  6.06 us
    ppermute x4, starting transfers between devices, band_hops(): lax.ppermute(jnp.concatenate([held[k] for k in keys], 0), 'band', [(i, i...  3.25 us
    ppermute x3, starting transfers between devices, band_swap(): got.append(lax.ppermute(x, 'band', [(i, i ^ k) for i in range(nbands)]))  3.09 us
  transfers between devices with their start and end apart: 8, of which 6 were waited for; matrix products, arithmetic and copies ran while one was open for 3% of the time, Pallas kernels for 0%

profile of v10, /device:TPU:0, one launch (start us, length us, event | category | flops | bytes accessed | tf_op | source)
XLA Modules:
  0.0 55.7 jit_solution(17367751041954464267)
XLA Ops:
  0.0 0.0 copy-start.3
  0.0 0.0 copy-start
  0.0 0.7 %broadcast_compare_fusion = pred[64]{0:T(512)(128)(4,1)S(1)} fusion(s32[64]{0:T(128)} %param.7), kind=kLoop, calls=%fused_computation.106 | loop fusion | flops 64 | bytes 320 | tf_op jit(solution)/shard_map/ge | solution.py:60
  0.7 0.0 copy-done.3
  0.8 0.9 %convert_element_type.86 = bf16[256,128]{1,0:T(8,128)(2,1)S(1)} convert(f32[256,128]{1,0:T(8,128)} %param.4) | non-fusion elementwise | flops 32768 | bytes 196608 | tf_op jit(solution)/shard_map/convert_element_type | solution.py:64
  1.7 0.0 copy-done
  1.7 0.0 copy-start.1
  1.7 0.6 %gather_fusion = bf16[64,128]{1,0:T(8,128)(2,1)S(1)} fusion(f32[256,128]{1,0:T(8,128)S(1)} %copy-done, s32[1024]{0:T(1024)S(1)} %pad_clamp_fusion.1), kind=kCustom, calls=%fused_computation | custom fusion | bytes 33024 | tf_op jit(solution)/shard_map/gather | solution.py:62
  2.3 0.1 select_convert_fusion.1
  2.4 0.1 copy-done.1
  2.6 0.7 %broadcast_in_dim.75 = bf16[8,65,128]{2,1,0:T(8,128)(2,1)} broadcast(bf16[65,128]{1,0:T(8,128)(2,1)S(1)} %pad_maximum_fusion.5), dimensions={1,2} | broadcast | bytes 149760 | tf_op jit(solution)/shard_map/broadcast_in_dim | solution.py:11
  3.3 0.5 collective-permute-start
  3.7 2.5 %collective-permute-start.1 = (bf16[512,128]{1,0:T(8,128)(2,1)S(1)}, bf16[512,128]{1,0:T(8,128)(2,1)S(1)}, u32[]{:S(2)}, u32[]{:S(2)}) collective-permute-start(bf16[512,128]{1,0:T(8,128)(2,1)S(1)} %pad_maximum_fusion.2), channel_id=1, source_target_pairs={{0,2},{1,3},{2,0},{3,1},{4,6},{5,7},{6,4},{7,5},{8,10},{9,11},{10,... | collective-permute-start | bytes 393224 | tf_op jit(solution)/shard_map/ppermute | solution.py:27
  6.2 0.1 collective-permute-start.2
  6.3 6.1 %all-to-all-start = ((bf16[8,65,128]{2,1,0:T(8,128)(2,1)}), bf16[8,65,128]{2,1,0:T(8,128)(2,1)S(1)}, u32[]{:S(2)}, u32[]{:S(2)}) async-start(bf16[8,65,128]{2,1,0:T(8,128)(2,1)} %broadcast_in_dim.75), calls=%async_computation | async-start | bytes 294912 | tf_op jit(solution)/shard_map/all_to_all | solution.py:15
  12.5 0.0 collective-permute-done
  12.5 0.0 collective-permute-done.1
  12.6 0.4 collective-permute-done.2
  13.1 0.6 %gather_fusion.1 = bf16[4,128,256]{2,1,0:T(8,128)(2,1)S(1)} fusion(bf16[4,128,256]{2,1,0:T(8,128)(2,1)S(1)} %pad_maximum_fusion, s32[1024]{0:T(1024)S(1)} %pad_clamp_fusion), kind=kCustom, calls=%fused_computation.1 | custom fusion | bytes 524304 | tf_op jit(solution)/shard_map/jit(_take)/gather | solution.py:70
  13.6 0.1 broadcast_select_fusion
  13.8 0.1 rev.11
  13.9 6.2 %all-to-all-done = bf16[8,65,128]{2,1,0:T(8,128)(2,1)S(1)} async-done(((bf16[8,65,128]{2,1,0:T(8,128)(2,1)}), bf16[8,65,128]{2,1,0:T(8,128)(2,1)S(1)}, u32[]{:S(2)}, u32[]{:S(2)}) %all-to-all-start) | async-done | bytes 133152 | tf_op jit(solution)/shard_map/all_to_all | solution.py:15
  20.2 1.6 %collective-permute-start.3 = (bf16[256,128]{1,0:T(8,128)(2,1)S(1)}, bf16[256,128]{1,0:T(8,128)(2,1)S(1)}, u32[]{:S(2)}, u32[]{:S(2)}) collective-permute-start(bf16[256,128]{1,0:T(8,128)(2,1)S(1)} %bitcast.58), channel_id=1, source_target_pairs={{0,2},{1,3},{2,0},{3,1},{4,6},{5,7},{6,4},{7,5},{8,10},{9,11},{10,... | collective-permute-start | bytes 196616 | tf_op jit(solution)/shard_map/ppermute | solution.py:43
  21.8 0.1 fusion.32
  21.9 0.2 fusion.1
  22.1 2.5 %collective-permute-done.3 = bf16[256,128]{1,0:T(8,128)(2,1)S(1)} collective-permute-done((bf16[256,128]{1,0:T(8,128)(2,1)S(1)}, bf16[256,128]{1,0:T(8,128)(2,1)S(1)}, u32[]{:S(2)}, u32[]{:S(2)}) %collective-permute-start.3) | collective-permute-done | bytes 65568 | tf_op jit(solution)/shard_map/ppermute | solution.py:43
  24.5 0.1 collective-permute-start.4
  24.6 0.2 fusion.9
  24.8 1.1 %collective-permute-done.4 = bf16[512,128]{1,0:T(8,128)(2,1)S(1)} collective-permute-done((bf16[512,128]{1,0:T(8,128)(2,1)S(1)}, bf16[512,128]{1,0:T(8,128)(2,1)S(1)}, u32[]{:S(2)}, u32[]{:S(2)}) %collective-permute-start.4) | collective-permute-done | bytes 131104 | tf_op jit(solution)/shard_map/ppermute | solution.py:43
  26.0 0.2 fusion.11
  26.1 0.0 copy-start.2
  26.2 0.7 %copy-done.2 = f32[256]{0:T(256)S(1)} copy-done((f32[256]{0:T(256)S(1)}, f32[256]{0:T(256)}, u32[]{:S(2)}) %copy-start.2) | copy-done | bytes 1048
  26.8 0.5 multiply_reduce_fusion.1
  27.3 0.6 %gather_fusion.2 = bf16[64,128]{1,0:T(8,128)(2,1)S(1)} fusion(f32[256,128]{1,0:T(8,128)S(1)} %get-tuple-element.13, s32[1024]{0:T(1024)S(1)} %pad_clamp_fusion.1), kind=kCustom, calls=%fused_computation.2 | custom fusion | bytes 33024 | tf_op jit(solution)/shard_map/gather | solution.py:81
  27.9 0.1 select_convert_fusion
  28.0 10.2 %all_to_all.15 = bf16[8,67,128]{2,1,0:T(8,128)(2,1)S(1)} all-to-all(bf16[8,67,128]{2,1,0:T(8,128)(2,1)S(1)} %broadcast_in_dim.79), channel_id=1, replica_groups=mesh['grid'=8,'band'=4] {'grid'}, dimensions={0} | all-to-all | bytes 274432 | tf_op jit(solution)/shard_map/all_to_all | solution.py:15
  38.4 1.6 %collective-permute-start.5 = (bf16[512,128]{1,0:T(8,128)(2,1)S(1)}, bf16[512,128]{1,0:T(8,128)(2,1)S(1)}, u32[]{:S(2)}, u32[]{:S(2)}) collective-permute-start(bf16[512,128]{1,0:T(8,128)(2,1)S(1)} %pad_maximum_fusion.4), channel_id=1, source_target_pairs={{0,2},{1,3},{2,0},{3,1},{4,6},{5,7},{6,4},{7,5},{8,10},{9,11},{10,... | collective-permute-start | bytes 393224 | tf_op jit(solution)/shard_map/ppermute | solution.py:43
  40.0 3.5 %collective-permute-done.5 = bf16[512,128]{1,0:T(8,128)(2,1)S(1)} collective-permute-done((bf16[512,128]{1,0:T(8,128)(2,1)S(1)}, bf16[512,128]{1,0:T(8,128)(2,1)S(1)}, u32[]{:S(2)}, u32[]{:S(2)}) %collective-permute-start.5) | collective-permute-done | bytes 131104 | tf_op jit(solution)/shard_map/ppermute | solution.py:43
  43.5 0.1 collective-permute-start.6
  43.6 0.2 fusion.13
  43.8 0.2 fusion.21
  44.0 1.1 %collective-permute-done.6 = bf16[1024,128]{1,0:T(8,128)(2,1)S(1)} collective-permute-done((bf16[1024,128]{1,0:T(8,128)(2,1)S(1)}, bf16[1024,128]{1,0:T(8,128)(2,1)S(1)}, u32[]{:S(2)}, u32[]{:S(2)}) %collective-permute-start.6) | collective-permute-done | bytes 262176 | tf_op jit(solution)/shard_map/ppermute | solution.py:43
  45.1 0.2 fusion.23
  45.3 0.5 multiply_reduce_fusion
  45.8 9.2 %all_to_all.16 = f32[8,1,128]{2,1,0:T(1,128)S(1)} all-to-all(f32[8,1,128]{2,1,0:T(1,128)S(1)} %broadcast_in_dim.80), channel_id=1, replica_groups=mesh['grid'=8,'band'=4] {'grid'}, dimensions={0} | all-to-all | bytes 8192 | tf_op jit(solution)/shard_map/all_to_all | solution.py:15
  55.0 0.7 %broadcast_multiply_fusion = f32[256,128]{1,0:T(8,128)} fusion(f32[256,128]{1,0:T(8,128)S(1)} %get-tuple-element.15, f32[128]{0:T(128)S(1)} %add_rsqrt_fusion), kind=kLoop, calls=%fused_computation.77 | loop fusion | flops 32768 | bytes 262656 | tf_op jit(solution)/shard_map/mul | solution.py:114
  (44 shorter events, 0.6 us)
Async XLA Ops:
  0.0 0.7 %copy-start.3 = (s32[64]{0:T(128)S(1)}, s32[64]{0:T(128)}, u32[]{:S(2)}) copy-start(s32[64]{0:T(128)} %param.7) | copy-start | bytes 772
  0.0 1.7 %copy-start = (f32[256,128]{1,0:T(8,128)S(1)}, f32[256,128]{1,0:T(8,128)}, u32[]{:S(2)}) copy-start(f32[256,128]{1,0:T(8,128)} %param.4) | copy-start | bytes 393220
  1.7 0.8 %copy-start.1 = (bf16[128,256]{1,0:T(8,128)(2,1)S(1)}, bf16[128,256]{1,0:T(8,128)(2,1)}, u32[]{:S(2)}) copy-start(bf16[128,256]{1,0:T(8,128)(2,1)} %param.6) | copy-start | bytes 196612
  3.3 9.2 %collective-permute-start = (bf16[512,128]{1,0:T(8,128)(2,1)S(1)}, bf16[512,128]{1,0:T(8,128)(2,1)S(1)}, u32[]{:S(2)}, u32[]{:S(2)}) collective-permute-start(bf16[512,128]{1,0:T(8,128)(2,1)S(1)} %pad_maximum_fusion.2), channel_id=1, source_target_pairs={{0,1},{1,0},{2,3},{3,2},{4,5},{5,4},{6,7},{7,6},{8,9},{9,8},{10,11... | collective-permute-start | bytes 393224 | tf_op jit(solution)/shard_map/ppermute | solution.py:27
  3.7 8.8 %collective-permute-start.1 = (bf16[512,128]{1,0:T(8,128)(2,1)S(1)}, bf16[512,128]{1,0:T(8,128)(2,1)S(1)}, u32[]{:S(2)}, u32[]{:S(2)}) collective-permute-start(bf16[512,128]{1,0:T(8,128)(2,1)S(1)} %pad_maximum_fusion.2), channel_id=1, source_target_pairs={{0,2},{1,3},{2,0},{3,1},{4,6},{5,7},{6,4},{7,5},{8,10},{9,11},{10,... | collective-permute-start | bytes 393224 | tf_op jit(solution)/shard_map/ppermute | solution.py:27
  6.2 6.8 %collective-permute-start.2 = (bf16[512,128]{1,0:T(8,128)(2,1)S(1)}, bf16[512,128]{1,0:T(8,128)(2,1)S(1)}, u32[]{:S(2)}, u32[]{:S(2)}) collective-permute-start(bf16[512,128]{1,0:T(8,128)(2,1)S(1)} %pad_maximum_fusion.2), channel_id=1, source_target_pairs={{0,3},{1,2},{2,1},{3,0},{4,7},{5,6},{6,5},{7,4},{8,11},{9,10},{10,... | collective-permute-start | bytes 393224 | tf_op jit(solution)/shard_map/ppermute | solution.py:27
  6.3 13.7 %all-to-all-start = ((bf16[8,65,128]{2,1,0:T(8,128)(2,1)}), bf16[8,65,128]{2,1,0:T(8,128)(2,1)S(1)}, u32[]{:S(2)}, u32[]{:S(2)}) async-start(bf16[8,65,128]{2,1,0:T(8,128)(2,1)} %broadcast_in_dim.75), calls=%async_computation | async-start | bytes 294912 | tf_op jit(solution)/shard_map/all_to_all | solution.py:15
  20.2 4.3 %collective-permute-start.3 = (bf16[256,128]{1,0:T(8,128)(2,1)S(1)}, bf16[256,128]{1,0:T(8,128)(2,1)S(1)}, u32[]{:S(2)}, u32[]{:S(2)}) collective-permute-start(bf16[256,128]{1,0:T(8,128)(2,1)S(1)} %bitcast.58), channel_id=1, source_target_pairs={{0,2},{1,3},{2,0},{3,1},{4,6},{5,7},{6,4},{7,5},{8,10},{9,11},{10,... | collective-permute-start | bytes 196616 | tf_op jit(solution)/shard_map/ppermute | solution.py:43
  24.5 1.4 %collective-permute-start.4 = (bf16[512,128]{1,0:T(8,128)(2,1)S(1)}, bf16[512,128]{1,0:T(8,128)(2,1)S(1)}, u32[]{:S(2)}, u32[]{:S(2)}) collective-permute-start(bf16[512,128]{1,0:T(8,128)(2,1)S(1)} %pad_maximum_fusion.3), channel_id=1, source_target_pairs={{0,1},{1,0},{2,3},{3,2},{4,5},{5,4},{6,7},{7,6},{8,9},{9,8},{10,11... | collective-permute-start | bytes 393224 | tf_op jit(solution)/shard_map/ppermute | solution.py:43
  26.1 0.7 %copy-start.2 = (f32[256]{0:T(256)S(1)}, f32[256]{0:T(256)}, u32[]{:S(2)}) copy-start(f32[256]{0:T(256)} %param.5) | copy-start | bytes 3076
  38.4 5.0 %collective-permute-start.5 = (bf16[512,128]{1,0:T(8,128)(2,1)S(1)}, bf16[512,128]{1,0:T(8,128)(2,1)S(1)}, u32[]{:S(2)}, u32[]{:S(2)}) collective-permute-start(bf16[512,128]{1,0:T(8,128)(2,1)S(1)} %pad_maximum_fusion.4), channel_id=1, source_target_pairs={{0,2},{1,3},{2,0},{3,1},{4,6},{5,7},{6,4},{7,5},{8,10},{9,11},{10,... | collective-permute-start | bytes 393224 | tf_op jit(solution)/shard_map/ppermute | solution.py:43
  43.5 1.6 %collective-permute-start.6 = (bf16[1024,128]{1,0:T(8,128)(2,1)S(1)}, bf16[1024,128]{1,0:T(8,128)(2,1)S(1)}, u32[]{:S(2)}, u32[]{:S(2)}) collective-permute-start(bf16[1024,128]{1,0:T(8,128)(2,1)S(1)} %pad_maximum_fusion.1), channel_id=1, source_target_pairs={{0,1},{1,0},{2,3},{3,2},{4,5},{5,4},{6,7},{7,6},{8,9},{9,8},{10,11... | collective-permute-start | bytes 786440 | tf_op jit(solution)/shard_map/ppermute | solution.py:43

commit v11 on v10

--- a/solution.py
+++ b/solution.py
@@ -58,10 +58,11 @@
     band = lax.axis_index("band")
     total_orbitals = block_width * nbands
     valid_mask = points >= 0
-    safe_idx = jnp.where(valid_mask, points, 0)
-    selected = jnp.where(valid_mask[:, None], orbitals[safe_idx], 0.0).astype(jnp.bfloat16)
+    picks = (points[:, None] == jnp.arange(rows, dtype=points.dtype)[None, :]).astype(jnp.bfloat16)
+    rows_b16 = orbitals.astype(jnp.bfloat16)
+    selected = jnp.dot(picks, rows_b16, preferred_element_type=jnp.float32).astype(jnp.bfloat16)
     filled = jnp.pad(valid_mask.astype(jnp.bfloat16), (0, block_width - nslots))
-    to_band = jnp.concatenate([orbitals.astype(jnp.bfloat16), fitted.reshape(-1, block_width)], 0)
+    to_band = jnp.concatenate([rows_b16, fitted.reshape(-1, block_width)], 0)
     sent, to_band = lax.optimization_barrier((grid_copies(jnp.concatenate([selected, filled[None]], 0)), to_band))
     got = grid_exchange(sent).reshape(ngroups, nslots + 1, block_width)
     swapped = band_swap(to_band)
@@ -78,7 +79,7 @@
     pot = potential[:, None]
     for step in range(ITERS):
         if step:
-            at_slots = jnp.where(valid_mask[:, None], psi[safe_idx], 0.0).astype(jnp.bfloat16)
+            at_slots = jnp.dot(picks, psi, preferred_element_type=jnp.float32).astype(jnp.bfloat16)
             high = lax.reduce_precision(sq, exponent_bits=8, mantissa_bits=7)
             rest = sq - high
             middle = lax.reduce_precision(rest, exponent_bits=8, mantissa_bits=7)

time: 56 us -> 54.8 us (0.979)
  other arithmetic: 2.96 us -> 2.1 us
  local copies, waits for them, and re-layouts: 3.72 us -> 2.97 us
    gather x2 -> x0, local copies, waits for them, and re-layouts: 1.21 us -> none  [the longest x1 0.61 us: body(): psi[safe_idx]]
    ge x1, other arithmetic: 0.73 us -> 0.01 us  [body(): valid_mask = points >= 0]
where the time goes in v11:
time: 54.8 us; the launch traced here: 54.5 us
  blocking collectives  19.4 us (35%)
  waiting for transfers between devices  14.8 us (27%)
  starting transfers between devices  12.4 us (23%)
  local copies, waits for them, and re-layouts  2.97 us (5%)
  matrix products  2.42 us (4%)
  other arithmetic  2.1 us (4%)
    all_to_all x2, blocking collectives, grid_exchange(): got = lax.all_to_all(sent, 'grid', 0, 0, tiled=True)  19.4 us
    ppermute x4, waiting for transfers between devices, band_hops(): lax.ppermute(jnp.concatenate([held[k] for k in keys], 0), 'band', [(i, i...  8.21 us
    all_to_all x1, waiting for transfers between devices, grid_exchange(): got = lax.all_to_all(sent, 'grid', 0, 0, tiled=True)  6.17 us
    all_to_all x1, starting transfers between devices, grid_exchange(): got = lax.all_to_all(sent, 'grid', 0, 0, tiled=True)  6.06 us
    ppermute x4, starting transfers between devices, band_hops(): lax.ppermute(jnp.concatenate([held[k] for k in keys], 0), 'band', [(i, i...  3.25 us
    ppermute x3, starting transfers between devices, band_swap(): got.append(lax.ppermute(x, 'band', [(i, i ^ k) for i in range(nbands)]))  3.09 us
    unnamed x10, local copies, waits for them, and re-layouts  1.3 us
    dot_general x6, matrix products, body(): lax.dot_general(coll[:, k * block_width:(k + 1) * block_width], rows_b[:,...  1.12 us
  transfers between devices with their start and end apart: 8, of which 6 were waited for; matrix products, arithmetic and copies ran while one was open for 3% of the time, Pallas kernels for 0%

profile of v11, /device:TPU:0, one launch (start us, length us, event | category | flops | bytes accessed | tf_op | source)
XLA Modules:
  0.0 54.5 jit_solution(15975107753947176133)
XLA Ops:
  0.0 0.0 copy-start.1
  0.0 0.9 %convert_element_type.86 = bf16[256,128]{1,0:T(8,128)(2,1)S(1)} convert(f32[256,128]{1,0:T(8,128)} %param.4) | non-fusion elementwise | flops 32768 | bytes 196608 | tf_op jit(solution)/shard_map/convert_element_type | solution.py:62
  0.9 0.0 copy-done.1
  1.0 0.0 copy-start.3
  1.0 0.6 %copy-done.3 = s32[64]{0:T(128)S(1)} copy-done((s32[64]{0:T(128)S(1)}, s32[64]{0:T(128)}, u32[]{:S(2)}) %copy-start.3) | copy-done | bytes 280
  1.6 0.2 convolution_convert_fusion.1
  1.9 0.7 %broadcast_in_dim.50 = bf16[8,65,128]{2,1,0:T(8,128)(2,1)} broadcast(bf16[65,128]{1,0:T(8,128)(2,1)S(1)} %pad_maximum_fusion.5), dimensions={1,2} | broadcast | bytes 149760 | tf_op jit(solution)/shard_map/broadcast_in_dim | solution.py:11
  2.5 0.5 collective-permute-start
  3.0 2.5 %collective-permute-start.1 = (bf16[512,128]{1,0:T(8,128)(2,1)S(1)}, bf16[512,128]{1,0:T(8,128)(2,1)S(1)}, u32[]{:S(2)}, u32[]{:S(2)}) collective-permute-start(bf16[512,128]{1,0:T(8,128)(2,1)S(1)} %pad_maximum_fusion.2), channel_id=1, source_target_pairs={{0,2},{1,3},{2,0},{3,1},{4,6},{5,7},{6,4},{7,5},{8,10},{9,11},{10,... | collective-permute-start | bytes 393224 | tf_op jit(solution)/shard_map/ppermute | solution.py:27
  5.5 0.1 collective-permute-start.2
  5.6 6.1 %all-to-all-start = ((bf16[8,65,128]{2,1,0:T(8,128)(2,1)}), bf16[8,65,128]{2,1,0:T(8,128)(2,1)S(1)}, u32[]{:S(2)}, u32[]{:S(2)}) async-start(bf16[8,65,128]{2,1,0:T(8,128)(2,1)} %broadcast_in_dim.50), calls=%async_computation | async-start | bytes 294912 | tf_op jit(solution)/shard_map/all_to_all | solution.py:15
  11.8 0.0 collective-permute-done
  11.8 0.0 collective-permute-done.1
  11.9 0.4 collective-permute-done.2
  12.3 0.6 %gather_fusion = bf16[4,128,256]{2,1,0:T(8,128)(2,1)S(1)} fusion(bf16[4,128,256]{2,1,0:T(8,128)(2,1)S(1)} %pad_maximum_fusion, s32[1024]{0:T(1024)S(1)} %pad_clamp_fusion), kind=kCustom, calls=%fused_computation | custom fusion | bytes 524304 | tf_op jit(solution)/shard_map/jit(_take)/gather | solution.py:71
  12.9 0.1 broadcast_select_fusion
  13.0 0.1 rev.11
  13.2 6.2 %all-to-all-done = bf16[8,65,128]{2,1,0:T(8,128)(2,1)S(1)} async-done(((bf16[8,65,128]{2,1,0:T(8,128)(2,1)}), bf16[8,65,128]{2,1,0:T(8,128)(2,1)S(1)}, u32[]{:S(2)}, u32[]{:S(2)}) %all-to-all-start) | async-done | bytes 133152 | tf_op jit(solution)/shard_map/all_to_all | solution.py:15
  19.5 1.6 %collective-permute-start.3 = (bf16[256,128]{1,0:T(8,128)(2,1)S(1)}, bf16[256,128]{1,0:T(8,128)(2,1)S(1)}, u32[]{:S(2)}, u32[]{:S(2)}) collective-permute-start(bf16[256,128]{1,0:T(8,128)(2,1)S(1)} %bitcast.60), channel_id=1, source_target_pairs={{0,2},{1,3},{2,0},{3,1},{4,6},{5,7},{6,4},{7,5},{8,10},{9,11},{10,... | collective-permute-start | bytes 196616 | tf_op jit(solution)/shard_map/ppermute | solution.py:43
  21.0 0.1 fusion.32
  21.1 0.2 fusion.1
  21.3 2.5 %collective-permute-done.3 = bf16[256,128]{1,0:T(8,128)(2,1)S(1)} collective-permute-done((bf16[256,128]{1,0:T(8,128)(2,1)S(1)}, bf16[256,128]{1,0:T(8,128)(2,1)S(1)}, u32[]{:S(2)}, u32[]{:S(2)}) %collective-permute-start.3) | collective-permute-done | bytes 65568 | tf_op jit(solution)/shard_map/ppermute | solution.py:43
  23.8 0.1 collective-permute-start.4
  23.9 0.2 fusion.9
  24.1 0.0 copy-start
  24.1 1.1 %collective-permute-done.4 = bf16[512,128]{1,0:T(8,128)(2,1)S(1)} collective-permute-done((bf16[512,128]{1,0:T(8,128)(2,1)S(1)}, bf16[512,128]{1,0:T(8,128)(2,1)S(1)}, u32[]{:S(2)}, u32[]{:S(2)}) %collective-permute-start.4) | collective-permute-done | bytes 131104 | tf_op jit(solution)/shard_map/ppermute | solution.py:43
  25.2 0.2 fusion.11
  25.4 0.0 copy-start.2
  25.4 0.0 copy-done
  25.4 0.7 %copy-done.2 = f32[256]{0:T(256)S(1)} copy-done((f32[256]{0:T(256)S(1)}, f32[256]{0:T(256)}, u32[]{:S(2)}) %copy-start.2) | copy-done | bytes 1048
  26.1 0.5 multiply_reduce_fusion.1
  26.6 0.2 convolution_convert_fusion
  26.8 10.2 %all_to_all.15 = bf16[8,67,128]{2,1,0:T(8,128)(2,1)S(1)} all-to-all(bf16[8,67,128]{2,1,0:T(8,128)(2,1)S(1)} %broadcast_in_dim.54), channel_id=1, replica_groups=mesh['grid'=8,'band'=4] {'grid'}, dimensions={0} | all-to-all | bytes 274432 | tf_op jit(solution)/shard_map/all_to_all | solution.py:15
  37.2 1.6 %collective-permute-start.5 = (bf16[512,128]{1,0:T(8,128)(2,1)S(1)}, bf16[512,128]{1,0:T(8,128)(2,1)S(1)}, u32[]{:S(2)}, u32[]{:S(2)}) collective-permute-start(bf16[512,128]{1,0:T(8,128)(2,1)S(1)} %pad_maximum_fusion.4), channel_id=1, source_target_pairs={{0,2},{1,3},{2,0},{3,1},{4,6},{5,7},{6,4},{7,5},{8,10},{9,11},{10,... | collective-permute-start | bytes 393224 | tf_op jit(solution)/shard_map/ppermute | solution.py:43
  38.8 3.5 %collective-permute-done.5 = bf16[512,128]{1,0:T(8,128)(2,1)S(1)} collective-permute-done((bf16[512,128]{1,0:T(8,128)(2,1)S(1)}, bf16[512,128]{1,0:T(8,128)(2,1)S(1)}, u32[]{:S(2)}, u32[]{:S(2)}) %collective-permute-start.5) | collective-permute-done | bytes 131104 | tf_op jit(solution)/shard_map/ppermute | solution.py:43
  42.3 0.1 collective-permute-start.6
  42.4 0.2 fusion.13
  42.6 0.2 fusion.21
  42.8 1.1 %collective-permute-done.6 = bf16[1024,128]{1,0:T(8,128)(2,1)S(1)} collective-permute-done((bf16[1024,128]{1,0:T(8,128)(2,1)S(1)}, bf16[1024,128]{1,0:T(8,128)(2,1)S(1)}, u32[]{:S(2)}, u32[]{:S(2)}) %collective-permute-start.6) | collective-permute-done | bytes 262176 | tf_op jit(solution)/shard_map/ppermute | solution.py:43
  43.9 0.2 fusion.23
  44.1 0.5 multiply_reduce_fusion
  44.5 9.2 %all_to_all.16 = f32[8,1,128]{2,1,0:T(1,128)S(1)} all-to-all(f32[8,1,128]{2,1,0:T(1,128)S(1)} %broadcast_in_dim.55), channel_id=1, replica_groups=mesh['grid'=8,'band'=4] {'grid'}, dimensions={0} | all-to-all | bytes 8192 | tf_op jit(solution)/shard_map/all_to_all | solution.py:15
  53.8 0.7 %broadcast_multiply_fusion = f32[256,128]{1,0:T(8,128)} fusion(f32[256,128]{1,0:T(8,128)S(1)} %get-tuple-element.15, f32[128]{0:T(128)S(1)} %add_rsqrt_fusion), kind=kLoop, calls=%fused_computation.77 | loop fusion | flops 32768 | bytes 262656 | tf_op jit(solution)/shard_map/mul | solution.py:115
  (43 shorter events, 0.6 us)
Async XLA Ops:
  0.0 0.9 %copy-start.1 = (bf16[128,256]{1,0:T(8,128)(2,1)S(1)}, bf16[128,256]{1,0:T(8,128)(2,1)}, u32[]{:S(2)}) copy-start(bf16[128,256]{1,0:T(8,128)(2,1)} %param.6) | copy-start | bytes 196612
  1.0 0.7 %copy-start.3 = (s32[64]{0:T(128)S(1)}, s32[64]{0:T(128)}, u32[]{:S(2)}) copy-start(s32[64]{0:T(128)} %param.7) | copy-start | bytes 772
  2.5 9.2 %collective-permute-start = (bf16[512,128]{1,0:T(8,128)(2,1)S(1)}, bf16[512,128]{1,0:T(8,128)(2,1)S(1)}, u32[]{:S(2)}, u32[]{:S(2)}) collective-permute-start(bf16[512,128]{1,0:T(8,128)(2,1)S(1)} %pad_maximum_fusion.2), channel_id=1, source_target_pairs={{0,1},{1,0},{2,3},{3,2},{4,5},{5,4},{6,7},{7,6},{8,9},{9,8},{10,11... | collective-permute-start | bytes 393224 | tf_op jit(solution)/shard_map/ppermute | solution.py:27
  3.0 8.8 %collective-permute-start.1 = (bf16[512,128]{1,0:T(8,128)(2,1)S(1)}, bf16[512,128]{1,0:T(8,128)(2,1)S(1)}, u32[]{:S(2)}, u32[]{:S(2)}) collective-permute-start(bf16[512,128]{1,0:T(8,128)(2,1)S(1)} %pad_maximum_fusion.2), channel_id=1, source_target_pairs={{0,2},{1,3},{2,0},{3,1},{4,6},{5,7},{6,4},{7,5},{8,10},{9,11},{10,... | collective-permute-start | bytes 393224 | tf_op jit(solution)/shard_map/ppermute | solution.py:27
  5.5 6.8 %collective-permute-start.2 = (bf16[512,128]{1,0:T(8,128)(2,1)S(1)}, bf16[512,128]{1,0:T(8,128)(2,1)S(1)}, u32[]{:S(2)}, u32[]{:S(2)}) collective-permute-start(bf16[512,128]{1,0:T(8,128)(2,1)S(1)} %pad_maximum_fusion.2), channel_id=1, source_target_pairs={{0,3},{1,2},{2,1},{3,0},{4,7},{5,6},{6,5},{7,4},{8,11},{9,10},{10,... | collective-permute-start | bytes 393224 | tf_op jit(solution)/shard_map/ppermute | solution.py:27
  5.6 13.7 %all-to-all-start = ((bf16[8,65,128]{2,1,0:T(8,128)(2,1)}), bf16[8,65,128]{2,1,0:T(8,128)(2,1)S(1)}, u32[]{:S(2)}, u32[]{:S(2)}) async-start(bf16[8,65,128]{2,1,0:T(8,128)(2,1)} %broadcast_in_dim.50), calls=%async_computation | async-start | bytes 294912 | tf_op jit(solution)/shard_map/all_to_all | solution.py:15
  19.5 4.3 %collective-permute-start.3 = (bf16[256,128]{1,0:T(8,128)(2,1)S(1)}, bf16[256,128]{1,0:T(8,128)(2,1)S(1)}, u32[]{:S(2)}, u32[]{:S(2)}) collective-permute-start(bf16[256,128]{1,0:T(8,128)(2,1)S(1)} %bitcast.60), channel_id=1, source_target_pairs={{0,2},{1,3},{2,0},{3,1},{4,6},{5,7},{6,4},{7,5},{8,10},{9,11},{10,... | collective-permute-start | bytes 196616 | tf_op jit(solution)/shard_map/ppermute | solution.py:43
  23.8 1.4 %collective-permute-start.4 = (bf16[512,128]{1,0:T(8,128)(2,1)S(1)}, bf16[512,128]{1,0:T(8,128)(2,1)S(1)}, u32[]{:S(2)}, u32[]{:S(2)}) collective-permute-start(bf16[512,128]{1,0:T(8,128)(2,1)S(1)} %pad_maximum_fusion.3), channel_id=1, source_target_pairs={{0,1},{1,0},{2,3},{3,2},{4,5},{5,4},{6,7},{7,6},{8,9},{9,8},{10,11... | collective-permute-start | bytes 393224 | tf_op jit(solution)/shard_map/ppermute | solution.py:43
  24.1 1.3 %copy-start = (f32[256,128]{1,0:T(8,128)S(1)}, f32[256,128]{1,0:T(8,128)}, u32[]{:S(2)}) copy-start(f32[256,128]{1,0:T(8,128)} %param.4) | copy-start | bytes 393220
  25.4 0.7 %copy-start.2 = (f32[256]{0:T(256)S(1)}, f32[256]{0:T(256)}, u32[]{:S(2)}) copy-start(f32[256]{0:T(256)} %param.5) | copy-start | bytes 3076
  37.2 5.0 %collective-permute-start.5 = (bf16[512,128]{1,0:T(8,128)(2,1)S(1)}, bf16[512,128]{1,0:T(8,128)(2,1)S(1)}, u32[]{:S(2)}, u32[]{:S(2)}) collective-permute-start(bf16[512,128]{1,0:T(8,128)(2,1)S(1)} %pad_maximum_fusion.4), channel_id=1, source_target_pairs={{0,2},{1,3},{2,0},{3,1},{4,6},{5,7},{6,4},{7,5},{8,10},{9,11},{10,... | collective-permute-start | bytes 393224 | tf_op jit(solution)/shard_map/ppermute | solution.py:43
  42.3 1.6 %collective-permute-start.6 = (bf16[1024,128]{1,0:T(8,128)(2,1)S(1)}, bf16[1024,128]{1,0:T(8,128)(2,1)S(1)}, u32[]{:S(2)}, u32[]{:S(2)}) collective-permute-start(bf16[1024,128]{1,0:T(8,128)(2,1)S(1)} %pad_maximum_fusion.1), channel_id=1, source_target_pairs={{0,1},{1,0},{2,3},{3,2},{4,5},{5,4},{6,7},{7,6},{8,9},{9,8},{10,11... | collective-permute-start | bytes 786440 | tf_op jit(solution)/shard_map/ppermute | solution.py:43

commit v12 on v11

--- a/solution.py
+++ b/solution.py
@@ -59,25 +59,23 @@
     total_orbitals = block_width * nbands
     valid_mask = points >= 0
     picks = (points[:, None] == jnp.arange(rows, dtype=points.dtype)[None, :]).astype(jnp.bfloat16)
-    rows_b16 = orbitals.astype(jnp.bfloat16)
-    selected = jnp.dot(picks, rows_b16, preferred_element_type=jnp.float32).astype(jnp.bfloat16)
+    selected = jnp.dot(picks, orbitals.astype(jnp.bfloat16), preferred_element_type=jnp.float32).astype(jnp.bfloat16)
     filled = jnp.pad(valid_mask.astype(jnp.bfloat16), (0, block_width - nslots))
-    to_band = jnp.concatenate([rows_b16, fitted.reshape(-1, block_width)], 0)
+    to_band = jnp.concatenate([orbitals, fitted.reshape(-1, block_width).astype(jnp.float32)], 0)
     sent, to_band = lax.optimization_barrier((grid_copies(jnp.concatenate([selected, filled[None]], 0)), to_band))
     got = grid_exchange(sent).reshape(ngroups, nslots + 1, block_width)
     swapped = band_swap(to_band)
-    rows_b = jnp.concatenate([part[:rows] for part in swapped], 1)
+    psi = jnp.concatenate([part[:rows] for part in swapped], 1)
     fitted_got = jnp.stack([part[rows:].reshape(fitted.shape) for part in swapped], 0)
     fitted_all = jnp.take(fitted_got, jnp.arange(nbands, dtype=jnp.int32) ^ band, axis=0)
     fitted_all = fitted_all.reshape(ngroups // 2, 2, nslots, fitted.shape[1])
     coll = jnp.concatenate(band_hops(pair_up(got[:, :nslots])), 1)
     first_filled = got[:, nslots, :nslots].reshape(ngroups // 2, 2, nslots)[:, 0] > 0
-    fitted_all = jnp.where(
-        first_filled[:, :, None], fitted_all[:, 0], jnp.flip(fitted_all[:, 1], axis=1)
-    ).reshape(-1, fitted.shape[1]).astype(jnp.float32)
-    psi = orbitals
+    fitted_all = jnp.where(first_filled[:, :, None], fitted_all[:, 0], jnp.flip(fitted_all[:, 1], axis=1))
+    fitted_all = fitted_all.reshape(-1, fitted.shape[1])
     pot = potential[:, None]
     for step in range(ITERS):
+        last = step == ITERS - 1
         if step:
             at_slots = jnp.dot(picks, psi, preferred_element_type=jnp.float32).astype(jnp.bfloat16)
             high = lax.reduce_precision(sq, exponent_bits=8, mantissa_bits=7)
@@ -85,16 +83,13 @@
             middle = lax.reduce_precision(rest, exponent_bits=8, mantissa_bits=7)
             low = lax.reduce_precision(rest - middle, exponent_bits=8, mantissa_bits=7)
             parts = jnp.stack([high, middle, low], 0).astype(jnp.bfloat16)
-            got = grid_gather(jnp.concatenate([at_slots, parts], 0)).reshape(ngroups, nslots + 3, block_width)
+            got = grid_gather(jnp.concatenate([at_slots, parts], 0)).reshape(ngroups, nslots + 3, total_orbitals)
             sums = got[:, nslots:].astype(jnp.float32)
             total = jnp.sum((sums[:, 0] + sums[:, 1]) + sums[:, 2], axis=0)
             scale = lax.rsqrt(total / (rows * ngroups) + 1e-06)
-            coll_own = pair_up((got[:, :nslots].astype(jnp.float32) * scale).astype(jnp.bfloat16))
+            coll = pair_up((got[:, :nslots].astype(jnp.float32) * scale).astype(jnp.bfloat16))
             psi = psi * scale
-            ncoll = coll_own.shape[0]
-            swapped = band_hops(jnp.concatenate([coll_own, psi.astype(jnp.bfloat16)], 0))
-            coll = jnp.concatenate([part[:ncoll] for part in swapped], 1)
-            rows_b = jnp.concatenate([part[ncoll:] for part in swapped], 1)
+        rows_b = psi.astype(jnp.bfloat16)
         proj = None
         for k in range(nbands):
             part = lax.dot_general(
@@ -106,8 +101,11 @@
             part = (part / total_orbitals).astype(jnp.bfloat16).astype(jnp.float32)
             proj = part if proj is None else proj + part
         tile_blocks = (fitted_all * proj).astype(jnp.bfloat16)
+        if last:
+            coll = coll[:, :block_width]
+            psi = psi[:, :block_width]
         applied = lax.dot_general(
-            tile_blocks, coll[:, :block_width], (((0,), (0,)), ((), ())), preferred_element_type=jnp.float32
+            tile_blocks, coll, (((0,), (0,)), ((), ())), preferred_element_type=jnp.float32
         )
         psi = psi - 0.25 * (pot * psi - applied)
         sq = jnp.sum(psi * psi, axis=0)

time: 54.8 us -> 57.6 us (1.051)
  blocking collectives: 19.4 us -> 28.8 us
  waiting for transfers between devices: 14.8 us -> 10 us
  starting transfers between devices: 12.4 us -> 10.8 us
  other arithmetic: 2.1 us -> 1.37 us
  local copies, waits for them, and re-layouts: 2.97 us -> 3.58 us
    all_to_all x2, blocking collectives: 19.4 us -> 28.8 us  [grid_exchange(): got = lax.all_to_all(sent, 'grid', 0, 0, tiled=True)]
    ppermute x4 -> x2, waiting for transfers between devices: 8.21 us -> 2.45 us  [band_hops(): lax.ppermute(jnp.concatenate([held[k] for k in keys], 0), 'band', [(i, i...]
    ppermute x4 -> x2, starting transfers between devices: 3.25 us -> 1.63 us  [band_hops(): lax.ppermute(jnp.concatenate([held[k] for k in keys], 0), 'band', [(i, i...]
    all_to_all x1, waiting for transfers between devices: 6.17 us -> 7.56 us  [grid_exchange(): got = lax.all_to_all(sent, 'grid', 0, 0, tiled=True)]
    convert_element_type x0 -> x1, local copies, waits for them, and re-layouts: none -> 0.9 us  [body(): fitted.reshape(-1, block_width).astype(jnp.float32)]
    convert_element_type x2, other arithmetic: 0.96 us -> 0.11 us  [body(): rows_b = psi.astype(jnp.bfloat16)]
    unnamed x10 -> x8, local copies, waits for them, and re-layouts: 1.3 us -> 0.71 us
  transfers between devices with their start and end apart: 8 -> 6, of which waited for: 6 -> 3; matrix products, arithmetic and copies ran while one was open for 3% -> 3% of each run, Pallas kernels for 0% -> 0%
where the time goes in v12:
time: 57.6 us; the launch traced here: 57.3 us
  blocking collectives  28.8 us (50%)
  starting transfers between devices  10.8 us (19%)
  waiting for transfers between devices  10 us (17%)
  local copies, waits for them, and re-layouts  3.58 us (6%)
  matrix products  2.45 us (4%)
  other arithmetic  1.37 us (2%)
    all_to_all x2, blocking collectives, grid_exchange(): got = lax.all_to_all(sent, 'grid', 0, 0, tiled=True)  28.8 us
    all_to_all x1, waiting for transfers between devices, grid_exchange(): got = lax.all_to_all(sent, 'grid', 0, 0, tiled=True)  7.56 us
    all_to_all x1, starting transfers between devices, grid_exchange(): got = lax.all_to_all(sent, 'grid', 0, 0, tiled=True)  6.06 us
    ppermute x3, starting transfers between devices, band_swap(): got.append(lax.ppermute(x, 'band', [(i, i ^ k) for i in range(nbands)]))  3.09 us
    ppermute x2, waiting for transfers between devices, band_hops(): lax.ppermute(jnp.concatenate([held[k] for k in keys], 0), 'band', [(i, i...  2.45 us
    ppermute x2, starting transfers between devices, band_hops(): lax.ppermute(jnp.concatenate([held[k] for k in keys], 0), 'band', [(i, i...  1.63 us
  transfers between devices with their start and end apart: 6, of which 3 were waited for; matrix products, arithmetic and copies ran while one was open for 3% of the time, Pallas kernels for 0%

profile of v12, /device:TPU:0, one launch (start us, length us, event | category | flops | bytes accessed | tf_op | source)
XLA Modules:
  0.0 57.3 jit_solution(7517178837185336686)
XLA Ops:
  0.0 0.0 copy-start.1
  0.0 0.0 copy-start
  0.0 0.9 %reshape.106 = f32[256,128]{1,0:T(8,128)S(1)} reshape(bf16[128,256]{1,0:T(8,128)(2,1)} %param.6) | data formatting | bytes 196608 | tf_op jit(solution)/shard_map/convert_element_type | solution.py:64
  0.9 0.0 copy-done.1
  0.9 0.0 copy-done
  1.0 0.2 convolution_convert_fusion.1
  1.2 0.7 %broadcast_in_dim.50 = bf16[8,65,128]{2,1,0:T(8,128)(2,1)} broadcast(bf16[65,128]{1,0:T(8,128)(2,1)S(1)} %pad_maximum_fusion.5), dimensions={1,2} | broadcast | bytes 149760 | tf_op jit(solution)/shard_map/broadcast_in_dim | solution.py:11
  1.9 0.5 collective-permute-start
  2.3 2.5 %collective-permute-start.1 = (f32[512,128]{1,0:T(8,128)S(1)}, f32[512,128]{1,0:T(8,128)S(1)}, u32[]{:S(2)}, u32[]{:S(2)}) collective-permute-start(f32[512,128]{1,0:T(8,128)S(1)} %pad_maximum_fusion.2), channel_id=1, source_target_pairs={{0,2},{1,3},{2,0},{3,1},{4,6},{5,7},{6,4},{7,5},{8,10},{9,11},{10,... | collective-permute-start | bytes 786440 | tf_op jit(solution)/shard_map/ppermute | solution.py:27
  4.8 0.1 collective-permute-start.2
  5.0 6.1 %all-to-all-start = ((bf16[8,65,128]{2,1,0:T(8,128)(2,1)}), bf16[8,65,128]{2,1,0:T(8,128)(2,1)S(1)}, u32[]{:S(2)}, u32[]{:S(2)}) async-start(bf16[8,65,128]{2,1,0:T(8,128)(2,1)} %broadcast_in_dim.50), calls=%async_computation | async-start | bytes 294912 | tf_op jit(solution)/shard_map/all_to_all | solution.py:15
  11.1 7.6 %all-to-all-done = bf16[8,65,128]{2,1,0:T(8,128)(2,1)S(1)} async-done(((bf16[8,65,128]{2,1,0:T(8,128)(2,1)}), bf16[8,65,128]{2,1,0:T(8,128)(2,1)S(1)}, u32[]{:S(2)}, u32[]{:S(2)}) %all-to-all-start) | async-done | bytes 133152 | tf_op jit(solution)/shard_map/all_to_all | solution.py:15
  18.8 1.6 %collective-permute-start.3 = (bf16[256,128]{1,0:T(8,128)(2,1)S(1)}, bf16[256,128]{1,0:T(8,128)(2,1)S(1)}, u32[]{:S(2)}, u32[]{:S(2)}) collective-permute-start(bf16[256,128]{1,0:T(8,128)(2,1)S(1)} %bitcast.49), channel_id=1, source_target_pairs={{0,2},{1,3},{2,0},{3,1},{4,6},{5,7},{6,4},{7,5},{8,10},{9,11},{10,... | collective-permute-start | bytes 196616 | tf_op jit(solution)/shard_map/ppermute | solution.py:43
  20.4 0.0 collective-permute-done
  20.5 0.0 collective-permute-done.1
  20.5 0.0 collective-permute-done.2
  20.7 0.6 %gather_fusion = f32[4,128,256]{2,1,0:T(8,128)S(1)} fusion(f32[4,128,256]{2,1,0:T(8,128)S(1)} %pad_maximum_fusion.1, s32[1024]{0:T(1024)S(1)} %pad_clamp_fusion), kind=kCustom, calls=%fused_computation | custom fusion | bytes 1048592 | tf_op jit(solution)/shard_map/jit(_take)/gather | solution.py:70
  21.3 0.1 broadcast_select_fusion
  21.4 0.1 rev.12
  21.5 0.1 fusion.31
  21.7 0.2 fusion.1
  21.8 1.3 %collective-permute-done.3 = bf16[256,128]{1,0:T(8,128)(2,1)S(1)} collective-permute-done((bf16[256,128]{1,0:T(8,128)(2,1)S(1)}, bf16[256,128]{1,0:T(8,128)(2,1)S(1)}, u32[]{:S(2)}, u32[]{:S(2)}) %collective-permute-start.3) | collective-permute-done | bytes 65568 | tf_op jit(solution)/shard_map/ppermute | solution.py:43
  23.2 0.1 collective-permute-start.4
  23.3 0.2 fusion.9
  23.4 1.1 %collective-permute-done.4 = bf16[512,128]{1,0:T(8,128)(2,1)S(1)} collective-permute-done((bf16[512,128]{1,0:T(8,128)(2,1)S(1)}, bf16[512,128]{1,0:T(8,128)(2,1)S(1)}, u32[]{:S(2)}, u32[]{:S(2)}) %collective-permute-start.4) | collective-permute-done | bytes 131104 | tf_op jit(solution)/shard_map/ppermute | solution.py:43
  24.6 0.2 fusion.11
  24.8 0.0 copy-start.2
  24.8 0.7 %copy-done.2 = f32[256]{0:T(256)S(1)} copy-done((f32[256]{0:T(256)S(1)}, f32[256]{0:T(256)}, u32[]{:S(2)}) %copy-start.2) | copy-done | bytes 1048
  25.5 0.5 multiply_reduce_fusion
  26.0 0.2 convolution_convert_fusion
  26.3 19.5 %all_to_all.15 = bf16[8,67,512]{2,1,0:T(8,128)(2,1)S(1)} all-to-all(bf16[8,67,512]{2,1,0:T(8,128)(2,1)S(1)} %broadcast_in_dim.54), channel_id=1, replica_groups=mesh['grid'=8,'band'=4] {'grid'}, dimensions={0} | all-to-all | bytes 1097728 | tf_op jit(solution)/shard_map/all_to_all | solution.py:15
  45.8 0.1 fusion.62
  45.8 0.1 fusion.71
  45.9 0.1 multiply_convert_fusion
  46.1 0.2 rev.14
  46.3 0.2 fusion.19
  46.5 0.2 fusion.21
  46.7 0.2 fusion.23
  46.9 0.5 multiply_reduce_fusion.1
  47.4 9.3 %all_to_all.16 = f32[8,1,128]{2,1,0:T(1,128)S(1)} all-to-all(f32[8,1,128]{2,1,0:T(1,128)S(1)} %broadcast_in_dim.55), channel_id=1, replica_groups=mesh['grid'=8,'band'=4] {'grid'}, dimensions={0} | all-to-all | bytes 8192 | tf_op jit(solution)/shard_map/all_to_all | solution.py:15
  56.7 0.7 %broadcast_multiply_fusion.1 = f32[256,128]{1,0:T(8,128)} fusion(f32[256,128]{1,0:T(8,128)S(1)} %get-tuple-element.27, f32[128]{0:T(128)S(1)} %add_rsqrt_fusion.1), kind=kLoop, calls=%fused_computation.83 | loop fusion | flops 32768 | bytes 262656 | tf_op jit(solution)/shard_map/mul | solution.py:113
  (38 shorter events, 0.6 us)
Async XLA Ops:
  0.0 0.9 %copy-start.1 = (s32[64]{0:T(128)S(1)}, s32[64]{0:T(128)}, u32[]{:S(2)}) copy-start(s32[64]{0:T(128)} %param.7) | copy-start | bytes 772
  0.0 0.9 %copy-start = (f32[256,128]{1,0:T(8,128)S(1)}, f32[256,128]{1,0:T(8,128)}, u32[]{:S(2)}) copy-start(f32[256,128]{1,0:T(8,128)} %param.4) | copy-start | bytes 393220
  1.9 18.5 %collective-permute-start = (f32[512,128]{1,0:T(8,128)S(1)}, f32[512,128]{1,0:T(8,128)S(1)}, u32[]{:S(2)}, u32[]{:S(2)}) collective-permute-start(f32[512,128]{1,0:T(8,128)S(1)} %pad_maximum_fusion.2), channel_id=1, source_target_pairs={{0,1},{1,0},{2,3},{3,2},{4,5},{5,4},{6,7},{7,6},{8,9},{9,8},{10,11... | collective-permute-start | bytes 786440 | tf_op jit(solution)/shard_map/ppermute | solution.py:27
  2.3 18.1 %collective-permute-start.1 = (f32[512,128]{1,0:T(8,128)S(1)}, f32[512,128]{1,0:T(8,128)S(1)}, u32[]{:S(2)}, u32[]{:S(2)}) collective-permute-start(f32[512,128]{1,0:T(8,128)S(1)} %pad_maximum_fusion.2), channel_id=1, source_target_pairs={{0,2},{1,3},{2,0},{3,1},{4,6},{5,7},{6,4},{7,5},{8,10},{9,11},{10,... | collective-permute-start | bytes 786440 | tf_op jit(solution)/shard_map/ppermute | solution.py:27
  4.8 15.7 %collective-permute-start.2 = (f32[512,128]{1,0:T(8,128)S(1)}, f32[512,128]{1,0:T(8,128)S(1)}, u32[]{:S(2)}, u32[]{:S(2)}) collective-permute-start(f32[512,128]{1,0:T(8,128)S(1)} %pad_maximum_fusion.2), channel_id=1, source_target_pairs={{0,3},{1,2},{2,1},{3,0},{4,7},{5,6},{6,5},{7,4},{8,11},{9,10},{10,... | collective-permute-start | bytes 786440 | tf_op jit(solution)/shard_map/ppermute | solution.py:27
  5.0 13.7 %all-to-all-start = ((bf16[8,65,128]{2,1,0:T(8,128)(2,1)}), bf16[8,65,128]{2,1,0:T(8,128)(2,1)S(1)}, u32[]{:S(2)}, u32[]{:S(2)}) async-start(bf16[8,65,128]{2,1,0:T(8,128)(2,1)} %broadcast_in_dim.50), calls=%async_computation | async-start | bytes 294912 | tf_op jit(solution)/shard_map/all_to_all | solution.py:15
  18.8 4.3 %collective-permute-start.3 = (bf16[256,128]{1,0:T(8,128)(2,1)S(1)}, bf16[256,128]{1,0:T(8,128)(2,1)S(1)}, u32[]{:S(2)}, u32[]{:S(2)}) collective-permute-start(bf16[256,128]{1,0:T(8,128)(2,1)S(1)} %bitcast.49), channel_id=1, source_target_pairs={{0,2},{1,3},{2,0},{3,1},{4,6},{5,7},{6,4},{7,5},{8,10},{9,11},{10,... | collective-permute-start | bytes 196616 | tf_op jit(solution)/shard_map/ppermute | solution.py:43
  23.2 1.4 %collective-permute-start.4 = (bf16[512,128]{1,0:T(8,128)(2,1)S(1)}, bf16[512,128]{1,0:T(8,128)(2,1)S(1)}, u32[]{:S(2)}, u32[]{:S(2)}) collective-permute-start(bf16[512,128]{1,0:T(8,128)(2,1)S(1)} %pad_maximum_fusion.3), channel_id=1, source_target_pairs={{0,1},{1,0},{2,3},{3,2},{4,5},{5,4},{6,7},{7,6},{8,9},{9,8},{10,11... | collective-permute-start | bytes 393224 | tf_op jit(solution)/shard_map/ppermute | solution.py:43
  24.8 0.7 %copy-start.2 = (f32[256]{0:T(256)S(1)}, f32[256]{0:T(256)}, u32[]{:S(2)}) copy-start(f32[256]{0:T(256)} %param.5) | copy-start | bytes 3076

commit v13 on v11

--- a/solution.py
+++ b/solution.py
@@ -65,7 +65,7 @@
     to_band = jnp.concatenate([rows_b16, fitted.reshape(-1, block_width)], 0)
     sent, to_band = lax.optimization_barrier((grid_copies(jnp.concatenate([selected, filled[None]], 0)), to_band))
     got = grid_exchange(sent).reshape(ngroups, nslots + 1, block_width)
-    swapped = band_swap(to_band)
+    swapped = band_hops(to_band)
     rows_b = jnp.concatenate([part[:rows] for part in swapped], 1)
     fitted_got = jnp.stack([part[rows:].reshape(fitted.shape) for part in swapped], 0)
     fitted_all = jnp.take(fitted_got, jnp.arange(nbands, dtype=jnp.int32) ^ band, axis=0)

time: 54.8 us -> 54.8 us (level)
  starting transfers between devices: 12.4 us -> 10.2 us
  waiting for transfers between devices: 14.8 us -> 16.3 us
  blocking collectives: 19.4 us -> 20 us
    ppermute x3 -> x0, starting transfers between devices: 3.09 us -> none  [band_swap(): got.append(lax.ppermute(x, 'band', [(i, i ^ k) for i in range(nbands)]))]
    ppermute x4 -> x6, starting transfers between devices: 3.25 us -> 4.35 us  [band_hops(): lax.ppermute(jnp.concatenate([held[k] for k in keys], 0), 'band', [(i, i...]
    all_to_all x1, waiting for transfers between devices: 6.17 us -> 7.2 us  [grid_exchange(): got = lax.all_to_all(sent, 'grid', 0, 0, tiled=True)]
    ppermute x4 -> x6, waiting for transfers between devices: 8.21 us -> 9.11 us  [band_hops(): lax.ppermute(jnp.concatenate([held[k] for k in keys], 0), 'band', [(i, i...]
    all_to_all x2, blocking collectives: 19.4 us -> 20 us  [grid_exchange(): got = lax.all_to_all(sent, 'grid', 0, 0, tiled=True)]
  transfers between devices with their start and end apart: 8 -> 7, of which waited for: 6 -> 4; matrix products, arithmetic and copies ran while one was open for 3% -> 4% of each run, Pallas kernels for 0% -> 0%
where the time goes in v13:
time: 54.8 us; the launch traced here: 54.4 us
  blocking collectives  20 us (36%)
  waiting for transfers between devices  16.3 us (30%)
  starting transfers between devices  10.2 us (19%)
  local copies, waits for them, and re-layouts  2.99 us (5%)
  matrix products  2.41 us (4%)
  other arithmetic  2.12 us (4%)
    all_to_all x2, blocking collectives, grid_exchange(): got = lax.all_to_all(sent, 'grid', 0, 0, tiled=True)  20 us
    ppermute x6, waiting for transfers between devices, band_hops(): lax.ppermute(jnp.concatenate([held[k] for k in keys], 0), 'band', [(i, i...  9.11 us
    all_to_all x1, waiting for transfers between devices, grid_exchange(): got = lax.all_to_all(sent, 'grid', 0, 0, tiled=True)  7.2 us
    all_to_all x1, starting transfers between devices, grid_exchange(): got = lax.all_to_all(sent, 'grid', 0, 0, tiled=True)  5.83 us
    ppermute x6, starting transfers between devices, band_hops(): lax.ppermute(jnp.concatenate([held[k] for k in keys], 0), 'band', [(i, i...  4.35 us
    unnamed x10, local copies, waits for them, and re-layouts  1.32 us
    dot_general x6, matrix products, body(): lax.dot_general(coll[:, k * block_width:(k + 1) * block_width], rows_b[:,...  1.11 us
  transfers between devices with their start and end apart: 7, of which 4 were waited for; matrix products, arithmetic and copies ran while one was open for 4% of the time, Pallas kernels for 0%

profile of v13, /device:TPU:0, one launch (start us, length us, event | category | flops | bytes accessed | tf_op | source)
XLA Modules:
  0.0 54.4 jit_solution(13812632545481627770)
XLA Ops:
  0.0 0.0 copy-start.1
  0.0 0.9 %convert_element_type.86 = bf16[256,128]{1,0:T(8,128)(2,1)S(1)} convert(f32[256,128]{1,0:T(8,128)} %param.4) | non-fusion elementwise | flops 32768 | bytes 196608 | tf_op jit(solution)/shard_map/convert_element_type | solution.py:62
  0.9 0.0 copy-done.1
  1.0 0.0 copy-start.3
  1.0 0.6 %copy-done.3 = s32[64]{0:T(128)S(1)} copy-done((s32[64]{0:T(128)S(1)}, s32[64]{0:T(128)}, u32[]{:S(2)}) %copy-start.3) | copy-done | bytes 280
  1.6 0.2 convolution_convert_fusion.1
  1.9 0.7 %broadcast_in_dim.50 = bf16[8,65,128]{2,1,0:T(8,128)(2,1)} broadcast(bf16[65,128]{1,0:T(8,128)(2,1)S(1)} %pad_maximum_fusion.6), dimensions={1,2} | broadcast | bytes 149760 | tf_op jit(solution)/shard_map/broadcast_in_dim | solution.py:11
  2.5 2.9 %collective-permute-start = (bf16[512,128]{1,0:T(8,128)(2,1)S(1)}, bf16[512,128]{1,0:T(8,128)(2,1)S(1)}, u32[]{:S(2)}, u32[]{:S(2)}) collective-permute-start(bf16[512,128]{1,0:T(8,128)(2,1)S(1)} %pad_maximum_fusion.3), channel_id=1, source_target_pairs={{0,2},{1,3},{2,0},{3,1},{4,6},{5,7},{6,4},{7,5},{8,10},{9,11},{10,... | collective-permute-start | bytes 393224 | tf_op jit(solution)/shard_map/ppermute | solution.py:43
  5.5 5.8 %all-to-all-start = ((bf16[8,65,128]{2,1,0:T(8,128)(2,1)}), bf16[8,65,128]{2,1,0:T(8,128)(2,1)S(1)}, u32[]{:S(2)}, u32[]{:S(2)}) async-start(bf16[8,65,128]{2,1,0:T(8,128)(2,1)} %broadcast_in_dim.50), calls=%async_computation | async-start | bytes 294912 | tf_op jit(solution)/shard_map/all_to_all | solution.py:15
  11.4 0.0 collective-permute-done
  11.4 0.1 collective-permute-start.1
  11.6 7.2 %all-to-all-done = bf16[8,65,128]{2,1,0:T(8,128)(2,1)S(1)} async-done(((bf16[8,65,128]{2,1,0:T(8,128)(2,1)}), bf16[8,65,128]{2,1,0:T(8,128)(2,1)S(1)}, u32[]{:S(2)}, u32[]{:S(2)}) %all-to-all-start) | async-done | bytes 133152 | tf_op jit(solution)/shard_map/all_to_all | solution.py:15
  18.8 0.6 %collective-permute-start.2 = (bf16[256,128]{1,0:T(8,128)(2,1)S(1)}, bf16[256,128]{1,0:T(8,128)(2,1)S(1)}, u32[]{:S(2)}, u32[]{:S(2)}) collective-permute-start(bf16[256,128]{1,0:T(8,128)(2,1)S(1)} %bitcast.60), channel_id=1, source_target_pairs={{0,2},{1,3},{2,0},{3,1},{4,6},{5,7},{6,4},{7,5},{8,10},{9,11},{10,... | collective-permute-start | bytes 196616 | tf_op jit(solution)/shard_map/ppermute | solution.py:43
  19.4 0.2 fusion.1
  19.7 3.5 %collective-permute-done.2 = bf16[256,128]{1,0:T(8,128)(2,1)S(1)} collective-permute-done((bf16[256,128]{1,0:T(8,128)(2,1)S(1)}, bf16[256,128]{1,0:T(8,128)(2,1)S(1)}, u32[]{:S(2)}, u32[]{:S(2)}) %collective-permute-start.2) | collective-permute-done | bytes 65568 | tf_op jit(solution)/shard_map/ppermute | solution.py:43
  23.2 0.1 collective-permute-start.3
  23.3 0.2 fusion.9
  23.5 0.0 collective-permute-done.1
  23.6 0.6 %gather_fusion = bf16[4,128,256]{2,1,0:T(8,128)(2,1)S(1)} fusion(bf16[4,128,256]{2,1,0:T(8,128)(2,1)S(1)} %pad_maximum_fusion.1, s32[1024]{0:T(1024)S(1)} %pad_clamp_fusion), kind=kCustom, calls=%fused_computation | custom fusion | bytes 524304 | tf_op jit(solution)/shard_map/jit(_take)/gather | solution.py:71
  24.2 0.1 broadcast_select_fusion
  24.3 0.1 rev.11
  24.4 0.1 fusion.32
  24.5 0.0 copy-start
  24.6 0.0 collective-permute-done.3
  24.6 0.2 fusion.11
  24.8 0.0 copy-start.2
  24.8 0.6 %copy-done = f32[256,128]{1,0:T(8,128)S(1)} copy-done((f32[256,128]{1,0:T(8,128)S(1)}, f32[256,128]{1,0:T(8,128)}, u32[]{:S(2)}) %copy-start) | copy-done | bytes 131096
  25.4 0.0 copy-done.2
  25.5 0.5 multiply_reduce_fusion.1
  25.9 0.2 convolution_convert_fusion
  26.2 10.5 %all_to_all.15 = bf16[8,67,128]{2,1,0:T(8,128)(2,1)S(1)} all-to-all(bf16[8,67,128]{2,1,0:T(8,128)(2,1)S(1)} %broadcast_in_dim.54), channel_id=1, replica_groups=mesh['grid'=8,'band'=4] {'grid'}, dimensions={0} | all-to-all | bytes 274432 | tf_op jit(solution)/shard_map/all_to_all | solution.py:15
  36.9 0.6 %collective-permute-start.4 = (bf16[512,128]{1,0:T(8,128)(2,1)S(1)}, bf16[512,128]{1,0:T(8,128)(2,1)S(1)}, u32[]{:S(2)}, u32[]{:S(2)}) collective-permute-start(bf16[512,128]{1,0:T(8,128)(2,1)S(1)} %pad_maximum_fusion.5), channel_id=1, source_target_pairs={{0,2},{1,3},{2,0},{3,1},{4,6},{5,7},{6,4},{7,5},{8,10},{9,11},{10,... | collective-permute-start | bytes 393224 | tf_op jit(solution)/shard_map/ppermute | solution.py:43
  37.5 4.4 %collective-permute-done.4 = bf16[512,128]{1,0:T(8,128)(2,1)S(1)} collective-permute-done((bf16[512,128]{1,0:T(8,128)(2,1)S(1)}, bf16[512,128]{1,0:T(8,128)(2,1)S(1)}, u32[]{:S(2)}, u32[]{:S(2)}) %collective-permute-start.4) | collective-permute-done | bytes 131104 | tf_op jit(solution)/shard_map/ppermute | solution.py:43
  42.0 0.1 collective-permute-start.5
  42.1 0.2 fusion.13
  42.2 0.2 fusion.21
  42.4 1.1 %collective-permute-done.5 = bf16[1024,128]{1,0:T(8,128)(2,1)S(1)} collective-permute-done((bf16[1024,128]{1,0:T(8,128)(2,1)S(1)}, bf16[1024,128]{1,0:T(8,128)(2,1)S(1)}, u32[]{:S(2)}, u32[]{:S(2)}) %collective-permute-start.5) | collective-permute-done | bytes 262176 | tf_op jit(solution)/shard_map/ppermute | solution.py:43
  43.6 0.2 fusion.23
  43.8 0.5 multiply_reduce_fusion
  44.2 9.5 %all_to_all.16 = f32[8,1,128]{2,1,0:T(1,128)S(1)} all-to-all(f32[8,1,128]{2,1,0:T(1,128)S(1)} %broadcast_in_dim.55), channel_id=1, replica_groups=mesh['grid'=8,'band'=4] {'grid'}, dimensions={0} | all-to-all | bytes 8192 | tf_op jit(solution)/shard_map/all_to_all | solution.py:15
  53.8 0.7 %broadcast_multiply_fusion = f32[256,128]{1,0:T(8,128)} fusion(f32[256,128]{1,0:T(8,128)S(1)} %get-tuple-element.17, f32[128]{0:T(128)S(1)} %add_rsqrt_fusion), kind=kLoop, calls=%fused_computation.78 | loop fusion | flops 32768 | bytes 262656 | tf_op jit(solution)/shard_map/mul | solution.py:115
  (43 shorter events, 0.6 us)
Async XLA Ops:
  0.0 0.9 %copy-start.1 = (bf16[128,256]{1,0:T(8,128)(2,1)S(1)}, bf16[128,256]{1,0:T(8,128)(2,1)}, u32[]{:S(2)}) copy-start(bf16[128,256]{1,0:T(8,128)(2,1)} %param.6) | copy-start | bytes 196612
  1.0 0.7 %copy-start.3 = (s32[64]{0:T(128)S(1)}, s32[64]{0:T(128)}, u32[]{:S(2)}) copy-start(s32[64]{0:T(128)} %param.7) | copy-start | bytes 772
  2.5 8.9 %collective-permute-start = (bf16[512,128]{1,0:T(8,128)(2,1)S(1)}, bf16[512,128]{1,0:T(8,128)(2,1)S(1)}, u32[]{:S(2)}, u32[]{:S(2)}) collective-permute-start(bf16[512,128]{1,0:T(8,128)(2,1)S(1)} %pad_maximum_fusion.3), channel_id=1, source_target_pairs={{0,2},{1,3},{2,0},{3,1},{4,6},{5,7},{6,4},{7,5},{8,10},{9,11},{10,... | collective-permute-start | bytes 393224 | tf_op jit(solution)/shard_map/ppermute | solution.py:43
  5.5 13.3 %all-to-all-start = ((bf16[8,65,128]{2,1,0:T(8,128)(2,1)}), bf16[8,65,128]{2,1,0:T(8,128)(2,1)S(1)}, u32[]{:S(2)}, u32[]{:S(2)}) async-start(bf16[8,65,128]{2,1,0:T(8,128)(2,1)} %broadcast_in_dim.50), calls=%async_computation | async-start | bytes 294912 | tf_op jit(solution)/shard_map/all_to_all | solution.py:15
  11.4 12.0 %collective-permute-start.1 = (bf16[1024,128]{1,0:T(8,128)(2,1)S(1)}, bf16[1024,128]{1,0:T(8,128)(2,1)S(1)}, u32[]{:S(2)}, u32[]{:S(2)}) collective-permute-start(bf16[1024,128]{1,0:T(8,128)(2,1)S(1)} %pad_maximum_fusion), channel_id=1, source_target_pairs={{0,1},{1,0},{2,3},{3,2},{4,5},{5,4},{6,7},{7,6},{8,9},{9,8},{10,11... | collective-permute-start | bytes 786440 | tf_op jit(solution)/shard_map/ppermute | solution.py:43
  18.8 4.3 %collective-permute-start.2 = (bf16[256,128]{1,0:T(8,128)(2,1)S(1)}, bf16[256,128]{1,0:T(8,128)(2,1)S(1)}, u32[]{:S(2)}, u32[]{:S(2)}) collective-permute-start(bf16[256,128]{1,0:T(8,128)(2,1)S(1)} %bitcast.60), channel_id=1, source_target_pairs={{0,2},{1,3},{2,0},{3,1},{4,6},{5,7},{6,4},{7,5},{8,10},{9,11},{10,... | collective-permute-start | bytes 196616 | tf_op jit(solution)/shard_map/ppermute | solution.py:43
  23.2 1.4 %collective-permute-start.3 = (bf16[512,128]{1,0:T(8,128)(2,1)S(1)}, bf16[512,128]{1,0:T(8,128)(2,1)S(1)}, u32[]{:S(2)}, u32[]{:S(2)}) collective-permute-start(bf16[512,128]{1,0:T(8,128)(2,1)S(1)} %pad_maximum_fusion.4), channel_id=1, source_target_pairs={{0,1},{1,0},{2,3},{3,2},{4,5},{5,4},{6,7},{7,6},{8,9},{9,8},{10,11... | collective-permute-start | bytes 393224 | tf_op jit(solution)/shard_map/ppermute | solution.py:43
  24.5 0.9 %copy-start = (f32[256,128]{1,0:T(8,128)S(1)}, f32[256,128]{1,0:T(8,128)}, u32[]{:S(2)}) copy-start(f32[256,128]{1,0:T(8,128)} %param.4) | copy-start | bytes 393220
  24.8 0.7 %copy-start.2 = (f32[256]{0:T(256)S(1)}, f32[256]{0:T(256)}, u32[]{:S(2)}) copy-start(f32[256]{0:T(256)} %param.5) | copy-start | bytes 3076
  36.9 5.0 %collective-permute-start.4 = (bf16[512,128]{1,0:T(8,128)(2,1)S(1)}, bf16[512,128]{1,0:T(8,128)(2,1)S(1)}, u32[]{:S(2)}, u32[]{:S(2)}) collective-permute-start(bf16[512,128]{1,0:T(8,128)(2,1)S(1)} %pad_maximum_fusion.5), channel_id=1, source_target_pairs={{0,2},{1,3},{2,0},{3,1},{4,6},{5,7},{6,4},{7,5},{8,10},{9,11},{10,... | collective-permute-start | bytes 393224 | tf_op jit(solution)/shard_map/ppermute | solution.py:43
  42.0 1.6 %collective-permute-start.5 = (bf16[1024,128]{1,0:T(8,128)(2,1)S(1)}, bf16[1024,128]{1,0:T(8,128)(2,1)S(1)}, u32[]{:S(2)}, u32[]{:S(2)}) collective-permute-start(bf16[1024,128]{1,0:T(8,128)(2,1)S(1)} %pad_maximum_fusion.2), channel_id=1, source_target_pairs={{0,1},{1,0},{2,3},{3,2},{4,5},{5,4},{6,7},{7,6},{8,9},{9,8},{10,11... | collective-permute-start | bytes 786440 | tf_op jit(solution)/shard_map/ppermute | solution.py:43

commit v14 on v13

--- a/solution.py
+++ b/solution.py
@@ -70,7 +70,7 @@
     fitted_got = jnp.stack([part[rows:].reshape(fitted.shape) for part in swapped], 0)
     fitted_all = jnp.take(fitted_got, jnp.arange(nbands, dtype=jnp.int32) ^ band, axis=0)
     fitted_all = fitted_all.reshape(ngroups // 2, 2, nslots, fitted.shape[1])
-    coll = jnp.concatenate(band_hops(pair_up(got[:, :nslots])), 1)
+    coll = jnp.concatenate(band_swap(pair_up(got[:, :nslots])), 1)
     first_filled = got[:, nslots, :nslots].reshape(ngroups // 2, 2, nslots)[:, 0] > 0
     fitted_all = jnp.where(
         first_filled[:, :, None], fitted_all[:, 0], jnp.flip(fitted_all[:, 1], axis=1)

time: 54.8 us -> 54.7 us (level)
  starting transfers between devices: 10.2 us -> 12.3 us
  waiting for transfers between devices: 16.3 us -> 14.9 us
  blocking collectives: 20 us -> 19.4 us
    ppermute x6 -> x4, waiting for transfers between devices: 9.11 us -> 4.82 us  [band_hops(): lax.ppermute(jnp.concatenate([held[k] for k in keys], 0), 'band', [(i, i...]
    ppermute x0 -> x3, waiting for transfers between devices: none -> 2.84 us  [band_swap(): got.append(lax.ppermute(x, 'band', [(i, i ^ k) for i in range(nbands)]))]
    ppermute x0 -> x3, starting transfers between devices: none -> 1.99 us  [band_swap(): got.append(lax.ppermute(x, 'band', [(i, i ^ k) for i in range(nbands)]))]
    all_to_all x2, blocking collectives: 20 us -> 19.4 us  [grid_exchange(): got = lax.all_to_all(sent, 'grid', 0, 0, tiled=True)]
    ppermute x6 -> x4, starting transfers between devices: 4.35 us -> 4.43 us  [band_hops(): lax.ppermute(jnp.concatenate([held[k] for k in keys], 0), 'band', [(i, i...]
  transfers between devices with their start and end apart: 7 -> 8, of which waited for: 4 -> 4; matrix products, arithmetic and copies ran while one was open for 4% -> 4% of each run, Pallas kernels for 0% -> 0%
where the time goes in v14:
time: 54.7 us; the launch traced here: 54.4 us
  blocking collectives  19.4 us (35%)
  waiting for transfers between devices  14.9 us (27%)
  starting transfers between devices  12.3 us (22%)
  local copies, waits for them, and re-layouts  2.98 us (5%)
  matrix products  2.42 us (4%)
  other arithmetic  2.12 us (4%)
    all_to_all x2, blocking collectives, grid_exchange(): got = lax.all_to_all(sent, 'grid', 0, 0, tiled=True)  19.4 us
    all_to_all x1, waiting for transfers between devices, grid_exchange(): got = lax.all_to_all(sent, 'grid', 0, 0, tiled=True)  7.2 us
    all_to_all x1, starting transfers between devices, grid_exchange(): got = lax.all_to_all(sent, 'grid', 0, 0, tiled=True)  5.83 us
    ppermute x4, waiting for transfers between devices, band_hops(): lax.ppermute(jnp.concatenate([held[k] for k in keys], 0), 'band', [(i, i...  4.82 us
    ppermute x4, starting transfers between devices, band_hops(): lax.ppermute(jnp.concatenate([held[k] for k in keys], 0), 'band', [(i, i...  4.43 us
    ppermute x3, waiting for transfers between devices, band_swap(): got.append(lax.ppermute(x, 'band', [(i, i ^ k) for i in range(nbands)]))  2.84 us
    ppermute x3, starting transfers between devices, band_swap(): got.append(lax.ppermute(x, 'band', [(i, i ^ k) for i in range(nbands)]))  1.99 us
    unnamed x10, local copies, waits for them, and re-layouts  1.31 us
  transfers between devices with their start and end apart: 8, of which 4 were waited for; matrix products, arithmetic and copies ran while one was open for 4% of the time, Pallas kernels for 0%

profile of v14, /device:TPU:0, one launch (start us, length us, event | category | flops | bytes accessed | tf_op | source)
XLA Modules:
  0.0 54.4 jit_solution(11479847196898735922)
XLA Ops:
  0.0 0.0 copy-start.1
  0.0 0.9 %convert_element_type.86 = bf16[256,128]{1,0:T(8,128)(2,1)S(1)} convert(f32[256,128]{1,0:T(8,128)} %param.4) | non-fusion elementwise | flops 32768 | bytes 196608 | tf_op jit(solution)/shard_map/convert_element_type | solution.py:62
  0.9 0.0 copy-done.1
  1.0 0.0 copy-start.3
  1.0 0.6 %copy-done.3 = s32[64]{0:T(128)S(1)} copy-done((s32[64]{0:T(128)S(1)}, s32[64]{0:T(128)}, u32[]{:S(2)}) %copy-start.3) | copy-done | bytes 280
  1.6 0.2 convolution_convert_fusion.1
  1.9 0.7 %broadcast_in_dim.50 = bf16[8,65,128]{2,1,0:T(8,128)(2,1)} broadcast(bf16[65,128]{1,0:T(8,128)(2,1)S(1)} %pad_maximum_fusion.5), dimensions={1,2} | broadcast | bytes 149760 | tf_op jit(solution)/shard_map/broadcast_in_dim | solution.py:11
  2.5 2.9 %collective-permute-start = (bf16[512,128]{1,0:T(8,128)(2,1)S(1)}, bf16[512,128]{1,0:T(8,128)(2,1)S(1)}, u32[]{:S(2)}, u32[]{:S(2)}) collective-permute-start(bf16[512,128]{1,0:T(8,128)(2,1)S(1)} %pad_maximum_fusion.3), channel_id=1, source_target_pairs={{0,2},{1,3},{2,0},{3,1},{4,6},{5,7},{6,4},{7,5},{8,10},{9,11},{10,... | collective-permute-start | bytes 393224 | tf_op jit(solution)/shard_map/ppermute | solution.py:43
  5.5 5.8 %all-to-all-start = ((bf16[8,65,128]{2,1,0:T(8,128)(2,1)}), bf16[8,65,128]{2,1,0:T(8,128)(2,1)S(1)}, u32[]{:S(2)}, u32[]{:S(2)}) async-start(bf16[8,65,128]{2,1,0:T(8,128)(2,1)} %broadcast_in_dim.50), calls=%async_computation | async-start | bytes 294912 | tf_op jit(solution)/shard_map/all_to_all | solution.py:15
  11.4 0.0 collective-permute-done
  11.4 0.1 collective-permute-start.1
  11.6 7.2 %all-to-all-done = bf16[8,65,128]{2,1,0:T(8,128)(2,1)S(1)} async-done(((bf16[8,65,128]{2,1,0:T(8,128)(2,1)}), bf16[8,65,128]{2,1,0:T(8,128)(2,1)S(1)}, u32[]{:S(2)}, u32[]{:S(2)}) %all-to-all-start) | async-done | bytes 133152 | tf_op jit(solution)/shard_map/all_to_all | solution.py:15
  18.8 0.1 collective-permute-start.4
  18.9 0.6 %collective-permute-start.3 = (bf16[256,128]{1,0:T(8,128)(2,1)S(1)}, bf16[256,128]{1,0:T(8,128)(2,1)S(1)}, u32[]{:S(2)}, u32[]{:S(2)}) collective-permute-start(bf16[256,128]{1,0:T(8,128)(2,1)S(1)} %bitcast.63), channel_id=1, source_target_pairs={{0,2},{1,3},{2,0},{3,1},{4,6},{5,7},{6,4},{7,5},{8,10},{9,11},{10,... | collective-permute-start | bytes 196616 | tf_op jit(solution)/shard_map/ppermute | solution.py:27
  19.5 0.2 fusion.1
  19.7 1.3 %collective-permute-start.2 = (bf16[256,128]{1,0:T(8,128)(2,1)S(1)}, bf16[256,128]{1,0:T(8,128)(2,1)S(1)}, u32[]{:S(2)}, u32[]{:S(2)}) collective-permute-start(bf16[256,128]{1,0:T(8,128)(2,1)S(1)} %bitcast.65), channel_id=1, source_target_pairs={{0,1},{1,0},{2,3},{3,2},{4,5},{5,4},{6,7},{7,6},{8,9},{9,8},{10,11... | collective-permute-start | bytes 196616 | tf_op jit(solution)/shard_map/ppermute | solution.py:27
  21.1 2.8 %collective-permute-done.3 = bf16[256,128]{1,0:T(8,128)(2,1)S(1)} collective-permute-done((bf16[256,128]{1,0:T(8,128)(2,1)S(1)}, bf16[256,128]{1,0:T(8,128)(2,1)S(1)}, u32[]{:S(2)}, u32[]{:S(2)}) %collective-permute-start.3) | collective-permute-done | bytes 65568 | tf_op jit(solution)/shard_map/ppermute | solution.py:27
  23.9 0.2 fusion.9
  24.1 0.0 collective-permute-done.1
  24.2 0.6 %gather_fusion = bf16[4,128,256]{2,1,0:T(8,128)(2,1)S(1)} fusion(bf16[4,128,256]{2,1,0:T(8,128)(2,1)S(1)} %pad_maximum_fusion.1, s32[1024]{0:T(1024)S(1)} %pad_clamp_fusion), kind=kCustom, calls=%fused_computation | custom fusion | bytes 524304 | tf_op jit(solution)/shard_map/jit(_take)/gather | solution.py:71
  24.8 0.1 broadcast_select_fusion
  24.9 0.1 rev.11
  25.1 0.1 fusion.32
  25.2 0.0 copy-start
  25.2 0.0 collective-permute-done.4
  25.2 0.2 fusion.11
  25.4 0.0 copy-start.2
  25.4 0.0 collective-permute-done.2
  25.4 0.7 %copy-done = f32[256,128]{1,0:T(8,128)S(1)} copy-done((f32[256,128]{1,0:T(8,128)S(1)}, f32[256,128]{1,0:T(8,128)}, u32[]{:S(2)}) %copy-start) | copy-done | bytes 131096
  26.1 0.0 copy-done.2
  26.1 0.5 multiply_reduce_fusion.1
  26.5 0.2 convolution_convert_fusion
  26.8 10.2 %all_to_all.15 = bf16[8,67,128]{2,1,0:T(8,128)(2,1)S(1)} all-to-all(bf16[8,67,128]{2,1,0:T(8,128)(2,1)S(1)} %broadcast_in_dim.54), channel_id=1, replica_groups=mesh['grid'=8,'band'=4] {'grid'}, dimensions={0} | all-to-all | bytes 274432 | tf_op jit(solution)/shard_map/all_to_all | solution.py:15
  37.2 1.4 %collective-permute-start.5 = (bf16[512,128]{1,0:T(8,128)(2,1)S(1)}, bf16[512,128]{1,0:T(8,128)(2,1)S(1)}, u32[]{:S(2)}, u32[]{:S(2)}) collective-permute-start(bf16[512,128]{1,0:T(8,128)(2,1)S(1)} %pad_maximum_fusion.4), channel_id=1, source_target_pairs={{0,2},{1,3},{2,0},{3,1},{4,6},{5,7},{6,4},{7,5},{8,10},{9,11},{10,... | collective-permute-start | bytes 393224 | tf_op jit(solution)/shard_map/ppermute | solution.py:43
  38.5 3.7 %collective-permute-done.5 = bf16[512,128]{1,0:T(8,128)(2,1)S(1)} collective-permute-done((bf16[512,128]{1,0:T(8,128)(2,1)S(1)}, bf16[512,128]{1,0:T(8,128)(2,1)S(1)}, u32[]{:S(2)}, u32[]{:S(2)}) %collective-permute-start.5) | collective-permute-done | bytes 131104 | tf_op jit(solution)/shard_map/ppermute | solution.py:43
  42.2 0.1 collective-permute-start.6
  42.3 0.2 fusion.13
  42.5 0.2 fusion.21
  42.7 1.1 %collective-permute-done.6 = bf16[1024,128]{1,0:T(8,128)(2,1)S(1)} collective-permute-done((bf16[1024,128]{1,0:T(8,128)(2,1)S(1)}, bf16[1024,128]{1,0:T(8,128)(2,1)S(1)}, u32[]{:S(2)}, u32[]{:S(2)}) %collective-permute-start.6) | collective-permute-done | bytes 262176 | tf_op jit(solution)/shard_map/ppermute | solution.py:43
  43.8 0.2 fusion.23
  44.0 0.5 multiply_reduce_fusion
  44.5 9.2 %all_to_all.16 = f32[8,1,128]{2,1,0:T(1,128)S(1)} all-to-all(f32[8,1,128]{2,1,0:T(1,128)S(1)} %broadcast_in_dim.55), channel_id=1, replica_groups=mesh['grid'=8,'band'=4] {'grid'}, dimensions={0} | all-to-all | bytes 8192 | tf_op jit(solution)/shard_map/all_to_all | solution.py:15
  53.8 0.7 %broadcast_multiply_fusion = f32[256,128]{1,0:T(8,128)} fusion(f32[256,128]{1,0:T(8,128)S(1)} %get-tuple-element.17, f32[128]{0:T(128)S(1)} %add_rsqrt_fusion), kind=kLoop, calls=%fused_computation.75 | loop fusion | flops 32768 | bytes 262656 | tf_op jit(solution)/shard_map/mul | solution.py:115
  (42 shorter events, 0.6 us)
Async XLA Ops:
  0.0 0.9 %copy-start.1 = (bf16[128,256]{1,0:T(8,128)(2,1)S(1)}, bf16[128,256]{1,0:T(8,128)(2,1)}, u32[]{:S(2)}) copy-start(bf16[128,256]{1,0:T(8,128)(2,1)} %param.6) | copy-start | bytes 196612
  1.0 0.7 %copy-start.3 = (s32[64]{0:T(128)S(1)}, s32[64]{0:T(128)}, u32[]{:S(2)}) copy-start(s32[64]{0:T(128)} %param.7) | copy-start | bytes 772
  2.5 8.9 %collective-permute-start = (bf16[512,128]{1,0:T(8,128)(2,1)S(1)}, bf16[512,128]{1,0:T(8,128)(2,1)S(1)}, u32[]{:S(2)}, u32[]{:S(2)}) collective-permute-start(bf16[512,128]{1,0:T(8,128)(2,1)S(1)} %pad_maximum_fusion.3), channel_id=1, source_target_pairs={{0,2},{1,3},{2,0},{3,1},{4,6},{5,7},{6,4},{7,5},{8,10},{9,11},{10,... | collective-permute-start | bytes 393224 | tf_op jit(solution)/shard_map/ppermute | solution.py:43
  5.5 13.3 %all-to-all-start = ((bf16[8,65,128]{2,1,0:T(8,128)(2,1)}), bf16[8,65,128]{2,1,0:T(8,128)(2,1)S(1)}, u32[]{:S(2)}, u32[]{:S(2)}) async-start(bf16[8,65,128]{2,1,0:T(8,128)(2,1)} %broadcast_in_dim.50), calls=%async_computation | async-start | bytes 294912 | tf_op jit(solution)/shard_map/all_to_all | solution.py:15
  11.4 12.7 %collective-permute-start.1 = (bf16[1024,128]{1,0:T(8,128)(2,1)S(1)}, bf16[1024,128]{1,0:T(8,128)(2,1)S(1)}, u32[]{:S(2)}, u32[]{:S(2)}) collective-permute-start(bf16[1024,128]{1,0:T(8,128)(2,1)S(1)} %pad_maximum_fusion), channel_id=1, source_target_pairs={{0,1},{1,0},{2,3},{3,2},{4,5},{5,4},{6,7},{7,6},{8,9},{9,8},{10,11... | collective-permute-start | bytes 786440 | tf_op jit(solution)/shard_map/ppermute | solution.py:43
  18.8 6.4 %collective-permute-start.4 = (bf16[256,128]{1,0:T(8,128)(2,1)S(1)}, bf16[256,128]{1,0:T(8,128)(2,1)S(1)}, u32[]{:S(2)}, u32[]{:S(2)}) collective-permute-start(bf16[256,128]{1,0:T(8,128)(2,1)S(1)} %bitcast.62), channel_id=1, source_target_pairs={{0,3},{1,2},{2,1},{3,0},{4,7},{5,6},{6,5},{7,4},{8,11},{9,10},{10,... | collective-permute-start | bytes 196616 | tf_op jit(solution)/shard_map/ppermute | solution.py:27
  18.9 5.0 %collective-permute-start.3 = (bf16[256,128]{1,0:T(8,128)(2,1)S(1)}, bf16[256,128]{1,0:T(8,128)(2,1)S(1)}, u32[]{:S(2)}, u32[]{:S(2)}) collective-permute-start(bf16[256,128]{1,0:T(8,128)(2,1)S(1)} %bitcast.63), channel_id=1, source_target_pairs={{0,2},{1,3},{2,0},{3,1},{4,6},{5,7},{6,4},{7,5},{8,10},{9,11},{10,... | collective-permute-start | bytes 196616 | tf_op jit(solution)/shard_map/ppermute | solution.py:27
  19.7 5.7 %collective-permute-start.2 = (bf16[256,128]{1,0:T(8,128)(2,1)S(1)}, bf16[256,128]{1,0:T(8,128)(2,1)S(1)}, u32[]{:S(2)}, u32[]{:S(2)}) collective-permute-start(bf16[256,128]{1,0:T(8,128)(2,1)S(1)} %bitcast.65), channel_id=1, source_target_pairs={{0,1},{1,0},{2,3},{3,2},{4,5},{5,4},{6,7},{7,6},{8,9},{9,8},{10,11... | collective-permute-start | bytes 196616 | tf_op jit(solution)/shard_map/ppermute | solution.py:27
  25.2 0.9 %copy-start = (f32[256,128]{1,0:T(8,128)S(1)}, f32[256,128]{1,0:T(8,128)}, u32[]{:S(2)}) copy-start(f32[256,128]{1,0:T(8,128)} %param.4) | copy-start | bytes 393220
  25.4 0.7 %copy-start.2 = (f32[256]{0:T(256)S(1)}, f32[256]{0:T(256)}, u32[]{:S(2)}) copy-start(f32[256]{0:T(256)} %param.5) | copy-start | bytes 3076
  37.2 5.0 %collective-permute-start.5 = (bf16[512,128]{1,0:T(8,128)(2,1)S(1)}, bf16[512,128]{1,0:T(8,128)(2,1)S(1)}, u32[]{:S(2)}, u32[]{:S(2)}) collective-permute-start(bf16[512,128]{1,0:T(8,128)(2,1)S(1)} %pad_maximum_fusion.4), channel_id=1, source_target_pairs={{0,2},{1,3},{2,0},{3,1},{4,6},{5,7},{6,4},{7,5},{8,10},{9,11},{10,... | collective-permute-start | bytes 393224 | tf_op jit(solution)/shard_map/ppermute | solution.py:43
  42.2 1.6 %collective-permute-start.6 = (bf16[1024,128]{1,0:T(8,128)(2,1)S(1)}, bf16[1024,128]{1,0:T(8,128)(2,1)S(1)}, u32[]{:S(2)}, u32[]{:S(2)}) collective-permute-start(bf16[1024,128]{1,0:T(8,128)(2,1)S(1)} %pad_maximum_fusion.2), channel_id=1, source_target_pairs={{0,1},{1,0},{2,3},{3,2},{4,5},{5,4},{6,7},{7,6},{8,9},{9,8},{10,11... | collective-permute-start | bytes 786440 | tf_op jit(solution)/shard_map/ppermute | solution.py:43

commit v15 on v13

--- a/solution.py
+++ b/solution.py
@@ -59,12 +59,13 @@
     total_orbitals = block_width * nbands
     valid_mask = points >= 0
     picks = (points[:, None] == jnp.arange(rows, dtype=points.dtype)[None, :]).astype(jnp.bfloat16)
-    rows_b16 = orbitals.astype(jnp.bfloat16)
-    selected = jnp.dot(picks, rows_b16, preferred_element_type=jnp.float32).astype(jnp.bfloat16)
+    selected = jnp.dot(picks, orbitals, preferred_element_type=jnp.float32).astype(jnp.bfloat16)
     filled = jnp.pad(valid_mask.astype(jnp.bfloat16), (0, block_width - nslots))
-    to_band = jnp.concatenate([rows_b16, fitted.reshape(-1, block_width)], 0)
-    sent, to_band = lax.optimization_barrier((grid_copies(jnp.concatenate([selected, filled[None]], 0)), to_band))
+    sent = lax.optimization_barrier(grid_copies(jnp.concatenate([selected, filled[None]], 0)))
     got = grid_exchange(sent).reshape(ngroups, nslots + 1, block_width)
+    to_band = jnp.concatenate([orbitals.astype(jnp.bfloat16), fitted.reshape(-1, block_width)], 0)
+    pot = potential[:, None]
+    got, first_pot_psi = lax.optimization_barrier((got, pot * orbitals))
     swapped = band_hops(to_band)
     rows_b = jnp.concatenate([part[:rows] for part in swapped], 1)
     fitted_got = jnp.stack([part[rows:].reshape(fitted.shape) for part in swapped], 0)
@@ -76,7 +77,6 @@
         first_filled[:, :, None], fitted_all[:, 0], jnp.flip(fitted_all[:, 1], axis=1)
     ).reshape(-1, fitted.shape[1]).astype(jnp.float32)
     psi = orbitals
-    pot = potential[:, None]
     for step in range(ITERS):
         if step:
             at_slots = jnp.dot(picks, psi, preferred_element_type=jnp.float32).astype(jnp.bfloat16)
@@ -109,7 +109,8 @@
         applied = lax.dot_general(
             tile_blocks, coll[:, :block_width], (((0,), (0,)), ((), ())), preferred_element_type=jnp.float32
         )
-        psi = psi - 0.25 * (pot * psi - applied)
+        pot_psi = first_pot_psi if step == 0 else pot * psi
+        psi = psi - 0.25 * (pot_psi - applied)
         sq = jnp.sum(psi * psi, axis=0)
     total = jnp.sum(grid_gather(sq[None]), axis=0)
     return psi * lax.rsqrt(total / (rows * ngroups) + 1e-06)

time: 54.8 us -> 55.2 us (level)
    reshape x1, local copies, waits for them, and re-layouts: 0.03 us -> 0.9 us  [body(): fitted.reshape(-1, block_width)]
    unnamed x10 -> x9, local copies, waits for them, and re-layouts: 1.32 us -> 0.85 us
  transfers between devices with their start and end apart: 7 -> 7, of which waited for: 4 -> 4; matrix products, arithmetic and copies ran while one was open for 4% -> 5% of each run, Pallas kernels for 0% -> 0%
where the time goes in v15:
time: 55.2 us; the launch traced here: 54.8 us
  blocking collectives  20.1 us (36%)
  waiting for transfers between devices  16.3 us (30%)
  starting transfers between devices  10.3 us (19%)
  local copies, waits for them, and re-layouts  3.37 us (6%)
  matrix products  2.42 us (4%)
  other arithmetic  1.95 us (4%)
    all_to_all x2, blocking collectives, grid_exchange(): got = lax.all_to_all(sent, 'grid', 0, 0, tiled=True)  20.1 us
    ppermute x6, waiting for transfers between devices, band_hops(): lax.ppermute(jnp.concatenate([held[k] for k in keys], 0), 'band', [(i, i...  9.02 us
    all_to_all x1, waiting for transfers between devices, grid_exchange(): got = lax.all_to_all(sent, 'grid', 0, 0, tiled=True)  7.25 us
    all_to_all x1, starting transfers between devices, grid_exchange(): got = lax.all_to_all(sent, 'grid', 0, 0, tiled=True)  5.83 us
    ppermute x6, starting transfers between devices, band_hops(): lax.ppermute(jnp.concatenate([held[k] for k in keys], 0), 'band', [(i, i...  4.46 us
    dot_general x6, matrix products, body(): lax.dot_general(coll[:, k * block_width:(k + 1) * block_width], rows_b[:,...  1.11 us
  transfers between devices with their start and end apart: 7, of which 4 were waited for; matrix products, arithmetic and copies ran while one was open for 5% of the time, Pallas kernels for 0%

profile of v15, /device:TPU:0, one launch (start us, length us, event | category | flops | bytes accessed | tf_op | source)
XLA Modules:
  0.0 54.8 jit_solution(15972527590867206774)
XLA Ops:
  0.0 0.0 copy-start
  0.0 0.9 %reshape.100 = bf16[256,128]{1,0:T(8,128)(2,1)S(1)} reshape(bf16[128,256]{1,0:T(8,128)(2,1)} %param.6) | data formatting | bytes 131072 | tf_op jit(solution)/shard_map/reshape | solution.py:66
  0.9 0.0 copy-done
  0.9 0.8 %fusion.62 = (bf16[256,128]{1,0:T(8,128)(2,1)S(1)}, f32[256,128]{1,0:T(8,128)S(1)}) fusion(f32[256,128]{1,0:T(8,128)S(1)} %copy-done, f32[256]{0:T(256)} %param.5), kind=kLoop, calls=%fused_computation.110 | loop fusion | flops 65536 | bytes 328704 | tf_op jit(solution)/shard_map/convert_element_type | solution.py:66
  1.7 0.0 copy-start.3
  1.7 3.0 %collective-permute-start = (bf16[512,128]{1,0:T(8,128)(2,1)S(1)}, bf16[512,128]{1,0:T(8,128)(2,1)S(1)}, u32[]{:S(2)}, u32[]{:S(2)}) collective-permute-start(bf16[512,128]{1,0:T(8,128)(2,1)S(1)} %pad_maximum_fusion.3), channel_id=1, source_target_pairs={{0,2},{1,3},{2,0},{3,1},{4,6},{5,7},{6,4},{7,5},{8,10},{9,11},{10,... | collective-permute-start | bytes 393224 | tf_op jit(solution)/shard_map/ppermute | solution.py:43
  4.8 0.0 copy-done.3
  4.8 0.2 convolution_convert_fusion.1
  5.0 0.7 %broadcast_in_dim.50 = bf16[8,65,128]{2,1,0:T(8,128)(2,1)} broadcast(bf16[65,128]{1,0:T(8,128)(2,1)S(1)} %pad_maximum_fusion.6), dimensions={1,2} | broadcast | bytes 149760 | tf_op jit(solution)/shard_map/broadcast_in_dim | solution.py:11
  5.7 5.8 %all-to-all-start = ((bf16[8,65,128]{2,1,0:T(8,128)(2,1)}), bf16[8,65,128]{2,1,0:T(8,128)(2,1)S(1)}, u32[]{:S(2)}, u32[]{:S(2)}) async-start(bf16[8,65,128]{2,1,0:T(8,128)(2,1)} %broadcast_in_dim.50), calls=%async_computation | async-start | bytes 294912 | tf_op jit(solution)/shard_map/all_to_all | solution.py:15
  11.5 0.0 collective-permute-done
  11.6 0.1 collective-permute-start.1
  11.7 7.3 %all-to-all-done = bf16[8,65,128]{2,1,0:T(8,128)(2,1)S(1)} async-done(((bf16[8,65,128]{2,1,0:T(8,128)(2,1)}), bf16[8,65,128]{2,1,0:T(8,128)(2,1)S(1)}, u32[]{:S(2)}, u32[]{:S(2)}) %all-to-all-start) | async-done | bytes 133152 | tf_op jit(solution)/shard_map/all_to_all | solution.py:15
  19.1 0.6 %collective-permute-start.2 = (bf16[256,128]{1,0:T(8,128)(2,1)S(1)}, bf16[256,128]{1,0:T(8,128)(2,1)S(1)}, u32[]{:S(2)}, u32[]{:S(2)}) collective-permute-start(bf16[256,128]{1,0:T(8,128)(2,1)S(1)} %bitcast.60), channel_id=1, source_target_pairs={{0,2},{1,3},{2,0},{3,1},{4,6},{5,7},{6,4},{7,5},{8,10},{9,11},{10,... | collective-permute-start | bytes 196616 | tf_op jit(solution)/shard_map/ppermute | solution.py:43
  19.7 0.2 fusion.1
  19.9 3.5 %collective-permute-done.2 = bf16[256,128]{1,0:T(8,128)(2,1)S(1)} collective-permute-done((bf16[256,128]{1,0:T(8,128)(2,1)S(1)}, bf16[256,128]{1,0:T(8,128)(2,1)S(1)}, u32[]{:S(2)}, u32[]{:S(2)}) %collective-permute-start.2) | collective-permute-done | bytes 65568 | tf_op jit(solution)/shard_map/ppermute | solution.py:43
  23.4 0.1 collective-permute-start.3
  23.5 0.2 fusion.9
  23.7 0.0 collective-permute-done.1
  23.7 0.0 copy-start.1
  23.8 0.8 %copy-done.1 = bf16[128,256]{1,0:T(8,128)(2,1)S(1)} copy-done((bf16[128,256]{1,0:T(8,128)(2,1)S(1)}, bf16[128,256]{1,0:T(8,128)(2,1)}, u32[]{:S(2)}) %copy-start.1) | copy-done | bytes 65560
  24.6 0.6 %gather_fusion = bf16[4,128,256]{2,1,0:T(8,128)(2,1)S(1)} fusion(bf16[4,128,256]{2,1,0:T(8,128)(2,1)S(1)} %pad_maximum_fusion.1, s32[1024]{0:T(1024)S(1)} %pad_clamp_fusion), kind=kCustom, calls=%fused_computation | custom fusion | bytes 524304 | tf_op jit(solution)/shard_map/jit(_take)/gather | solution.py:72
  25.2 0.1 copy_select_fusion
  25.3 0.1 rev.11
  25.5 0.1 fusion.32
  25.6 0.0 collective-permute-done.3
  25.6 0.2 fusion.11
  25.8 0.5 multiply_reduce_fusion.1
  26.2 0.2 convolution_convert_fusion
  26.5 10.6 %all_to_all.15 = bf16[8,67,128]{2,1,0:T(8,128)(2,1)S(1)} all-to-all(bf16[8,67,128]{2,1,0:T(8,128)(2,1)S(1)} %broadcast_in_dim.54), channel_id=1, replica_groups=mesh['grid'=8,'band'=4] {'grid'}, dimensions={0} | all-to-all | bytes 274432 | tf_op jit(solution)/shard_map/all_to_all | solution.py:15
  37.2 0.6 %collective-permute-start.4 = (bf16[512,128]{1,0:T(8,128)(2,1)S(1)}, bf16[512,128]{1,0:T(8,128)(2,1)S(1)}, u32[]{:S(2)}, u32[]{:S(2)}) collective-permute-start(bf16[512,128]{1,0:T(8,128)(2,1)S(1)} %pad_maximum_fusion.5), channel_id=1, source_target_pairs={{0,2},{1,3},{2,0},{3,1},{4,6},{5,7},{6,4},{7,5},{8,10},{9,11},{10,... | collective-permute-start | bytes 393224 | tf_op jit(solution)/shard_map/ppermute | solution.py:43
  37.9 4.4 %collective-permute-done.4 = bf16[512,128]{1,0:T(8,128)(2,1)S(1)} collective-permute-done((bf16[512,128]{1,0:T(8,128)(2,1)S(1)}, bf16[512,128]{1,0:T(8,128)(2,1)S(1)}, u32[]{:S(2)}, u32[]{:S(2)}) %collective-permute-start.4) | collective-permute-done | bytes 131104 | tf_op jit(solution)/shard_map/ppermute | solution.py:43
  42.3 0.1 collective-permute-start.5
  42.4 0.2 fusion.13
  42.6 0.2 fusion.21
  42.8 0.0 copy-start.2
  42.8 1.1 %collective-permute-done.5 = bf16[1024,128]{1,0:T(8,128)(2,1)S(1)} collective-permute-done((bf16[1024,128]{1,0:T(8,128)(2,1)S(1)}, bf16[1024,128]{1,0:T(8,128)(2,1)S(1)}, u32[]{:S(2)}, u32[]{:S(2)}) %collective-permute-start.5) | collective-permute-done | bytes 262176 | tf_op jit(solution)/shard_map/ppermute | solution.py:43
  43.9 0.2 fusion.23
  44.1 0.0 copy-done.2
  44.1 0.5 multiply_reduce_fusion
  44.6 9.5 %all_to_all.16 = f32[8,1,128]{2,1,0:T(1,128)S(1)} all-to-all(f32[8,1,128]{2,1,0:T(1,128)S(1)} %broadcast_in_dim.55), channel_id=1, replica_groups=mesh['grid'=8,'band'=4] {'grid'}, dimensions={0} | all-to-all | bytes 8192 | tf_op jit(solution)/shard_map/all_to_all | solution.py:15
  54.1 0.7 %broadcast_multiply_fusion = f32[256,128]{1,0:T(8,128)} fusion(f32[256,128]{1,0:T(8,128)S(1)} %get-tuple-element.19, f32[128]{0:T(128)S(1)} %add_rsqrt_fusion), kind=kLoop, calls=%fused_computation.78 | loop fusion | flops 32768 | bytes 262656 | tf_op jit(solution)/shard_map/mul | solution.py:116
  (40 shorter events, 0.6 us)
Async XLA Ops:
  0.0 0.9 %copy-start = (f32[256,128]{1,0:T(8,128)S(1)}, f32[256,128]{1,0:T(8,128)}, u32[]{:S(2)}) copy-start(f32[256,128]{1,0:T(8,128)} %param.4) | copy-start | bytes 393220
  1.7 3.0 %copy-start.3 = (s32[64]{0:T(128)S(1)}, s32[64]{0:T(128)}, u32[]{:S(2)}) copy-start(s32[64]{0:T(128)} %param.7) | copy-start | bytes 772
  1.7 9.8 %collective-permute-start = (bf16[512,128]{1,0:T(8,128)(2,1)S(1)}, bf16[512,128]{1,0:T(8,128)(2,1)S(1)}, u32[]{:S(2)}, u32[]{:S(2)}) collective-permute-start(bf16[512,128]{1,0:T(8,128)(2,1)S(1)} %pad_maximum_fusion.3), channel_id=1, source_target_pairs={{0,2},{1,3},{2,0},{3,1},{4,6},{5,7},{6,4},{7,5},{8,10},{9,11},{10,... | collective-permute-start | bytes 393224 | tf_op jit(solution)/shard_map/ppermute | solution.py:43
  5.7 13.3 %all-to-all-start = ((bf16[8,65,128]{2,1,0:T(8,128)(2,1)}), bf16[8,65,128]{2,1,0:T(8,128)(2,1)S(1)}, u32[]{:S(2)}, u32[]{:S(2)}) async-start(bf16[8,65,128]{2,1,0:T(8,128)(2,1)} %broadcast_in_dim.50), calls=%async_computation | async-start | bytes 294912 | tf_op jit(solution)/shard_map/all_to_all | solution.py:15
  11.6 12.1 %collective-permute-start.1 = (bf16[1024,128]{1,0:T(8,128)(2,1)S(1)}, bf16[1024,128]{1,0:T(8,128)(2,1)S(1)}, u32[]{:S(2)}, u32[]{:S(2)}) collective-permute-start(bf16[1024,128]{1,0:T(8,128)(2,1)S(1)} %pad_maximum_fusion), channel_id=1, source_target_pairs={{0,1},{1,0},{2,3},{3,2},{4,5},{5,4},{6,7},{7,6},{8,9},{9,8},{10,11... | collective-permute-start | bytes 786440 | tf_op jit(solution)/shard_map/ppermute | solution.py:43
  19.1 4.3 %collective-permute-start.2 = (bf16[256,128]{1,0:T(8,128)(2,1)S(1)}, bf16[256,128]{1,0:T(8,128)(2,1)S(1)}, u32[]{:S(2)}, u32[]{:S(2)}) collective-permute-start(bf16[256,128]{1,0:T(8,128)(2,1)S(1)} %bitcast.60), channel_id=1, source_target_pairs={{0,2},{1,3},{2,0},{3,1},{4,6},{5,7},{6,4},{7,5},{8,10},{9,11},{10,... | collective-permute-start | bytes 196616 | tf_op jit(solution)/shard_map/ppermute | solution.py:43
  23.4 2.2 %collective-permute-start.3 = (bf16[512,128]{1,0:T(8,128)(2,1)S(1)}, bf16[512,128]{1,0:T(8,128)(2,1)S(1)}, u32[]{:S(2)}, u32[]{:S(2)}) collective-permute-start(bf16[512,128]{1,0:T(8,128)(2,1)S(1)} %pad_maximum_fusion.4), channel_id=1, source_target_pairs={{0,1},{1,0},{2,3},{3,2},{4,5},{5,4},{6,7},{7,6},{8,9},{9,8},{10,11... | collective-permute-start | bytes 393224 | tf_op jit(solution)/shard_map/ppermute | solution.py:43
  23.7 0.8 %copy-start.1 = (bf16[128,256]{1,0:T(8,128)(2,1)S(1)}, bf16[128,256]{1,0:T(8,128)(2,1)}, u32[]{:S(2)}) copy-start(bf16[128,256]{1,0:T(8,128)(2,1)} %param.6) | copy-start | bytes 196612
  37.2 5.0 %collective-permute-start.4 = (bf16[512,128]{1,0:T(8,128)(2,1)S(1)}, bf16[512,128]{1,0:T(8,128)(2,1)S(1)}, u32[]{:S(2)}, u32[]{:S(2)}) collective-permute-start(bf16[512,128]{1,0:T(8,128)(2,1)S(1)} %pad_maximum_fusion.5), channel_id=1, source_target_pairs={{0,2},{1,3},{2,0},{3,1},{4,6},{5,7},{6,4},{7,5},{8,10},{9,11},{10,... | collective-permute-start | bytes 393224 | tf_op jit(solution)/shard_map/ppermute | solution.py:43
  42.3 1.6 %collective-permute-start.5 = (bf16[1024,128]{1,0:T(8,128)(2,1)S(1)}, bf16[1024,128]{1,0:T(8,128)(2,1)S(1)}, u32[]{:S(2)}, u32[]{:S(2)}) collective-permute-start(bf16[1024,128]{1,0:T(8,128)(2,1)S(1)} %pad_maximum_fusion.2), channel_id=1, source_target_pairs={{0,1},{1,0},{2,3},{3,2},{4,5},{5,4},{6,7},{7,6},{8,9},{9,8},{10,11... | collective-permute-start | bytes 786440 | tf_op jit(solution)/shard_map/ppermute | solution.py:43
  42.8 1.3 %copy-start.2 = (f32[256]{0:T(256)S(1)}, f32[256]{0:T(256)}, u32[]{:S(2)}) copy-start(f32[256]{0:T(256)} %param.5) | copy-start | bytes 3076

commit v16 on v13

--- a/solution.py
+++ b/solution.py
@@ -79,6 +79,7 @@
     pot = potential[:, None]
     for step in range(ITERS):
         if step:
+            fresh_swapped = band_hops(psi)
             at_slots = jnp.dot(picks, psi, preferred_element_type=jnp.float32).astype(jnp.bfloat16)
             high = lax.reduce_precision(sq, exponent_bits=8, mantissa_bits=7)
             rest = sq - high
@@ -90,11 +91,20 @@
             total = jnp.sum((sums[:, 0] + sums[:, 1]) + sums[:, 2], axis=0)
             scale = lax.rsqrt(total / (rows * ngroups) + 1e-06)
             coll_own = pair_up((got[:, :nslots].astype(jnp.float32) * scale).astype(jnp.bfloat16))
+            ncoll = coll_own.shape[0]
+            high = lax.reduce_precision(scale, exponent_bits=8, mantissa_bits=7)
+            rest = scale - high
+            middle = lax.reduce_precision(rest, exponent_bits=8, mantissa_bits=7)
+            low = lax.reduce_precision(rest - middle, exponent_bits=8, mantissa_bits=7)
+            scale_parts = jnp.stack([high, middle, low], 0).astype(jnp.bfloat16)
+            swapped = band_hops(jnp.concatenate([coll_own, scale_parts], 0))
+            coll = jnp.concatenate([part[:ncoll] for part in swapped], 1)
+            scaled = []
+            for part, fresh_rows in zip(swapped, fresh_swapped):
+                got_scale = part[ncoll:].astype(jnp.float32)
+                scaled.append((fresh_rows * ((got_scale[0] + got_scale[1]) + got_scale[2])).astype(jnp.bfloat16))
+            rows_b = jnp.concatenate(scaled, 1)
             psi = psi * scale
-            ncoll = coll_own.shape[0]
-            swapped = band_hops(jnp.concatenate([coll_own, psi.astype(jnp.bfloat16)], 0))
-            coll = jnp.concatenate([part[:ncoll] for part in swapped], 1)
-            rows_b = jnp.concatenate([part[ncoll:] for part in swapped], 1)
         proj = None
         for k in range(nbands):
             part = lax.dot_general(

time: 54.8 us -> 56.4 us (1.029)
  blocking collectives: 20 us -> 9.08 us
  starting transfers between devices: 10.2 us -> 16.7 us
  waiting for transfers between devices: 16.3 us -> 20.5 us
  local copies, waits for them, and re-layouts: 2.99 us -> 4.13 us
  other arithmetic: 2.12 us -> 2.8 us
    all_to_all x2 -> x1, blocking collectives: 20 us -> 9.08 us  [grid_exchange(): got = lax.all_to_all(sent, 'grid', 0, 0, tiled=True)]
    all_to_all x1 -> x2, starting transfers between devices: 5.83 us -> 11.2 us  [grid_exchange(): got = lax.all_to_all(sent, 'grid', 0, 0, tiled=True)]
    all_to_all x1 -> x2, waiting for transfers between devices: 7.2 us -> 9.8 us  [grid_exchange(): got = lax.all_to_all(sent, 'grid', 0, 0, tiled=True)]
    ppermute x6 -> x8, waiting for transfers between devices: 9.11 us -> 10.7 us  [band_hops(): lax.ppermute(jnp.concatenate([held[k] for k in keys], 0), 'band', [(i, i...]
    ppermute x6 -> x8, starting transfers between devices: 4.35 us -> 5.48 us  [band_hops(): lax.ppermute(jnp.concatenate([held[k] for k in keys], 0), 'band', [(i, i...]
    broadcast_in_dim x3, local copies, waits for them, and re-layouts: 0.7 us -> 1.36 us  [grid_copies(): return jnp.broadcast_to(x[None], (ngroups,) + x.shape)]
    ge x1, other arithmetic: 0.01 us -> 0.66 us  [body(): valid_mask = points >= 0]
  transfers between devices with their start and end apart: 7 -> 10, of which waited for: 4 -> 6; matrix products, arithmetic and copies ran while one was open for 4% -> 6% of each run, Pallas kernels for 0% -> 0%
where the time goes in v16:
time: 56.4 us; the launch traced here: 56 us
  waiting for transfers between devices  20.5 us (36%)
  starting transfers between devices  16.7 us (30%)
  blocking collectives  9.08 us (16%)
  local copies, waits for them, and re-layouts  4.13 us (7%)
  other arithmetic  2.8 us (5%)
  matrix products  2.43 us (4%)
    all_to_all x2, starting transfers between devices, grid_exchange(): got = lax.all_to_all(sent, 'grid', 0, 0, tiled=True)  11.2 us
    ppermute x8, waiting for transfers between devices, band_hops(): lax.ppermute(jnp.concatenate([held[k] for k in keys], 0), 'band', [(i, i...  10.7 us
    all_to_all x2, waiting for transfers between devices, grid_exchange(): got = lax.all_to_all(sent, 'grid', 0, 0, tiled=True)  9.8 us
    all_to_all x1, blocking collectives, grid_exchange(): got = lax.all_to_all(sent, 'grid', 0, 0, tiled=True)  9.08 us
    ppermute x8, starting transfers between devices, band_hops(): lax.ppermute(jnp.concatenate([held[k] for k in keys], 0), 'band', [(i, i...  5.48 us
    broadcast_in_dim x3, local copies, waits for them, and re-layouts, grid_copies(): return jnp.broadcast_to(x[None], (ngroups,) + x.shape)  1.36 us
    unnamed x10, local copies, waits for them, and re-layouts  1.34 us
  transfers between devices with their start and end apart: 10, of which 6 were waited for; matrix products, arithmetic and copies ran while one was open for 6% of the time, Pallas kernels for 0%

profile of v16, /device:TPU:0, one launch (start us, length us, event | category | flops | bytes accessed | tf_op | source)
XLA Modules:
  0.0 56.0 jit_solution(2790851836292182738)
XLA Ops:
  0.0 0.7 %broadcast_compare_fusion = pred[64]{0:T(512)(128)(4,1)S(1)} fusion(s32[64]{0:T(128)} %param.7), kind=kLoop, calls=%fused_computation.126 | loop fusion | flops 64 | bytes 320 | tf_op jit(solution)/shard_map/ge | solution.py:60
  0.7 0.9 %convert_element_type.108 = bf16[256,128]{1,0:T(8,128)(2,1)S(1)} convert(f32[256,128]{1,0:T(8,128)} %param.4) | non-fusion elementwise | flops 32768 | bytes 196608 | tf_op jit(solution)/shard_map/convert_element_type | solution.py:62
  1.6 0.0 copy-done.3
  1.6 0.0 copy-start.1
  1.6 0.2 convolution_convert_fusion.1
  1.8 0.6 %copy-done.1 = bf16[128,256]{1,0:T(8,128)(2,1)S(1)} copy-done((bf16[128,256]{1,0:T(8,128)(2,1)S(1)}, bf16[128,256]{1,0:T(8,128)(2,1)}, u32[]{:S(2)}) %copy-start.1) | copy-done | bytes 65560
  2.5 0.7 %broadcast_in_dim.31 = bf16[8,65,128]{2,1,0:T(8,128)(2,1)} broadcast(bf16[65,128]{1,0:T(8,128)(2,1)S(1)} %pad_maximum_fusion.6), dimensions={1,2} | broadcast | bytes 149760 | tf_op jit(solution)/shard_map/broadcast_in_dim | solution.py:11
  3.2 7.3 %all-to-all-start = ((bf16[8,65,128]{2,1,0:T(8,128)(2,1)}), bf16[8,65,128]{2,1,0:T(8,128)(2,1)S(1)}, u32[]{:S(2)}, u32[]{:S(2)}) async-start(bf16[8,65,128]{2,1,0:T(8,128)(2,1)} %broadcast_in_dim.31), calls=%async_computation | async-start | bytes 294912 | tf_op jit(solution)/shard_map/all_to_all | solution.py:15
  10.5 1.5 %collective-permute-start = (bf16[512,128]{1,0:T(8,128)(2,1)S(1)}, bf16[512,128]{1,0:T(8,128)(2,1)S(1)}, u32[]{:S(2)}, u32[]{:S(2)}) collective-permute-start(bf16[512,128]{1,0:T(8,128)(2,1)S(1)} %pad_maximum_fusion.3), channel_id=1, source_target_pairs={{0,2},{1,3},{2,0},{3,1},{4,6},{5,7},{6,4},{7,5},{8,10},{9,11},{10,... | collective-permute-start | bytes 393224 | tf_op jit(solution)/shard_map/ppermute | solution.py:43
  12.0 3.4 %collective-permute-done = bf16[512,128]{1,0:T(8,128)(2,1)S(1)} collective-permute-done((bf16[512,128]{1,0:T(8,128)(2,1)S(1)}, bf16[512,128]{1,0:T(8,128)(2,1)S(1)}, u32[]{:S(2)}, u32[]{:S(2)}) %collective-permute-start) | collective-permute-done | bytes 131104 | tf_op jit(solution)/shard_map/ppermute | solution.py:43
  15.5 0.1 collective-permute-start.1
  15.6 2.3 %all-to-all-done = bf16[8,65,128]{2,1,0:T(8,128)(2,1)S(1)} async-done(((bf16[8,65,128]{2,1,0:T(8,128)(2,1)}), bf16[8,65,128]{2,1,0:T(8,128)(2,1)S(1)}, u32[]{:S(2)}, u32[]{:S(2)}) %all-to-all-start) | async-done | bytes 133152 | tf_op jit(solution)/shard_map/all_to_all | solution.py:15
  18.0 1.6 %collective-permute-start.2 = (bf16[256,128]{1,0:T(8,128)(2,1)S(1)}, bf16[256,128]{1,0:T(8,128)(2,1)S(1)}, u32[]{:S(2)}, u32[]{:S(2)}) collective-permute-start(bf16[256,128]{1,0:T(8,128)(2,1)S(1)} %bitcast.74), channel_id=1, source_target_pairs={{0,2},{1,3},{2,0},{3,1},{4,6},{5,7},{6,4},{7,5},{8,10},{9,11},{10,... | collective-permute-start | bytes 196616 | tf_op jit(solution)/shard_map/ppermute | solution.py:43
  19.6 0.2 fusion.1
  19.8 2.5 %collective-permute-done.2 = bf16[256,128]{1,0:T(8,128)(2,1)S(1)} collective-permute-done((bf16[256,128]{1,0:T(8,128)(2,1)S(1)}, bf16[256,128]{1,0:T(8,128)(2,1)S(1)}, u32[]{:S(2)}, u32[]{:S(2)}) %collective-permute-start.2) | collective-permute-done | bytes 65568 | tf_op jit(solution)/shard_map/ppermute | solution.py:43
  22.3 0.1 collective-permute-start.3
  22.4 0.2 fusion.9
  22.6 0.0 collective-permute-done.1
  22.8 0.6 %gather_fusion = bf16[4,128,256]{2,1,0:T(8,128)(2,1)S(1)} fusion(bf16[4,128,256]{2,1,0:T(8,128)(2,1)S(1)} %pad_maximum_fusion.1, s32[1024]{0:T(1024)S(1)} %pad_clamp_fusion), kind=kCustom, calls=%fused_computation | custom fusion | bytes 524304 | tf_op jit(solution)/shard_map/jit(_take)/gather | solution.py:71
  23.3 0.1 broadcast_select_fusion
  23.5 0.1 rev.11
  23.6 0.1 fusion.34
  23.7 0.0 copy-start
  23.7 0.0 collective-permute-done.3
  23.8 0.2 fusion.11
  24.0 0.0 copy-start.2
  24.0 0.6 %copy-done = f32[256,128]{1,0:T(8,128)S(1)} copy-done((f32[256,128]{1,0:T(8,128)S(1)}, f32[256,128]{1,0:T(8,128)}, u32[]{:S(2)}) %copy-start) | copy-done | bytes 131096
  24.6 0.0 copy-done.2
  24.6 0.5 multiply_reduce_fusion.1
  25.1 0.2 convolution_convert_fusion
  25.3 1.6 %collective-permute-start.6 = (f32[256,128]{1,0:T(8,128)S(1)}, f32[256,128]{1,0:T(8,128)S(1)}, u32[]{:S(2)}, u32[]{:S(2)}) collective-permute-start(f32[256,128]{1,0:T(8,128)S(1)} %get-tuple-element.21), channel_id=1, source_target_pairs={{0,2},{1,3},{2,0},{3,1},{4,6},{5,7},{6,4},{7,5},{8,10},{9,11},{10,... | collective-permute-start | bytes 393224 | tf_op jit(solution)/shard_map/ppermute | solution.py:43
  26.9 0.7 %broadcast_in_dim.58 = bf16[8,67,128]{2,1,0:T(8,128)(2,1)} broadcast(bf16[67,128]{1,0:T(8,128)(2,1)S(1)} %pad_maximum_fusion.7), dimensions={1,2} | broadcast | bytes 154368 | tf_op jit(solution)/shard_map/broadcast_in_dim | solution.py:11
  27.6 3.9 %all-to-all-start.1 = ((bf16[8,67,128]{2,1,0:T(8,128)(2,1)}), bf16[8,67,128]{2,1,0:T(8,128)(2,1)S(1)}, u32[]{:S(2)}, u32[]{:S(2)}) async-start(bf16[8,67,128]{2,1,0:T(8,128)(2,1)} %broadcast_in_dim.58), calls=%async_computation.1 | async-start | bytes 294912 | tf_op jit(solution)/shard_map/all_to_all | solution.py:15
  31.5 0.0 collective-permute-done.6
  31.5 0.1 collective-permute-start.7
  31.6 7.5 %all-to-all-done.1 = bf16[8,67,128]{2,1,0:T(8,128)(2,1)S(1)} async-done(((bf16[8,67,128]{2,1,0:T(8,128)(2,1)}), bf16[8,67,128]{2,1,0:T(8,128)(2,1)S(1)}, u32[]{:S(2)}, u32[]{:S(2)}) %all-to-all-start.1) | async-done | bytes 137248 | tf_op jit(solution)/shard_map/all_to_all | solution.py:15
  39.2 0.6 %collective-permute-start.4 = (bf16[259,128]{1,0:T(8,128)(2,1)S(1)}, bf16[259,128]{1,0:T(8,128)(2,1)S(1)}, u32[]{:S(2)}, u32[]{:S(2)}) collective-permute-start(bf16[259,128]{1,0:T(8,128)(2,1)S(1)} %pad_maximum_fusion.5), channel_id=1, source_target_pairs={{0,2},{1,3},{2,0},{3,1},{4,6},{5,7},{6,4},{7,5},{8,10},{9,11},{10,... | collective-permute-start | bytes 198920 | tf_op jit(solution)/shard_map/ppermute | solution.py:43
  39.8 0.2 fusion.13
  40.0 3.6 %collective-permute-done.4 = bf16[259,128]{1,0:T(8,128)(2,1)S(1)} collective-permute-done((bf16[259,128]{1,0:T(8,128)(2,1)S(1)}, bf16[259,128]{1,0:T(8,128)(2,1)S(1)}, u32[]{:S(2)}, u32[]{:S(2)}) %collective-permute-start.4) | collective-permute-done | bytes 66336 | tf_op jit(solution)/shard_map/ppermute | solution.py:43
  43.6 0.5 concatenate.34
  44.1 0.1 collective-permute-start.5
  44.2 0.2 fusion.21
  44.4 1.1 %collective-permute-done.5 = bf16[518,128]{1,0:T(8,128)(2,1)S(1)} collective-permute-done((bf16[518,128]{1,0:T(8,128)(2,1)S(1)}, bf16[518,128]{1,0:T(8,128)(2,1)S(1)}, u32[]{:S(2)}, u32[]{:S(2)}) %collective-permute-start.5) | collective-permute-done | bytes 132640 | tf_op jit(solution)/shard_map/ppermute | solution.py:43
  45.5 0.0 collective-permute-done.7
  45.5 0.2 fusion.23
  45.7 0.5 multiply_reduce_fusion
  46.2 9.1 %all_to_all.15 = f32[8,1,128]{2,1,0:T(1,128)S(1)} all-to-all(f32[8,1,128]{2,1,0:T(1,128)S(1)} %broadcast_in_dim.59), channel_id=1, replica_groups=mesh['grid'=8,'band'=4] {'grid'}, dimensions={0} | all-to-all | bytes 8192 | tf_op jit(solution)/shard_map/all_to_all | solution.py:15
  55.3 0.7 %broadcast_multiply_fusion = f32[256,128]{1,0:T(8,128)} fusion(f32[256,128]{1,0:T(8,128)S(1)} %get-tuple-element.23, f32[128]{0:T(128)S(1)} %add_rsqrt_fusion), kind=kLoop, calls=%fused_computation.80 | loop fusion | flops 32768 | bytes 262656 | tf_op jit(solution)/shard_map/mul | solution.py:125
  (48 shorter events, 0.6 us)
Async XLA Ops:
  0.7 0.9 %copy-start.3 = (s32[64]{0:T(128)S(1)}, s32[64]{0:T(128)}, u32[]{:S(2)}) copy-start(s32[64]{0:T(128)} %param.7) | copy-start | bytes 772
  1.6 0.8 %copy-start.1 = (bf16[128,256]{1,0:T(8,128)(2,1)S(1)}, bf16[128,256]{1,0:T(8,128)(2,1)}, u32[]{:S(2)}) copy-start(bf16[128,256]{1,0:T(8,128)(2,1)} %param.6) | copy-start | bytes 196612
  3.2 14.7 %all-to-all-start = ((bf16[8,65,128]{2,1,0:T(8,128)(2,1)}), bf16[8,65,128]{2,1,0:T(8,128)(2,1)S(1)}, u32[]{:S(2)}, u32[]{:S(2)}) async-start(bf16[8,65,128]{2,1,0:T(8,128)(2,1)} %broadcast_in_dim.31), calls=%async_computation | async-start | bytes 294912 | tf_op jit(solution)/shard_map/all_to_all | solution.py:15
  10.5 5.0 %collective-permute-start = (bf16[512,128]{1,0:T(8,128)(2,1)S(1)}, bf16[512,128]{1,0:T(8,128)(2,1)S(1)}, u32[]{:S(2)}, u32[]{:S(2)}) collective-permute-start(bf16[512,128]{1,0:T(8,128)(2,1)S(1)} %pad_maximum_fusion.3), channel_id=1, source_target_pairs={{0,2},{1,3},{2,0},{3,1},{4,6},{5,7},{6,4},{7,5},{8,10},{9,11},{10,... | collective-permute-start | bytes 393224 | tf_op jit(solution)/shard_map/ppermute | solution.py:43
  15.5 7.1 %collective-permute-start.1 = (bf16[1024,128]{1,0:T(8,128)(2,1)S(1)}, bf16[1024,128]{1,0:T(8,128)(2,1)S(1)}, u32[]{:S(2)}, u32[]{:S(2)}) collective-permute-start(bf16[1024,128]{1,0:T(8,128)(2,1)S(1)} %pad_maximum_fusion), channel_id=1, source_target_pairs={{0,1},{1,0},{2,3},{3,2},{4,5},{5,4},{6,7},{7,6},{8,9},{9,8},{10,11... | collective-permute-start | bytes 786440 | tf_op jit(solution)/shard_map/ppermute | solution.py:43
  18.0 4.3 %collective-permute-start.2 = (bf16[256,128]{1,0:T(8,128)(2,1)S(1)}, bf16[256,128]{1,0:T(8,128)(2,1)S(1)}, u32[]{:S(2)}, u32[]{:S(2)}) collective-permute-start(bf16[256,128]{1,0:T(8,128)(2,1)S(1)} %bitcast.74), channel_id=1, source_target_pairs={{0,2},{1,3},{2,0},{3,1},{4,6},{5,7},{6,4},{7,5},{8,10},{9,11},{10,... | collective-permute-start | bytes 196616 | tf_op jit(solution)/shard_map/ppermute | solution.py:43
  22.3 1.4 %collective-permute-start.3 = (bf16[512,128]{1,0:T(8,128)(2,1)S(1)}, bf16[512,128]{1,0:T(8,128)(2,1)S(1)}, u32[]{:S(2)}, u32[]{:S(2)}) collective-permute-start(bf16[512,128]{1,0:T(8,128)(2,1)S(1)} %pad_maximum_fusion.4), channel_id=1, source_target_pairs={{0,1},{1,0},{2,3},{3,2},{4,5},{5,4},{6,7},{7,6},{8,9},{9,8},{10,11... | collective-permute-start | bytes 393224 | tf_op jit(solution)/shard_map/ppermute | solution.py:43
  23.7 0.9 %copy-start = (f32[256,128]{1,0:T(8,128)S(1)}, f32[256,128]{1,0:T(8,128)}, u32[]{:S(2)}) copy-start(f32[256,128]{1,0:T(8,128)} %param.4) | copy-start | bytes 393220
  24.0 0.7 %copy-start.2 = (f32[256]{0:T(256)S(1)}, f32[256]{0:T(256)}, u32[]{:S(2)}) copy-start(f32[256]{0:T(256)} %param.5) | copy-start | bytes 3076
  25.3 6.1 %collective-permute-start.6 = (f32[256,128]{1,0:T(8,128)S(1)}, f32[256,128]{1,0:T(8,128)S(1)}, u32[]{:S(2)}, u32[]{:S(2)}) collective-permute-start(f32[256,128]{1,0:T(8,128)S(1)} %get-tuple-element.21), channel_id=1, source_target_pairs={{0,2},{1,3},{2,0},{3,1},{4,6},{5,7},{6,4},{7,5},{8,10},{9,11},{10,... | collective-permute-start | bytes 393224 | tf_op jit(solution)/shard_map/ppermute | solution.py:43
  27.6 11.5 %all-to-all-start.1 = ((bf16[8,67,128]{2,1,0:T(8,128)(2,1)}), bf16[8,67,128]{2,1,0:T(8,128)(2,1)S(1)}, u32[]{:S(2)}, u32[]{:S(2)}) async-start(bf16[8,67,128]{2,1,0:T(8,128)(2,1)} %broadcast_in_dim.58), calls=%async_computation.1 | async-start | bytes 294912 | tf_op jit(solution)/shard_map/all_to_all | solution.py:15
  31.5 14.0 %collective-permute-start.7 = (f32[512,128]{1,0:T(8,128)S(1)}, f32[512,128]{1,0:T(8,128)S(1)}, u32[]{:S(2)}, u32[]{:S(2)}) collective-permute-start(f32[512,128]{1,0:T(8,128)S(1)} %pad_maximum_fusion.2), channel_id=1, source_target_pairs={{0,1},{1,0},{2,3},{3,2},{4,5},{5,4},{6,7},{7,6},{8,9},{9,8},{10,11... | collective-permute-start | bytes 786440 | tf_op jit(solution)/shard_map/ppermute | solution.py:43
  39.2 4.4 %collective-permute-start.4 = (bf16[259,128]{1,0:T(8,128)(2,1)S(1)}, bf16[259,128]{1,0:T(8,128)(2,1)S(1)}, u32[]{:S(2)}, u32[]{:S(2)}) collective-permute-start(bf16[259,128]{1,0:T(8,128)(2,1)S(1)} %pad_maximum_fusion.5), channel_id=1, source_target_pairs={{0,2},{1,3},{2,0},{3,1},{4,6},{5,7},{6,4},{7,5},{8,10},{9,11},{10,... | collective-permute-start | bytes 198920 | tf_op jit(solution)/shard_map/ppermute | solution.py:43
  44.1 1.4 %collective-permute-start.5 = (bf16[518,128]{1,0:T(8,128)(2,1)S(1)}, bf16[518,128]{1,0:T(8,128)(2,1)S(1)}, u32[]{:S(2)}, u32[]{:S(2)}) collective-permute-start(bf16[518,128]{1,0:T(8,128)(2,1)S(1)} %concatenate.34), channel_id=1, source_target_pairs={{0,1},{1,0},{2,3},{3,2},{4,5},{5,4},{6,7},{7,6},{8,9},{9,8},{10,11... | collective-permute-start | bytes 397832 | tf_op jit(solution)/shard_map/ppermute | solution.py:43

commit v17 on v14

--- a/solution.py
+++ b/solution.py
@@ -47,12 +47,41 @@
     return [held[k] for k in range(nbands)]
 
 
+def tree_gather(slots, extra, merge_first, merge_extra):
+    ngroups = lax.axis_size("grid")
+    g = lax.axis_index("grid")
+    nslots = slots.shape[0]
+    got = lax.ppermute(jnp.concatenate([slots, extra], 0), "grid", [(i, i ^ 1) for i in range(ngroups)])
+    lower = (g & 1) == 1
+    first = jnp.where(lower, got[:nslots], slots)
+    second = jnp.where(lower, slots, got[:nslots])
+    cur = first + jnp.flip(second, axis=0)
+    extra = merge_first(extra, got[nslots:], lower)
+    step = 2
+    while step < ngroups:
+        got = lax.ppermute(jnp.concatenate([cur, extra], 0), "grid", [(i, i ^ step) for i in range(ngroups)])
+        lower = (g & step) != 0
+        n = cur.shape[0]
+        cur = jnp.where(lower, jnp.concatenate([got[:n], cur], 0), jnp.concatenate([cur, got[:n]], 0))
+        extra = merge_extra(extra, got[n:], lower)
+        step *= 2
+    return cur, extra
+
+
+def pick_first(own, got, lower):
+    return jnp.where(lower, got, own)
+
+
+def in_order(own, got, lower):
+    return jnp.where(lower, jnp.concatenate([got, own], 0), jnp.concatenate([own, got], 0))
+
+
 def body(orbitals, potential, fitted, points):
     ngroups = lax.axis_size("grid")
     nbands = lax.axis_size("band")
     nslots = points.shape[0]
     block_width = orbitals.shape[1]
-    if ngroups > 8 or ngroups % 2 or nbands & (nbands - 1) or nslots > block_width:
+    if ngroups > 8 or ngroups & (ngroups - 1) or nbands & (nbands - 1) or nslots > block_width:
         return body_spread(orbitals, potential, fitted, points)
     rows = orbitals.shape[0]
     band = lax.axis_index("band")
@@ -63,15 +92,15 @@
     selected = jnp.dot(picks, rows_b16, preferred_element_type=jnp.float32).astype(jnp.bfloat16)
     filled = jnp.pad(valid_mask.astype(jnp.bfloat16), (0, block_width - nslots))
     to_band = jnp.concatenate([rows_b16, fitted.reshape(-1, block_width)], 0)
-    sent, to_band = lax.optimization_barrier((grid_copies(jnp.concatenate([selected, filled[None]], 0)), to_band))
-    got = grid_exchange(sent).reshape(ngroups, nslots + 1, block_width)
+    sel, mask_row, to_band = lax.optimization_barrier((selected, filled[None], to_band))
+    merged, first_rows = tree_gather(sel, mask_row, pick_first, in_order)
     swapped = band_hops(to_band)
     rows_b = jnp.concatenate([part[:rows] for part in swapped], 1)
     fitted_got = jnp.stack([part[rows:].reshape(fitted.shape) for part in swapped], 0)
     fitted_all = jnp.take(fitted_got, jnp.arange(nbands, dtype=jnp.int32) ^ band, axis=0)
     fitted_all = fitted_all.reshape(ngroups // 2, 2, nslots, fitted.shape[1])
-    coll = jnp.concatenate(band_swap(pair_up(got[:, :nslots])), 1)
-    first_filled = got[:, nslots, :nslots].reshape(ngroups // 2, 2, nslots)[:, 0] > 0
+    coll = jnp.concatenate(band_hops(merged), 1)
+    first_filled = first_rows[:, :nslots] > 0
     fitted_all = jnp.where(
         first_filled[:, :, None], fitted_all[:, 0], jnp.flip(fitted_all[:, 1], axis=1)
     ).reshape(-1, fitted.shape[1]).astype(jnp.float32)

time: 54.7 us -> 55.7 us (1.018)
  waiting for transfers between devices: 14.9 us -> 10.8 us
  blocking collectives: 19.4 us -> 23.3 us
  starting transfers between devices: 12.3 us -> 13.4 us
  other arithmetic: 2.12 us -> 2.84 us
  local copies, waits for them, and re-layouts: 2.98 us -> 2.31 us
    all_to_all x1 -> x0, waiting for transfers between devices: 7.2 us -> none  [grid_exchange(): got = lax.all_to_all(sent, 'grid', 0, 0, tiled=True)]
    ppermute x3, starting transfers between devices: 1.99 us -> 8.27 us  [the longest x2 5.24 us: tree_gather(): lax.ppermute(jnp.concatenate([cur, extra], 0), 'grid', [(i, i ^ step) for...]
    all_to_all x1 -> x0, starting transfers between devices: 5.83 us -> none  [grid_exchange(): got = lax.all_to_all(sent, 'grid', 0, 0, tiled=True)]
    all_to_all x2, blocking collectives: 19.4 us -> 23.3 us  [grid_exchange(): got = lax.all_to_all(sent, 'grid', 0, 0, tiled=True)]
    ppermute x4 -> x6, waiting for transfers between devices: 4.82 us -> 6.94 us  [band_hops(): lax.ppermute(jnp.concatenate([held[k] for k in keys], 0), 'band', [(i, i...]
    ppermute x3, waiting for transfers between devices: 2.84 us -> 3.84 us  [the longest x2 3.59 us: tree_gather(): lax.ppermute(jnp.concatenate([cur, extra], 0), 'grid', [(i, i ^ step) for...]
    ppermute x4 -> x6, starting transfers between devices: 4.43 us -> 5.15 us  [band_hops(): lax.ppermute(jnp.concatenate([held[k] for k in keys], 0), 'band', [(i, i...]
    broadcast_in_dim x3 -> x2, local copies, waits for them, and re-layouts: 0.7 us -> 0.03 us  [grid_copies(): return jnp.broadcast_to(x[None], (ngroups,) + x.shape)]
  transfers between devices with their start and end apart: 8 -> 9, of which waited for: 4 -> 7; matrix products, arithmetic and copies ran while one was open for 4% -> 3% of each run, Pallas kernels for 0% -> 0%
where the time goes in v17:
time: 55.7 us; the launch traced here: 55.5 us
  blocking collectives  23.3 us (42%)
  starting transfers between devices  13.4 us (24%)
  waiting for transfers between devices  10.8 us (19%)
  other arithmetic  2.84 us (5%)
  matrix products  2.42 us (4%)
  local copies, waits for them, and re-layouts  2.31 us (4%)
    all_to_all x2, blocking collectives, grid_exchange(): got = lax.all_to_all(sent, 'grid', 0, 0, tiled=True)  23.3 us
    ppermute x6, waiting for transfers between devices, band_hops(): lax.ppermute(jnp.concatenate([held[k] for k in keys], 0), 'band', [(i, i...  6.94 us
    ppermute x2, starting transfers between devices, tree_gather(): lax.ppermute(jnp.concatenate([cur, extra], 0), 'grid', [(i, i ^ step) for...  5.24 us
    ppermute x6, starting transfers between devices, band_hops(): lax.ppermute(jnp.concatenate([held[k] for k in keys], 0), 'band', [(i, i...  5.15 us
    ppermute x2, waiting for transfers between devices, tree_gather(): lax.ppermute(jnp.concatenate([cur, extra], 0), 'grid', [(i, i ^ step) for...  3.59 us
    ppermute x1, starting transfers between devices, tree_gather(): lax.ppermute(jnp.concatenate([slots, extra], 0), 'grid', [(i, i ^ 1) for...  3.03 us
    unnamed x8, local copies, waits for them, and re-layouts  1.34 us
    dot_general x6, matrix products, body(): lax.dot_general(coll[:, k * block_width:(k + 1) * block_width], rows_b[:,...  1.12 us
  transfers between devices with their start and end apart: 9, of which 7 were waited for; matrix products, arithmetic and copies ran while one was open for 3% of the time, Pallas kernels for 0%

profile of v17, /device:TPU:0, one launch (start us, length us, event | category | flops | bytes accessed | tf_op | source)
XLA Modules:
  0.0 55.5 jit_solution(9301085336450021830)
XLA Ops:
  0.0 0.7 %broadcast_compare_fusion = pred[64]{0:T(512)(128)(4,1)S(1)} fusion(s32[64]{0:T(128)} %param.7), kind=kLoop, calls=%fused_computation.111 | loop fusion | flops 64 | bytes 320 | tf_op jit(solution)/shard_map/ge | solution.py:89
  0.7 0.0 copy-start.3
  0.7 0.9 %convert_element_type.86 = bf16[256,128]{1,0:T(8,128)(2,1)S(1)} convert(f32[256,128]{1,0:T(8,128)} %param.4) | non-fusion elementwise | flops 32768 | bytes 196608 | tf_op jit(solution)/shard_map/convert_element_type | solution.py:91
  1.6 0.0 copy-done.3
  1.6 0.0 copy-start.1
  1.6 0.2 convolution_convert_fusion.1
  1.8 0.6 %copy-done.1 = bf16[128,256]{1,0:T(8,128)(2,1)S(1)} copy-done((bf16[128,256]{1,0:T(8,128)(2,1)S(1)}, bf16[128,256]{1,0:T(8,128)(2,1)}, u32[]{:S(2)}) %copy-start.1) | copy-done | bytes 65560
  2.5 3.0 %collective-permute-start = (bf16[65,128]{1,0:T(8,128)(2,1)S(1)}, bf16[65,128]{1,0:T(8,128)(2,1)S(1)}, u32[]{:S(2)}, u32[]{:S(2)}) collective-permute-start(bf16[65,128]{1,0:T(8,128)(2,1)S(1)} %pad_maximum_fusion.7), channel_id=1, source_target_pairs={{0,4},{4,0},{8,12},{12,8},{16,20},{20,16},{24,28},{28,24},{1,5},{5... | collective-permute-start | bytes 49928 | tf_op jit(solution)/shard_map/ppermute | solution.py:54
  5.5 1.5 %collective-permute-start.3 = (bf16[512,128]{1,0:T(8,128)(2,1)S(1)}, bf16[512,128]{1,0:T(8,128)(2,1)S(1)}, u32[]{:S(2)}, u32[]{:S(2)}) collective-permute-start(bf16[512,128]{1,0:T(8,128)(2,1)S(1)} %pad_maximum_fusion.3), channel_id=1, source_target_pairs={{0,2},{1,3},{2,0},{3,1},{4,6},{5,7},{6,4},{7,5},{8,10},{9,11},{10,... | collective-permute-start | bytes 393224 | tf_op jit(solution)/shard_map/ppermute | solution.py:43
  7.0 0.2 collective-permute-done
  7.4 2.1 %collective-permute-start.1 = (bf16[65,128]{1,0:T(8,128)(2,1)S(1)}, bf16[65,128]{1,0:T(8,128)(2,1)S(1)}, u32[]{:S(2)}, u32[]{:S(2)}) collective-permute-start(bf16[65,128]{1,0:T(8,128)(2,1)S(1)} %pad_maximum_fusion.8), channel_id=1, source_target_pairs={{0,8},{4,12},{8,0},{12,4},{16,24},{20,28},{24,16},{28,20},{1,9},{5... | collective-permute-start | bytes 49928 | tf_op jit(solution)/shard_map/ppermute | solution.py:62
  9.5 1.7 %collective-permute-done.1 = bf16[65,128]{1,0:T(8,128)(2,1)S(1)} collective-permute-done((bf16[65,128]{1,0:T(8,128)(2,1)S(1)}, bf16[65,128]{1,0:T(8,128)(2,1)S(1)}, u32[]{:S(2)}, u32[]{:S(2)}) %collective-permute-start.1) | collective-permute-done | bytes 16672 | tf_op jit(solution)/shard_map/ppermute | solution.py:62
  11.3 3.1 %collective-permute-start.2 = (bf16[130,128]{1,0:T(8,128)(2,1)S(1)}, bf16[130,128]{1,0:T(8,128)(2,1)S(1)}, u32[]{:S(2)}, u32[]{:S(2)}) collective-permute-start(bf16[130,128]{1,0:T(8,128)(2,1)S(1)} %pad_maximum_fusion.6), channel_id=1, source_target_pairs={{0,16},{4,20},{8,24},{12,28},{16,0},{20,4},{24,8},{28,12},{1,17},{... | collective-permute-start | bytes 99848 | tf_op jit(solution)/shard_map/ppermute | solution.py:62
  14.5 1.9 %collective-permute-done.2 = bf16[130,128]{1,0:T(8,128)(2,1)S(1)} collective-permute-done((bf16[130,128]{1,0:T(8,128)(2,1)S(1)}, bf16[130,128]{1,0:T(8,128)(2,1)S(1)}, u32[]{:S(2)}, u32[]{:S(2)}) %collective-permute-start.2) | collective-permute-done | bytes 33312 | tf_op jit(solution)/shard_map/ppermute | solution.py:62
  16.4 1.9 %collective-permute-start.5 = (bf16[256,128]{1,0:T(8,128)(2,1)S(1)}, bf16[256,128]{1,0:T(8,128)(2,1)S(1)}, u32[]{:S(2)}, u32[]{:S(2)}) collective-permute-start(bf16[256,128]{1,0:T(8,128)(2,1)S(1)} %maximum_select_fusion), channel_id=1, source_target_pairs={{0,2},{1,3},{2,0},{3,1},{4,6},{5,7},{6,4},{7,5},{8,10},{9,11},{10,... | collective-permute-start | bytes 196616 | tf_op jit(solution)/shard_map/ppermute | solution.py:43
  18.3 0.0 collective-permute-done.3
  18.3 0.1 collective-permute-start.4
  18.4 2.3 %collective-permute-done.5 = bf16[256,128]{1,0:T(8,128)(2,1)S(1)} collective-permute-done((bf16[256,128]{1,0:T(8,128)(2,1)S(1)}, bf16[256,128]{1,0:T(8,128)(2,1)S(1)}, u32[]{:S(2)}, u32[]{:S(2)}) %collective-permute-start.5) | collective-permute-done | bytes 65568 | tf_op jit(solution)/shard_map/ppermute | solution.py:43
  20.7 0.1 collective-permute-start.6
  20.8 0.2 fusion.9
  21.0 0.0 collective-permute-done.4
  21.1 0.6 %gather_fusion = bf16[4,128,256]{2,1,0:T(8,128)(2,1)S(1)} fusion(bf16[4,128,256]{2,1,0:T(8,128)(2,1)S(1)} %pad_maximum_fusion.1, s32[1024]{0:T(1024)S(1)} %pad_clamp_fusion), kind=kCustom, calls=%fused_computation | custom fusion | bytes 524304 | tf_op jit(solution)/shard_map/jit(_take)/gather | solution.py:100
  21.7 0.1 broadcast_select_fusion
  21.8 0.1 rev.13
  22.0 0.1 fusion.32
  22.1 0.1 collective-permute-done.6
  22.1 0.2 fusion.7
  22.3 0.0 copy-start
  22.3 0.2 fusion.11
  22.5 0.0 copy-start.2
  22.5 0.7 %copy-done = f32[256,128]{1,0:T(8,128)S(1)} copy-done((f32[256,128]{1,0:T(8,128)S(1)}, f32[256,128]{1,0:T(8,128)}, u32[]{:S(2)}) %copy-start) | copy-done | bytes 131096
  23.2 0.0 copy-done.2
  23.2 0.5 multiply_reduce_fusion.1
  23.7 0.2 convolution_convert_fusion
  23.9 14.1 %all_to_all.10 = bf16[8,67,128]{2,1,0:T(8,128)(2,1)S(1)} all-to-all(bf16[8,67,128]{2,1,0:T(8,128)(2,1)S(1)} %broadcast_in_dim.47), channel_id=1, replica_groups=mesh['grid'=8,'band'=4] {'grid'}, dimensions={0} | all-to-all | bytes 274432 | tf_op jit(solution)/shard_map/all_to_all | solution.py:15
  38.2 1.6 %collective-permute-start.7 = (bf16[512,128]{1,0:T(8,128)(2,1)S(1)}, bf16[512,128]{1,0:T(8,128)(2,1)S(1)}, u32[]{:S(2)}, u32[]{:S(2)}) collective-permute-start(bf16[512,128]{1,0:T(8,128)(2,1)S(1)} %pad_maximum_fusion.5), channel_id=1, source_target_pairs={{0,2},{1,3},{2,0},{3,1},{4,6},{5,7},{6,4},{7,5},{8,10},{9,11},{10,... | collective-permute-start | bytes 393224 | tf_op jit(solution)/shard_map/ppermute | solution.py:43
  39.8 3.5 %collective-permute-done.7 = bf16[512,128]{1,0:T(8,128)(2,1)S(1)} collective-permute-done((bf16[512,128]{1,0:T(8,128)(2,1)S(1)}, bf16[512,128]{1,0:T(8,128)(2,1)S(1)}, u32[]{:S(2)}, u32[]{:S(2)}) %collective-permute-start.7) | collective-permute-done | bytes 131104 | tf_op jit(solution)/shard_map/ppermute | solution.py:43
  43.2 0.1 collective-permute-start.8
  43.3 0.2 fusion.13
  43.5 0.2 fusion.21
  43.7 1.1 %collective-permute-done.8 = bf16[1024,128]{1,0:T(8,128)(2,1)S(1)} collective-permute-done((bf16[1024,128]{1,0:T(8,128)(2,1)S(1)}, bf16[1024,128]{1,0:T(8,128)(2,1)S(1)}, u32[]{:S(2)}, u32[]{:S(2)}) %collective-permute-start.8) | collective-permute-done | bytes 262176 | tf_op jit(solution)/shard_map/ppermute | solution.py:43
  44.8 0.2 fusion.23
  45.0 0.5 multiply_reduce_fusion
  45.5 9.2 %all_to_all.11 = f32[8,1,128]{2,1,0:T(1,128)S(1)} all-to-all(f32[8,1,128]{2,1,0:T(1,128)S(1)} %broadcast_in_dim.48), channel_id=1, replica_groups=mesh['grid'=8,'band'=4] {'grid'}, dimensions={0} | all-to-all | bytes 8192 | tf_op jit(solution)/shard_map/all_to_all | solution.py:15
  54.8 0.7 %broadcast_multiply_fusion = f32[256,128]{1,0:T(8,128)} fusion(f32[256,128]{1,0:T(8,128)S(1)} %get-tuple-element.19, f32[128]{0:T(128)S(1)} %add_rsqrt_fusion), kind=kLoop, calls=%fused_computation.76 | loop fusion | flops 32768 | bytes 262656 | tf_op jit(solution)/shard_map/mul | solution.py:144
  (49 shorter events, 0.7 us)
Async XLA Ops:
  0.7 0.9 %copy-start.3 = (s32[64]{0:T(128)S(1)}, s32[64]{0:T(128)}, u32[]{:S(2)}) copy-start(s32[64]{0:T(128)} %param.7) | copy-start | bytes 772
  1.6 0.8 %copy-start.1 = (bf16[128,256]{1,0:T(8,128)(2,1)S(1)}, bf16[128,256]{1,0:T(8,128)(2,1)}, u32[]{:S(2)}) copy-start(bf16[128,256]{1,0:T(8,128)(2,1)} %param.6) | copy-start | bytes 196612
  2.5 4.8 %collective-permute-start = (bf16[65,128]{1,0:T(8,128)(2,1)S(1)}, bf16[65,128]{1,0:T(8,128)(2,1)S(1)}, u32[]{:S(2)}, u32[]{:S(2)}) collective-permute-start(bf16[65,128]{1,0:T(8,128)(2,1)S(1)} %pad_maximum_fusion.7), channel_id=1, source_target_pairs={{0,4},{4,0},{8,12},{12,8},{16,20},{20,16},{24,28},{28,24},{1,5},{5... | collective-permute-start | bytes 49928 | tf_op jit(solution)/shard_map/ppermute | solution.py:54
  5.5 12.7 %collective-permute-start.3 = (bf16[512,128]{1,0:T(8,128)(2,1)S(1)}, bf16[512,128]{1,0:T(8,128)(2,1)S(1)}, u32[]{:S(2)}, u32[]{:S(2)}) collective-permute-start(bf16[512,128]{1,0:T(8,128)(2,1)S(1)} %pad_maximum_fusion.3), channel_id=1, source_target_pairs={{0,2},{1,3},{2,0},{3,1},{4,6},{5,7},{6,4},{7,5},{8,10},{9,11},{10,... | collective-permute-start | bytes 393224 | tf_op jit(solution)/shard_map/ppermute | solution.py:43
  7.4 3.9 %collective-permute-start.1 = (bf16[65,128]{1,0:T(8,128)(2,1)S(1)}, bf16[65,128]{1,0:T(8,128)(2,1)S(1)}, u32[]{:S(2)}, u32[]{:S(2)}) collective-permute-start(bf16[65,128]{1,0:T(8,128)(2,1)S(1)} %pad_maximum_fusion.8), channel_id=1, source_target_pairs={{0,8},{4,12},{8,0},{12,4},{16,24},{20,28},{24,16},{28,20},{1,9},{5... | collective-permute-start | bytes 49928 | tf_op jit(solution)/shard_map/ppermute | solution.py:62
  11.3 5.0 %collective-permute-start.2 = (bf16[130,128]{1,0:T(8,128)(2,1)S(1)}, bf16[130,128]{1,0:T(8,128)(2,1)S(1)}, u32[]{:S(2)}, u32[]{:S(2)}) collective-permute-start(bf16[130,128]{1,0:T(8,128)(2,1)S(1)} %pad_maximum_fusion.6), channel_id=1, source_target_pairs={{0,16},{4,20},{8,24},{12,28},{16,0},{20,4},{24,8},{28,12},{1,17},{... | collective-permute-start | bytes 99848 | tf_op jit(solution)/shard_map/ppermute | solution.py:62
  16.4 4.3 %collective-permute-start.5 = (bf16[256,128]{1,0:T(8,128)(2,1)S(1)}, bf16[256,128]{1,0:T(8,128)(2,1)S(1)}, u32[]{:S(2)}, u32[]{:S(2)}) collective-permute-start(bf16[256,128]{1,0:T(8,128)(2,1)S(1)} %maximum_select_fusion), channel_id=1, source_target_pairs={{0,2},{1,3},{2,0},{3,1},{4,6},{5,7},{6,4},{7,5},{8,10},{9,11},{10,... | collective-permute-start | bytes 196616 | tf_op jit(solution)/shard_map/ppermute | solution.py:43
  18.3 2.6 %collective-permute-start.4 = (bf16[1024,128]{1,0:T(8,128)(2,1)S(1)}, bf16[1024,128]{1,0:T(8,128)(2,1)S(1)}, u32[]{:S(2)}, u32[]{:S(2)}) collective-permute-start(bf16[1024,128]{1,0:T(8,128)(2,1)S(1)} %pad_maximum_fusion), channel_id=1, source_target_pairs={{0,1},{1,0},{2,3},{3,2},{4,5},{5,4},{6,7},{7,6},{8,9},{9,8},{10,11... | collective-permute-start | bytes 786440 | tf_op jit(solution)/shard_map/ppermute | solution.py:43
  20.7 1.4 %collective-permute-start.6 = (bf16[512,128]{1,0:T(8,128)(2,1)S(1)}, bf16[512,128]{1,0:T(8,128)(2,1)S(1)}, u32[]{:S(2)}, u32[]{:S(2)}) collective-permute-start(bf16[512,128]{1,0:T(8,128)(2,1)S(1)} %pad_maximum_fusion.4), channel_id=1, source_target_pairs={{0,1},{1,0},{2,3},{3,2},{4,5},{5,4},{6,7},{7,6},{8,9},{9,8},{10,11... | collective-permute-start | bytes 393224 | tf_op jit(solution)/shard_map/ppermute | solution.py:43
  22.3 0.9 %copy-start = (f32[256,128]{1,0:T(8,128)S(1)}, f32[256,128]{1,0:T(8,128)}, u32[]{:S(2)}) copy-start(f32[256,128]{1,0:T(8,128)} %param.4) | copy-start | bytes 393220
  22.5 0.7 %copy-start.2 = (f32[256]{0:T(256)S(1)}, f32[256]{0:T(256)}, u32[]{:S(2)}) copy-start(f32[256]{0:T(256)} %param.5) | copy-start | bytes 3076
  38.2 5.0 %collective-permute-start.7 = (bf16[512,128]{1,0:T(8,128)(2,1)S(1)}, bf16[512,128]{1,0:T(8,128)(2,1)S(1)}, u32[]{:S(2)}, u32[]{:S(2)}) collective-permute-start(bf16[512,128]{1,0:T(8,128)(2,1)S(1)} %pad_maximum_fusion.5), channel_id=1, source_target_pairs={{0,2},{1,3},{2,0},{3,1},{4,6},{5,7},{6,4},{7,5},{8,10},{9,11},{10,... | collective-permute-start | bytes 393224 | tf_op jit(solution)/shard_map/ppermute | solution.py:43
  43.2 1.6 %collective-permute-start.8 = (bf16[1024,128]{1,0:T(8,128)(2,1)S(1)}, bf16[1024,128]{1,0:T(8,128)(2,1)S(1)}, u32[]{:S(2)}, u32[]{:S(2)}) collective-permute-start(bf16[1024,128]{1,0:T(8,128)(2,1)S(1)} %pad_maximum_fusion.2), channel_id=1, source_target_pairs={{0,1},{1,0},{2,3},{3,2},{4,5},{5,4},{6,7},{7,6},{8,9},{9,8},{10,11... | collective-permute-start | bytes 786440 | tf_op jit(solution)/shard_map/ppermute | solution.py:43

commit v18 on v13

--- a/solution.py
+++ b/solution.py
@@ -65,6 +65,8 @@
     to_band = jnp.concatenate([rows_b16, fitted.reshape(-1, block_width)], 0)
     sent, to_band = lax.optimization_barrier((grid_copies(jnp.concatenate([selected, filled[None]], 0)), to_band))
     got = grid_exchange(sent).reshape(ngroups, nslots + 1, block_width)
+    pot = potential[:, None]
+    got, first_pot_psi = lax.optimization_barrier((got, pot * orbitals))
     swapped = band_hops(to_band)
     rows_b = jnp.concatenate([part[:rows] for part in swapped], 1)
     fitted_got = jnp.stack([part[rows:].reshape(fitted.shape) for part in swapped], 0)
@@ -76,7 +78,6 @@
         first_filled[:, :, None], fitted_all[:, 0], jnp.flip(fitted_all[:, 1], axis=1)
     ).reshape(-1, fitted.shape[1]).astype(jnp.float32)
     psi = orbitals
-    pot = potential[:, None]
     for step in range(ITERS):
         if step:
             at_slots = jnp.dot(picks, psi, preferred_element_type=jnp.float32).astype(jnp.bfloat16)
@@ -109,7 +110,8 @@
         applied = lax.dot_general(
             tile_blocks, coll[:, :block_width], (((0,), (0,)), ((), ())), preferred_element_type=jnp.float32
         )
-        psi = psi - 0.25 * (pot * psi - applied)
+        pot_psi = first_pot_psi if step == 0 else pot * psi
+        psi = psi - 0.25 * (pot_psi - applied)
         sq = jnp.sum(psi * psi, axis=0)
     total = jnp.sum(grid_gather(sq[None]), axis=0)
     return psi * lax.rsqrt(total / (rows * ngroups) + 1e-06)

time: 54.8 us -> 54.2 us (0.989)
  other arithmetic: 2.12 us -> 1.27 us
    convert_element_type x1 -> x0, other arithmetic: 0.94 us -> none  [body(): rows_b16 = orbitals.astype(jnp.bfloat16)]
    reshape x1, local copies, waits for them, and re-layouts: 0.03 us -> 0.9 us  [body(): to_band = jnp.concatenate([rows_b16, fitted.reshape(-1, block_width)], 0)]
    unnamed x10 -> x7, local copies, waits for them, and re-layouts: 1.32 us -> 0.68 us
  transfers between devices with their start and end apart: 7 -> 7, of which waited for: 4 -> 5; matrix products, arithmetic and copies ran while one was open for 4% -> 4% of each run, Pallas kernels for 0% -> 0%
where the time goes in v18:
time: 54.2 us; the launch traced here: 53.9 us
  blocking collectives  20 us (37%)
  waiting for transfers between devices  16.3 us (30%)
  starting transfers between devices  10.2 us (19%)
  local copies, waits for them, and re-layouts  3.23 us (6%)
  matrix products  2.42 us (4%)
  other arithmetic  1.27 us (2%)
    all_to_all x2, blocking collectives, grid_exchange(): got = lax.all_to_all(sent, 'grid', 0, 0, tiled=True)  20 us
    ppermute x6, waiting for transfers between devices, band_hops(): lax.ppermute(jnp.concatenate([held[k] for k in keys], 0), 'band', [(i, i...  9.12 us
    all_to_all x1, waiting for transfers between devices, grid_exchange(): got = lax.all_to_all(sent, 'grid', 0, 0, tiled=True)  7.2 us
    all_to_all x1, starting transfers between devices, grid_exchange(): got = lax.all_to_all(sent, 'grid', 0, 0, tiled=True)  5.83 us
    ppermute x6, starting transfers between devices, band_hops(): lax.ppermute(jnp.concatenate([held[k] for k in keys], 0), 'band', [(i, i...  4.35 us
    dot_general x6, matrix products, body(): lax.dot_general(coll[:, k * block_width:(k + 1) * block_width], rows_b[:,...  1.11 us
  transfers between devices with their start and end apart: 7, of which 5 were waited for; matrix products, arithmetic and copies ran while one was open for 4% of the time, Pallas kernels for 0%

profile of v18, /device:TPU:0, one launch (start us, length us, event | category | flops | bytes accessed | tf_op | source)
XLA Modules:
  0.0 53.9 jit_solution(3888882936275514853)
XLA Ops:
  0.0 0.0 copy-start.2
  0.0 0.0 copy-start
  0.0 0.9 %reshape.100 = bf16[256,128]{1,0:T(8,128)(2,1)S(1)} reshape(bf16[128,256]{1,0:T(8,128)(2,1)} %param.6) | data formatting | bytes 131072 | tf_op jit(solution)/shard_map/reshape | solution.py:65
  0.9 0.0 copy-done.2
  0.9 0.0 copy-start.1
  0.9 0.0 copy-done
  1.0 0.7 %copy-done.1 = f32[256]{0:T(256)S(1)} copy-done((f32[256]{0:T(256)S(1)}, f32[256]{0:T(256)}, u32[]{:S(2)}) %copy-start.1) | copy-done | bytes 1048
  1.6 0.1 broadcast_multiply_fusion.1
  1.7 0.2 convolution_convert_fusion.1
  2.0 0.7 %broadcast_in_dim.50 = bf16[8,65,128]{2,1,0:T(8,128)(2,1)} broadcast(bf16[65,128]{1,0:T(8,128)(2,1)S(1)} %pad_maximum_fusion.6), dimensions={1,2} | broadcast | bytes 149760 | tf_op jit(solution)/shard_map/broadcast_in_dim | solution.py:11
  2.6 2.9 %collective-permute-start = (bf16[512,128]{1,0:T(8,128)(2,1)S(1)}, bf16[512,128]{1,0:T(8,128)(2,1)S(1)}, u32[]{:S(2)}, u32[]{:S(2)}) collective-permute-start(bf16[512,128]{1,0:T(8,128)(2,1)S(1)} %pad_maximum_fusion.3), channel_id=1, source_target_pairs={{0,2},{1,3},{2,0},{3,1},{4,6},{5,7},{6,4},{7,5},{8,10},{9,11},{10,... | collective-permute-start | bytes 393224 | tf_op jit(solution)/shard_map/ppermute | solution.py:43
  5.6 5.8 %all-to-all-start = ((bf16[8,65,128]{2,1,0:T(8,128)(2,1)}), bf16[8,65,128]{2,1,0:T(8,128)(2,1)S(1)}, u32[]{:S(2)}, u32[]{:S(2)}) async-start(bf16[8,65,128]{2,1,0:T(8,128)(2,1)} %broadcast_in_dim.50), calls=%async_computation | async-start | bytes 294912 | tf_op jit(solution)/shard_map/all_to_all | solution.py:15
  11.5 0.0 collective-permute-done
  11.5 0.1 collective-permute-start.1
  11.7 7.2 %all-to-all-done = bf16[8,65,128]{2,1,0:T(8,128)(2,1)S(1)} async-done(((bf16[8,65,128]{2,1,0:T(8,128)(2,1)}), bf16[8,65,128]{2,1,0:T(8,128)(2,1)S(1)}, u32[]{:S(2)}, u32[]{:S(2)}) %all-to-all-start) | async-done | bytes 133152 | tf_op jit(solution)/shard_map/all_to_all | solution.py:15
  19.0 0.6 %collective-permute-start.2 = (bf16[256,128]{1,0:T(8,128)(2,1)S(1)}, bf16[256,128]{1,0:T(8,128)(2,1)S(1)}, u32[]{:S(2)}, u32[]{:S(2)}) collective-permute-start(bf16[256,128]{1,0:T(8,128)(2,1)S(1)} %bitcast.60), channel_id=1, source_target_pairs={{0,2},{1,3},{2,0},{3,1},{4,6},{5,7},{6,4},{7,5},{8,10},{9,11},{10,... | collective-permute-start | bytes 196616 | tf_op jit(solution)/shard_map/ppermute | solution.py:43
  19.6 0.2 fusion.1
  19.8 3.5 %collective-permute-done.2 = bf16[256,128]{1,0:T(8,128)(2,1)S(1)} collective-permute-done((bf16[256,128]{1,0:T(8,128)(2,1)S(1)}, bf16[256,128]{1,0:T(8,128)(2,1)S(1)}, u32[]{:S(2)}, u32[]{:S(2)}) %collective-permute-start.2) | collective-permute-done | bytes 65568 | tf_op jit(solution)/shard_map/ppermute | solution.py:43
  23.3 0.1 collective-permute-start.3
  23.4 0.2 fusion.9
  23.6 0.0 collective-permute-done.1
  23.7 0.6 %gather_fusion = bf16[4,128,256]{2,1,0:T(8,128)(2,1)S(1)} fusion(bf16[4,128,256]{2,1,0:T(8,128)(2,1)S(1)} %pad_maximum_fusion.1, s32[1024]{0:T(1024)S(1)} %pad_clamp_fusion), kind=kCustom, calls=%fused_computation | custom fusion | bytes 524304 | tf_op jit(solution)/shard_map/jit(_take)/gather | solution.py:73
  24.3 0.1 broadcast_select_fusion
  24.4 0.1 rev.11
  24.6 0.1 fusion.32
  24.7 0.1 collective-permute-done.3
  24.7 0.2 fusion.11
  24.9 0.5 multiply_reduce_fusion.1
  25.4 0.2 convolution_convert_fusion
  25.6 10.5 %all_to_all.15 = bf16[8,67,128]{2,1,0:T(8,128)(2,1)S(1)} all-to-all(bf16[8,67,128]{2,1,0:T(8,128)(2,1)S(1)} %broadcast_in_dim.54), channel_id=1, replica_groups=mesh['grid'=8,'band'=4] {'grid'}, dimensions={0} | all-to-all | bytes 274432 | tf_op jit(solution)/shard_map/all_to_all | solution.py:15
  36.3 0.6 %collective-permute-start.4 = (bf16[512,128]{1,0:T(8,128)(2,1)S(1)}, bf16[512,128]{1,0:T(8,128)(2,1)S(1)}, u32[]{:S(2)}, u32[]{:S(2)}) collective-permute-start(bf16[512,128]{1,0:T(8,128)(2,1)S(1)} %pad_maximum_fusion.5), channel_id=1, source_target_pairs={{0,2},{1,3},{2,0},{3,1},{4,6},{5,7},{6,4},{7,5},{8,10},{9,11},{10,... | collective-permute-start | bytes 393224 | tf_op jit(solution)/shard_map/ppermute | solution.py:43
  36.9 4.4 %collective-permute-done.4 = bf16[512,128]{1,0:T(8,128)(2,1)S(1)} collective-permute-done((bf16[512,128]{1,0:T(8,128)(2,1)S(1)}, bf16[512,128]{1,0:T(8,128)(2,1)S(1)}, u32[]{:S(2)}, u32[]{:S(2)}) %collective-permute-start.4) | collective-permute-done | bytes 131104 | tf_op jit(solution)/shard_map/ppermute | solution.py:43
  41.4 0.1 collective-permute-start.5
  41.5 0.2 fusion.13
  41.7 0.2 fusion.21
  41.9 1.1 %collective-permute-done.5 = bf16[1024,128]{1,0:T(8,128)(2,1)S(1)} collective-permute-done((bf16[1024,128]{1,0:T(8,128)(2,1)S(1)}, bf16[1024,128]{1,0:T(8,128)(2,1)S(1)}, u32[]{:S(2)}, u32[]{:S(2)}) %collective-permute-start.5) | collective-permute-done | bytes 262176 | tf_op jit(solution)/shard_map/ppermute | solution.py:43
  43.0 0.2 fusion.23
  43.2 0.5 multiply_reduce_fusion
  43.7 9.5 %all_to_all.16 = f32[8,1,128]{2,1,0:T(1,128)S(1)} all-to-all(f32[8,1,128]{2,1,0:T(1,128)S(1)} %broadcast_in_dim.55), channel_id=1, replica_groups=mesh['grid'=8,'band'=4] {'grid'}, dimensions={0} | all-to-all | bytes 8192 | tf_op jit(solution)/shard_map/all_to_all | solution.py:15
  53.2 0.7 %broadcast_multiply_fusion = f32[256,128]{1,0:T(8,128)} fusion(f32[256,128]{1,0:T(8,128)S(1)} %get-tuple-element.23, f32[128]{0:T(128)S(1)} %add_rsqrt_fusion), kind=kLoop, calls=%fused_computation.78 | loop fusion | flops 32768 | bytes 262656 | tf_op jit(solution)/shard_map/mul | solution.py:117
  (42 shorter events, 0.6 us)
Async XLA Ops:
  0.0 0.9 %copy-start.2 = (s32[64]{0:T(128)S(1)}, s32[64]{0:T(128)}, u32[]{:S(2)}) copy-start(s32[64]{0:T(128)} %param.7) | copy-start | bytes 772
  0.0 0.9 %copy-start = (f32[256,128]{1,0:T(8,128)S(1)}, f32[256,128]{1,0:T(8,128)}, u32[]{:S(2)}) copy-start(f32[256,128]{1,0:T(8,128)} %param.4) | copy-start | bytes 393220
  0.9 0.7 %copy-start.1 = (f32[256]{0:T(256)S(1)}, f32[256]{0:T(256)}, u32[]{:S(2)}) copy-start(f32[256]{0:T(256)} %param.5) | copy-start | bytes 3076
  2.6 8.9 %collective-permute-start = (bf16[512,128]{1,0:T(8,128)(2,1)S(1)}, bf16[512,128]{1,0:T(8,128)(2,1)S(1)}, u32[]{:S(2)}, u32[]{:S(2)}) collective-permute-start(bf16[512,128]{1,0:T(8,128)(2,1)S(1)} %pad_maximum_fusion.3), channel_id=1, source_target_pairs={{0,2},{1,3},{2,0},{3,1},{4,6},{5,7},{6,4},{7,5},{8,10},{9,11},{10,... | collective-permute-start | bytes 393224 | tf_op jit(solution)/shard_map/ppermute | solution.py:43
  5.6 13.3 %all-to-all-start = ((bf16[8,65,128]{2,1,0:T(8,128)(2,1)}), bf16[8,65,128]{2,1,0:T(8,128)(2,1)S(1)}, u32[]{:S(2)}, u32[]{:S(2)}) async-start(bf16[8,65,128]{2,1,0:T(8,128)(2,1)} %broadcast_in_dim.50), calls=%async_computation | async-start | bytes 294912 | tf_op jit(solution)/shard_map/all_to_all | solution.py:15
  11.5 12.1 %collective-permute-start.1 = (bf16[1024,128]{1,0:T(8,128)(2,1)S(1)}, bf16[1024,128]{1,0:T(8,128)(2,1)S(1)}, u32[]{:S(2)}, u32[]{:S(2)}) collective-permute-start(bf16[1024,128]{1,0:T(8,128)(2,1)S(1)} %pad_maximum_fusion), channel_id=1, source_target_pairs={{0,1},{1,0},{2,3},{3,2},{4,5},{5,4},{6,7},{7,6},{8,9},{9,8},{10,11... | collective-permute-start | bytes 786440 | tf_op jit(solution)/shard_map/ppermute | solution.py:43
  19.0 4.3 %collective-permute-start.2 = (bf16[256,128]{1,0:T(8,128)(2,1)S(1)}, bf16[256,128]{1,0:T(8,128)(2,1)S(1)}, u32[]{:S(2)}, u32[]{:S(2)}) collective-permute-start(bf16[256,128]{1,0:T(8,128)(2,1)S(1)} %bitcast.60), channel_id=1, source_target_pairs={{0,2},{1,3},{2,0},{3,1},{4,6},{5,7},{6,4},{7,5},{8,10},{9,11},{10,... | collective-permute-start | bytes 196616 | tf_op jit(solution)/shard_map/ppermute | solution.py:43
  23.3 1.4 %collective-permute-start.3 = (bf16[512,128]{1,0:T(8,128)(2,1)S(1)}, bf16[512,128]{1,0:T(8,128)(2,1)S(1)}, u32[]{:S(2)}, u32[]{:S(2)}) collective-permute-start(bf16[512,128]{1,0:T(8,128)(2,1)S(1)} %pad_maximum_fusion.4), channel_id=1, source_target_pairs={{0,1},{1,0},{2,3},{3,2},{4,5},{5,4},{6,7},{7,6},{8,9},{9,8},{10,11... | collective-permute-start | bytes 393224 | tf_op jit(solution)/shard_map/ppermute | solution.py:43
  36.3 5.0 %collective-permute-start.4 = (bf16[512,128]{1,0:T(8,128)(2,1)S(1)}, bf16[512,128]{1,0:T(8,128)(2,1)S(1)}, u32[]{:S(2)}, u32[]{:S(2)}) collective-permute-start(bf16[512,128]{1,0:T(8,128)(2,1)S(1)} %pad_maximum_fusion.5), channel_id=1, source_target_pairs={{0,2},{1,3},{2,0},{3,1},{4,6},{5,7},{6,4},{7,5},{8,10},{9,11},{10,... | collective-permute-start | bytes 393224 | tf_op jit(solution)/shard_map/ppermute | solution.py:43
  41.4 1.6 %collective-permute-start.5 = (bf16[1024,128]{1,0:T(8,128)(2,1)S(1)}, bf16[1024,128]{1,0:T(8,128)(2,1)S(1)}, u32[]{:S(2)}, u32[]{:S(2)}) collective-permute-start(bf16[1024,128]{1,0:T(8,128)(2,1)S(1)} %pad_maximum_fusion.2), channel_id=1, source_target_pairs={{0,1},{1,0},{2,3},{3,2},{4,5},{5,4},{6,7},{7,6},{8,9},{9,8},{10,11... | collective-permute-start | bytes 786440 | tf_op jit(solution)/shard_map/ppermute | solution.py:43

commit v19 on v18

--- a/solution.py
+++ b/solution.py
@@ -66,13 +66,14 @@
     sent, to_band = lax.optimization_barrier((grid_copies(jnp.concatenate([selected, filled[None]], 0)), to_band))
     got = grid_exchange(sent).reshape(ngroups, nslots + 1, block_width)
     pot = potential[:, None]
-    got, first_pot_psi = lax.optimization_barrier((got, pot * orbitals))
+    got, orbitals_later = lax.optimization_barrier((got, orbitals))
     swapped = band_hops(to_band)
     rows_b = jnp.concatenate([part[:rows] for part in swapped], 1)
     fitted_got = jnp.stack([part[rows:].reshape(fitted.shape) for part in swapped], 0)
     fitted_all = jnp.take(fitted_got, jnp.arange(nbands, dtype=jnp.int32) ^ band, axis=0)
     fitted_all = fitted_all.reshape(ngroups // 2, 2, nslots, fitted.shape[1])
     coll = jnp.concatenate(band_hops(pair_up(got[:, :nslots])), 1)
+    coll, first_pot_psi = lax.optimization_barrier((coll, pot * orbitals_later))
     first_filled = got[:, nslots, :nslots].reshape(ngroups // 2, 2, nslots)[:, 0] > 0
     fitted_all = jnp.where(
         first_filled[:, :, None], fitted_all[:, 0], jnp.flip(fitted_all[:, 1], axis=1)

time: 54.2 us -> 54.3 us (level)
  waiting for transfers between devices: 16.3 us -> 13.2 us
  starting transfers between devices: 10.2 us -> 12.1 us
  other arithmetic: 1.27 us -> 2.89 us
  local copies, waits for them, and re-layouts: 3.23 us -> 2.33 us
  blocking collectives: 20 us -> 20.6 us
    all_to_all x1, waiting for transfers between devices: 7.2 us -> 2.34 us  [grid_exchange(): got = lax.all_to_all(sent, 'grid', 0, 0, tiled=True)]
    ppermute x6, waiting for transfers between devices: 9.12 us -> 10.9 us  [band_hops(): lax.ppermute(jnp.concatenate([held[k] for k in keys], 0), 'band', [(i, i...]
    all_to_all x1, starting transfers between devices: 5.83 us -> 7.28 us  [grid_exchange(): got = lax.all_to_all(sent, 'grid', 0, 0, tiled=True)]
    convert_element_type x0 -> x1, other arithmetic: none -> 0.93 us  [body(): rows_b16 = orbitals.astype(jnp.bfloat16)]
    reshape x1, local copies, waits for them, and re-layouts: 0.9 us -> 0.03 us  [body(): to_band = jnp.concatenate([rows_b16, fitted.reshape(-1, block_width)], 0)]
    ge x1, other arithmetic: 0.01 us -> 0.66 us  [body(): valid_mask = points >= 0]
    all_to_all x2, blocking collectives: 20 us -> 20.6 us  [grid_exchange(): got = lax.all_to_all(sent, 'grid', 0, 0, tiled=True)]
  transfers between devices with their start and end apart: 7 -> 7, of which waited for: 5 -> 6; matrix products, arithmetic and copies ran while one was open for 4% -> 3% of each run, Pallas kernels for 0% -> 0%
where the time goes in v19:
time: 54.3 us; the launch traced here: 53.9 us
  blocking collectives  20.6 us (38%)
  waiting for transfers between devices  13.2 us (24%)
  starting transfers between devices  12.1 us (22%)
  other arithmetic  2.89 us (5%)
  matrix products  2.43 us (4%)
  local copies, waits for them, and re-layouts  2.33 us (4%)
    all_to_all x2, blocking collectives, grid_exchange(): got = lax.all_to_all(sent, 'grid', 0, 0, tiled=True)  20.6 us
    ppermute x6, waiting for transfers between devices, band_hops(): lax.ppermute(jnp.concatenate([held[k] for k in keys], 0), 'band', [(i, i...  10.9 us
    all_to_all x1, starting transfers between devices, grid_exchange(): got = lax.all_to_all(sent, 'grid', 0, 0, tiled=True)  7.28 us
    ppermute x6, starting transfers between devices, band_hops(): lax.ppermute(jnp.concatenate([held[k] for k in keys], 0), 'band', [(i, i...  4.81 us
    all_to_all x1, waiting for transfers between devices, grid_exchange(): got = lax.all_to_all(sent, 'grid', 0, 0, tiled=True)  2.34 us
    dot_general x6, matrix products, body(): lax.dot_general(coll[:, k * block_width:(k + 1) * block_width], rows_b[:,...  1.12 us
  transfers between devices with their start and end apart: 7, of which 6 were waited for; matrix products, arithmetic and copies ran while one was open for 3% of the time, Pallas kernels for 0%

profile of v19, /device:TPU:0, one launch (start us, length us, event | category | flops | bytes accessed | tf_op | source)
XLA Modules:
  0.0 53.9 jit_solution(4338269417233846948)
XLA Ops:
  0.0 0.7 %broadcast_compare_fusion = pred[64]{0:T(512)(128)(4,1)S(1)} fusion(s32[64]{0:T(128)} %param.7), kind=kLoop, calls=%fused_computation.111 | loop fusion | flops 64 | bytes 320 | tf_op jit(solution)/shard_map/ge | solution.py:60
  0.7 0.0 copy-start.3
  0.7 0.9 %convert_element_type.86 = bf16[256,128]{1,0:T(8,128)(2,1)S(1)} convert(f32[256,128]{1,0:T(8,128)} %param.4) | non-fusion elementwise | flops 32768 | bytes 196608 | tf_op jit(solution)/shard_map/convert_element_type | solution.py:62
  1.6 0.0 copy-done.3
  1.6 0.0 copy-start.1
  1.6 0.2 convolution_convert_fusion.1
  1.8 0.6 %copy-done.1 = bf16[128,256]{1,0:T(8,128)(2,1)S(1)} copy-done((bf16[128,256]{1,0:T(8,128)(2,1)S(1)}, bf16[128,256]{1,0:T(8,128)(2,1)}, u32[]{:S(2)}) %copy-start.1) | copy-done | bytes 65560
  2.5 0.7 %broadcast_in_dim.50 = bf16[8,65,128]{2,1,0:T(8,128)(2,1)} broadcast(bf16[65,128]{1,0:T(8,128)(2,1)S(1)} %pad_maximum_fusion.7), dimensions={1,2} | broadcast | bytes 149760 | tf_op jit(solution)/shard_map/broadcast_in_dim | solution.py:11
  3.2 7.3 %all-to-all-start = ((bf16[8,65,128]{2,1,0:T(8,128)(2,1)}), bf16[8,65,128]{2,1,0:T(8,128)(2,1)S(1)}, u32[]{:S(2)}, u32[]{:S(2)}) async-start(bf16[8,65,128]{2,1,0:T(8,128)(2,1)} %broadcast_in_dim.50), calls=%async_computation | async-start | bytes 294912 | tf_op jit(solution)/shard_map/all_to_all | solution.py:15
  10.5 1.5 %collective-permute-start.2 = (bf16[512,128]{1,0:T(8,128)(2,1)S(1)}, bf16[512,128]{1,0:T(8,128)(2,1)S(1)}, u32[]{:S(2)}, u32[]{:S(2)}) collective-permute-start(bf16[512,128]{1,0:T(8,128)(2,1)S(1)} %pad_maximum_fusion.4), channel_id=1, source_target_pairs={{0,2},{1,3},{2,0},{3,1},{4,6},{5,7},{6,4},{7,5},{8,10},{9,11},{10,... | collective-permute-start | bytes 393224 | tf_op jit(solution)/shard_map/ppermute | solution.py:43
  12.0 3.4 %collective-permute-done.2 = bf16[512,128]{1,0:T(8,128)(2,1)S(1)} collective-permute-done((bf16[512,128]{1,0:T(8,128)(2,1)S(1)}, bf16[512,128]{1,0:T(8,128)(2,1)S(1)}, u32[]{:S(2)}, u32[]{:S(2)}) %collective-permute-start.2) | collective-permute-done | bytes 131104 | tf_op jit(solution)/shard_map/ppermute | solution.py:43
  15.5 0.1 collective-permute-start.3
  15.6 2.3 %all-to-all-done = bf16[8,65,128]{2,1,0:T(8,128)(2,1)S(1)} async-done(((bf16[8,65,128]{2,1,0:T(8,128)(2,1)}), bf16[8,65,128]{2,1,0:T(8,128)(2,1)S(1)}, u32[]{:S(2)}, u32[]{:S(2)}) %all-to-all-start) | async-done | bytes 133152 | tf_op jit(solution)/shard_map/all_to_all | solution.py:15
  18.0 0.0 copy-start
  18.0 0.0 copy-start.2
  18.0 1.6 %collective-permute-start = (bf16[256,128]{1,0:T(8,128)(2,1)S(1)}, bf16[256,128]{1,0:T(8,128)(2,1)S(1)}, u32[]{:S(2)}, u32[]{:S(2)}) collective-permute-start(bf16[256,128]{1,0:T(8,128)(2,1)S(1)} %bitcast.57), channel_id=1, source_target_pairs={{0,2},{1,3},{2,0},{3,1},{4,6},{5,7},{6,4},{7,5},{8,10},{9,11},{10,... | collective-permute-start | bytes 196616 | tf_op jit(solution)/shard_map/ppermute | solution.py:43
  19.6 0.0 copy-done
  19.6 0.0 copy-done.2
  19.6 0.1 broadcast_multiply_fusion.1
  19.7 2.6 %collective-permute-done = bf16[256,128]{1,0:T(8,128)(2,1)S(1)} collective-permute-done((bf16[256,128]{1,0:T(8,128)(2,1)S(1)}, bf16[256,128]{1,0:T(8,128)(2,1)S(1)}, u32[]{:S(2)}, u32[]{:S(2)}) %collective-permute-start) | collective-permute-done | bytes 65568 | tf_op jit(solution)/shard_map/ppermute | solution.py:43
  22.4 0.1 collective-permute-start.1
  22.5 0.0 collective-permute-done.3
  22.6 0.6 %gather_fusion = bf16[4,128,256]{2,1,0:T(8,128)(2,1)S(1)} fusion(bf16[4,128,256]{2,1,0:T(8,128)(2,1)S(1)} %pad_maximum_fusion.2, s32[1024]{0:T(1024)S(1)} %pad_clamp_fusion), kind=kCustom, calls=%fused_computation | custom fusion | bytes 524304 | tf_op jit(solution)/shard_map/jit(_take)/gather | solution.py:73
  23.2 0.1 broadcast_select_fusion
  23.3 0.1 rev.12
  23.4 0.1 fusion.32
  23.5 0.3 collective-permute-done.1
  23.8 0.2 fusion.1
  24.0 0.2 fusion.9
  24.2 0.2 fusion.11
  24.4 0.5 multiply_reduce_fusion.1
  24.9 0.2 convolution_convert_fusion
  25.2 11.3 %all_to_all.15 = bf16[8,67,128]{2,1,0:T(8,128)(2,1)S(1)} all-to-all(bf16[8,67,128]{2,1,0:T(8,128)(2,1)S(1)} %broadcast_in_dim.54), channel_id=1, replica_groups=mesh['grid'=8,'band'=4] {'grid'}, dimensions={0} | all-to-all | bytes 274432 | tf_op jit(solution)/shard_map/all_to_all | solution.py:15
  36.7 1.6 %collective-permute-start.4 = (bf16[512,128]{1,0:T(8,128)(2,1)S(1)}, bf16[512,128]{1,0:T(8,128)(2,1)S(1)}, u32[]{:S(2)}, u32[]{:S(2)}) collective-permute-start(bf16[512,128]{1,0:T(8,128)(2,1)S(1)} %pad_maximum_fusion.6), channel_id=1, source_target_pairs={{0,2},{1,3},{2,0},{3,1},{4,6},{5,7},{6,4},{7,5},{8,10},{9,11},{10,... | collective-permute-start | bytes 393224 | tf_op jit(solution)/shard_map/ppermute | solution.py:43
  38.2 3.5 %collective-permute-done.4 = bf16[512,128]{1,0:T(8,128)(2,1)S(1)} collective-permute-done((bf16[512,128]{1,0:T(8,128)(2,1)S(1)}, bf16[512,128]{1,0:T(8,128)(2,1)S(1)}, u32[]{:S(2)}, u32[]{:S(2)}) %collective-permute-start.4) | collective-permute-done | bytes 131104 | tf_op jit(solution)/shard_map/ppermute | solution.py:43
  41.7 0.1 collective-permute-start.5
  41.8 0.2 fusion.13
  42.0 0.2 fusion.21
  42.2 1.1 %collective-permute-done.5 = bf16[1024,128]{1,0:T(8,128)(2,1)S(1)} collective-permute-done((bf16[1024,128]{1,0:T(8,128)(2,1)S(1)}, bf16[1024,128]{1,0:T(8,128)(2,1)S(1)}, u32[]{:S(2)}, u32[]{:S(2)}) %collective-permute-start.5) | collective-permute-done | bytes 262176 | tf_op jit(solution)/shard_map/ppermute | solution.py:43
  43.3 0.2 fusion.23
  43.5 0.5 multiply_reduce_fusion
  44.0 9.2 %all_to_all.16 = f32[8,1,128]{2,1,0:T(1,128)S(1)} all-to-all(f32[8,1,128]{2,1,0:T(1,128)S(1)} %broadcast_in_dim.55), channel_id=1, replica_groups=mesh['grid'=8,'band'=4] {'grid'}, dimensions={0} | all-to-all | bytes 8192 | tf_op jit(solution)/shard_map/all_to_all | solution.py:15
  53.3 0.7 %broadcast_multiply_fusion = f32[256,128]{1,0:T(8,128)} fusion(f32[256,128]{1,0:T(8,128)S(1)} %get-tuple-element.27, f32[128]{0:T(128)S(1)} %add_rsqrt_fusion), kind=kLoop, calls=%fused_computation.77 | loop fusion | flops 32768 | bytes 262656 | tf_op jit(solution)/shard_map/mul | solution.py:118
  (44 shorter events, 0.6 us)
Async XLA Ops:
  0.7 0.9 %copy-start.3 = (s32[64]{0:T(128)S(1)}, s32[64]{0:T(128)}, u32[]{:S(2)}) copy-start(s32[64]{0:T(128)} %param.7) | copy-start | bytes 772
  1.6 0.8 %copy-start.1 = (bf16[128,256]{1,0:T(8,128)(2,1)S(1)}, bf16[128,256]{1,0:T(8,128)(2,1)}, u32[]{:S(2)}) copy-start(bf16[128,256]{1,0:T(8,128)(2,1)} %param.6) | copy-start | bytes 196612
  3.2 14.7 %all-to-all-start = ((bf16[8,65,128]{2,1,0:T(8,128)(2,1)}), bf16[8,65,128]{2,1,0:T(8,128)(2,1)S(1)}, u32[]{:S(2)}, u32[]{:S(2)}) async-start(bf16[8,65,128]{2,1,0:T(8,128)(2,1)} %broadcast_in_dim.50), calls=%async_computation | async-start | bytes 294912 | tf_op jit(solution)/shard_map/all_to_all | solution.py:15
  10.5 5.0 %collective-permute-start.2 = (bf16[512,128]{1,0:T(8,128)(2,1)S(1)}, bf16[512,128]{1,0:T(8,128)(2,1)S(1)}, u32[]{:S(2)}, u32[]{:S(2)}) collective-permute-start(bf16[512,128]{1,0:T(8,128)(2,1)S(1)} %pad_maximum_fusion.4), channel_id=1, source_target_pairs={{0,2},{1,3},{2,0},{3,1},{4,6},{5,7},{6,4},{7,5},{8,10},{9,11},{10,... | collective-permute-start | bytes 393224 | tf_op jit(solution)/shard_map/ppermute | solution.py:43
  15.5 7.0 %collective-permute-start.3 = (bf16[1024,128]{1,0:T(8,128)(2,1)S(1)}, bf16[1024,128]{1,0:T(8,128)(2,1)S(1)}, u32[]{:S(2)}, u32[]{:S(2)}) collective-permute-start(bf16[1024,128]{1,0:T(8,128)(2,1)S(1)} %pad_maximum_fusion.1), channel_id=1, source_target_pairs={{0,1},{1,0},{2,3},{3,2},{4,5},{5,4},{6,7},{7,6},{8,9},{9,8},{10,11... | collective-permute-start | bytes 786440 | tf_op jit(solution)/shard_map/ppermute | solution.py:43
  18.0 1.6 %copy-start = (f32[256,128]{1,0:T(8,128)S(1)}, f32[256,128]{1,0:T(8,128)}, u32[]{:S(2)}) copy-start(f32[256,128]{1,0:T(8,128)} %param.4) | copy-start | bytes 393220
  18.0 1.6 %copy-start.2 = (f32[256]{0:T(256)S(1)}, f32[256]{0:T(256)}, u32[]{:S(2)}) copy-start(f32[256]{0:T(256)} %param.5) | copy-start | bytes 3076
  18.0 4.3 %collective-permute-start = (bf16[256,128]{1,0:T(8,128)(2,1)S(1)}, bf16[256,128]{1,0:T(8,128)(2,1)S(1)}, u32[]{:S(2)}, u32[]{:S(2)}) collective-permute-start(bf16[256,128]{1,0:T(8,128)(2,1)S(1)} %bitcast.57), channel_id=1, source_target_pairs={{0,2},{1,3},{2,0},{3,1},{4,6},{5,7},{6,4},{7,5},{8,10},{9,11},{10,... | collective-permute-start | bytes 196616 | tf_op jit(solution)/shard_map/ppermute | solution.py:43
  22.4 1.4 %collective-permute-start.1 = (bf16[512,128]{1,0:T(8,128)(2,1)S(1)}, bf16[512,128]{1,0:T(8,128)(2,1)S(1)}, u32[]{:S(2)}, u32[]{:S(2)}) collective-permute-start(bf16[512,128]{1,0:T(8,128)(2,1)S(1)} %pad_maximum_fusion.5), channel_id=1, source_target_pairs={{0,1},{1,0},{2,3},{3,2},{4,5},{5,4},{6,7},{7,6},{8,9},{9,8},{10,11... | collective-permute-start | bytes 393224 | tf_op jit(solution)/shard_map/ppermute | solution.py:43
  36.7 5.0 %collective-permute-start.4 = (bf16[512,128]{1,0:T(8,128)(2,1)S(1)}, bf16[512,128]{1,0:T(8,128)(2,1)S(1)}, u32[]{:S(2)}, u32[]{:S(2)}) collective-permute-start(bf16[512,128]{1,0:T(8,128)(2,1)S(1)} %pad_maximum_fusion.6), channel_id=1, source_target_pairs={{0,2},{1,3},{2,0},{3,1},{4,6},{5,7},{6,4},{7,5},{8,10},{9,11},{10,... | collective-permute-start | bytes 393224 | tf_op jit(solution)/shard_map/ppermute | solution.py:43
  41.7 1.6 %collective-permute-start.5 = (bf16[1024,128]{1,0:T(8,128)(2,1)S(1)}, bf16[1024,128]{1,0:T(8,128)(2,1)S(1)}, u32[]{:S(2)}, u32[]{:S(2)}) collective-permute-start(bf16[1024,128]{1,0:T(8,128)(2,1)S(1)} %pad_maximum_fusion.3), channel_id=1, source_target_pairs={{0,1},{1,0},{2,3},{3,2},{4,5},{5,4},{6,7},{7,6},{8,9},{9,8},{10,11... | collective-permute-start | bytes 786440 | tf_op jit(solution)/shard_map/ppermute | solution.py:43

commit v20 on v19

--- a/solution.py
+++ b/solution.py
@@ -67,12 +67,20 @@
     got = grid_exchange(sent).reshape(ngroups, nslots + 1, block_width)
     pot = potential[:, None]
     got, orbitals_later = lax.optimization_barrier((got, orbitals))
-    swapped = band_hops(to_band)
+    nband_rows = to_band.shape[0]
+    across = lax.ppermute(to_band, "band", [(i, i ^ 2) for i in range(nbands)]) if nbands == 4 else None
+    paired = pair_up(got[:, :nslots])
+    if nbands == 4:
+        paired, across = lax.optimization_barrier((paired, across))
+        on_chip = lax.ppermute(jnp.concatenate([to_band, across], 0), "band", [(i, i ^ 1) for i in range(nbands)])
+        swapped = [to_band, on_chip[:nband_rows], across, on_chip[nband_rows:]]
+    else:
+        swapped = band_hops(to_band)
     rows_b = jnp.concatenate([part[:rows] for part in swapped], 1)
     fitted_got = jnp.stack([part[rows:].reshape(fitted.shape) for part in swapped], 0)
     fitted_all = jnp.take(fitted_got, jnp.arange(nbands, dtype=jnp.int32) ^ band, axis=0)
     fitted_all = fitted_all.reshape(ngroups // 2, 2, nslots, fitted.shape[1])
-    coll = jnp.concatenate(band_hops(pair_up(got[:, :nslots])), 1)
+    coll = jnp.concatenate(band_hops(paired), 1)
     coll, first_pot_psi = lax.optimization_barrier((coll, pot * orbitals_later))
     first_filled = got[:, nslots, :nslots].reshape(ngroups // 2, 2, nslots)[:, 0] > 0
     fitted_all = jnp.where(

time: 54.3 us -> 54.3 us (level)
  waiting for transfers between devices: 13.2 us -> 14.6 us
  other arithmetic: 2.89 us -> 2.25 us
  blocking collectives: 20.6 us -> 20 us
    all_to_all x1, waiting for transfers between devices: 2.34 us -> 5.89 us  [grid_exchange(): got = lax.all_to_all(sent, 'grid', 0, 0, tiled=True)]
    ppermute x6 -> x4, waiting for transfers between devices: 10.9 us -> 8.67 us  [band_hops(): lax.ppermute(jnp.concatenate([held[k] for k in keys], 0), 'band', [(i, i...]
    ppermute x6 -> x4, starting transfers between devices: 4.81 us -> 3.25 us  [band_hops(): lax.ppermute(jnp.concatenate([held[k] for k in keys], 0), 'band', [(i, i...]
    ppermute x0 -> x2, starting transfers between devices: none -> 1.56 us  [the longest x1 1.49 us: body(): lax.ppermute(to_band, 'band', [(i, i ^ 2) for i in range(nbands)])]
    ge x1, other arithmetic: 0.66 us -> 0.01 us  [body(): valid_mask = points >= 0]
    all_to_all x2, blocking collectives: 20.6 us -> 20 us  [grid_exchange(): got = lax.all_to_all(sent, 'grid', 0, 0, tiled=True)]
  transfers between devices with their start and end apart: 7 -> 7, of which waited for: 6 -> 5; matrix products, arithmetic and copies ran while one was open for 3% -> 2% of each run, Pallas kernels for 0% -> 0%
where the time goes in v20:
time: 54.3 us; the launch traced here: 54 us
  blocking collectives  20 us (37%)
  waiting for transfers between devices  14.6 us (27%)
  starting transfers between devices  12.1 us (22%)
  matrix products  2.42 us (4%)
  local copies, waits for them, and re-layouts  2.31 us (4%)
  other arithmetic  2.25 us (4%)
    all_to_all x2, blocking collectives, grid_exchange(): got = lax.all_to_all(sent, 'grid', 0, 0, tiled=True)  20 us
    ppermute x4, waiting for transfers between devices, band_hops(): lax.ppermute(jnp.concatenate([held[k] for k in keys], 0), 'band', [(i, i...  8.67 us
    all_to_all x1, starting transfers between devices, grid_exchange(): got = lax.all_to_all(sent, 'grid', 0, 0, tiled=True)  7.28 us
    all_to_all x1, waiting for transfers between devices, grid_exchange(): got = lax.all_to_all(sent, 'grid', 0, 0, tiled=True)  5.89 us
    ppermute x4, starting transfers between devices, band_hops(): lax.ppermute(jnp.concatenate([held[k] for k in keys], 0), 'band', [(i, i...  3.25 us
    ppermute x1, starting transfers between devices, body(): lax.ppermute(to_band, 'band', [(i, i ^ 2) for i in range(nbands)])  1.49 us
    dot_general x6, matrix products, body(): lax.dot_general(coll[:, k * block_width:(k + 1) * block_width], rows_b[:,...  1.12 us
  transfers between devices with their start and end apart: 7, of which 5 were waited for; matrix products, arithmetic and copies ran while one was open for 2% of the time, Pallas kernels for 0%

profile of v20, /device:TPU:0, one launch (start us, length us, event | category | flops | bytes accessed | tf_op | source)
XLA Modules:
  0.0 54.0 jit_solution(3577867151436024943)
XLA Ops:
  0.0 0.0 copy-start.1
  0.0 0.9 %convert_element_type.86 = bf16[256,128]{1,0:T(8,128)(2,1)S(1)} convert(f32[256,128]{1,0:T(8,128)} %param.4) | non-fusion elementwise | flops 32768 | bytes 196608 | tf_op jit(solution)/shard_map/convert_element_type | solution.py:62
  0.9 0.0 copy-done.1
  1.0 0.0 copy-start.3
  1.0 0.6 %copy-done.3 = s32[64]{0:T(128)S(1)} copy-done((s32[64]{0:T(128)S(1)}, s32[64]{0:T(128)}, u32[]{:S(2)}) %copy-start.3) | copy-done | bytes 280
  1.6 0.2 convolution_convert_fusion.1
  1.9 0.7 %broadcast_in_dim.50 = bf16[8,65,128]{2,1,0:T(8,128)(2,1)} broadcast(bf16[65,128]{1,0:T(8,128)(2,1)S(1)} %pad_maximum_fusion.7), dimensions={1,2} | broadcast | bytes 149760 | tf_op jit(solution)/shard_map/broadcast_in_dim | solution.py:11
  2.5 7.3 %all-to-all-start = ((bf16[8,65,128]{2,1,0:T(8,128)(2,1)}), bf16[8,65,128]{2,1,0:T(8,128)(2,1)S(1)}, u32[]{:S(2)}, u32[]{:S(2)}) async-start(bf16[8,65,128]{2,1,0:T(8,128)(2,1)} %broadcast_in_dim.50), calls=%async_computation | async-start | bytes 294912 | tf_op jit(solution)/shard_map/all_to_all | solution.py:15
  9.8 1.5 %collective-permute-start = (bf16[512,128]{1,0:T(8,128)(2,1)S(1)}, bf16[512,128]{1,0:T(8,128)(2,1)S(1)}, u32[]{:S(2)}, u32[]{:S(2)}) collective-permute-start(bf16[512,128]{1,0:T(8,128)(2,1)S(1)} %pad_maximum_fusion.4), channel_id=1, source_target_pairs={{0,2},{1,3},{2,0},{3,1},{4,6},{5,7},{6,4},{7,5},{8,10},{9,11},{10,... | collective-permute-start | bytes 393224 | tf_op jit(solution)/shard_map/ppermute | solution.py:71
  11.4 5.9 %all-to-all-done = bf16[8,65,128]{2,1,0:T(8,128)(2,1)S(1)} async-done(((bf16[8,65,128]{2,1,0:T(8,128)(2,1)}), bf16[8,65,128]{2,1,0:T(8,128)(2,1)S(1)}, u32[]{:S(2)}, u32[]{:S(2)}) %all-to-all-start) | async-done | bytes 133152 | tf_op jit(solution)/shard_map/all_to_all | solution.py:15
  17.4 0.0 collective-permute-done
  17.4 0.1 collective-permute-start.3
  17.5 1.6 %collective-permute-start.1 = (bf16[256,128]{1,0:T(8,128)(2,1)S(1)}, bf16[256,128]{1,0:T(8,128)(2,1)S(1)}, u32[]{:S(2)}, u32[]{:S(2)}) collective-permute-start(bf16[256,128]{1,0:T(8,128)(2,1)S(1)} %bitcast.57), channel_id=1, source_target_pairs={{0,2},{1,3},{2,0},{3,1},{4,6},{5,7},{6,4},{7,5},{8,10},{9,11},{10,... | collective-permute-start | bytes 196616 | tf_op jit(solution)/shard_map/ppermute | solution.py:43
  19.1 0.0 copy-start
  19.1 0.0 copy-start.2
  19.1 2.8 %collective-permute-done.1 = bf16[256,128]{1,0:T(8,128)(2,1)S(1)} collective-permute-done((bf16[256,128]{1,0:T(8,128)(2,1)S(1)}, bf16[256,128]{1,0:T(8,128)(2,1)S(1)}, u32[]{:S(2)}, u32[]{:S(2)}) %collective-permute-start.1) | collective-permute-done | bytes 65568 | tf_op jit(solution)/shard_map/ppermute | solution.py:43
  22.0 0.1 collective-permute-start.2
  22.1 0.0 copy-done
  22.1 0.0 copy-done.2
  22.1 0.1 broadcast_multiply_fusion.1
  22.2 1.2 %collective-permute-done.2 = bf16[512,128]{1,0:T(8,128)(2,1)S(1)} collective-permute-done((bf16[512,128]{1,0:T(8,128)(2,1)S(1)}, bf16[512,128]{1,0:T(8,128)(2,1)S(1)}, u32[]{:S(2)}, u32[]{:S(2)}) %collective-permute-start.2) | collective-permute-done | bytes 131104 | tf_op jit(solution)/shard_map/ppermute | solution.py:43
  23.5 0.2 fusion.9
  23.7 0.2 fusion.1
  23.9 0.0 collective-permute-done.3
  24.0 0.6 %gather_fusion = bf16[4,128,256]{2,1,0:T(8,128)(2,1)S(1)} fusion(bf16[4,128,256]{2,1,0:T(8,128)(2,1)S(1)} %pad_maximum_fusion.2, s32[1024]{0:T(1024)S(1)} %pad_clamp_fusion), kind=kCustom, calls=%fused_computation | custom fusion | bytes 524304 | tf_op jit(solution)/shard_map/jit(_take)/gather | solution.py:81
  24.6 0.1 broadcast_select_fusion
  24.7 0.1 rev.12
  24.8 0.1 fusion.32
  24.9 0.2 fusion.11
  25.1 0.5 multiply_reduce_fusion.1
  25.6 0.2 convolution_convert_fusion
  25.9 10.7 %all_to_all.15 = bf16[8,67,128]{2,1,0:T(8,128)(2,1)S(1)} all-to-all(bf16[8,67,128]{2,1,0:T(8,128)(2,1)S(1)} %broadcast_in_dim.54), channel_id=1, replica_groups=mesh['grid'=8,'band'=4] {'grid'}, dimensions={0} | all-to-all | bytes 274432 | tf_op jit(solution)/shard_map/all_to_all | solution.py:15
  36.8 1.6 %collective-permute-start.4 = (bf16[512,128]{1,0:T(8,128)(2,1)S(1)}, bf16[512,128]{1,0:T(8,128)(2,1)S(1)}, u32[]{:S(2)}, u32[]{:S(2)}) collective-permute-start(bf16[512,128]{1,0:T(8,128)(2,1)S(1)} %pad_maximum_fusion.6), channel_id=1, source_target_pairs={{0,2},{1,3},{2,0},{3,1},{4,6},{5,7},{6,4},{7,5},{8,10},{9,11},{10,... | collective-permute-start | bytes 393224 | tf_op jit(solution)/shard_map/ppermute | solution.py:43
  38.3 3.5 %collective-permute-done.4 = bf16[512,128]{1,0:T(8,128)(2,1)S(1)} collective-permute-done((bf16[512,128]{1,0:T(8,128)(2,1)S(1)}, bf16[512,128]{1,0:T(8,128)(2,1)S(1)}, u32[]{:S(2)}, u32[]{:S(2)}) %collective-permute-start.4) | collective-permute-done | bytes 131104 | tf_op jit(solution)/shard_map/ppermute | solution.py:43
  41.9 0.1 collective-permute-start.5
  41.9 0.2 fusion.13
  42.1 0.2 fusion.21
  42.3 1.1 %collective-permute-done.5 = bf16[1024,128]{1,0:T(8,128)(2,1)S(1)} collective-permute-done((bf16[1024,128]{1,0:T(8,128)(2,1)S(1)}, bf16[1024,128]{1,0:T(8,128)(2,1)S(1)}, u32[]{:S(2)}, u32[]{:S(2)}) %collective-permute-start.5) | collective-permute-done | bytes 262176 | tf_op jit(solution)/shard_map/ppermute | solution.py:43
  43.5 0.2 fusion.23
  43.6 0.5 multiply_reduce_fusion
  44.1 9.2 %all_to_all.16 = f32[8,1,128]{2,1,0:T(1,128)S(1)} all-to-all(f32[8,1,128]{2,1,0:T(1,128)S(1)} %broadcast_in_dim.55), channel_id=1, replica_groups=mesh['grid'=8,'band'=4] {'grid'}, dimensions={0} | all-to-all | bytes 8192 | tf_op jit(solution)/shard_map/all_to_all | solution.py:15
  53.4 0.7 %broadcast_multiply_fusion = f32[256,128]{1,0:T(8,128)} fusion(f32[256,128]{1,0:T(8,128)S(1)} %get-tuple-element.31, f32[128]{0:T(128)S(1)} %add_rsqrt_fusion), kind=kLoop, calls=%fused_computation.76 | loop fusion | flops 32768 | bytes 262656 | tf_op jit(solution)/shard_map/mul | solution.py:126
  (45 shorter events, 0.7 us)
Async XLA Ops:
  0.0 0.9 %copy-start.1 = (bf16[128,256]{1,0:T(8,128)(2,1)S(1)}, bf16[128,256]{1,0:T(8,128)(2,1)}, u32[]{:S(2)}) copy-start(bf16[128,256]{1,0:T(8,128)(2,1)} %param.6) | copy-start | bytes 196612
  1.0 0.7 %copy-start.3 = (s32[64]{0:T(128)S(1)}, s32[64]{0:T(128)}, u32[]{:S(2)}) copy-start(s32[64]{0:T(128)} %param.7) | copy-start | bytes 772
  2.5 14.7 %all-to-all-start = ((bf16[8,65,128]{2,1,0:T(8,128)(2,1)}), bf16[8,65,128]{2,1,0:T(8,128)(2,1)S(1)}, u32[]{:S(2)}, u32[]{:S(2)}) async-start(bf16[8,65,128]{2,1,0:T(8,128)(2,1)} %broadcast_in_dim.50), calls=%async_computation | async-start | bytes 294912 | tf_op jit(solution)/shard_map/all_to_all | solution.py:15
  9.8 7.6 %collective-permute-start = (bf16[512,128]{1,0:T(8,128)(2,1)S(1)}, bf16[512,128]{1,0:T(8,128)(2,1)S(1)}, u32[]{:S(2)}, u32[]{:S(2)}) collective-permute-start(bf16[512,128]{1,0:T(8,128)(2,1)S(1)} %pad_maximum_fusion.4), channel_id=1, source_target_pairs={{0,2},{1,3},{2,0},{3,1},{4,6},{5,7},{6,4},{7,5},{8,10},{9,11},{10,... | collective-permute-start | bytes 393224 | tf_op jit(solution)/shard_map/ppermute | solution.py:71
  17.4 6.5 %collective-permute-start.3 = (bf16[1024,128]{1,0:T(8,128)(2,1)S(1)}, bf16[1024,128]{1,0:T(8,128)(2,1)S(1)}, u32[]{:S(2)}, u32[]{:S(2)}) collective-permute-start(bf16[1024,128]{1,0:T(8,128)(2,1)S(1)} %pad_maximum_fusion.1), channel_id=1, source_target_pairs={{0,1},{1,0},{2,3},{3,2},{4,5},{5,4},{6,7},{7,6},{8,9},{9,8},{10,11... | collective-permute-start | bytes 786440 | tf_op jit(solution)/shard_map/ppermute | solution.py:75
  17.5 4.5 %collective-permute-start.1 = (bf16[256,128]{1,0:T(8,128)(2,1)S(1)}, bf16[256,128]{1,0:T(8,128)(2,1)S(1)}, u32[]{:S(2)}, u32[]{:S(2)}) collective-permute-start(bf16[256,128]{1,0:T(8,128)(2,1)S(1)} %bitcast.57), channel_id=1, source_target_pairs={{0,2},{1,3},{2,0},{3,1},{4,6},{5,7},{6,4},{7,5},{8,10},{9,11},{10,... | collective-permute-start | bytes 196616 | tf_op jit(solution)/shard_map/ppermute | solution.py:43
  19.1 3.0 %copy-start = (f32[256,128]{1,0:T(8,128)S(1)}, f32[256,128]{1,0:T(8,128)}, u32[]{:S(2)}) copy-start(f32[256,128]{1,0:T(8,128)} %param.4) | copy-start | bytes 393220
  19.1 3.0 %copy-start.2 = (f32[256]{0:T(256)S(1)}, f32[256]{0:T(256)}, u32[]{:S(2)}) copy-start(f32[256]{0:T(256)} %param.5) | copy-start | bytes 3076
  22.0 1.4 %collective-permute-start.2 = (bf16[512,128]{1,0:T(8,128)(2,1)S(1)}, bf16[512,128]{1,0:T(8,128)(2,1)S(1)}, u32[]{:S(2)}, u32[]{:S(2)}) collective-permute-start(bf16[512,128]{1,0:T(8,128)(2,1)S(1)} %pad_maximum_fusion.5), channel_id=1, source_target_pairs={{0,1},{1,0},{2,3},{3,2},{4,5},{5,4},{6,7},{7,6},{8,9},{9,8},{10,11... | collective-permute-start | bytes 393224 | tf_op jit(solution)/shard_map/ppermute | solution.py:43
  36.8 5.0 %collective-permute-start.4 = (bf16[512,128]{1,0:T(8,128)(2,1)S(1)}, bf16[512,128]{1,0:T(8,128)(2,1)S(1)}, u32[]{:S(2)}, u32[]{:S(2)}) collective-permute-start(bf16[512,128]{1,0:T(8,128)(2,1)S(1)} %pad_maximum_fusion.6), channel_id=1, source_target_pairs={{0,2},{1,3},{2,0},{3,1},{4,6},{5,7},{6,4},{7,5},{8,10},{9,11},{10,... | collective-permute-start | bytes 393224 | tf_op jit(solution)/shard_map/ppermute | solution.py:43
  41.9 1.6 %collective-permute-start.5 = (bf16[1024,128]{1,0:T(8,128)(2,1)S(1)}, bf16[1024,128]{1,0:T(8,128)(2,1)S(1)}, u32[]{:S(2)}, u32[]{:S(2)}) collective-permute-start(bf16[1024,128]{1,0:T(8,128)(2,1)S(1)} %pad_maximum_fusion.3), channel_id=1, source_target_pairs={{0,1},{1,0},{2,3},{3,2},{4,5},{5,4},{6,7},{7,6},{8,9},{9,8},{10,11... | collective-permute-start | bytes 786440 | tf_op jit(solution)/shard_map/ppermute | solution.py:43

commit v21 on v19

--- a/solution.py
+++ b/solution.py
@@ -57,13 +57,15 @@
     rows = orbitals.shape[0]
     band = lax.axis_index("band")
     total_orbitals = block_width * nbands
-    valid_mask = points >= 0
     picks = (points[:, None] == jnp.arange(rows, dtype=points.dtype)[None, :]).astype(jnp.bfloat16)
     rows_b16 = orbitals.astype(jnp.bfloat16)
     selected = jnp.dot(picks, rows_b16, preferred_element_type=jnp.float32).astype(jnp.bfloat16)
-    filled = jnp.pad(valid_mask.astype(jnp.bfloat16), (0, block_width - nslots))
+    filled = lax.dot_general(
+        jnp.ones((1, rows), jnp.bfloat16), picks, (((1,), (1,)), ((), ())), preferred_element_type=jnp.float32
+    ).astype(jnp.bfloat16)
+    filled = jnp.pad(filled, ((0, 0), (0, block_width - nslots)))
     to_band = jnp.concatenate([rows_b16, fitted.reshape(-1, block_width)], 0)
-    sent, to_band = lax.optimization_barrier((grid_copies(jnp.concatenate([selected, filled[None]], 0)), to_band))
+    sent, to_band = lax.optimization_barrier((grid_copies(jnp.concatenate([selected, filled], 0)), to_band))
     got = grid_exchange(sent).reshape(ngroups, nslots + 1, block_width)
     pot = potential[:, None]
     got, orbitals_later = lax.optimization_barrier((got, orbitals))

time: 54.3 us -> 54.5 us (level)
  matrix products: 2.43 us -> 3.27 us
  other arithmetic: 2.89 us -> 2.23 us
    dot_general x0 -> x1, matrix products: none -> 0.85 us  [body(): lax.dot_general(jnp.ones((1, rows), jnp.bfloat16), picks, (((1,), (1,)),...]
    ge x1 -> x0, other arithmetic: 0.66 us -> none  [body(): valid_mask = points >= 0]
where the time goes in v21:
time: 54.5 us; the launch traced here: 54.1 us
  blocking collectives  20.6 us (38%)
  waiting for transfers between devices  13.2 us (24%)
  starting transfers between devices  12.1 us (22%)
  matrix products  3.27 us (6%)
  local copies, waits for them, and re-layouts  2.33 us (4%)
  other arithmetic  2.23 us (4%)
    all_to_all x2, blocking collectives, grid_exchange(): got = lax.all_to_all(sent, 'grid', 0, 0, tiled=True)  20.6 us
    ppermute x6, waiting for transfers between devices, band_hops(): lax.ppermute(jnp.concatenate([held[k] for k in keys], 0), 'band', [(i, i...  10.9 us
    all_to_all x1, starting transfers between devices, grid_exchange(): got = lax.all_to_all(sent, 'grid', 0, 0, tiled=True)  7.28 us
    ppermute x6, starting transfers between devices, band_hops(): lax.ppermute(jnp.concatenate([held[k] for k in keys], 0), 'band', [(i, i...  4.82 us
    all_to_all x1, waiting for transfers between devices, grid_exchange(): got = lax.all_to_all(sent, 'grid', 0, 0, tiled=True)  2.34 us
    dot_general x6, matrix products, body(): lax.dot_general(coll[:, k * block_width:(k + 1) * block_width], rows_b[:,...  1.11 us
  transfers between devices with their start and end apart: 7, of which 6 were waited for; matrix products, arithmetic and copies ran while one was open for 3% of the time, Pallas kernels for 0%

profile of v21, /device:TPU:0, one launch (start us, length us, event | category | flops | bytes accessed | tf_op | source)
XLA Modules:
  0.0 54.1 jit_solution(15400088769074653427)
XLA Ops:
  0.0 0.8 %fusion.31 = bf16[1,64]{1,0:T(2,128)(2,1)S(1)} fusion(s32[64]{0:T(128)} %param.7), kind=kOutput, calls=%fused_computation.45 | convolution fusion | flops 49216 | bytes 384 | tf_op jit(solution)/shard_map/dot_general | solution.py:63
  0.8 0.0 copy-start.3
  0.9 0.9 %convert_element_type.91 = bf16[256,128]{1,0:T(8,128)(2,1)S(1)} convert(f32[256,128]{1,0:T(8,128)} %param.4) | non-fusion elementwise | flops 32768 | bytes 196608 | tf_op jit(solution)/shard_map/convert_element_type | solution.py:61
  1.8 0.0 copy-done.3
  1.8 0.0 copy-start.1
  1.8 0.2 convolution_convert_fusion.1
  2.0 0.6 %copy-done.1 = bf16[128,256]{1,0:T(8,128)(2,1)S(1)} copy-done((bf16[128,256]{1,0:T(8,128)(2,1)S(1)}, bf16[128,256]{1,0:T(8,128)(2,1)}, u32[]{:S(2)}) %copy-start.1) | copy-done | bytes 65560
  2.7 0.7 %broadcast_in_dim.27 = bf16[8,65,128]{2,1,0:T(8,128)(2,1)} broadcast(bf16[65,128]{1,0:T(8,128)(2,1)S(1)} %fusion.62), dimensions={1,2} | broadcast | bytes 149760 | tf_op jit(solution)/shard_map/broadcast_in_dim | solution.py:11
  3.4 7.3 %all-to-all-start = ((bf16[8,65,128]{2,1,0:T(8,128)(2,1)}), bf16[8,65,128]{2,1,0:T(8,128)(2,1)S(1)}, u32[]{:S(2)}, u32[]{:S(2)}) async-start(bf16[8,65,128]{2,1,0:T(8,128)(2,1)} %broadcast_in_dim.27), calls=%async_computation | async-start | bytes 294912 | tf_op jit(solution)/shard_map/all_to_all | solution.py:15
  10.7 1.5 %collective-permute-start.2 = (bf16[512,128]{1,0:T(8,128)(2,1)S(1)}, bf16[512,128]{1,0:T(8,128)(2,1)S(1)}, u32[]{:S(2)}, u32[]{:S(2)}) collective-permute-start(bf16[512,128]{1,0:T(8,128)(2,1)S(1)} %pad_maximum_fusion.4), channel_id=1, source_target_pairs={{0,2},{1,3},{2,0},{3,1},{4,6},{5,7},{6,4},{7,5},{8,10},{9,11},{10,... | collective-permute-start | bytes 393224 | tf_op jit(solution)/shard_map/ppermute | solution.py:43
  12.2 3.4 %collective-permute-done.2 = bf16[512,128]{1,0:T(8,128)(2,1)S(1)} collective-permute-done((bf16[512,128]{1,0:T(8,128)(2,1)S(1)}, bf16[512,128]{1,0:T(8,128)(2,1)S(1)}, u32[]{:S(2)}, u32[]{:S(2)}) %collective-permute-start.2) | collective-permute-done | bytes 131104 | tf_op jit(solution)/shard_map/ppermute | solution.py:43
  15.7 0.1 collective-permute-start.3
  15.8 2.3 %all-to-all-done = bf16[8,65,128]{2,1,0:T(8,128)(2,1)S(1)} async-done(((bf16[8,65,128]{2,1,0:T(8,128)(2,1)}), bf16[8,65,128]{2,1,0:T(8,128)(2,1)S(1)}, u32[]{:S(2)}, u32[]{:S(2)}) %all-to-all-start) | async-done | bytes 133152 | tf_op jit(solution)/shard_map/all_to_all | solution.py:15
  18.2 0.0 copy-start
  18.2 0.0 copy-start.2
  18.2 1.6 %collective-permute-start = (bf16[256,128]{1,0:T(8,128)(2,1)S(1)}, bf16[256,128]{1,0:T(8,128)(2,1)S(1)}, u32[]{:S(2)}, u32[]{:S(2)}) collective-permute-start(bf16[256,128]{1,0:T(8,128)(2,1)S(1)} %bitcast.63), channel_id=1, source_target_pairs={{0,2},{1,3},{2,0},{3,1},{4,6},{5,7},{6,4},{7,5},{8,10},{9,11},{10,... | collective-permute-start | bytes 196616 | tf_op jit(solution)/shard_map/ppermute | solution.py:43
  19.8 0.0 copy-done
  19.8 0.0 copy-done.2
  19.8 0.1 broadcast_multiply_fusion.1
  19.9 2.6 %collective-permute-done = bf16[256,128]{1,0:T(8,128)(2,1)S(1)} collective-permute-done((bf16[256,128]{1,0:T(8,128)(2,1)S(1)}, bf16[256,128]{1,0:T(8,128)(2,1)S(1)}, u32[]{:S(2)}, u32[]{:S(2)}) %collective-permute-start) | collective-permute-done | bytes 65568 | tf_op jit(solution)/shard_map/ppermute | solution.py:43
  22.6 0.1 collective-permute-start.1
  22.7 0.0 collective-permute-done.3
  22.8 0.6 %gather_fusion = bf16[4,128,256]{2,1,0:T(8,128)(2,1)S(1)} fusion(bf16[4,128,256]{2,1,0:T(8,128)(2,1)S(1)} %pad_maximum_fusion.2, s32[1024]{0:T(1024)S(1)} %pad_clamp_fusion), kind=kCustom, calls=%fused_computation | custom fusion | bytes 524304 | tf_op jit(solution)/shard_map/jit(_take)/gather | solution.py:75
  23.4 0.1 broadcast_select_fusion
  23.5 0.1 rev.12
  23.6 0.1 fusion.34
  23.7 0.3 collective-permute-done.1
  24.0 0.2 fusion.1
  24.2 0.2 fusion.9
  24.4 0.2 fusion.11
  24.6 0.5 multiply_reduce_fusion.1
  25.1 0.2 convolution_convert_fusion
  25.3 11.3 %all_to_all.15 = bf16[8,67,128]{2,1,0:T(8,128)(2,1)S(1)} all-to-all(bf16[8,67,128]{2,1,0:T(8,128)(2,1)S(1)} %broadcast_in_dim.50), channel_id=1, replica_groups=mesh['grid'=8,'band'=4] {'grid'}, dimensions={0} | all-to-all | bytes 274432 | tf_op jit(solution)/shard_map/all_to_all | solution.py:15
  36.9 1.6 %collective-permute-start.4 = (bf16[512,128]{1,0:T(8,128)(2,1)S(1)}, bf16[512,128]{1,0:T(8,128)(2,1)S(1)}, u32[]{:S(2)}, u32[]{:S(2)}) collective-permute-start(bf16[512,128]{1,0:T(8,128)(2,1)S(1)} %pad_maximum_fusion.6), channel_id=1, source_target_pairs={{0,2},{1,3},{2,0},{3,1},{4,6},{5,7},{6,4},{7,5},{8,10},{9,11},{10,... | collective-permute-start | bytes 393224 | tf_op jit(solution)/shard_map/ppermute | solution.py:43
  38.4 3.5 %collective-permute-done.4 = bf16[512,128]{1,0:T(8,128)(2,1)S(1)} collective-permute-done((bf16[512,128]{1,0:T(8,128)(2,1)S(1)}, bf16[512,128]{1,0:T(8,128)(2,1)S(1)}, u32[]{:S(2)}, u32[]{:S(2)}) %collective-permute-start.4) | collective-permute-done | bytes 131104 | tf_op jit(solution)/shard_map/ppermute | solution.py:43
  41.9 0.1 collective-permute-start.5
  42.0 0.2 fusion.13
  42.2 0.2 fusion.21
  42.4 1.1 %collective-permute-done.5 = bf16[1024,128]{1,0:T(8,128)(2,1)S(1)} collective-permute-done((bf16[1024,128]{1,0:T(8,128)(2,1)S(1)}, bf16[1024,128]{1,0:T(8,128)(2,1)S(1)}, u32[]{:S(2)}, u32[]{:S(2)}) %collective-permute-start.5) | collective-permute-done | bytes 262176 | tf_op jit(solution)/shard_map/ppermute | solution.py:43
  43.5 0.2 fusion.23
  43.7 0.5 multiply_reduce_fusion
  44.2 9.2 %all_to_all.16 = f32[8,1,128]{2,1,0:T(1,128)S(1)} all-to-all(f32[8,1,128]{2,1,0:T(1,128)S(1)} %broadcast_in_dim.51), channel_id=1, replica_groups=mesh['grid'=8,'band'=4] {'grid'}, dimensions={0} | all-to-all | bytes 8192 | tf_op jit(solution)/shard_map/all_to_all | solution.py:15
  53.4 0.7 %broadcast_multiply_fusion = f32[256,128]{1,0:T(8,128)} fusion(f32[256,128]{1,0:T(8,128)S(1)} %get-tuple-element.27, f32[128]{0:T(128)S(1)} %add_rsqrt_fusion), kind=kLoop, calls=%fused_computation.80 | loop fusion | flops 32768 | bytes 262656 | tf_op jit(solution)/shard_map/mul | solution.py:120
  (43 shorter events, 0.6 us)
Async XLA Ops:
  0.8 0.9 %copy-start.3 = (s32[64]{0:T(128)S(1)}, s32[64]{0:T(128)}, u32[]{:S(2)}) copy-start(s32[64]{0:T(128)} %param.7) | copy-start | bytes 772
  1.8 0.8 %copy-start.1 = (bf16[128,256]{1,0:T(8,128)(2,1)S(1)}, bf16[128,256]{1,0:T(8,128)(2,1)}, u32[]{:S(2)}) copy-start(bf16[128,256]{1,0:T(8,128)(2,1)} %param.6) | copy-start | bytes 196612
  3.4 14.7 %all-to-all-start = ((bf16[8,65,128]{2,1,0:T(8,128)(2,1)}), bf16[8,65,128]{2,1,0:T(8,128)(2,1)S(1)}, u32[]{:S(2)}, u32[]{:S(2)}) async-start(bf16[8,65,128]{2,1,0:T(8,128)(2,1)} %broadcast_in_dim.27), calls=%async_computation | async-start | bytes 294912 | tf_op jit(solution)/shard_map/all_to_all | solution.py:15
  10.7 5.0 %collective-permute-start.2 = (bf16[512,128]{1,0:T(8,128)(2,1)S(1)}, bf16[512,128]{1,0:T(8,128)(2,1)S(1)}, u32[]{:S(2)}, u32[]{:S(2)}) collective-permute-start(bf16[512,128]{1,0:T(8,128)(2,1)S(1)} %pad_maximum_fusion.4), channel_id=1, source_target_pairs={{0,2},{1,3},{2,0},{3,1},{4,6},{5,7},{6,4},{7,5},{8,10},{9,11},{10,... | collective-permute-start | bytes 393224 | tf_op jit(solution)/shard_map/ppermute | solution.py:43
  15.7 7.0 %collective-permute-start.3 = (bf16[1024,128]{1,0:T(8,128)(2,1)S(1)}, bf16[1024,128]{1,0:T(8,128)(2,1)S(1)}, u32[]{:S(2)}, u32[]{:S(2)}) collective-permute-start(bf16[1024,128]{1,0:T(8,128)(2,1)S(1)} %pad_maximum_fusion.1), channel_id=1, source_target_pairs={{0,1},{1,0},{2,3},{3,2},{4,5},{5,4},{6,7},{7,6},{8,9},{9,8},{10,11... | collective-permute-start | bytes 786440 | tf_op jit(solution)/shard_map/ppermute | solution.py:43
  18.2 1.6 %copy-start = (f32[256,128]{1,0:T(8,128)S(1)}, f32[256,128]{1,0:T(8,128)}, u32[]{:S(2)}) copy-start(f32[256,128]{1,0:T(8,128)} %param.4) | copy-start | bytes 393220
  18.2 1.6 %copy-start.2 = (f32[256]{0:T(256)S(1)}, f32[256]{0:T(256)}, u32[]{:S(2)}) copy-start(f32[256]{0:T(256)} %param.5) | copy-start | bytes 3076
  18.2 4.3 %collective-permute-start = (bf16[256,128]{1,0:T(8,128)(2,1)S(1)}, bf16[256,128]{1,0:T(8,128)(2,1)S(1)}, u32[]{:S(2)}, u32[]{:S(2)}) collective-permute-start(bf16[256,128]{1,0:T(8,128)(2,1)S(1)} %bitcast.63), channel_id=1, source_target_pairs={{0,2},{1,3},{2,0},{3,1},{4,6},{5,7},{6,4},{7,5},{8,10},{9,11},{10,... | collective-permute-start | bytes 196616 | tf_op jit(solution)/shard_map/ppermute | solution.py:43
  22.6 1.4 %collective-permute-start.1 = (bf16[512,128]{1,0:T(8,128)(2,1)S(1)}, bf16[512,128]{1,0:T(8,128)(2,1)S(1)}, u32[]{:S(2)}, u32[]{:S(2)}) collective-permute-start(bf16[512,128]{1,0:T(8,128)(2,1)S(1)} %pad_maximum_fusion.5), channel_id=1, source_target_pairs={{0,1},{1,0},{2,3},{3,2},{4,5},{5,4},{6,7},{7,6},{8,9},{9,8},{10,11... | collective-permute-start | bytes 393224 | tf_op jit(solution)/shard_map/ppermute | solution.py:43
  36.9 5.0 %collective-permute-start.4 = (bf16[512,128]{1,0:T(8,128)(2,1)S(1)}, bf16[512,128]{1,0:T(8,128)(2,1)S(1)}, u32[]{:S(2)}, u32[]{:S(2)}) collective-permute-start(bf16[512,128]{1,0:T(8,128)(2,1)S(1)} %pad_maximum_fusion.6), channel_id=1, source_target_pairs={{0,2},{1,3},{2,0},{3,1},{4,6},{5,7},{6,4},{7,5},{8,10},{9,11},{10,... | collective-permute-start | bytes 393224 | tf_op jit(solution)/shard_map/ppermute | solution.py:43
  41.9 1.6 %collective-permute-start.5 = (bf16[1024,128]{1,0:T(8,128)(2,1)S(1)}, bf16[1024,128]{1,0:T(8,128)(2,1)S(1)}, u32[]{:S(2)}, u32[]{:S(2)}) collective-permute-start(bf16[1024,128]{1,0:T(8,128)(2,1)S(1)} %pad_maximum_fusion.3), channel_id=1, source_target_pairs={{0,1},{1,0},{2,3},{3,2},{4,5},{5,4},{6,7},{7,6},{8,9},{9,8},{10,11... | collective-permute-start | bytes 786440 | tf_op jit(solution)/shard_map/ppermute | solution.py:43

commit v22 on v19

--- a/solution.py
+++ b/solution.py
@@ -67,7 +67,7 @@
     got = grid_exchange(sent).reshape(ngroups, nslots + 1, block_width)
     pot = potential[:, None]
     got, orbitals_later = lax.optimization_barrier((got, orbitals))
-    swapped = band_hops(to_band)
+    swapped = band_swap(to_band)
     rows_b = jnp.concatenate([part[:rows] for part in swapped], 1)
     fitted_got = jnp.stack([part[rows:].reshape(fitted.shape) for part in swapped], 0)
     fitted_all = jnp.take(fitted_got, jnp.arange(nbands, dtype=jnp.int32) ^ band, axis=0)

time: 54.3 us -> 55.1 us (1.015)
  waiting for transfers between devices: 13.2 us -> 15 us
  blocking collectives: 20.6 us -> 19.4 us
    all_to_all x1, waiting for transfers between devices: 2.34 us -> 6.43 us  [grid_exchange(): got = lax.all_to_all(sent, 'grid', 0, 0, tiled=True)]
    ppermute x0 -> x3, starting transfers between devices: none -> 3.06 us  [band_swap(): got.append(lax.ppermute(x, 'band', [(i, i ^ k) for i in range(nbands)]))]
    ppermute x6 -> x4, waiting for transfers between devices: 10.9 us -> 8.57 us  [band_hops(): lax.ppermute(jnp.concatenate([held[k] for k in keys], 0), 'band', [(i, i...]
    ppermute x6 -> x4, starting transfers between devices: 4.81 us -> 3.15 us  [band_hops(): lax.ppermute(jnp.concatenate([held[k] for k in keys], 0), 'band', [(i, i...]
    all_to_all x1, starting transfers between devices: 7.28 us -> 6.09 us  [grid_exchange(): got = lax.all_to_all(sent, 'grid', 0, 0, tiled=True)]
    all_to_all x2, blocking collectives: 20.6 us -> 19.4 us  [grid_exchange(): got = lax.all_to_all(sent, 'grid', 0, 0, tiled=True)]
  transfers between devices with their start and end apart: 7 -> 8, of which waited for: 6 -> 5; matrix products, arithmetic and copies ran while one was open for 3% -> 3% of each run, Pallas kernels for 0% -> 0%
where the time goes in v22:
time: 55.1 us; the launch traced here: 54.8 us
  blocking collectives  19.4 us (35%)
  waiting for transfers between devices  15 us (27%)
  starting transfers between devices  12.3 us (22%)
  other arithmetic  2.87 us (5%)
  matrix products  2.42 us (4%)
  local copies, waits for them, and re-layouts  2.33 us (4%)
    all_to_all x2, blocking collectives, grid_exchange(): got = lax.all_to_all(sent, 'grid', 0, 0, tiled=True)  19.4 us
    ppermute x4, waiting for transfers between devices, band_hops(): lax.ppermute(jnp.concatenate([held[k] for k in keys], 0), 'band', [(i, i...  8.57 us
    all_to_all x1, waiting for transfers between devices, grid_exchange(): got = lax.all_to_all(sent, 'grid', 0, 0, tiled=True)  6.43 us
    all_to_all x1, starting transfers between devices, grid_exchange(): got = lax.all_to_all(sent, 'grid', 0, 0, tiled=True)  6.09 us
    ppermute x4, starting transfers between devices, band_hops(): lax.ppermute(jnp.concatenate([held[k] for k in keys], 0), 'band', [(i, i...  3.15 us
    ppermute x3, starting transfers between devices, band_swap(): got.append(lax.ppermute(x, 'band', [(i, i ^ k) for i in range(nbands)]))  3.06 us
    dot_general x6, matrix products, body(): lax.dot_general(coll[:, k * block_width:(k + 1) * block_width], rows_b[:,...  1.11 us
  transfers between devices with their start and end apart: 8, of which 5 were waited for; matrix products, arithmetic and copies ran while one was open for 3% of the time, Pallas kernels for 0%

profile of v22, /device:TPU:0, one launch (start us, length us, event | category | flops | bytes accessed | tf_op | source)
XLA Modules:
  0.0 54.8 jit_solution(5865023173551044221)
XLA Ops:
  0.0 0.7 %broadcast_compare_fusion = pred[64]{0:T(512)(128)(4,1)S(1)} fusion(s32[64]{0:T(128)} %param.7), kind=kLoop, calls=%fused_computation.110 | loop fusion | flops 64 | bytes 320 | tf_op jit(solution)/shard_map/ge | solution.py:60
  0.7 0.0 copy-start.3
  0.7 0.9 %convert_element_type.86 = bf16[256,128]{1,0:T(8,128)(2,1)S(1)} convert(f32[256,128]{1,0:T(8,128)} %param.4) | non-fusion elementwise | flops 32768 | bytes 196608 | tf_op jit(solution)/shard_map/convert_element_type | solution.py:62
  1.6 0.0 copy-done.3
  1.6 0.0 copy-start.1
  1.6 0.2 convolution_convert_fusion.1
  1.8 0.6 %copy-done.1 = bf16[128,256]{1,0:T(8,128)(2,1)S(1)} copy-done((bf16[128,256]{1,0:T(8,128)(2,1)S(1)}, bf16[128,256]{1,0:T(8,128)(2,1)}, u32[]{:S(2)}) %copy-start.1) | copy-done | bytes 65560
  2.5 0.7 %broadcast_in_dim.50 = bf16[8,65,128]{2,1,0:T(8,128)(2,1)} broadcast(bf16[65,128]{1,0:T(8,128)(2,1)S(1)} %pad_maximum_fusion.6), dimensions={1,2} | broadcast | bytes 149760 | tf_op jit(solution)/shard_map/broadcast_in_dim | solution.py:11
  3.2 2.4 %collective-permute-start.4 = (bf16[512,128]{1,0:T(8,128)(2,1)S(1)}, bf16[512,128]{1,0:T(8,128)(2,1)S(1)}, u32[]{:S(2)}, u32[]{:S(2)}) collective-permute-start(bf16[512,128]{1,0:T(8,128)(2,1)S(1)} %pad_maximum_fusion.3), channel_id=1, source_target_pairs={{0,3},{1,2},{2,1},{3,0},{4,7},{5,6},{6,5},{7,4},{8,11},{9,10},{10,... | collective-permute-start | bytes 393224 | tf_op jit(solution)/shard_map/ppermute | solution.py:27
  5.6 0.6 %collective-permute-start.3 = (bf16[512,128]{1,0:T(8,128)(2,1)S(1)}, bf16[512,128]{1,0:T(8,128)(2,1)S(1)}, u32[]{:S(2)}, u32[]{:S(2)}) collective-permute-start(bf16[512,128]{1,0:T(8,128)(2,1)S(1)} %pad_maximum_fusion.3), channel_id=1, source_target_pairs={{0,2},{1,3},{2,0},{3,1},{4,6},{5,7},{6,4},{7,5},{8,10},{9,11},{10,... | collective-permute-start | bytes 393224 | tf_op jit(solution)/shard_map/ppermute | solution.py:27
  6.2 0.1 collective-permute-start.2
  6.2 6.1 %all-to-all-start = ((bf16[8,65,128]{2,1,0:T(8,128)(2,1)}), bf16[8,65,128]{2,1,0:T(8,128)(2,1)S(1)}, u32[]{:S(2)}, u32[]{:S(2)}) async-start(bf16[8,65,128]{2,1,0:T(8,128)(2,1)} %broadcast_in_dim.50), calls=%async_computation | async-start | bytes 294912 | tf_op jit(solution)/shard_map/all_to_all | solution.py:15
  12.4 0.0 collective-permute-done.4
  12.5 0.0 collective-permute-done.3
  12.5 0.0 collective-permute-done.2
  12.6 0.6 %gather_fusion = bf16[4,128,256]{2,1,0:T(8,128)(2,1)S(1)} fusion(bf16[4,128,256]{2,1,0:T(8,128)(2,1)S(1)} %pad_maximum_fusion.1, s32[1024]{0:T(1024)S(1)} %pad_clamp_fusion), kind=kCustom, calls=%fused_computation | custom fusion | bytes 524304 | tf_op jit(solution)/shard_map/jit(_take)/gather | solution.py:73
  13.2 0.1 broadcast_select_fusion
  13.3 0.1 rev.12
  13.5 6.4 %all-to-all-done = bf16[8,65,128]{2,1,0:T(8,128)(2,1)S(1)} async-done(((bf16[8,65,128]{2,1,0:T(8,128)(2,1)}), bf16[8,65,128]{2,1,0:T(8,128)(2,1)S(1)}, u32[]{:S(2)}, u32[]{:S(2)}) %all-to-all-start) | async-done | bytes 133152 | tf_op jit(solution)/shard_map/all_to_all | solution.py:15
  20.0 1.5 %collective-permute-start = (bf16[256,128]{1,0:T(8,128)(2,1)S(1)}, bf16[256,128]{1,0:T(8,128)(2,1)S(1)}, u32[]{:S(2)}, u32[]{:S(2)}) collective-permute-start(bf16[256,128]{1,0:T(8,128)(2,1)S(1)} %bitcast.57), channel_id=1, source_target_pairs={{0,2},{1,3},{2,0},{3,1},{4,6},{5,7},{6,4},{7,5},{8,10},{9,11},{10,... | collective-permute-start | bytes 196616 | tf_op jit(solution)/shard_map/ppermute | solution.py:43
  21.5 0.1 fusion.32
  21.6 0.0 copy-start
  21.6 0.0 copy-start.2
  21.6 2.7 %collective-permute-done = bf16[256,128]{1,0:T(8,128)(2,1)S(1)} collective-permute-done((bf16[256,128]{1,0:T(8,128)(2,1)S(1)}, bf16[256,128]{1,0:T(8,128)(2,1)S(1)}, u32[]{:S(2)}, u32[]{:S(2)}) %collective-permute-start) | collective-permute-done | bytes 65568 | tf_op jit(solution)/shard_map/ppermute | solution.py:43
  24.4 0.1 collective-permute-start.1
  24.4 0.0 copy-done
  24.4 0.0 copy-done.2
  24.5 0.1 broadcast_multiply_fusion.1
  24.6 1.2 %collective-permute-done.1 = bf16[512,128]{1,0:T(8,128)(2,1)S(1)} collective-permute-done((bf16[512,128]{1,0:T(8,128)(2,1)S(1)}, bf16[512,128]{1,0:T(8,128)(2,1)S(1)}, u32[]{:S(2)}, u32[]{:S(2)}) %collective-permute-start.1) | collective-permute-done | bytes 131104 | tf_op jit(solution)/shard_map/ppermute | solution.py:43
  25.8 0.2 fusion.1
  26.0 0.2 fusion.11
  26.2 0.2 fusion.9
  26.4 0.5 multiply_reduce_fusion.1
  26.9 0.2 convolution_convert_fusion
  27.1 10.2 %all_to_all.15 = bf16[8,67,128]{2,1,0:T(8,128)(2,1)S(1)} all-to-all(bf16[8,67,128]{2,1,0:T(8,128)(2,1)S(1)} %broadcast_in_dim.54), channel_id=1, replica_groups=mesh['grid'=8,'band'=4] {'grid'}, dimensions={0} | all-to-all | bytes 274432 | tf_op jit(solution)/shard_map/all_to_all | solution.py:15
  37.5 1.5 %collective-permute-start.5 = (bf16[512,128]{1,0:T(8,128)(2,1)S(1)}, bf16[512,128]{1,0:T(8,128)(2,1)S(1)}, u32[]{:S(2)}, u32[]{:S(2)}) collective-permute-start(bf16[512,128]{1,0:T(8,128)(2,1)S(1)} %pad_maximum_fusion.5), channel_id=1, source_target_pairs={{0,2},{1,3},{2,0},{3,1},{4,6},{5,7},{6,4},{7,5},{8,10},{9,11},{10,... | collective-permute-start | bytes 393224 | tf_op jit(solution)/shard_map/ppermute | solution.py:43
  39.0 3.5 %collective-permute-done.5 = bf16[512,128]{1,0:T(8,128)(2,1)S(1)} collective-permute-done((bf16[512,128]{1,0:T(8,128)(2,1)S(1)}, bf16[512,128]{1,0:T(8,128)(2,1)S(1)}, u32[]{:S(2)}, u32[]{:S(2)}) %collective-permute-start.5) | collective-permute-done | bytes 131104 | tf_op jit(solution)/shard_map/ppermute | solution.py:43
  42.6 0.1 collective-permute-start.6
  42.7 0.2 fusion.13
  42.9 0.2 fusion.21
  43.0 1.1 %collective-permute-done.6 = bf16[1024,128]{1,0:T(8,128)(2,1)S(1)} collective-permute-done((bf16[1024,128]{1,0:T(8,128)(2,1)S(1)}, bf16[1024,128]{1,0:T(8,128)(2,1)S(1)}, u32[]{:S(2)}, u32[]{:S(2)}) %collective-permute-start.6) | collective-permute-done | bytes 262176 | tf_op jit(solution)/shard_map/ppermute | solution.py:43
  44.2 0.2 fusion.23
  44.4 0.5 multiply_reduce_fusion
  44.8 9.2 %all_to_all.16 = f32[8,1,128]{2,1,0:T(1,128)S(1)} all-to-all(f32[8,1,128]{2,1,0:T(1,128)S(1)} %broadcast_in_dim.55), channel_id=1, replica_groups=mesh['grid'=8,'band'=4] {'grid'}, dimensions={0} | all-to-all | bytes 8192 | tf_op jit(solution)/shard_map/all_to_all | solution.py:15
  54.1 0.7 %broadcast_multiply_fusion = f32[256,128]{1,0:T(8,128)} fusion(f32[256,128]{1,0:T(8,128)S(1)} %get-tuple-element.25, f32[128]{0:T(128)S(1)} %add_rsqrt_fusion), kind=kLoop, calls=%fused_computation.76 | loop fusion | flops 32768 | bytes 262656 | tf_op jit(solution)/shard_map/mul | solution.py:118
  (44 shorter events, 0.6 us)
Async XLA Ops:
  0.7 0.9 %copy-start.3 = (s32[64]{0:T(128)S(1)}, s32[64]{0:T(128)}, u32[]{:S(2)}) copy-start(s32[64]{0:T(128)} %param.7) | copy-start | bytes 772
  1.6 0.8 %copy-start.1 = (bf16[128,256]{1,0:T(8,128)(2,1)S(1)}, bf16[128,256]{1,0:T(8,128)(2,1)}, u32[]{:S(2)}) copy-start(bf16[128,256]{1,0:T(8,128)(2,1)} %param.6) | copy-start | bytes 196612
  3.2 9.2 %collective-permute-start.4 = (bf16[512,128]{1,0:T(8,128)(2,1)S(1)}, bf16[512,128]{1,0:T(8,128)(2,1)S(1)}, u32[]{:S(2)}, u32[]{:S(2)}) collective-permute-start(bf16[512,128]{1,0:T(8,128)(2,1)S(1)} %pad_maximum_fusion.3), channel_id=1, source_target_pairs={{0,3},{1,2},{2,1},{3,0},{4,7},{5,6},{6,5},{7,4},{8,11},{9,10},{10,... | collective-permute-start | bytes 393224 | tf_op jit(solution)/shard_map/ppermute | solution.py:27
  5.6 6.9 %collective-permute-start.3 = (bf16[512,128]{1,0:T(8,128)(2,1)S(1)}, bf16[512,128]{1,0:T(8,128)(2,1)S(1)}, u32[]{:S(2)}, u32[]{:S(2)}) collective-permute-start(bf16[512,128]{1,0:T(8,128)(2,1)S(1)} %pad_maximum_fusion.3), channel_id=1, source_target_pairs={{0,2},{1,3},{2,0},{3,1},{4,6},{5,7},{6,4},{7,5},{8,10},{9,11},{10,... | collective-permute-start | bytes 393224 | tf_op jit(solution)/shard_map/ppermute | solution.py:27
  6.2 6.4 %collective-permute-start.2 = (bf16[512,128]{1,0:T(8,128)(2,1)S(1)}, bf16[512,128]{1,0:T(8,128)(2,1)S(1)}, u32[]{:S(2)}, u32[]{:S(2)}) collective-permute-start(bf16[512,128]{1,0:T(8,128)(2,1)S(1)} %pad_maximum_fusion.3), channel_id=1, source_target_pairs={{0,1},{1,0},{2,3},{3,2},{4,5},{5,4},{6,7},{7,6},{8,9},{9,8},{10,11... | collective-permute-start | bytes 393224 | tf_op jit(solution)/shard_map/ppermute | solution.py:27
  6.2 13.6 %all-to-all-start = ((bf16[8,65,128]{2,1,0:T(8,128)(2,1)}), bf16[8,65,128]{2,1,0:T(8,128)(2,1)S(1)}, u32[]{:S(2)}, u32[]{:S(2)}) async-start(bf16[8,65,128]{2,1,0:T(8,128)(2,1)} %broadcast_in_dim.50), calls=%async_computation | async-start | bytes 294912 | tf_op jit(solution)/shard_map/all_to_all | solution.py:15
  20.0 4.3 %collective-permute-start = (bf16[256,128]{1,0:T(8,128)(2,1)S(1)}, bf16[256,128]{1,0:T(8,128)(2,1)S(1)}, u32[]{:S(2)}, u32[]{:S(2)}) collective-permute-start(bf16[256,128]{1,0:T(8,128)(2,1)S(1)} %bitcast.57), channel_id=1, source_target_pairs={{0,2},{1,3},{2,0},{3,1},{4,6},{5,7},{6,4},{7,5},{8,10},{9,11},{10,... | collective-permute-start | bytes 196616 | tf_op jit(solution)/shard_map/ppermute | solution.py:43
  21.6 2.8 %copy-start = (f32[256,128]{1,0:T(8,128)S(1)}, f32[256,128]{1,0:T(8,128)}, u32[]{:S(2)}) copy-start(f32[256,128]{1,0:T(8,128)} %param.4) | copy-start | bytes 393220
  21.6 2.8 %copy-start.2 = (f32[256]{0:T(256)S(1)}, f32[256]{0:T(256)}, u32[]{:S(2)}) copy-start(f32[256]{0:T(256)} %param.5) | copy-start | bytes 3076
  24.4 1.4 %collective-permute-start.1 = (bf16[512,128]{1,0:T(8,128)(2,1)S(1)}, bf16[512,128]{1,0:T(8,128)(2,1)S(1)}, u32[]{:S(2)}, u32[]{:S(2)}) collective-permute-start(bf16[512,128]{1,0:T(8,128)(2,1)S(1)} %pad_maximum_fusion.4), channel_id=1, source_target_pairs={{0,1},{1,0},{2,3},{3,2},{4,5},{5,4},{6,7},{7,6},{8,9},{9,8},{10,11... | collective-permute-start | bytes 393224 | tf_op jit(solution)/shard_map/ppermute | solution.py:43
  37.5 5.0 %collective-permute-start.5 = (bf16[512,128]{1,0:T(8,128)(2,1)S(1)}, bf16[512,128]{1,0:T(8,128)(2,1)S(1)}, u32[]{:S(2)}, u32[]{:S(2)}) collective-permute-start(bf16[512,128]{1,0:T(8,128)(2,1)S(1)} %pad_maximum_fusion.5), channel_id=1, source_target_pairs={{0,2},{1,3},{2,0},{3,1},{4,6},{5,7},{6,4},{7,5},{8,10},{9,11},{10,... | collective-permute-start | bytes 393224 | tf_op jit(solution)/shard_map/ppermute | solution.py:43
  42.6 1.6 %collective-permute-start.6 = (bf16[1024,128]{1,0:T(8,128)(2,1)S(1)}, bf16[1024,128]{1,0:T(8,128)(2,1)S(1)}, u32[]{:S(2)}, u32[]{:S(2)}) collective-permute-start(bf16[1024,128]{1,0:T(8,128)(2,1)S(1)} %pad_maximum_fusion.2), channel_id=1, source_target_pairs={{0,1},{1,0},{2,3},{3,2},{4,5},{5,4},{6,7},{7,6},{8,9},{9,8},{10,11... | collective-permute-start | bytes 786440 | tf_op jit(solution)/shard_map/ppermute | solution.py:43

commit v23 on v19

--- a/solution.py
+++ b/solution.py
@@ -70,8 +70,13 @@
     swapped = band_hops(to_band)
     rows_b = jnp.concatenate([part[:rows] for part in swapped], 1)
     fitted_got = jnp.stack([part[rows:].reshape(fitted.shape) for part in swapped], 0)
-    fitted_all = jnp.take(fitted_got, jnp.arange(nbands, dtype=jnp.int32) ^ band, axis=0)
-    fitted_all = fitted_all.reshape(ngroups // 2, 2, nslots, fitted.shape[1])
+    ordered = []
+    for j in range(nbands):
+        pick = fitted_got[nbands - 1]
+        for k in range(nbands - 2, -1, -1):
+            pick = jnp.where(band == (j ^ k), fitted_got[k], pick)
+        ordered.append(pick)
+    fitted_all = jnp.stack(ordered, 0).reshape(ngroups // 2, 2, nslots, fitted.shape[1])
     coll = jnp.concatenate(band_hops(pair_up(got[:, :nslots])), 1)
     coll, first_pot_psi = lax.optimization_barrier((coll, pot * orbitals_later))
     first_filled = got[:, nslots, :nslots].reshape(ngroups // 2, 2, nslots)[:, 0] > 0

time: 54.3 us -> 54 us (level)
  waiting for transfers between devices: 13.2 us -> 17.1 us
  starting transfers between devices: 12.1 us -> 10.2 us
  blocking collectives: 20.6 us -> 19.4 us
  other arithmetic: 2.89 us -> 2.18 us
    all_to_all x1, waiting for transfers between devices: 2.34 us -> 7.34 us  [grid_exchange(): got = lax.all_to_all(sent, 'grid', 0, 0, tiled=True)]
    all_to_all x1, starting transfers between devices: 7.28 us -> 5.83 us  [grid_exchange(): got = lax.all_to_all(sent, 'grid', 0, 0, tiled=True)]
    ppermute x6, waiting for transfers between devices: 10.9 us -> 9.71 us  [band_hops(): lax.ppermute(jnp.concatenate([held[k] for k in keys], 0), 'band', [(i, i...]
    all_to_all x2, blocking collectives: 20.6 us -> 19.4 us  [grid_exchange(): got = lax.all_to_all(sent, 'grid', 0, 0, tiled=True)]
    ge x1, other arithmetic: 0.66 us -> 0.01 us  [body(): valid_mask = points >= 0]
    gather x1 -> x0, local copies, waits for them, and re-layouts: 0.56 us -> none  [body(): jnp.take(fitted_got, jnp.arange(nbands, dtype=jnp.int32) ^ band, axis=0)]
  transfers between devices with their start and end apart: 7 -> 7, of which waited for: 6 -> 5; matrix products, arithmetic and copies ran while one was open for 3% -> 2% of each run, Pallas kernels for 0% -> 0%
where the time goes in v23:
time: 54 us; the launch traced here: 53.7 us
  blocking collectives  19.4 us (36%)
  waiting for transfers between devices  17.1 us (32%)
  starting transfers between devices  10.2 us (19%)
  matrix products  2.42 us (4%)
  other arithmetic  2.18 us (4%)
  local copies, waits for them, and re-layouts  1.99 us (4%)
    all_to_all x2, blocking collectives, grid_exchange(): got = lax.all_to_all(sent, 'grid', 0, 0, tiled=True)  19.4 us
    ppermute x6, waiting for transfers between devices, band_hops(): lax.ppermute(jnp.concatenate([held[k] for k in keys], 0), 'band', [(i, i...  9.71 us
    all_to_all x1, waiting for transfers between devices, grid_exchange(): got = lax.all_to_all(sent, 'grid', 0, 0, tiled=True)  7.34 us
    all_to_all x1, starting transfers between devices, grid_exchange(): got = lax.all_to_all(sent, 'grid', 0, 0, tiled=True)  5.83 us
    ppermute x6, starting transfers between devices, band_hops(): lax.ppermute(jnp.concatenate([held[k] for k in keys], 0), 'band', [(i, i...  4.35 us
    dot_general x6, matrix products, body(): lax.dot_general(coll[:, k * block_width:(k + 1) * block_width], rows_b[:,...  1.12 us
  transfers between devices with their start and end apart: 7, of which 5 were waited for; matrix products, arithmetic and copies ran while one was open for 2% of the time, Pallas kernels for 0%

profile of v23, /device:TPU:0, one launch (start us, length us, event | category | flops | bytes accessed | tf_op | source)
XLA Modules:
  0.0 53.7 jit_solution(6885919632119356243)
XLA Ops:
  0.0 0.0 copy-start.1
  0.0 0.9 %convert_element_type.86 = bf16[256,128]{1,0:T(8,128)(2,1)S(1)} convert(f32[256,128]{1,0:T(8,128)} %param.4) | non-fusion elementwise | flops 32768 | bytes 196608 | tf_op jit(solution)/shard_map/convert_element_type | solution.py:62
  0.9 0.0 copy-done.1
  1.0 0.0 copy-start.3
  1.0 0.6 %copy-done.3 = s32[64]{0:T(128)S(1)} copy-done((s32[64]{0:T(128)S(1)}, s32[64]{0:T(128)}, u32[]{:S(2)}) %copy-start.3) | copy-done | bytes 280
  1.6 0.2 convolution_convert_fusion.1
  1.9 0.7 %broadcast_in_dim.21 = bf16[8,65,128]{2,1,0:T(8,128)(2,1)} broadcast(bf16[65,128]{1,0:T(8,128)(2,1)S(1)} %pad_maximum_fusion.7), dimensions={1,2} | broadcast | bytes 149760 | tf_op jit(solution)/shard_map/broadcast_in_dim | solution.py:11
  2.5 2.9 %collective-permute-start.2 = (bf16[512,128]{1,0:T(8,128)(2,1)S(1)}, bf16[512,128]{1,0:T(8,128)(2,1)S(1)}, u32[]{:S(2)}, u32[]{:S(2)}) collective-permute-start(bf16[512,128]{1,0:T(8,128)(2,1)S(1)} %pad_maximum_fusion.4), channel_id=1, source_target_pairs={{0,2},{1,3},{2,0},{3,1},{4,6},{5,7},{6,4},{7,5},{8,10},{9,11},{10,... | collective-permute-start | bytes 393224 | tf_op jit(solution)/shard_map/ppermute | solution.py:43
  5.5 5.8 %all-to-all-start = ((bf16[8,65,128]{2,1,0:T(8,128)(2,1)}), bf16[8,65,128]{2,1,0:T(8,128)(2,1)S(1)}, u32[]{:S(2)}, u32[]{:S(2)}) async-start(bf16[8,65,128]{2,1,0:T(8,128)(2,1)} %broadcast_in_dim.21), calls=%async_computation | async-start | bytes 294912 | tf_op jit(solution)/shard_map/all_to_all | solution.py:15
  11.3 0.0 collective-permute-done.2
  11.3 0.1 collective-permute-start.3
  11.4 7.3 %all-to-all-done = bf16[8,65,128]{2,1,0:T(8,128)(2,1)S(1)} async-done(((bf16[8,65,128]{2,1,0:T(8,128)(2,1)}), bf16[8,65,128]{2,1,0:T(8,128)(2,1)S(1)}, u32[]{:S(2)}, u32[]{:S(2)}) %all-to-all-start) | async-done | bytes 133152 | tf_op jit(solution)/shard_map/all_to_all | solution.py:15
  18.8 0.0 copy-start
  18.9 0.0 copy-start.2
  18.9 0.6 %collective-permute-start = (bf16[256,128]{1,0:T(8,128)(2,1)S(1)}, bf16[256,128]{1,0:T(8,128)(2,1)S(1)}, u32[]{:S(2)}, u32[]{:S(2)}) collective-permute-start(bf16[256,128]{1,0:T(8,128)(2,1)S(1)} %bitcast.55), channel_id=1, source_target_pairs={{0,2},{1,3},{2,0},{3,1},{4,6},{5,7},{6,4},{7,5},{8,10},{9,11},{10,... | collective-permute-start | bytes 196616 | tf_op jit(solution)/shard_map/ppermute | solution.py:43
  19.5 0.3 copy-done
  19.7 0.0 copy-done.2
  19.7 0.1 broadcast_multiply_fusion.1
  19.9 3.3 %collective-permute-done = bf16[256,128]{1,0:T(8,128)(2,1)S(1)} collective-permute-done((bf16[256,128]{1,0:T(8,128)(2,1)S(1)}, bf16[256,128]{1,0:T(8,128)(2,1)S(1)}, u32[]{:S(2)}, u32[]{:S(2)}) %collective-permute-start) | collective-permute-done | bytes 65568 | tf_op jit(solution)/shard_map/ppermute | solution.py:43
  23.2 0.1 collective-permute-start.1
  23.3 0.0 collective-permute-done.3
  23.6 0.1 rev.12
  23.7 0.1 fusion.32
  23.8 0.8 %collective-permute-done.1 = bf16[512,128]{1,0:T(8,128)(2,1)S(1)} collective-permute-done((bf16[512,128]{1,0:T(8,128)(2,1)S(1)}, bf16[512,128]{1,0:T(8,128)(2,1)S(1)}, u32[]{:S(2)}, u32[]{:S(2)}) %collective-permute-start.1) | collective-permute-done | bytes 131104 | tf_op jit(solution)/shard_map/ppermute | solution.py:43
  24.7 0.2 fusion.1
  24.9 0.2 fusion.11
  25.1 0.2 fusion.9
  25.3 0.5 multiply_reduce_fusion.1
  25.7 0.2 convolution_convert_fusion
  26.0 10.2 %all_to_all.15 = bf16[8,67,128]{2,1,0:T(8,128)(2,1)S(1)} all-to-all(bf16[8,67,128]{2,1,0:T(8,128)(2,1)S(1)} %broadcast_in_dim.23), channel_id=1, replica_groups=mesh['grid'=8,'band'=4] {'grid'}, dimensions={0} | all-to-all | bytes 274432 | tf_op jit(solution)/shard_map/all_to_all | solution.py:15
  36.4 0.6 %collective-permute-start.4 = (bf16[512,128]{1,0:T(8,128)(2,1)S(1)}, bf16[512,128]{1,0:T(8,128)(2,1)S(1)}, u32[]{:S(2)}, u32[]{:S(2)}) collective-permute-start(bf16[512,128]{1,0:T(8,128)(2,1)S(1)} %pad_maximum_fusion.6), channel_id=1, source_target_pairs={{0,2},{1,3},{2,0},{3,1},{4,6},{5,7},{6,4},{7,5},{8,10},{9,11},{10,... | collective-permute-start | bytes 393224 | tf_op jit(solution)/shard_map/ppermute | solution.py:43
  37.0 4.4 %collective-permute-done.4 = bf16[512,128]{1,0:T(8,128)(2,1)S(1)} collective-permute-done((bf16[512,128]{1,0:T(8,128)(2,1)S(1)}, bf16[512,128]{1,0:T(8,128)(2,1)S(1)}, u32[]{:S(2)}, u32[]{:S(2)}) %collective-permute-start.4) | collective-permute-done | bytes 131104 | tf_op jit(solution)/shard_map/ppermute | solution.py:43
  41.5 0.1 collective-permute-start.5
  41.5 0.2 fusion.13
  41.7 0.2 fusion.21
  41.9 1.1 %collective-permute-done.5 = bf16[1024,128]{1,0:T(8,128)(2,1)S(1)} collective-permute-done((bf16[1024,128]{1,0:T(8,128)(2,1)S(1)}, bf16[1024,128]{1,0:T(8,128)(2,1)S(1)}, u32[]{:S(2)}, u32[]{:S(2)}) %collective-permute-start.5) | collective-permute-done | bytes 262176 | tf_op jit(solution)/shard_map/ppermute | solution.py:43
  43.1 0.2 fusion.23
  43.3 0.5 multiply_reduce_fusion
  43.7 9.2 %all_to_all.16 = f32[8,1,128]{2,1,0:T(1,128)S(1)} all-to-all(f32[8,1,128]{2,1,0:T(1,128)S(1)} %broadcast_in_dim.24), channel_id=1, replica_groups=mesh['grid'=8,'band'=4] {'grid'}, dimensions={0} | all-to-all | bytes 8192 | tf_op jit(solution)/shard_map/all_to_all | solution.py:15
  53.0 0.7 %broadcast_multiply_fusion = f32[256,128]{1,0:T(8,128)} fusion(f32[256,128]{1,0:T(8,128)S(1)} %get-tuple-element.28, f32[128]{0:T(128)S(1)} %add_rsqrt_fusion), kind=kLoop, calls=%fused_computation.75 | loop fusion | flops 32768 | bytes 262656 | tf_op jit(solution)/shard_map/mul | solution.py:123
  (41 shorter events, 0.7 us)
Async XLA Ops:
  0.0 0.9 %copy-start.1 = (bf16[128,256]{1,0:T(8,128)(2,1)S(1)}, bf16[128,256]{1,0:T(8,128)(2,1)}, u32[]{:S(2)}) copy-start(bf16[128,256]{1,0:T(8,128)(2,1)} %param.6) | copy-start | bytes 196612
  1.0 0.7 %copy-start.3 = (s32[64]{0:T(128)S(1)}, s32[64]{0:T(128)}, u32[]{:S(2)}) copy-start(s32[64]{0:T(128)} %param.7) | copy-start | bytes 772
  2.5 8.8 %collective-permute-start.2 = (bf16[512,128]{1,0:T(8,128)(2,1)S(1)}, bf16[512,128]{1,0:T(8,128)(2,1)S(1)}, u32[]{:S(2)}, u32[]{:S(2)}) collective-permute-start(bf16[512,128]{1,0:T(8,128)(2,1)S(1)} %pad_maximum_fusion.4), channel_id=1, source_target_pairs={{0,2},{1,3},{2,0},{3,1},{4,6},{5,7},{6,4},{7,5},{8,10},{9,11},{10,... | collective-permute-start | bytes 393224 | tf_op jit(solution)/shard_map/ppermute | solution.py:43
  5.5 13.3 %all-to-all-start = ((bf16[8,65,128]{2,1,0:T(8,128)(2,1)}), bf16[8,65,128]{2,1,0:T(8,128)(2,1)S(1)}, u32[]{:S(2)}, u32[]{:S(2)}) async-start(bf16[8,65,128]{2,1,0:T(8,128)(2,1)} %broadcast_in_dim.21), calls=%async_computation | async-start | bytes 294912 | tf_op jit(solution)/shard_map/all_to_all | solution.py:15
  11.3 12.0 %collective-permute-start.3 = (bf16[1024,128]{1,0:T(8,128)(2,1)S(1)}, bf16[1024,128]{1,0:T(8,128)(2,1)S(1)}, u32[]{:S(2)}, u32[]{:S(2)}) collective-permute-start(bf16[1024,128]{1,0:T(8,128)(2,1)S(1)} %pad_maximum_fusion.1), channel_id=1, source_target_pairs={{0,1},{1,0},{2,3},{3,2},{4,5},{5,4},{6,7},{7,6},{8,9},{9,8},{10,11... | collective-permute-start | bytes 786440 | tf_op jit(solution)/shard_map/ppermute | solution.py:43
  18.8 0.9 %copy-start = (f32[256,128]{1,0:T(8,128)S(1)}, f32[256,128]{1,0:T(8,128)}, u32[]{:S(2)}) copy-start(f32[256,128]{1,0:T(8,128)} %param.4) | copy-start | bytes 393220
  18.9 0.9 %copy-start.2 = (f32[256]{0:T(256)S(1)}, f32[256]{0:T(256)}, u32[]{:S(2)}) copy-start(f32[256]{0:T(256)} %param.5) | copy-start | bytes 3076
  18.9 4.3 %collective-permute-start = (bf16[256,128]{1,0:T(8,128)(2,1)S(1)}, bf16[256,128]{1,0:T(8,128)(2,1)S(1)}, u32[]{:S(2)}, u32[]{:S(2)}) collective-permute-start(bf16[256,128]{1,0:T(8,128)(2,1)S(1)} %bitcast.55), channel_id=1, source_target_pairs={{0,2},{1,3},{2,0},{3,1},{4,6},{5,7},{6,4},{7,5},{8,10},{9,11},{10,... | collective-permute-start | bytes 196616 | tf_op jit(solution)/shard_map/ppermute | solution.py:43
  23.2 1.4 %collective-permute-start.1 = (bf16[512,128]{1,0:T(8,128)(2,1)S(1)}, bf16[512,128]{1,0:T(8,128)(2,1)S(1)}, u32[]{:S(2)}, u32[]{:S(2)}) collective-permute-start(bf16[512,128]{1,0:T(8,128)(2,1)S(1)} %pad_maximum_fusion.5), channel_id=1, source_target_pairs={{0,1},{1,0},{2,3},{3,2},{4,5},{5,4},{6,7},{7,6},{8,9},{9,8},{10,11... | collective-permute-start | bytes 393224 | tf_op jit(solution)/shard_map/ppermute | solution.py:43
  36.4 5.0 %collective-permute-start.4 = (bf16[512,128]{1,0:T(8,128)(2,1)S(1)}, bf16[512,128]{1,0:T(8,128)(2,1)S(1)}, u32[]{:S(2)}, u32[]{:S(2)}) collective-permute-start(bf16[512,128]{1,0:T(8,128)(2,1)S(1)} %pad_maximum_fusion.6), channel_id=1, source_target_pairs={{0,2},{1,3},{2,0},{3,1},{4,6},{5,7},{6,4},{7,5},{8,10},{9,11},{10,... | collective-permute-start | bytes 393224 | tf_op jit(solution)/shard_map/ppermute | solution.py:43
  41.5 1.6 %collective-permute-start.5 = (bf16[1024,128]{1,0:T(8,128)(2,1)S(1)}, bf16[1024,128]{1,0:T(8,128)(2,1)S(1)}, u32[]{:S(2)}, u32[]{:S(2)}) collective-permute-start(bf16[1024,128]{1,0:T(8,128)(2,1)S(1)} %pad_maximum_fusion.3), channel_id=1, source_target_pairs={{0,1},{1,0},{2,3},{3,2},{4,5},{5,4},{6,7},{7,6},{8,9},{9,8},{10,11... | collective-permute-start | bytes 786440 | tf_op jit(solution)/shard_map/ppermute | solution.py:43
